TPU v7x, 32 devices: a whole 2x2x4 slice. The times are simulated.
32 devices in a mesh: ctx: 8 (over y, x, core), head: 4 (over z).
Axes of the slice: x: 2, y: 2, z: 4, core: 2. Of those that a mesh axis runs over, the one named last changes fastest.
Arguments:
- doc_lengths: int32 [6], replicated, may hold values from 1 to 512, 1024 in all
- lin_q: bfloat16 [1024, 8192], P('ctx', 'head'), may hold values from -6 to 6
- lin_k: bfloat16 [1024, 8192], P('ctx', 'head'), may hold values from -6 to 6
- lin_v: bfloat16 [1024, 8192], P('ctx', 'head'), may hold values from -6 to 6
- log_decay: float32 [64, 1024], P('head', 'ctx'), may hold values from -0.8 to 0
- out_gate: bfloat16 [1024, 8192], P('ctx', 'head'), may hold values from -6 to 6
- lin_gain: float32 [8192], P('head'), may hold values from 0.5 to 1.5
- soft_q: bfloat16 [1024, 8192], P('ctx', 'head'), may hold values from -200 to 200
- soft_k: bfloat16 [1024, 1024], P('ctx', 'head'), may hold values from -7 to 7
- soft_v: bfloat16 [1024, 1024], P('ctx', 'head'), may hold values from -6 to 6
Outputs:
- lin_out: bfloat16 [1024, 8192], P('ctx', 'head')
- soft_out: bfloat16 [1024, 8192], P('ctx', 'head')
Inputs may be any that keep to these rules, and one draw needn't show every extreme that they name: `doc_lengths`: the documents lie end to end and fill all 1024 positions; the longest has exactly 512 positions.
All inputs are finite; a program needn't handle non-finite values.
Results may differ from a plain program's by a relative error of at most 0.0054.
Values may be sent and summed in bfloat16 or wider, within the bound.
No kernel may reach another device: no remote copies, remote signals or barrier semaphores. Data moves between devices by JAX's collectives and lax.ppermute only.
A program may use at most 64 MiB of HBM per device.

v0:
```python
import jax
import jax.numpy as jnp
from jax import lax
from jax.sharding import PartitionSpec as P

DH = 128
SPAN = 4


def from_behind(shard, axis, by):
    count = lax.axis_size(axis)
    pairs = [(i, i + by) for i in range(count) if 0 <= i + by < count]
    return lax.ppermute(shard, axis, pairs)


def document_of(positions, doc_lengths):
    ends = jnp.cumsum(doc_lengths)
    return jnp.sum((ends[None, :] <= positions[:, None]).astype(jnp.int32), axis=1)


def block_terms(query, lookup_array, values, decay, docs, before):
    rows = docs.shape[0]
    level = jnp.cumsum(decay, axis=1)
    order = jnp.arange(rows)
    same = (docs[:, None] == docs[None, :]) & (order[None, :] <= order[:, None])
    scores = jnp.einsum("thd,shd->hts", query, lookup_array, preferred_element_type=jnp.float32)
    fade = jnp.exp(jnp.minimum(level[:, :, None] - level[:, None, :], 0.0))
    weights = jnp.where(same[None], scores * fade, 0.0).astype(jnp.bfloat16)
    inner = jnp.einsum("hts,shd->thd", weights, values, preferred_element_type=jnp.float32)
    carried = docs == before
    closing = (docs == docs[-1]).astype(jnp.float32)
    tail = jnp.exp(level[:, -1:] - level) * closing[None, :]
    weighted = (lookup_array.astype(jnp.float32) * tail.T[:, :, None]).astype(jnp.bfloat16)
    state = jnp.einsum("shd,she->hde", weighted, values, preferred_element_type=jnp.float32)
    shrinkage_multiplier = jnp.exp(level[:, -1]) * carried[-1].astype(jnp.float32)
    return (inner, level, carried, shrinkage_multiplier, state)


def local(doc_lengths, lin_q, lin_k, lin_v, log_decay, out_gate, lin_gain, soft_q, soft_k, soft_v):
    rows = lin_q.shape[0]
    heads_here = lin_q.shape[1] // DH
    kv_here = soft_k.shape[1] // DH
    group = soft_q.shape[1] // (kv_here * DH)
    shard = lax.axis_index("ctx")
    positions = shard * rows + jnp.arange(rows, dtype=jnp.int32)
    docs = document_of(positions, doc_lengths)
    before = jnp.where(shard > 0, document_of(positions[:1] - 1, doc_lengths)[0], -1)
    query = lin_q.reshape(rows, heads_here, DH)
    lookup_array = lin_k.reshape(rows, heads_here, DH)
    values = lin_v.reshape(rows, heads_here, DH)
    inner, level, carried, shrinkage_multiplier, state = block_terms(
        query, lookup_array, values, log_decay, docs, before
    )
    key_blocks = [soft_k]
    value_blocks = [soft_v]
    incoming = jnp.zeros((heads_here, DH, DH), jnp.float32)
    running = jnp.ones((heads_here,), jnp.float32)
    for step in range(1, SPAN + 1):
        far_keys, far_values = from_behind((soft_k, soft_v), "ctx", step)
        key_blocks.append(far_keys)
        value_blocks.append(far_values)
        far_factor, far_state = from_behind((shrinkage_multiplier, state), "ctx", step)
        incoming = incoming + running[:, None, None] * far_state
        running = running * far_factor
    outer = jnp.einsum(
        "thd,hde->the", query, incoming.astype(jnp.bfloat16), preferred_element_type=jnp.float32
    )
    outer = outer * (jnp.exp(level).T * carried[:, None].astype(jnp.float32))[:, :, None]
    mixed = inner + outer
    local_sq = jnp.sum(mixed * mixed, axis=(1, 2))
    total_sq = lax.psum(local_sq, "head")
    mean_sq = total_sq / (lax.axis_size("head") * heads_here * DH)
    flat = mixed.reshape(rows, heads_here * DH)
    normed = (
        flat
        * lax.rsqrt(mean_sq + 1e-06)[:, None]
        * lin_gain[None, :]
        * jax.nn.sigmoid(out_gate.astype(jnp.float32))
    )
    lin_out = normed.astype(jnp.bfloat16)
    span_rows = (SPAN + 1) * rows
    all_keys = jnp.concatenate(key_blocks[::-1], axis=0).reshape(span_rows, kv_here, DH)
    all_values = jnp.concatenate(value_blocks[::-1], axis=0).reshape(span_rows, kv_here, DH)
    key_pos = shard * rows - SPAN * rows + jnp.arange(span_rows, dtype=jnp.int32)
    key_docs = jnp.where(key_pos >= 0, document_of(key_pos, doc_lengths), -1)
    allowed = (key_docs[None, :] == docs[:, None]) & (key_pos[None, :] <= positions[:, None])
    soft_query = soft_q.reshape(rows, kv_here, group, DH)
    scores = jnp.einsum(
        "tkgd,skd->kgts", soft_query, all_keys, preferred_element_type=jnp.float32
    ) * DH ** (-0.5)
    top = jnp.max(jnp.where(allowed, scores, -1e30), axis=-1, keepdims=True)
    expd = jnp.where(allowed, jnp.exp(jnp.minimum(scores - top, 0.0)), 0.0)
    total = jnp.sum(expd, axis=-1)
    attended = jnp.einsum(
        "kgts,skd->tkgd", expd.astype(jnp.bfloat16), all_values, preferred_element_type=jnp.float32
    )
    attended = attended / total.transpose(2, 0, 1)[..., None]
    soft_out = attended.reshape(rows, kv_here * group * DH).astype(jnp.bfloat16)
    return (lin_out, soft_out)


def solution(mesh):
    in_specs = (
        P(),
        P("ctx", "head"),
        P("ctx", "head"),
        P("ctx", "head"),
        P("head", "ctx"),
        P("ctx", "head"),
        P("head"),
        P("ctx", "head"),
        P("ctx", "head"),
        P("ctx", "head"),
    )
    out_specs = (P("ctx", "head"), P("ctx", "head"))
    return jax.shard_map(local, mesh=mesh, in_specs=in_specs, out_specs=out_specs, check_vma=False)
```

profile of v0, /device:TPU:4, one launch (start us, length us, event | category | flops | bytes accessed | tf_op | source)
XLA Modules:
  0.0 174.1 jit_solution(5694177750652210288)
XLA Ops:
  0.7 0.9 reduce-window.4
  1.7 0.7 slice.14
  2.4 0.6 fusion.56
  3.7 0.7 fusion.61
  4.4 0.6 slice.16
  5.6 1.0 reduce_window_sum.20
  6.8 1.9 %collective-permute-start.1 = (f32[16]{0:T(128)S(1)}, f32[16]{0:T(128)S(1)}, u32[]{:S(2)}, u32[]{:S(2)}) collective-permute-start(f32[16]{0:T(128)S(1)} %exponential_multiply_fusion), channel_id=1, source_target_pairs={{0,4},{4,8},{8,12},{12,16},{16,20},{20,24},{24,28},{1,5},{5,9},{9,... | collective-permute-start | bytes 200 | tf_op jit(solution)/shard_map/ppermute | solution.py:13
  8.7 3.4 %collective-permute-start.3 = (f32[16]{0:T(128)S(1)}, f32[16]{0:T(128)S(1)}, u32[]{:S(2)}, u32[]{:S(2)}) collective-permute-start(f32[16]{0:T(128)S(1)} %exponential_multiply_fusion), channel_id=1, source_target_pairs={{0,8},{4,12},{8,16},{12,20},{16,24},{20,28},{1,9},{5,13},{9,17},{1... | collective-permute-start | bytes 200 | tf_op jit(solution)/shard_map/ppermute | solution.py:13
  12.1 1.9 %collective-permute-start.5 = (f32[16]{0:T(128)S(1)}, f32[16]{0:T(128)S(1)}, u32[]{:S(2)}, u32[]{:S(2)}) collective-permute-start(f32[16]{0:T(128)S(1)} %exponential_multiply_fusion), channel_id=1, source_target_pairs={{0,12},{4,16},{8,20},{12,24},{16,28},{1,13},{5,17},{9,21},{13,25},... | collective-permute-start | bytes 200 | tf_op jit(solution)/shard_map/ppermute | solution.py:13
  14.1 1.3 copy.62
  15.5 2.4 %fusion.29 = f32[16,128,128]{2,1,0:T(8,128)} fusion(bf16[128,16,128]{0,2,1:T(8,128)(2,1)S(1)} %bitcast.91, f32[128,16]{0,1:T(8,128)S(1)} %get-tuple-element.13, bf16[128,2048]{1,0:T(8,128)(2,1)} %param.13), kind=kOutput, calls=%fused_computation.31 | convolution fusion | flops 67895296 | bytes 2105344 | tf_op jit(solution)/shard_map/shd,she->hde/dot_general | solution.py:34
  17.9 1.9 %collective-permute-start = (f32[16,128,128]{2,1,0:T(8,128)}, f32[16,128,128]{2,1,0:T(8,128)S(1)}, u32[]{:S(2)}, u32[]{:S(2)}) collective-permute-start(f32[16,128,128]{2,1,0:T(8,128)} %fusion.29), channel_id=1, source_target_pairs={{0,4},{4,8},{8,12},{12,16},{16,20},{20,24},{24,28},{1,5},{5,9},{9,... | collective-permute-start | bytes 3145736 | tf_op jit(solution)/shard_map/ppermute | solution.py:13
  19.8 1.9 %collective-permute-start.2 = (f32[16,128,128]{2,1,0:T(8,128)}, f32[16,128,128]{2,1,0:T(8,128)}, u32[]{:S(2)}, u32[]{:S(2)}) collective-permute-start(f32[16,128,128]{2,1,0:T(8,128)} %fusion.29), channel_id=1, source_target_pairs={{0,8},{4,12},{8,16},{12,20},{16,24},{20,28},{1,9},{5,13},{9,17},{1... | collective-permute-start | bytes 3145736 | tf_op jit(solution)/shard_map/ppermute | solution.py:13
  21.9 0.9 compare_and_fusion
  22.9 1.7 convolution_bitcast_fusion.1
  24.8 1.9 %collective-permute-start.4 = (f32[16,128,128]{2,1,0:T(8,128)}, f32[16,128,128]{2,1,0:T(8,128)S(1)}, u32[]{:S(2)}, u32[]{:S(2)}) collective-permute-start(f32[16,128,128]{2,1,0:T(8,128)} %fusion.29), channel_id=1, source_target_pairs={{0,12},{4,16},{8,20},{12,24},{16,28},{1,13},{5,17},{9,21},{13,25},... | collective-permute-start | bytes 3145736 | tf_op jit(solution)/shard_map/ppermute | solution.py:13
  26.7 1.3 collective-permute-start.6
  28.0 1.3 collective-permute-start.7
  29.3 0.5 fusion.60
  29.8 62.9 %collective-permute-done.7 = bf16[128,256]{1,0:T(8,128)(2,1)S(1)} collective-permute-done((bf16[128,256]{1,0:T(8,128)(2,1)}, bf16[128,256]{1,0:T(8,128)(2,1)S(1)}, u32[]{:S(2)}, u32[]{:S(2)}) %collective-permute-start.7) | collective-permute-done | bytes 65568 | tf_op jit(solution)/shard_map/ppermute | solution.py:13
  92.8 1.9 %collective-permute-start.8 = (bf16[128,256]{1,0:T(8,128)(2,1)}, bf16[128,256]{1,0:T(8,128)(2,1)S(1)}, u32[]{:S(2)}, u32[]{:S(2)}) collective-permute-start(bf16[128,256]{1,0:T(8,128)(2,1)} %param.19), channel_id=1, source_target_pairs={{0,12},{4,16},{8,20},{12,24},{16,28},{1,13},{5,17},{9,21},{13,25},... | collective-permute-start | bytes 196616 | tf_op jit(solution)/shard_map/ppermute | solution.py:13
  94.7 12.0 %collective-permute-done.8 = bf16[128,256]{1,0:T(8,128)(2,1)S(1)} collective-permute-done((bf16[128,256]{1,0:T(8,128)(2,1)}, bf16[128,256]{1,0:T(8,128)(2,1)S(1)}, u32[]{:S(2)}, u32[]{:S(2)}) %collective-permute-start.8) | collective-permute-done | bytes 65568 | tf_op jit(solution)/shard_map/ppermute | solution.py:13
  106.7 1.9 %collective-permute-start.9 = (bf16[128,256]{1,0:T(8,128)(2,1)}, bf16[128,256]{1,0:T(8,128)(2,1)S(1)}, u32[]{:S(2)}, u32[]{:S(2)}) collective-permute-start(bf16[128,256]{1,0:T(8,128)(2,1)} %param.19), channel_id=1, source_target_pairs={{0,8},{4,12},{8,16},{12,20},{16,24},{20,28},{1,9},{5,13},{9,17},{1... | collective-permute-start | bytes 196616 | tf_op jit(solution)/shard_map/ppermute | solution.py:13
  108.6 6.1 %collective-permute-done.9 = bf16[128,256]{1,0:T(8,128)(2,1)S(1)} collective-permute-done((bf16[128,256]{1,0:T(8,128)(2,1)}, bf16[128,256]{1,0:T(8,128)(2,1)S(1)}, u32[]{:S(2)}, u32[]{:S(2)}) %collective-permute-start.9) | collective-permute-done | bytes 65568 | tf_op jit(solution)/shard_map/ppermute | solution.py:13
  114.7 3.7 %collective-permute-start.10 = (bf16[128,256]{1,0:T(8,128)(2,1)}, bf16[128,256]{1,0:T(8,128)(2,1)S(1)}, u32[]{:S(2)}, u32[]{:S(2)}) collective-permute-start(bf16[128,256]{1,0:T(8,128)(2,1)} %param.19), channel_id=1, source_target_pairs={{0,4},{4,8},{8,12},{12,16},{16,20},{20,24},{24,28},{1,5},{5,9},{9,... | collective-permute-start | bytes 196616 | tf_op jit(solution)/shard_map/ppermute | solution.py:13
  118.4 3.0 %collective-permute-done.10 = bf16[128,256]{1,0:T(8,128)(2,1)S(1)} collective-permute-done((bf16[128,256]{1,0:T(8,128)(2,1)}, bf16[128,256]{1,0:T(8,128)(2,1)S(1)}, u32[]{:S(2)}, u32[]{:S(2)}) %collective-permute-start.10) | collective-permute-done | bytes 65568 | tf_op jit(solution)/shard_map/ppermute | solution.py:13
  121.4 1.3 collective-permute-start.11
  122.7 0.8 constant_dynamic-update-slice_fusion
  123.5 0.9 copy.46
  124.4 3.2 %collective-permute-done.11 = bf16[128,256]{0,1:T(8,128)(2,1)} collective-permute-done((bf16[128,256]{0,1:T(8,128)(2,1)S(1)}, bf16[128,256]{0,1:T(8,128)(2,1)}, u32[]{:S(2)}, u32[]{:S(2)}) %collective-permute-start.11) | collective-permute-done | bytes 65568 | tf_op jit(solution)/shard_map/ppermute | solution.py:13
  127.7 1.9 %collective-permute-start.12 = (bf16[128,256]{0,1:T(8,128)(2,1)S(1)}, bf16[128,256]{0,1:T(8,128)(2,1)S(1)}, u32[]{:S(2)}, u32[]{:S(2)}) collective-permute-start(bf16[128,256]{0,1:T(8,128)(2,1)S(1)} %copy.47), channel_id=1, source_target_pairs={{0,12},{4,16},{8,20},{12,24},{16,28},{1,13},{5,17},{9,21},{13,25},... | collective-permute-start | bytes 196616 | tf_op jit(solution)/shard_map/ppermute | solution.py:13
  129.6 1.5 constant_dynamic-update-slice_fusion.9
  131.0 2.2 %collective-permute-done.12 = bf16[128,256]{0,1:T(8,128)(2,1)S(1)} collective-permute-done((bf16[128,256]{0,1:T(8,128)(2,1)S(1)}, bf16[128,256]{0,1:T(8,128)(2,1)S(1)}, u32[]{:S(2)}, u32[]{:S(2)}) %collective-permute-start.12) | collective-permute-done | bytes 65568 | tf_op jit(solution)/shard_map/ppermute | solution.py:13
  133.2 2.7 %collective-permute-start.13 = (bf16[128,256]{0,1:T(8,128)(2,1)S(1)}, bf16[128,256]{0,1:T(8,128)(2,1)S(1)}, u32[]{:S(2)}, u32[]{:S(2)}) collective-permute-start(bf16[128,256]{0,1:T(8,128)(2,1)S(1)} %copy.47), channel_id=1, source_target_pairs={{0,8},{4,12},{8,16},{12,20},{16,24},{20,28},{1,9},{5,13},{9,17},{1... | collective-permute-start | bytes 196616 | tf_op jit(solution)/shard_map/ppermute | solution.py:13
  135.9 0.6 constant_dynamic-update-slice_fusion.8
  136.6 3.7 %collective-permute-done.13 = bf16[128,256]{0,1:T(8,128)(2,1)S(1)} collective-permute-done((bf16[128,256]{0,1:T(8,128)(2,1)S(1)}, bf16[128,256]{0,1:T(8,128)(2,1)S(1)}, u32[]{:S(2)}, u32[]{:S(2)}) %collective-permute-start.13) | collective-permute-done | bytes 65568 | tf_op jit(solution)/shard_map/ppermute | solution.py:13
  140.3 1.9 %collective-permute-start.14 = (bf16[128,256]{0,1:T(8,128)(2,1)S(1)}, bf16[128,256]{0,1:T(8,128)(2,1)S(1)}, u32[]{:S(2)}, u32[]{:S(2)}) collective-permute-start(bf16[128,256]{0,1:T(8,128)(2,1)S(1)} %copy.47), channel_id=1, source_target_pairs={{0,4},{4,8},{8,12},{12,16},{16,20},{20,24},{24,28},{1,5},{5,9},{9,... | collective-permute-start | bytes 196616 | tf_op jit(solution)/shard_map/ppermute | solution.py:13
  142.2 0.6 constant_dynamic-update-slice_fusion.7
  142.8 3.9 %collective-permute-done.14 = bf16[128,256]{0,1:T(8,128)(2,1)S(1)} collective-permute-done((bf16[128,256]{0,1:T(8,128)(2,1)S(1)}, bf16[128,256]{0,1:T(8,128)(2,1)S(1)}, u32[]{:S(2)}, u32[]{:S(2)}) %collective-permute-start.14) | collective-permute-done | bytes 65568 | tf_op jit(solution)/shard_map/ppermute | solution.py:13
  146.7 0.6 constant_dynamic-update-slice_fusion.6
  147.4 0.6 constant_dynamic-update-slice_fusion.5
  148.0 5.4 %fusion.62 = (f32[2,8,128]{2,1,0:T(8,128)S(1)}, bf16[2,8,128,640]{2,3,1,0:T(8,128)(2,1)}) fusion(pred[128,640]{0,1:T(8,128)(4,1)} %compare_and_fusion, bf16[640,2,128,1]{0,2,3,1:T(8,128)(2,1)} %bitcast.22, bf16[128,2,8,128]{3,2,1,0:T(8,128)(2,1)S(1)} %bitcast.94), kind=kOutput, calls=%fused_computation.83 | convolution fusion | flops 681575040 | bytes 3563520 | tf_op jit(solution)/shard_map/sub | solution.py:92
  153.4 2.3 %fusion.20 = bf16[128,2,8,128]{0,3,2,1:T(8,128)(2,1)S(1)} fusion(bf16[640,2,128,1]{0,2,3,1:T(8,128)(2,1)S(1)} %bitcast.96, bf16[2,8,128,640]{2,3,1,0:T(8,128)(2,1)} %get-tuple-element.18, f32[128,2,8]{0,2,1:T(8,128)S(1)} %bitcast.101), kind=kOutput, calls=%fused_computation.21 | convolution fusion | flops 336068608 | bytes 3481600 | tf_op jit(solution)/shard_map/kgts,skd->tkgd/dot_general | solution.py:94
  155.7 1.0 copy.55
  156.8 1.0 copy-done.1
  157.8 2.9 %multiply_reduce_fusion = (f32[128]{0:T(128)S(1)}, f32[128,16,128]{0,2,1:T(8,128)S(1)}) fusion(f32[128,16,128]{0,2,1:T(8,128)} %convolution_bitcast_fusion.1, f32[128,16]{0,1:T(8,128)S(1)} %get-tuple-element.12, f32[16,128,128]{2,1,0:T(8,128)} %collective-permute-done.6, f32[16,128,128]{2,1,0:T(8,128)} %copy-done.1, ...), kind=kOutput, calls=%fused_computation.24 | convolution fusion | flops 69992320 | bytes 6824640 | tf_op jit(solution)/shard_map/thd,hde->the/dot_general | solution.py:65
  161.0 12.0 %psum.7 = f32[128]{0:T(128)S(1)} all-reduce(f32[128]{0:T(128)S(1)} %get-tuple-element.15), channel_id=1, replica_groups=mesh['ctx'=8,'head'=4] {'head'}, use_global_device_ids=true, to_apply=%region_5.6 | all-reduce | flops 128 | bytes 1024 | tf_op jit(solution)/shard_map/psum | solution.py:71
  173.0 1.1 multiply_convert_fusion
  (41 shorter events, 1.2 us)
Async XLA Ops:
  0.6 22.3 %copy-start = (bf16[128,2048]{1,0:T(8,128)(2,1)S(1)}, bf16[128,2048]{1,0:T(8,128)(2,1)}, u32[]{:S(2)}) copy-start(bf16[128,2048]{1,0:T(8,128)(2,1)} %param.11) | copy-start | bytes 1572868
  0.6 22.3 %copy-start.4 = (bf16[128,2048]{1,0:T(8,128)(2,1)S(1)}, bf16[128,2048]{1,0:T(8,128)(2,1)}, u32[]{:S(2)}) copy-start(bf16[128,2048]{1,0:T(8,128)(2,1)} %param.13) | copy-start | bytes 1572868
  0.7 22.1 %copy-start.6 = (bf16[128,256]{1,0:T(8,128)(2,1)S(1)}, bf16[128,256]{1,0:T(8,128)(2,1)}, u32[]{:S(2)}) copy-start(bf16[128,256]{1,0:T(8,128)(2,1)} %param.18) | copy-start | bytes 196612
  6.8 18.0 %collective-permute-start.1 = (f32[16]{0:T(128)S(1)}, f32[16]{0:T(128)S(1)}, u32[]{:S(2)}, u32[]{:S(2)}) collective-permute-start(f32[16]{0:T(128)S(1)} %exponential_multiply_fusion), channel_id=1, source_target_pairs={{0,4},{4,8},{8,12},{12,16},{16,20},{20,24},{24,28},{1,5},{5,9},{9,... | collective-permute-start | bytes 200 | tf_op jit(solution)/shard_map/ppermute | solution.py:13
  8.7 18.0 %collective-permute-start.3 = (f32[16]{0:T(128)S(1)}, f32[16]{0:T(128)S(1)}, u32[]{:S(2)}, u32[]{:S(2)}) collective-permute-start(f32[16]{0:T(128)S(1)} %exponential_multiply_fusion), channel_id=1, source_target_pairs={{0,8},{4,12},{8,16},{12,20},{16,24},{20,28},{1,9},{5,13},{9,17},{1... | collective-permute-start | bytes 200 | tf_op jit(solution)/shard_map/ppermute | solution.py:13
  12.1 15.9 %collective-permute-start.5 = (f32[16]{0:T(128)S(1)}, f32[16]{0:T(128)S(1)}, u32[]{:S(2)}, u32[]{:S(2)}) collective-permute-start(f32[16]{0:T(128)S(1)} %exponential_multiply_fusion), channel_id=1, source_target_pairs={{0,12},{4,16},{8,20},{12,24},{16,28},{1,13},{5,17},{9,21},{13,25},... | collective-permute-start | bytes 200 | tf_op jit(solution)/shard_map/ppermute | solution.py:13
  15.4 9.2 %copy-start.3 = (bf16[128,2048]{1,0:T(8,128)(2,1)S(1)}, bf16[128,2048]{1,0:T(8,128)(2,1)}, u32[]{:S(2)}) copy-start(bf16[128,2048]{1,0:T(8,128)(2,1)} %param.17) | copy-start | bytes 1572868
  17.9 138.9 %collective-permute-start = (f32[16,128,128]{2,1,0:T(8,128)}, f32[16,128,128]{2,1,0:T(8,128)S(1)}, u32[]{:S(2)}, u32[]{:S(2)}) collective-permute-start(f32[16,128,128]{2,1,0:T(8,128)} %fusion.29), channel_id=1, source_target_pairs={{0,4},{4,8},{8,12},{12,16},{16,20},{20,24},{24,28},{1,5},{5,9},{9,... | collective-permute-start | bytes 3145736 | tf_op jit(solution)/shard_map/ppermute | solution.py:13
  19.8 137.0 %collective-permute-start.2 = (f32[16,128,128]{2,1,0:T(8,128)}, f32[16,128,128]{2,1,0:T(8,128)}, u32[]{:S(2)}, u32[]{:S(2)}) collective-permute-start(f32[16,128,128]{2,1,0:T(8,128)} %fusion.29), channel_id=1, source_target_pairs={{0,8},{4,12},{8,16},{12,20},{16,24},{20,28},{1,9},{5,13},{9,17},{1... | collective-permute-start | bytes 3145736 | tf_op jit(solution)/shard_map/ppermute | solution.py:13
  24.8 132.0 %collective-permute-start.4 = (f32[16,128,128]{2,1,0:T(8,128)}, f32[16,128,128]{2,1,0:T(8,128)S(1)}, u32[]{:S(2)}, u32[]{:S(2)}) collective-permute-start(f32[16,128,128]{2,1,0:T(8,128)} %fusion.29), channel_id=1, source_target_pairs={{0,12},{4,16},{8,20},{12,24},{16,28},{1,13},{5,17},{9,21},{13,25},... | collective-permute-start | bytes 3145736 | tf_op jit(solution)/shard_map/ppermute | solution.py:13
  26.7 130.1 %collective-permute-start.6 = (f32[16,128,128]{2,1,0:T(8,128)}, f32[16,128,128]{2,1,0:T(8,128)}, u32[]{:S(2)}, u32[]{:S(2)}) collective-permute-start(f32[16,128,128]{2,1,0:T(8,128)} %fusion.29), channel_id=1, source_target_pairs={{0,16},{4,20},{8,24},{12,28},{1,17},{5,21},{9,25},{13,29},{2,18},{... | collective-permute-start | bytes 3145736 | tf_op jit(solution)/shard_map/ppermute | solution.py:13
  28.0 64.8 %collective-permute-start.7 = (bf16[128,256]{1,0:T(8,128)(2,1)}, bf16[128,256]{1,0:T(8,128)(2,1)S(1)}, u32[]{:S(2)}, u32[]{:S(2)}) collective-permute-start(bf16[128,256]{1,0:T(8,128)(2,1)} %param.19), channel_id=1, source_target_pairs={{0,16},{4,20},{8,24},{12,28},{1,17},{5,21},{9,25},{13,29},{2,18},{... | collective-permute-start | bytes 196616 | tf_op jit(solution)/shard_map/ppermute | solution.py:13
  92.8 13.9 %collective-permute-start.8 = (bf16[128,256]{1,0:T(8,128)(2,1)}, bf16[128,256]{1,0:T(8,128)(2,1)S(1)}, u32[]{:S(2)}, u32[]{:S(2)}) collective-permute-start(bf16[128,256]{1,0:T(8,128)(2,1)} %param.19), channel_id=1, source_target_pairs={{0,12},{4,16},{8,20},{12,24},{16,28},{1,13},{5,17},{9,21},{13,25},... | collective-permute-start | bytes 196616 | tf_op jit(solution)/shard_map/ppermute | solution.py:13
  106.7 8.0 %collective-permute-start.9 = (bf16[128,256]{1,0:T(8,128)(2,1)}, bf16[128,256]{1,0:T(8,128)(2,1)S(1)}, u32[]{:S(2)}, u32[]{:S(2)}) collective-permute-start(bf16[128,256]{1,0:T(8,128)(2,1)} %param.19), channel_id=1, source_target_pairs={{0,8},{4,12},{8,16},{12,20},{16,24},{20,28},{1,9},{5,13},{9,17},{1... | collective-permute-start | bytes 196616 | tf_op jit(solution)/shard_map/ppermute | solution.py:13
  114.7 6.7 %collective-permute-start.10 = (bf16[128,256]{1,0:T(8,128)(2,1)}, bf16[128,256]{1,0:T(8,128)(2,1)S(1)}, u32[]{:S(2)}, u32[]{:S(2)}) collective-permute-start(bf16[128,256]{1,0:T(8,128)(2,1)} %param.19), channel_id=1, source_target_pairs={{0,4},{4,8},{8,12},{12,16},{16,20},{20,24},{24,28},{1,5},{5,9},{9,... | collective-permute-start | bytes 196616 | tf_op jit(solution)/shard_map/ppermute | solution.py:13
  121.4 6.3 %collective-permute-start.11 = (bf16[128,256]{0,1:T(8,128)(2,1)S(1)}, bf16[128,256]{0,1:T(8,128)(2,1)}, u32[]{:S(2)}, u32[]{:S(2)}) collective-permute-start(bf16[128,256]{0,1:T(8,128)(2,1)S(1)} %copy.47), channel_id=1, source_target_pairs={{0,16},{4,20},{8,24},{12,28},{1,17},{5,21},{9,25},{13,29},{2,18},{... | collective-permute-start | bytes 196616 | tf_op jit(solution)/shard_map/ppermute | solution.py:13
  127.7 5.6 %collective-permute-start.12 = (bf16[128,256]{0,1:T(8,128)(2,1)S(1)}, bf16[128,256]{0,1:T(8,128)(2,1)S(1)}, u32[]{:S(2)}, u32[]{:S(2)}) collective-permute-start(bf16[128,256]{0,1:T(8,128)(2,1)S(1)} %copy.47), channel_id=1, source_target_pairs={{0,12},{4,16},{8,20},{12,24},{16,28},{1,13},{5,17},{9,21},{13,25},... | collective-permute-start | bytes 196616 | tf_op jit(solution)/shard_map/ppermute | solution.py:13
  133.2 7.0 %collective-permute-start.13 = (bf16[128,256]{0,1:T(8,128)(2,1)S(1)}, bf16[128,256]{0,1:T(8,128)(2,1)S(1)}, u32[]{:S(2)}, u32[]{:S(2)}) collective-permute-start(bf16[128,256]{0,1:T(8,128)(2,1)S(1)} %copy.47), channel_id=1, source_target_pairs={{0,8},{4,12},{8,16},{12,20},{16,24},{20,28},{1,9},{5,13},{9,17},{1... | collective-permute-start | bytes 196616 | tf_op jit(solution)/shard_map/ppermute | solution.py:13
  140.3 6.5 %collective-permute-start.14 = (bf16[128,256]{0,1:T(8,128)(2,1)S(1)}, bf16[128,256]{0,1:T(8,128)(2,1)S(1)}, u32[]{:S(2)}, u32[]{:S(2)}) collective-permute-start(bf16[128,256]{0,1:T(8,128)(2,1)S(1)} %copy.47), channel_id=1, source_target_pairs={{0,4},{4,8},{8,12},{12,16},{16,20},{20,24},{24,28},{1,5},{5,9},{9,... | collective-permute-start | bytes 196616 | tf_op jit(solution)/shard_map/ppermute | solution.py:13
  148.0 5.4 %copy-start.5 = (bf16[640,256]{0,1:T(8,128)(2,1)S(1)}, bf16[640,256]{0,1:T(8,128)(2,1)}, u32[]{:S(2)}) copy-start(bf16[640,256]{0,1:T(8,128)(2,1)} %copy.46) | copy-start | bytes 983044
  153.4 4.3 %copy-start.8 = (f32[16]{0:T(128)S(1)}, f32[16]{0:T(128)}, u32[]{:S(2)}) copy-start(f32[16]{0:T(128)} %get-tuple-element.9) | copy-start | bytes 196
  156.8 1.0 copy-start.1
  157.8 15.3 %copy-start.2 = (bf16[128,2048]{1,0:T(8,128)(2,1)S(1)}, bf16[128,2048]{1,0:T(8,128)(2,1)}, u32[]{:S(2)}) copy-start(bf16[128,2048]{1,0:T(8,128)(2,1)} %param.15) | copy-start | bytes 1572868
  157.8 15.3 %copy-start.7 = (f32[2048]{0:T(1024)S(1)}, f32[2048]{0:T(1024)}, u32[]{:S(2)}) copy-start(f32[2048]{0:T(1024)} %param.16) | copy-start | bytes 24580
where the time goes:
time: 175 us; the launch traced here: 174 us
  waiting for transfers between devices  97 us (55%)
  starting transfers between devices  30.9 us (18%)
  matrix products  14.8 us (8%)
  blocking collectives  12 us (7%)
  local copies, waits for them, and re-layouts  11.1 us (6%)
  other arithmetic  6.08 us (3%)
  between operations  2.32 us (1%)
    ppermute x15, waiting for transfers between devices, from_behind(): return lax.ppermute(shard, axis, pairs)  97 us
    ppermute x15, starting transfers between devices, from_behind(): return lax.ppermute(shard, axis, pairs)  30.9 us
    psum x1, blocking collectives, local(): total_sq = lax.psum(local_sq, 'head')  12 us
    unnamed x29, local copies, waits for them, and re-layouts  5.65 us
    sub x1, matrix products, local(): expd = jnp.where(allowed, jnp.exp(jnp.minimum(scores - top, 0.0)), 0.0)  5.4 us
  transfers between devices with their start and end apart: 15, of which 8 were waited for; matrix products, arithmetic and copies ran while one was open for 13% of the time, Pallas kernels for 0%

commit v1 on v0

--- a/solution.py
+++ b/solution.py
@@ -11,6 +11,17 @@
     count = lax.axis_size(axis)
     pairs = [(i, i + by) for i in range(count) if 0 <= i + by < count]
     return lax.ppermute(shard, axis, pairs)
+
+
+def all_sum(x, axis):
+    count = lax.axis_size(axis)
+    me = lax.axis_index(axis)
+    parts = [x]
+    for by in range(1, count):
+        parts.append(lax.ppermute(x, axis, [(i, (i + by) % count) for i in range(count)]))
+    stacked = jnp.stack(parts)
+    order = (me - jnp.arange(count)) % count
+    return jnp.sum(stacked[order], axis=0)
 
 
 def document_of(positions, doc_lengths):
@@ -51,16 +62,18 @@
     inner, level, carried, shrinkage_multiplier, state = block_terms(
         query, lookup_array, values, log_decay, docs, before
     )
+    kv_width = soft_k.shape[1]
+    pair = jnp.concatenate([soft_k, soft_v], axis=1)
+    state_b = state.astype(jnp.bfloat16)
     key_blocks = [soft_k]
     value_blocks = [soft_v]
     incoming = jnp.zeros((heads_here, DH, DH), jnp.float32)
     running = jnp.ones((heads_here,), jnp.float32)
     for step in range(1, SPAN + 1):
-        far_keys, far_values = from_behind((soft_k, soft_v), "ctx", step)
-        key_blocks.append(far_keys)
-        value_blocks.append(far_values)
-        far_factor, far_state = from_behind((shrinkage_multiplier, state), "ctx", step)
-        incoming = incoming + running[:, None, None] * far_state
+        far_pair, far_factor, far_state = from_behind((pair, shrinkage_multiplier, state_b), "ctx", step)
+        key_blocks.append(far_pair[:, :kv_width])
+        value_blocks.append(far_pair[:, kv_width:])
+        incoming = incoming + running[:, None, None] * far_state.astype(jnp.float32)
         running = running * far_factor
     outer = jnp.einsum(
         "thd,hde->the", query, incoming.astype(jnp.bfloat16), preferred_element_type=jnp.float32
@@ -68,7 +81,7 @@
     outer = outer * (jnp.exp(level).T * carried[:, None].astype(jnp.float32))[:, :, None]
     mixed = inner + outer
     local_sq = jnp.sum(mixed * mixed, axis=(1, 2))
-    total_sq = lax.psum(local_sq, "head")
+    total_sq = all_sum(local_sq, "head")
     mean_sq = total_sq / (lax.axis_size("head") * heads_here * DH)
     flat = mixed.reshape(rows, heads_here * DH)
     normed = (

time: 175 us -> 86.3 us (0.49)
  the two profiles are of different devices: /device:TPU:4 before, /device:TPU:1 now
where the time goes in v1:
time: 86.3 us; the launch traced here: 85.7 us
  starting transfers between devices  32.6 us (38%)
  waiting for transfers between devices  26.2 us (30%)
  matrix products  11.3 us (13%)
  local copies, waits for them, and re-layouts  8.4 us (10%)
  other arithmetic  4.83 us (6%)
  between operations  2.36 us (3%)
    ppermute x11, starting transfers between devices, from_behind(): return lax.ppermute(shard, axis, pairs)  27.9 us
    ppermute x11, waiting for transfers between devices, from_behind(): return lax.ppermute(shard, axis, pairs)  26.2 us
    sub x1, matrix products, local(): expd = jnp.where(allowed, jnp.exp(jnp.minimum(scores - top, 0.0)), 0.0)  5.49 us
    unnamed x26, local copies, waits for them, and re-layouts  4.78 us
    ppermute x3, starting transfers between devices, all_sum(): lax.ppermute(x, axis, [(i, (i + by) % count) for i in range(count)])  4.73 us
    dot_general x1, matrix products, local(): jnp.einsum('thd,hde->the', query, incoming.astype(jnp.bfloat16), preferre...  2.15 us
  transfers between devices with their start and end apart: 14, of which 3 were waited for; matrix products, arithmetic and copies ran while one was open for 21% of the time, Pallas kernels for 0%

profile of v1, /device:TPU:1, one launch (start us, length us, event | category | flops | bytes accessed | tf_op | source)
XLA Modules:
  0.0 85.7 jit_solution(5499632390948967822)
XLA Ops:
  0.6 0.0 copy-start
  0.6 0.0 copy-start.2
  0.7 1.0 %copy.44 = bf16[128,256]{0,1:T(8,128)(2,1)S(1)} copy(bf16[128,256]{1,0:T(8,128)(2,1)} %param.18) | data formatting | bytes 131072 | tf_op args[8]
  1.7 1.0 %copy.45 = bf16[128,256]{0,1:T(8,128)(2,1)S(1)} copy(bf16[128,256]{1,0:T(8,128)(2,1)} %param.19) | data formatting | bytes 131072 | tf_op args[9]
  2.7 4.0 %collective-permute-start.10 = (bf16[128,512]{0,1:T(8,128)(2,1)S(1)}, bf16[128,512]{0,1:T(8,128)(2,1)S(1)}, u32[]{:S(2)}, u32[]{:S(2)}) collective-permute-start(bf16[128,512]{0,1:T(8,128)(2,1)S(1)} %pad_maximum_fusion), channel_id=1, source_target_pairs={{0,16},{4,20},{8,24},{12,28},{1,17},{5,21},{9,25},{13,29},{2,18},{... | collective-permute-start | bytes 393224 | tf_op jit(solution)/shard_map/ppermute | solution.py:13
  6.7 1.9 %collective-permute-start.11 = (bf16[128,512]{0,1:T(8,128)(2,1)S(1)}, bf16[128,512]{0,1:T(8,128)(2,1)S(1)}, u32[]{:S(2)}, u32[]{:S(2)}) collective-permute-start(bf16[128,512]{0,1:T(8,128)(2,1)S(1)} %pad_maximum_fusion), channel_id=1, source_target_pairs={{0,12},{4,16},{8,20},{12,24},{16,28},{1,13},{5,17},{9,21},{13,25},... | collective-permute-start | bytes 393224 | tf_op jit(solution)/shard_map/ppermute | solution.py:13
  8.5 3.2 %collective-permute-start.12 = (bf16[128,512]{0,1:T(8,128)(2,1)S(1)}, bf16[128,512]{0,1:T(8,128)(2,1)S(1)}, u32[]{:S(2)}, u32[]{:S(2)}) collective-permute-start(bf16[128,512]{0,1:T(8,128)(2,1)S(1)} %pad_maximum_fusion), channel_id=1, source_target_pairs={{0,8},{4,12},{8,16},{12,20},{16,24},{20,28},{1,9},{5,13},{9,17},{1... | collective-permute-start | bytes 393224 | tf_op jit(solution)/shard_map/ppermute | solution.py:13
  11.7 0.8 reduce-window.4
  12.6 0.1 convert_reduce_fusion.1
  12.7 0.6 slice.38
  13.3 0.6 fusion.55
  14.6 0.6 fusion.62
  15.2 0.6 slice.40
  16.5 1.0 %reduce_window_sum.20 = f32[16,128]{1,0:T(8,128)S(1)} reduce-window(f32[16,128]{1,0:T(8,128)} %param.14, f32[]{:T(128)} %constant.26.clone.1), window={size=1x128 pad=0_0x127_0}, to_apply=%region_2.3 | reduce-window | flops 260096 | bytes 16388 | tf_op jit(solution)/shard_map/jit(cumsum)/reduce_window_sum | solution.py:34
  17.4 0.2 slice_reduce_fusion
  17.6 3.0 %collective-permute-start.1 = (f32[16]{0:T(128)S(1)}, f32[16]{0:T(128)S(1)}, u32[]{:S(2)}, u32[]{:S(2)}) collective-permute-start(f32[16]{0:T(128)S(1)} %exponential_multiply_fusion), channel_id=1, source_target_pairs={{0,4},{4,8},{8,12},{12,16},{16,20},{20,24},{24,28},{1,5},{5,9},{9,... | collective-permute-start | bytes 200 | tf_op jit(solution)/shard_map/ppermute | solution.py:13
  20.6 1.6 %collective-permute-start.3 = (f32[16]{0:T(128)S(1)}, f32[16]{0:T(128)S(1)}, u32[]{:S(2)}, u32[]{:S(2)}) collective-permute-start(f32[16]{0:T(128)S(1)} %exponential_multiply_fusion), channel_id=1, source_target_pairs={{0,8},{4,12},{8,16},{12,20},{16,24},{20,28},{1,9},{5,13},{9,17},{1... | collective-permute-start | bytes 200 | tf_op jit(solution)/shard_map/ppermute | solution.py:13
  22.3 0.1 fusion.54
  22.4 0.1 convert_reduce_fusion
  22.5 0.2 compare_and_fusion
  22.7 1.3 %copy.58 = bf16[128,2048]{0,1:T(8,128)(2,1)S(1)} copy(bf16[128,2048]{1,0:T(8,128)(2,1)} %param.12) | data formatting | bytes 1048576 | tf_op jit(solution)/shard_map/reshape | solution.py:60
  24.1 0.0 copy-start.4
  24.1 0.1 multiply_bitcast_fusion
  24.2 1.4 %convolution_convert_fusion = bf16[16,128,128]{2,1,0:T(8,128)(2,1)S(1)} fusion(bf16[128,16,128]{0,2,1:T(8,128)(2,1)S(1)} %bitcast.97, f32[128,16]{0,1:T(8,128)S(1)} %get-tuple-element.21, bf16[128,2048]{1,0:T(8,128)(2,1)} %param.13), kind=kOutput, calls=%fused_computation.23 | convolution fusion | flops 68157440 | bytes 1581056 | tf_op jit(solution)/shard_map/shd,she->hde/dot_general | solution.py:45
  25.6 1.7 %convolution_bitcast_fusion.1 = f32[128,16,128]{0,2,1:T(8,128)} fusion(bf16[128,16,128]{0,2,1:T(8,128)(2,1)S(1)} %bitcast.98, f32[16,128]{1,0:T(8,128)S(1)} %reduce_window_sum.20, pred[128,128]{1,0:T(8,128)(4,1)S(1)} %fusion.54, bf16[128,2048]{1,0:T(8,128)(2,1)S(1)} %copy-done.2, bf16[128,2048]{1,0:T(8,128)(2,1)S(1)} %copy-done), kind=kOutput, calls=%fused_computation.17 | convolution fusion | flops 135528448 | bytes 2646016 | tf_op jit(solution)/shard_map/hts,shd->thd/dot_general | solution.py:40
  27.3 0.9 %copy.61 = bf16[16,8,16,128]{3,2,1,0:T(8,128)(2,1)} copy(bf16[16,8,16,128]{3,1,2,0:T(8,128)(2,1)S(1)} %bitcast.99) | data formatting | bytes 1048576
  28.2 1.3 %collective-permute-start.5 = (f32[16]{0:T(128)S(1)}, f32[16]{0:T(128)S(1)}, u32[]{:S(2)}, u32[]{:S(2)}) collective-permute-start(f32[16]{0:T(128)S(1)} %exponential_multiply_fusion), channel_id=1, source_target_pairs={{0,12},{4,16},{8,20},{12,24},{16,28},{1,13},{5,17},{9,21},{13,25},... | collective-permute-start | bytes 200 | tf_op jit(solution)/shard_map/ppermute | solution.py:13
  29.5 2.2 %collective-permute-start.13 = (bf16[128,512]{0,1:T(8,128)(2,1)S(1)}, bf16[128,512]{0,1:T(8,128)(2,1)S(1)}, u32[]{:S(2)}, u32[]{:S(2)}) collective-permute-start(bf16[128,512]{0,1:T(8,128)(2,1)S(1)} %pad_maximum_fusion), channel_id=1, source_target_pairs={{0,4},{4,8},{8,12},{12,16},{16,20},{20,24},{24,28},{1,5},{5,9},{9,... | collective-permute-start | bytes 393224 | tf_op jit(solution)/shard_map/ppermute | solution.py:13
  31.7 2.7 %collective-permute-start = (bf16[16,128,128]{2,1,0:T(8,128)(2,1)S(1)}, bf16[16,128,128]{2,1,0:T(8,128)(2,1)S(1)}, u32[]{:S(2)}, u32[]{:S(2)}) collective-permute-start(bf16[16,128,128]{2,1,0:T(8,128)(2,1)S(1)} %convolution_convert_fusion), channel_id=1, source_target_pairs={{0,4},{4,8},{8,12},{12,16},{16,20},{20,24},{24,28},{1,5},{5,9},{9,... | collective-permute-start | bytes 1572872 | tf_op jit(solution)/shard_map/ppermute | solution.py:13
  34.4 3.9 %collective-permute-start.2 = (bf16[16,128,128]{2,1,0:T(8,128)(2,1)S(1)}, bf16[16,128,128]{2,1,0:T(8,128)(2,1)}, u32[]{:S(2)}, u32[]{:S(2)}) collective-permute-start(bf16[16,128,128]{2,1,0:T(8,128)(2,1)S(1)} %convolution_convert_fusion), channel_id=1, source_target_pairs={{0,8},{4,12},{8,16},{12,20},{16,24},{20,28},{1,9},{5,13},{9,17},{1... | collective-permute-start | bytes 1572872 | tf_op jit(solution)/shard_map/ppermute | solution.py:13
  38.3 2.1 %collective-permute-start.4 = (bf16[16,128,128]{2,1,0:T(8,128)(2,1)S(1)}, bf16[16,128,128]{2,1,0:T(8,128)(2,1)}, u32[]{:S(2)}, u32[]{:S(2)}) collective-permute-start(bf16[16,128,128]{2,1,0:T(8,128)(2,1)S(1)} %convolution_convert_fusion), channel_id=1, source_target_pairs={{0,12},{4,16},{8,20},{12,24},{16,28},{1,13},{5,17},{9,21},{13,25},... | collective-permute-start | bytes 1572872 | tf_op jit(solution)/shard_map/ppermute | solution.py:13
  40.5 2.1 %collective-permute-start.6 = (bf16[16,128,128]{2,1,0:T(8,128)(2,1)S(1)}, bf16[16,128,128]{2,1,0:T(8,128)(2,1)}, u32[]{:S(2)}, u32[]{:S(2)}) collective-permute-start(bf16[16,128,128]{2,1,0:T(8,128)(2,1)S(1)} %convolution_convert_fusion), channel_id=1, source_target_pairs={{0,16},{4,20},{8,24},{12,28},{1,17},{5,21},{9,25},{13,29},{2,18},{... | collective-permute-start | bytes 1572872 | tf_op jit(solution)/shard_map/ppermute | solution.py:13
  42.7 0.0 copy-start.5
  42.7 0.7 copy-done.5
  43.4 5.5 %fusion.63 = (f32[2,8,128]{2,1,0:T(8,128)S(1)}, bf16[2,8,128,640]{2,3,1,0:T(8,128)(2,1)}) fusion(pred[128,640]{0,1:T(8,128)(4,1)S(1)} %compare_and_fusion, bf16[640,2,128,1]{0,2,3,1:T(8,128)(2,1)S(1)} %bitcast.102, bf16[128,2,8,128]{3,2,1,0:T(8,128)(2,1)} %bitcast.100), kind=kOutput, calls=%fused_computation.93 | convolution fusion | flops 681575040 | bytes 3563520 | tf_op jit(solution)/shard_map/sub | solution.py:105
  48.9 4.9 %collective-permute-done.2 = bf16[16,128,128]{2,1,0:T(8,128)(2,1)} collective-permute-done((bf16[16,128,128]{2,1,0:T(8,128)(2,1)S(1)}, bf16[16,128,128]{2,1,0:T(8,128)(2,1)}, u32[]{:S(2)}, u32[]{:S(2)}) %collective-permute-start.2) | collective-permute-done | bytes 524320 | tf_op jit(solution)/shard_map/ppermute | solution.py:13
  53.8 15.6 %collective-permute-done.4 = bf16[16,128,128]{2,1,0:T(8,128)(2,1)} collective-permute-done((bf16[16,128,128]{2,1,0:T(8,128)(2,1)S(1)}, bf16[16,128,128]{2,1,0:T(8,128)(2,1)}, u32[]{:S(2)}, u32[]{:S(2)}) %collective-permute-start.4) | collective-permute-done | bytes 524320 | tf_op jit(solution)/shard_map/ppermute | solution.py:13
  69.3 5.7 %collective-permute-done.6 = bf16[16,128,128]{2,1,0:T(8,128)(2,1)} collective-permute-done((bf16[16,128,128]{2,1,0:T(8,128)(2,1)S(1)}, bf16[16,128,128]{2,1,0:T(8,128)(2,1)}, u32[]{:S(2)}, u32[]{:S(2)}) %collective-permute-start.6) | collective-permute-done | bytes 524320 | tf_op jit(solution)/shard_map/ppermute | solution.py:13
  75.1 2.2 %multiply_reduce_fusion = (f32[128]{0:T(128)S(1)}, f32[128,16,128]{0,2,1:T(8,128)S(1)}) fusion(f32[128,16,128]{0,2,1:T(8,128)S(1)} %copy-done.1, f32[128,16]{0,1:T(8,128)S(1)} %get-tuple-element.20, bf16[16,128,128]{2,1,0:T(8,128)(2,1)} %collective-permute-done.6, bf16[16,128,128]{2,1,0:T(8,128)(2,1)} %collective-permute-done.4, ...), kind=kOutput, calls=%fused_computation.26 | convolution fusion | flops 71040896 | bytes 4727488 | tf_op jit(solution)/shard_map/thd,hde->the/dot_general | solution.py:78
  77.2 1.4 %collective-permute-start.7 = (f32[128]{0:T(128)S(1)}, f32[128]{0:T(128)S(1)}, u32[]{:S(2)}, u32[]{:S(2)}) collective-permute-start(f32[128]{0:T(128)S(1)} %get-tuple-element.23), channel_id=1, source_target_pairs={{0,1},{1,2},{2,3},{3,0},{4,5},{5,6},{6,7},{7,4},{8,9},{9,10},{10,1... | collective-permute-start | bytes 1544 | tf_op jit(solution)/shard_map/ppermute | solution.py:21
  78.6 2.3 %collective-permute-start.8 = (f32[128]{0:T(128)S(1)}, f32[128]{0:T(128)S(1)}, u32[]{:S(2)}, u32[]{:S(2)}) collective-permute-start(f32[128]{0:T(128)S(1)} %get-tuple-element.23), channel_id=1, source_target_pairs={{0,2},{1,3},{2,0},{3,1},{4,6},{5,7},{6,4},{7,5},{8,10},{9,11},{10,... | collective-permute-start | bytes 1544 | tf_op jit(solution)/shard_map/ppermute | solution.py:21
  80.9 1.1 %collective-permute-start.9 = (f32[128]{0:T(128)S(1)}, f32[128]{0:T(128)S(1)}, u32[]{:S(2)}, u32[]{:S(2)}) collective-permute-start(f32[128]{0:T(128)S(1)} %get-tuple-element.23), channel_id=1, source_target_pairs={{0,3},{1,0},{2,1},{3,2},{4,7},{5,4},{6,5},{7,6},{8,11},{9,8},{10,9... | collective-permute-start | bytes 1544 | tf_op jit(solution)/shard_map/ppermute | solution.py:21
  82.0 0.6 fusion.20
  82.5 0.0 copy-start.7
  82.6 1.0 %copy.51 = bf16[128,2048]{1,0:T(8,128)(2,1)} copy(bf16[128,2048]{0,1:T(8,128)(2,1)S(1)} %bitcast.101) | data formatting | bytes 1048576
  83.6 0.3 copy.43
  84.0 0.6 gather_fusion
  84.6 1.1 %multiply_convert_fusion = bf16[128,2048]{1,0:T(8,128)(2,1)} fusion(bf16[128,2048]{1,0:T(8,128)(2,1)S(1)} %copy-done.3, f32[128,2048]{1,0:T(8,128)S(1)} %copy.43, f32[2048]{0:T(1024)S(1)} %copy-done.7, f32[128]{0:T(128)S(1)} %add_rsqrt_fusion), kind=kLoop, calls=%fused_computation.25 | loop fusion | flops 2097152 | bytes 2105856 | tf_op jit(solution)/shard_map/convert_element_type | solution.py:93
  (39 shorter events, 0.3 us)
Async XLA Ops:
  0.6 24.9 %copy-start = (bf16[128,2048]{1,0:T(8,128)(2,1)S(1)}, bf16[128,2048]{1,0:T(8,128)(2,1)}, u32[]{:S(2)}) copy-start(bf16[128,2048]{1,0:T(8,128)(2,1)} %param.11) | copy-start | bytes 1572868
  0.6 24.9 %copy-start.2 = (bf16[128,2048]{1,0:T(8,128)(2,1)S(1)}, bf16[128,2048]{1,0:T(8,128)(2,1)}, u32[]{:S(2)}) copy-start(bf16[128,2048]{1,0:T(8,128)(2,1)} %param.13) | copy-start | bytes 1572868
  2.7 31.7 %collective-permute-start.10 = (bf16[128,512]{0,1:T(8,128)(2,1)S(1)}, bf16[128,512]{0,1:T(8,128)(2,1)S(1)}, u32[]{:S(2)}, u32[]{:S(2)}) collective-permute-start(bf16[128,512]{0,1:T(8,128)(2,1)S(1)} %pad_maximum_fusion), channel_id=1, source_target_pairs={{0,16},{4,20},{8,24},{12,28},{1,17},{5,21},{9,25},{13,29},{2,18},{... | collective-permute-start | bytes 393224 | tf_op jit(solution)/shard_map/ppermute | solution.py:13
  6.7 31.7 %collective-permute-start.11 = (bf16[128,512]{0,1:T(8,128)(2,1)S(1)}, bf16[128,512]{0,1:T(8,128)(2,1)S(1)}, u32[]{:S(2)}, u32[]{:S(2)}) collective-permute-start(bf16[128,512]{0,1:T(8,128)(2,1)S(1)} %pad_maximum_fusion), channel_id=1, source_target_pairs={{0,12},{4,16},{8,20},{12,24},{16,28},{1,13},{5,17},{9,21},{13,25},... | collective-permute-start | bytes 393224 | tf_op jit(solution)/shard_map/ppermute | solution.py:13
  8.5 31.9 %collective-permute-start.12 = (bf16[128,512]{0,1:T(8,128)(2,1)S(1)}, bf16[128,512]{0,1:T(8,128)(2,1)S(1)}, u32[]{:S(2)}, u32[]{:S(2)}) collective-permute-start(bf16[128,512]{0,1:T(8,128)(2,1)S(1)} %pad_maximum_fusion), channel_id=1, source_target_pairs={{0,8},{4,12},{8,16},{12,20},{16,24},{20,28},{1,9},{5,13},{9,17},{1... | collective-permute-start | bytes 393224 | tf_op jit(solution)/shard_map/ppermute | solution.py:13
  17.6 10.6 %collective-permute-start.1 = (f32[16]{0:T(128)S(1)}, f32[16]{0:T(128)S(1)}, u32[]{:S(2)}, u32[]{:S(2)}) collective-permute-start(f32[16]{0:T(128)S(1)} %exponential_multiply_fusion), channel_id=1, source_target_pairs={{0,4},{4,8},{8,12},{12,16},{16,20},{20,24},{24,28},{1,5},{5,9},{9,... | collective-permute-start | bytes 200 | tf_op jit(solution)/shard_map/ppermute | solution.py:13
  20.6 8.9 %collective-permute-start.3 = (f32[16]{0:T(128)S(1)}, f32[16]{0:T(128)S(1)}, u32[]{:S(2)}, u32[]{:S(2)}) collective-permute-start(f32[16]{0:T(128)S(1)} %exponential_multiply_fusion), channel_id=1, source_target_pairs={{0,8},{4,12},{8,16},{12,20},{16,24},{20,28},{1,9},{5,13},{9,17},{1... | collective-permute-start | bytes 200 | tf_op jit(solution)/shard_map/ppermute | solution.py:13
  24.1 3.3 %copy-start.4 = (bf16[128,2048]{1,0:T(8,128)(2,1)S(1)}, bf16[128,2048]{1,0:T(8,128)(2,1)}, u32[]{:S(2)}) copy-start(bf16[128,2048]{1,0:T(8,128)(2,1)} %param.17) | copy-start | bytes 1572868
  28.2 3.5 %collective-permute-start.5 = (f32[16]{0:T(128)S(1)}, f32[16]{0:T(128)S(1)}, u32[]{:S(2)}, u32[]{:S(2)}) collective-permute-start(f32[16]{0:T(128)S(1)} %exponential_multiply_fusion), channel_id=1, source_target_pairs={{0,12},{4,16},{8,20},{12,24},{16,28},{1,13},{5,17},{9,21},{13,25},... | collective-permute-start | bytes 200 | tf_op jit(solution)/shard_map/ppermute | solution.py:13
  29.5 13.1 %collective-permute-start.13 = (bf16[128,512]{0,1:T(8,128)(2,1)S(1)}, bf16[128,512]{0,1:T(8,128)(2,1)S(1)}, u32[]{:S(2)}, u32[]{:S(2)}) collective-permute-start(bf16[128,512]{0,1:T(8,128)(2,1)S(1)} %pad_maximum_fusion), channel_id=1, source_target_pairs={{0,4},{4,8},{8,12},{12,16},{16,20},{20,24},{24,28},{1,5},{5,9},{9,... | collective-permute-start | bytes 393224 | tf_op jit(solution)/shard_map/ppermute | solution.py:13
  31.7 17.2 %collective-permute-start = (bf16[16,128,128]{2,1,0:T(8,128)(2,1)S(1)}, bf16[16,128,128]{2,1,0:T(8,128)(2,1)S(1)}, u32[]{:S(2)}, u32[]{:S(2)}) collective-permute-start(bf16[16,128,128]{2,1,0:T(8,128)(2,1)S(1)} %convolution_convert_fusion), channel_id=1, source_target_pairs={{0,4},{4,8},{8,12},{12,16},{16,20},{20,24},{24,28},{1,5},{5,9},{9,... | collective-permute-start | bytes 1572872 | tf_op jit(solution)/shard_map/ppermute | solution.py:13
  34.4 19.4 %collective-permute-start.2 = (bf16[16,128,128]{2,1,0:T(8,128)(2,1)S(1)}, bf16[16,128,128]{2,1,0:T(8,128)(2,1)}, u32[]{:S(2)}, u32[]{:S(2)}) collective-permute-start(bf16[16,128,128]{2,1,0:T(8,128)(2,1)S(1)} %convolution_convert_fusion), channel_id=1, source_target_pairs={{0,8},{4,12},{8,16},{12,20},{16,24},{20,28},{1,9},{5,13},{9,17},{1... | collective-permute-start | bytes 1572872 | tf_op jit(solution)/shard_map/ppermute | solution.py:13
  38.3 31.0 %collective-permute-start.4 = (bf16[16,128,128]{2,1,0:T(8,128)(2,1)S(1)}, bf16[16,128,128]{2,1,0:T(8,128)(2,1)}, u32[]{:S(2)}, u32[]{:S(2)}) collective-permute-start(bf16[16,128,128]{2,1,0:T(8,128)(2,1)S(1)} %convolution_convert_fusion), channel_id=1, source_target_pairs={{0,12},{4,16},{8,20},{12,24},{16,28},{1,13},{5,17},{9,21},{13,25},... | collective-permute-start | bytes 1572872 | tf_op jit(solution)/shard_map/ppermute | solution.py:13
  40.5 34.6 %collective-permute-start.6 = (bf16[16,128,128]{2,1,0:T(8,128)(2,1)S(1)}, bf16[16,128,128]{2,1,0:T(8,128)(2,1)}, u32[]{:S(2)}, u32[]{:S(2)}) collective-permute-start(bf16[16,128,128]{2,1,0:T(8,128)(2,1)S(1)} %convolution_convert_fusion), channel_id=1, source_target_pairs={{0,16},{4,20},{8,24},{12,28},{1,17},{5,21},{9,25},{13,29},{2,18},{... | collective-permute-start | bytes 1572872 | tf_op jit(solution)/shard_map/ppermute | solution.py:13
  42.7 0.7 copy-start.5
  43.4 31.6 %copy-start.1 = (f32[128,16,128]{0,2,1:T(8,128)S(1)}, f32[128,16,128]{0,2,1:T(8,128)}, u32[]{:S(2)}) copy-start(f32[128,16,128]{0,2,1:T(8,128)} %convolution_bitcast_fusion.1) | copy-start | bytes 3145732
  48.9 33.0 %copy-start.6 = (bf16[640,256]{0,1:T(8,128)(2,1)S(1)}, bf16[640,256]{0,1:T(8,128)(2,1)}, u32[]{:S(2)}) copy-start(bf16[640,256]{0,1:T(8,128)(2,1)} %copy-done.5) | copy-start | bytes 983044
  48.9 33.0 %copy-start.8 = (bf16[2,8,128,640]{2,3,1,0:T(8,128)(2,1)S(1)}, bf16[2,8,128,640]{2,3,1,0:T(8,128)(2,1)}, u32[]{:S(2)}) copy-start(bf16[2,8,128,640]{2,3,1,0:T(8,128)(2,1)} %get-tuple-element.26) | copy-start | bytes 7864324
  77.2 6.7 %collective-permute-start.7 = (f32[128]{0:T(128)S(1)}, f32[128]{0:T(128)S(1)}, u32[]{:S(2)}, u32[]{:S(2)}) collective-permute-start(f32[128]{0:T(128)S(1)} %get-tuple-element.23), channel_id=1, source_target_pairs={{0,1},{1,2},{2,3},{3,0},{4,5},{5,6},{6,7},{7,4},{8,9},{9,10},{10,1... | collective-permute-start | bytes 1544 | tf_op jit(solution)/shard_map/ppermute | solution.py:21
  78.6 5.4 %collective-permute-start.8 = (f32[128]{0:T(128)S(1)}, f32[128]{0:T(128)S(1)}, u32[]{:S(2)}, u32[]{:S(2)}) collective-permute-start(f32[128]{0:T(128)S(1)} %get-tuple-element.23), channel_id=1, source_target_pairs={{0,2},{1,3},{2,0},{3,1},{4,6},{5,7},{6,4},{7,5},{8,10},{9,11},{10,... | collective-permute-start | bytes 1544 | tf_op jit(solution)/shard_map/ppermute | solution.py:21
  80.9 3.1 %collective-permute-start.9 = (f32[128]{0:T(128)S(1)}, f32[128]{0:T(128)S(1)}, u32[]{:S(2)}, u32[]{:S(2)}) collective-permute-start(f32[128]{0:T(128)S(1)} %get-tuple-element.23), channel_id=1, source_target_pairs={{0,3},{1,0},{2,1},{3,2},{4,7},{5,4},{6,5},{7,6},{8,11},{9,8},{10,9... | collective-permute-start | bytes 1544 | tf_op jit(solution)/shard_map/ppermute | solution.py:21
  82.5 2.0 %copy-start.3 = (bf16[128,2048]{1,0:T(8,128)(2,1)S(1)}, bf16[128,2048]{1,0:T(8,128)(2,1)}, u32[]{:S(2)}) copy-start(bf16[128,2048]{1,0:T(8,128)(2,1)} %param.15) | copy-start | bytes 1572868
  82.5 2.0 %copy-start.7 = (f32[2048]{0:T(1024)S(1)}, f32[2048]{0:T(1024)}, u32[]{:S(2)}) copy-start(f32[2048]{0:T(1024)} %param.16) | copy-start | bytes 24580

commit v2 on v1

--- a/solution.py
+++ b/solution.py
@@ -62,19 +62,53 @@
     inner, level, carried, shrinkage_multiplier, state = block_terms(
         query, lookup_array, values, log_decay, docs, before
     )
+    count = lax.axis_size("ctx")
+    odd = (shard % 2) == 1
+    pair = jnp.concatenate([soft_k, soft_v], axis=1)
     kv_width = soft_k.shape[1]
-    pair = jnp.concatenate([soft_k, soft_v], axis=1)
-    state_b = state.astype(jnp.bfloat16)
-    key_blocks = [soft_k]
-    value_blocks = [soft_v]
-    incoming = jnp.zeros((heads_here, DH, DH), jnp.float32)
-    running = jnp.ones((heads_here,), jnp.float32)
-    for step in range(1, SPAN + 1):
-        far_pair, far_factor, far_state = from_behind((pair, shrinkage_multiplier, state_b), "ctx", step)
-        key_blocks.append(far_pair[:, :kv_width])
-        value_blocks.append(far_pair[:, kv_width:])
-        incoming = incoming + running[:, None, None] * far_state.astype(jnp.float32)
-        running = running * far_factor
+    n_state = state.size
+    n_factor = heads_here
+    evens = [(i, i + 1) for i in range(0, count, 2)]
+    first = jnp.concatenate(
+        [state.reshape(-1), shrinkage_multiplier, pair.astype(jnp.float32).reshape(-1)]
+    )
+    got = lax.ppermute(first, "ctx", evens)
+    state_prev = got[:n_state].reshape(state.shape)
+    factor_prev = got[n_state : n_state + n_factor]
+    pair_prev = got[n_state + n_factor :].reshape(pair.shape).astype(jnp.bfloat16)
+    chip_state = shrinkage_multiplier[:, None, None] * state_prev + state
+    chip_factor = shrinkage_multiplier * factor_prev
+    factor_hi = chip_factor.astype(jnp.bfloat16)
+    factor_lo = (chip_factor - factor_hi.astype(jnp.float32)).astype(jnp.bfloat16)
+    packet = jnp.concatenate(
+        [chip_state.astype(jnp.bfloat16).reshape(-1), factor_hi, factor_lo,
+         pair_prev.reshape(-1), pair.reshape(-1)]
+    )
+    near = lax.ppermute(packet, "ctx", [(i, i + 1) for i in range(1, count - 1, 2)])
+    far = lax.ppermute(packet, "ctx", [(i, i + 3) for i in range(1, count - 3, 2)])
+
+    def unpack(got_packet):
+        chip = got_packet[:n_state].reshape(state.shape).astype(jnp.float32)
+        hi = got_packet[n_state : n_state + n_factor].astype(jnp.float32)
+        lo = got_packet[n_state + n_factor : n_state + 2 * n_factor].astype(jnp.float32)
+        blocks = got_packet[n_state + 2 * n_factor :].reshape((2,) + pair.shape)
+        return chip, hi + lo, blocks
+
+    state_near, factor_near, pairs_near = unpack(near)
+    state_far, _, pairs_far = unpack(far)
+    incoming_even = state_near + factor_near[:, None, None] * state_far
+    onward = shrinkage_multiplier[:, None, None] * incoming_even + state
+    fourth = jnp.concatenate(
+        [onward.reshape(-1), pairs_far[1].astype(jnp.float32).reshape(-1),
+         pairs_near.astype(jnp.float32).reshape(-1)]
+    )
+    back = lax.ppermute(fourth, "ctx", evens)
+    incoming_odd = back[:n_state].reshape(state.shape)
+    pairs_odd = back[n_state:].reshape((3,) + pair.shape).astype(jnp.bfloat16)
+    incoming = jnp.where(odd, incoming_odd, incoming_even)
+    window_even = jnp.concatenate([pairs_far[0], pairs_far[1], pairs_near[0], pairs_near[1]], axis=0)
+    window_odd = jnp.concatenate([pairs_odd[0], pairs_odd[1], pairs_odd[2], pair_prev], axis=0)
+    window = jnp.concatenate([jnp.where(odd, window_odd, window_even), pair], axis=0)
     outer = jnp.einsum(
         "thd,hde->the", query, incoming.astype(jnp.bfloat16), preferred_element_type=jnp.float32
     )
@@ -92,8 +126,8 @@
     )
     lin_out = normed.astype(jnp.bfloat16)
     span_rows = (SPAN + 1) * rows
-    all_keys = jnp.concatenate(key_blocks[::-1], axis=0).reshape(span_rows, kv_here, DH)
-    all_values = jnp.concatenate(value_blocks[::-1], axis=0).reshape(span_rows, kv_here, DH)
+    all_keys = window[:, :kv_width].reshape(span_rows, kv_here, DH)
+    all_values = window[:, kv_width:].reshape(span_rows, kv_here, DH)
     key_pos = shard * rows - SPAN * rows + jnp.arange(span_rows, dtype=jnp.int32)
     key_docs = jnp.where(key_pos >= 0, document_of(key_pos, doc_lengths), -1)
     allowed = (key_docs[None, :] == docs[:, None]) & (key_pos[None, :] <= positions[:, None])

time: 86.3 us -> 91.4 us (1.059)
  the two profiles are of different devices: /device:TPU:1 before, /device:TPU:0 now
where the time goes in v2:
time: 91.4 us; the launch traced here: 90.5 us
  local copies, waits for them, and re-layouts  34.5 us (38%)
  starting transfers between devices  25.4 us (28%)
  matrix products  14.6 us (16%)
  other arithmetic  13.7 us (15%)
  between operations  2.32 us (3%)
    ppermute x1, starting transfers between devices, local(): back = lax.ppermute(fourth, 'ctx', evens)  14.9 us
    concatenate x1, local copies, waits for them, and re-layouts, local(): jnp.concatenate([chip_state.astype(jnp.bfloat16).reshape(-1), factor_hi,...  10.6 us
    unnamed x38, local copies, waits for them, and re-layouts  6.48 us
    sub x1, matrix products, local(): expd = jnp.where(allowed, jnp.exp(jnp.minimum(scores - top, 0.0)), 0.0)  5.47 us
    ppermute x3, starting transfers between devices, all_sum(): lax.ppermute(x, axis, [(i, (i + by) % count) for i in range(count)])  4.67 us
    ppermute x1, starting transfers between devices, local(): got = lax.ppermute(first, 'ctx', evens)  3.44 us
    dot_general x1, matrix products, local(): jnp.einsum('kgts,skd->tkgd', expd.astype(jnp.bfloat16), all_values, prefe...  3.11 us
    slice x2, local copies, waits for them, and re-layouts, local(): pairs_far[0]  2.77 us
  transfers between devices with their start and end apart: 7, of which 0 were waited for; matrix products, arithmetic and copies ran while one was open for 30% of the time, Pallas kernels for 0%

profile of v2, /device:TPU:0, one launch (start us, length us, event | category | flops | bytes accessed | tf_op | source)
XLA Modules:
  0.0 90.5 jit_solution(1472744428152179331)
XLA Ops:
  0.6 1.4 %copy.54 = bf16[128,2048]{0,1:T(8,128)(2,1)S(1)} copy(bf16[128,2048]{1,0:T(8,128)(2,1)} %param.12) | data formatting | bytes 1048576 | tf_op jit(solution)/shard_map/reshape | solution.py:60
  2.1 0.8 reduce-window.4
  3.0 0.6 fusion.57
  3.6 0.6 slice.118
  4.2 1.0 %reduce_window_sum.20 = f32[16,128]{1,0:T(8,128)S(1)} reduce-window(f32[16,128]{1,0:T(8,128)} %param.14, f32[]{:T(128)} %constant.61.clone.1), window={size=1x128 pad=0_0x127_0}, to_apply=%region_2.3 | reduce-window | flops 260096 | bytes 16388 | tf_op jit(solution)/shard_map/jit(cumsum)/reduce_window_sum | solution.py:34
  6.0 0.7 fusion.65
  6.7 0.6 slice.117
  8.0 0.8 constant_dynamic-update-slice_fusion.1
  8.8 0.8 constant_dynamic-update-slice_fusion
  9.7 0.6 multiply_bitcast_fusion
  10.3 1.3 %fusion.30 = f32[16,128,128]{2,1,0:T(8,128)S(1)} fusion(bf16[128,16,128]{0,2,1:T(8,128)(2,1)S(1)} %bitcast.116, f32[128,16]{0,1:T(8,128)S(1)} %get-tuple-element.23, bf16[128,2048]{1,0:T(8,128)(2,1)} %param.13), kind=kOutput, calls=%fused_computation.39 | convolution fusion | flops 67895296 | bytes 2105344 | tf_op jit(solution)/shard_map/shd,she->hde/dot_general | solution.py:45
  11.7 1.7 %concatenate.25 = f32[327696]{0:T(1024)S(1)} concatenate(f32[262144]{0:T(1024)S(1)} %bitcast.107, f32[16]{0:T(128)S(1)} %exponential_multiply_fusion, bf16[65536]{0:T(1024)(128)(2,1)S(1)} %bitcast.119), dimensions={0} | concatenate | bytes 2490496 | tf_op jit(solution)/shard_map/concatenate | solution.py:72
  13.4 3.4 %collective-permute-start = (f32[327696]{0:T(1024)S(1)}, f32[327696]{0:T(1024)}, u32[]{:S(2)}, u32[]{:S(2)}) collective-permute-start(f32[327696]{0:T(1024)S(1)} %concatenate.25), channel_id=1, source_target_pairs={{0,4},{8,12},{16,20},{24,28},{1,5},{9,13},{17,21},{25,29},{2,6},{1... | collective-permute-start | bytes 3932360 | tf_op jit(solution)/shard_map/ppermute | solution.py:75
  16.8 1.3 %convert_reduce_fusion = s32[640]{0:T(1024)} fusion(s32[640]{0:T(1024)S(1)} %iota_add_fusion, s32[6]{0:T(128)} %bitcast.130), kind=kLoop, calls=%fused_computation.66 | loop fusion | flops 10880 | bytes 5144 | tf_op jit(solution)/shard_map/reduce_sum | solution.py:29
  18.1 1.4 %fusion.56 = pred[128,128]{1,0:T(8,128)(4,1)} fusion(s32[128]{0:T(128)} %copy-done.9), kind=kLoop, calls=%fused_computation.65 | loop fusion | flops 49152 | bytes 16896 | tf_op jit(solution)/shard_map/and | solution.py:36
  19.5 1.3 %slice.144 = f32[262144]{0:T(1024)S(1)} slice(f32[327696]{0:T(1024)} %collective-permute-done), slice={[0:262144]} | slice | bytes 2097152 | tf_op jit(solution)/shard_map/slice | solution.py:76
  20.7 0.9 add_convert_fusion
  21.6 0.7 subtract_convert_fusion
  22.3 1.1 %slice.184 = bf16[65536]{0:T(1024)(128)(2,1)S(1)} slice(f32[327696]{0:T(1024)} %collective-permute-done), slice={[262160:327696]} | slice | bytes 262144 | tf_op jit(solution)/shard_map/slice | solution.py:78
  23.4 0.6 copy-done.1
  24.1 10.6 %concatenate.26 = bf16[393248]{0:T(1024)(128)(2,1)} concatenate(bf16[262144]{0:T(1024)(128)(2,1)S(1)} %bitcast.118, bf16[16]{0:T(256)(128)(2,1)S(1)} %get-tuple-element.11, bf16[16]{0:T(256)(128)(2,1)S(1)} %get-tuple-element.10, bf16[65536]{0:T(1024)(128)(2,1)S(1)} %slice.184, bf16[65536]{0:T(1024)(128)(2,1)S(1)} %bitcast.120), dimensions={0} | concatenate | bytes 1572992 | tf_op jit(solution)/shard_map/concatenate | solution.py:83
  34.7 0.8 collective-permute-start.1
  35.5 0.7 compare_select_fusion
  36.2 1.6 %collective-permute-start.2 = (bf16[393248]{0:T(1024)(128)(2,1)}, bf16[393248]{0:T(1024)(128)(2,1)}, u32[]{:S(2)}, u32[]{:S(2)}) collective-permute-start(bf16[393248]{0:T(1024)(128)(2,1)} %concatenate.26), channel_id=1, source_target_pairs={{4,16},{12,24},{5,17},{13,25},{6,18},{14,26},{7,19},{15,27}} | collective-permute-start | bytes 2359496 | tf_op jit(solution)/shard_map/ppermute | solution.py:88
  37.8 0.6 pad_clamp_fusion
  38.4 1.9 %copy.58 = bf16[16,8,16,128]{3,2,1,0:T(8,128)(2,1)} copy(bf16[16,8,16,128]{3,1,2,0:T(8,128)(2,1)} %bitcast.122) | data formatting | bytes 1048576
  40.3 1.5 %compare_and_fusion = pred[128,640]{0,1:T(8,128)(4,1)} fusion(s32[128]{0:T(128)} %copy-done.15, s32[128]{0:T(128)} %copy-done.9, s32[640]{0:T(1024)S(1)} %iota_add_fusion, s32[640]{0:T(1024)S(1)} %compare_select_fusion), kind=kLoop, calls=%fused_computation.61 | loop fusion | flops 245760 | bytes 88064 | tf_op jit(solution)/shard_map/and | solution.py:133
  41.9 2.8 %convolution_bitcast_fusion.1 = f32[128,16,128]{0,2,1:T(8,128)} fusion(bf16[128,16,128]{0,2,1:T(8,128)(2,1)S(1)} %bitcast.117, f32[16,128]{1,0:T(8,128)S(1)} %reduce_window_sum.20, pred[128,128]{1,0:T(8,128)(4,1)} %fusion.56, bf16[128,2048]{1,0:T(8,128)(2,1)} %param.13, bf16[128,2048]{1,0:T(8,128)(2,1)S(1)} %copy-done), kind=kOutput, calls=%fused_computation.18 | convolution fusion | flops 135528448 | bytes 2646016 | tf_op jit(solution)/shard_map/hts,shd->thd/dot_general | solution.py:40
  44.9 1.1 %slice.150 = bf16[262144]{0:T(1024)(128)(2,1)S(1)} slice(bf16[393248]{0:T(1024)(128)(2,1)} %collective-permute-done.2), slice={[0:262144]} | slice | bytes 1048576 | tf_op jit(solution)/shard_map/slice | solution.py:91
  46.0 0.4 multiply_add_fusion
  46.6 1.8 %fusion.67 = (bf16[65536]{0:T(1024)(128)(2,1)}, bf16[65536]{0:T(1024)(128)(2,1)S(1)}) fusion(bf16[393248]{0:T(1024)(128)(2,1)} %collective-permute-done.2), kind=kLoop, calls=%fused_computation.102 | loop fusion | bytes 524288 | tf_op jit(solution)/shard_map/slice | solution.py:109
  48.4 1.0 %pad_maximum_fusion = bf16[458752]{0:T(1024)(128)(2,1)} fusion(bf16[131072]{0:T(1024)(128)(2,1)S(1)} %slice.183, bf16[65536]{0:T(1024)(128)(2,1)S(1)} %get-tuple-element.16, bf16[262144]{0:T(1024)(128)(2,1)S(1)} %bitcast.114), kind=kLoop, calls=%fused_computation.14 | loop fusion | flops 2752512 | bytes 1835008 | tf_op jit(solution)/shard_map/concatenate | solution.py:101
  49.4 14.9 %collective-permute-start.3 = (bf16[458752]{0:T(1024)(128)(2,1)}, bf16[458752]{0:T(1024)(128)(2,1)S(1)}, u32[]{:S(2)}, u32[]{:S(2)}) collective-permute-start(bf16[458752]{0:T(1024)(128)(2,1)} %pad_maximum_fusion), channel_id=1, source_target_pairs={{0,4},{8,12},{16,20},{24,28},{1,5},{9,13},{17,21},{25,29},{2,6},{1... | collective-permute-start | bytes 2752520 | tf_op jit(solution)/shard_map/ppermute | solution.py:105
  64.2 0.8 fusion.68
  65.1 1.0 %slice.138 = bf16[128,512]{1,0:T(8,128)(2,1)S(1)} reshape(bf16[65536]{0:T(1024)(128)(2,1)} %get-tuple-element.19) | data formatting | bytes 262144 | tf_op jit(solution)/shard_map/slice | solution.py:109
  66.1 1.0 %slice.136 = bf16[128,512]{1,0:T(8,128)(2,1)S(1)} reshape(bf16[65536]{0:T(1024)(128)(2,1)} %get-tuple-element.18) | data formatting | bytes 262144 | tf_op jit(solution)/shard_map/slice | solution.py:109
  67.2 1.0 %slice.134 = bf16[128,512]{1,0:T(8,128)(2,1)S(1)} reshape(bf16[65536]{0:T(1024)(128)(2,1)} %get-tuple-element.15) | data formatting | bytes 262144 | tf_op jit(solution)/shard_map/slice | solution.py:109
  68.2 0.9 copy-done.3
  69.1 1.9 %multiply_reduce_fusion = (f32[128]{0:T(128)S(1)}, f32[128,16,128]{0,2,1:T(8,128)S(1)}) fusion(f32[128,16,128]{0,2,1:T(8,128)} %convolution_bitcast_fusion.1, f32[128,16]{0,1:T(8,128)S(1)} %copy-done.7, bf16[16,128,128]{2,1,0:T(8,128)(2,1)S(1)} %bitcast.115, bf16[16,128,128]{2,1,0:T(8,128)(2,1)S(1)} %bitcast.111, bf16[16,128,128]{2,1,0:T(8,128)(2,1)S(1)} %bitcast.109, ...), kind=kOutput, calls=%fused_computation.28 | convolution fusion | flops 69468032 | bytes 4203073 | tf_op jit(solution)/shard_map/thd,hde->the/dot_general | solution.py:112
  71.0 3.7 %collective-permute-start.6 = (f32[128]{0:T(128)S(1)}, f32[128]{0:T(128)S(1)}, u32[]{:S(2)}, u32[]{:S(2)}) collective-permute-start(f32[128]{0:T(128)S(1)} %get-tuple-element.25), channel_id=1, source_target_pairs={{0,3},{1,0},{2,1},{3,2},{4,7},{5,4},{6,5},{7,6},{8,11},{9,8},{10,9... | collective-permute-start | bytes 1544 | tf_op jit(solution)/shard_map/ppermute | solution.py:21
  74.7 1.0 %collective-permute-start.4 = (f32[128]{0:T(128)S(1)}, f32[128]{0:T(128)S(1)}, u32[]{:S(2)}, u32[]{:S(2)}) collective-permute-start(f32[128]{0:T(128)S(1)} %get-tuple-element.25), channel_id=1, source_target_pairs={{0,1},{1,2},{2,3},{3,0},{4,5},{5,6},{6,7},{7,4},{8,9},{9,10},{10,1... | collective-permute-start | bytes 1544 | tf_op jit(solution)/shard_map/ppermute | solution.py:21
  75.7 1.1 %fusion.66 = (bf16[65536]{0:T(1024)(128)(2,1)S(1)}, bf16[65536]{0:T(1024)(128)(2,1)S(1)}, bf16[65536]{0:T(1024)(128)(2,1)S(1)}) fusion(bf16[458752]{0:T(1024)(128)(2,1)} %copy-done.3), kind=kLoop, calls=%fused_computation.101 | loop fusion | bytes 786432 | tf_op jit(solution)/shard_map/slice | solution.py:110
  77.7 5.5 %fusion.69 = (f32[2,8,128]{2,1,0:T(8,128)S(1)}, bf16[2,8,128,640]{2,3,1,0:T(8,128)(2,1)}) fusion(pred[128,640]{0,1:T(8,128)(4,1)} %compare_and_fusion, bf16[640,2,128,1]{0,2,3,1:T(8,128)(2,1)S(1)} %bitcast.126, bf16[128,2,8,128]{3,2,1,0:T(8,128)(2,1)} %bitcast.123), kind=kOutput, calls=%fused_computation.104 | convolution fusion | flops 681575040 | bytes 3563520 | tf_op jit(solution)/shard_map/sub | solution.py:139
  83.1 3.1 %fusion.20 = bf16[128,2,8,128]{0,3,2,1:T(8,128)(2,1)} fusion(bf16[640,2,128,1]{0,2,3,1:T(8,128)(2,1)S(1)} %bitcast.125, bf16[2,8,128,640]{2,3,1,0:T(8,128)(2,1)} %get-tuple-element.28, f32[128,2,8]{0,2,1:T(8,128)S(1)} %bitcast.135), kind=kOutput, calls=%fused_computation.23 | convolution fusion | flops 336068608 | bytes 3481600 | tf_op jit(solution)/shard_map/kgts,skd->tkgd/dot_general | solution.py:141
  86.2 0.3 copy.41
  86.6 2.0 %copy.47 = bf16[128,2048]{1,0:T(8,128)(2,1)} copy(bf16[128,2048]{0,1:T(8,128)(2,1)} %bitcast.124) | data formatting | bytes 1048576
  88.7 0.7 gather_fusion
  89.4 1.1 %multiply_convert_fusion = bf16[128,2048]{1,0:T(8,128)(2,1)} fusion(bf16[128,2048]{1,0:T(8,128)(2,1)S(1)} %copy-done.6, f32[128,2048]{1,0:T(8,128)S(1)} %copy.41, f32[2048]{0:T(1024)S(1)} %copy-done.8, f32[128]{0:T(128)S(1)} %add_rsqrt_fusion), kind=kLoop, calls=%fused_computation.27 | loop fusion | flops 2097152 | bytes 2105856 | tf_op jit(solution)/shard_map/convert_element_type | solution.py:127
  (63 shorter events, 1.8 us)
Async XLA Ops:
  0.6 41.3 %copy-start = (bf16[128,2048]{1,0:T(8,128)(2,1)S(1)}, bf16[128,2048]{1,0:T(8,128)(2,1)}, u32[]{:S(2)}) copy-start(bf16[128,2048]{1,0:T(8,128)(2,1)} %param.11) | copy-start | bytes 1572868
  2.0 5.3 %copy-start.15 = (s32[128]{0:T(128)}, s32[128]{0:T(128)S(1)}, u32[]{:S(2)}) copy-start(s32[128]{0:T(128)S(1)} %iota_add_fusion.1) | copy-start | bytes 1540
  2.9 4.4 %copy-start.16 = (s32[6,1]{0,1:T(1,128)}, s32[6,1]{0,1:T(1,128)S(1)}, u32[]{:S(2)}) copy-start(s32[6,1]{0,1:T(1,128)S(1)} %reduce-window.4) | copy-start | bytes 76
  3.0 4.3 %copy-start.9 = (s32[128]{0:T(128)}, s32[128]{0:T(128)S(1)}, u32[]{:S(2)}) copy-start(s32[128]{0:T(128)S(1)} %convert_reduce_fusion.1) | copy-start | bytes 1540
  5.4 4.9 %copy-start.10 = (f32[16]{0:T(128)}, f32[16]{0:T(128)S(1)}, u32[]{:S(2)}) copy-start(f32[16]{0:T(128)S(1)} %slice_reduce_fusion) | copy-start | bytes 196
  9.6 0.7 copy-start.4
  9.7 7.1 %copy-start.11 = (f32[16]{0:T(128)}, f32[16]{0:T(128)S(1)}, u32[]{:S(2)}) copy-start(f32[16]{0:T(128)S(1)} %exponential_multiply_fusion) | copy-start | bytes 196
  13.4 6.1 %collective-permute-start = (f32[327696]{0:T(1024)S(1)}, f32[327696]{0:T(1024)}, u32[]{:S(2)}, u32[]{:S(2)}) collective-permute-start(f32[327696]{0:T(1024)S(1)} %concatenate.25), channel_id=1, source_target_pairs={{0,4},{8,12},{16,20},{24,28},{1,5},{9,13},{17,21},{25,29},{2,6},{1... | collective-permute-start | bytes 3932360 | tf_op jit(solution)/shard_map/ppermute | solution.py:75
  23.4 0.7 copy-start.1
  34.7 10.0 %copy-start.2 = (bf16[65536]{0:T(1024)(128)(2,1)S(1)}, bf16[65536]{0:T(1024)(128)(2,1)}, u32[]{:S(2)}) copy-start(bf16[65536]{0:T(1024)(128)(2,1)} %copy-done.1) | copy-start | bytes 393220
  34.7 10.1 %collective-permute-start.1 = (bf16[393248]{0:T(1024)(128)(2,1)}, bf16[393248]{0:T(1024)(128)(2,1)S(1)}, u32[]{:S(2)}, u32[]{:S(2)}) collective-permute-start(bf16[393248]{0:T(1024)(128)(2,1)} %concatenate.26), channel_id=1, source_target_pairs={{4,8},{12,16},{20,24},{5,9},{13,17},{21,25},{6,10},{14,18},{22,26}... | collective-permute-start | bytes 2359496 | tf_op jit(solution)/shard_map/ppermute | solution.py:87
  36.2 8.6 %collective-permute-start.2 = (bf16[393248]{0:T(1024)(128)(2,1)}, bf16[393248]{0:T(1024)(128)(2,1)}, u32[]{:S(2)}, u32[]{:S(2)}) collective-permute-start(bf16[393248]{0:T(1024)(128)(2,1)} %concatenate.26), channel_id=1, source_target_pairs={{4,16},{12,24},{5,17},{13,25},{6,18},{14,26},{7,19},{15,27}} | collective-permute-start | bytes 2359496 | tf_op jit(solution)/shard_map/ppermute | solution.py:88
  41.9 4.1 %copy-start.12 = (f32[16]{0:T(128)S(1)}, f32[16]{0:T(128)}, u32[]{:S(2)}) copy-start(f32[16]{0:T(128)} %copy-done.11) | copy-start | bytes 196
  44.9 1.5 %copy-start.13 = (f32[16]{0:T(128)}, f32[16]{0:T(128)S(1)}, u32[]{:S(2)}) copy-start(f32[16]{0:T(128)S(1)} %fusion.60) | copy-start | bytes 196
  46.6 22.5 %copy-start.7 = (f32[128,16]{0,1:T(8,128)S(1)}, f32[128,16]{0,1:T(8,128)}, u32[]{:S(2)}) copy-start(f32[128,16]{0,1:T(8,128)} %get-tuple-element.22) | copy-start | bytes 24580
  46.6 22.5 %copy-start.14 = (f32[16]{0:T(128)S(1)}, f32[16]{0:T(128)}, u32[]{:S(2)}) copy-start(f32[16]{0:T(128)} %copy-done.13) | copy-start | bytes 196
  49.4 18.8 %collective-permute-start.3 = (bf16[458752]{0:T(1024)(128)(2,1)}, bf16[458752]{0:T(1024)(128)(2,1)S(1)}, u32[]{:S(2)}, u32[]{:S(2)}) collective-permute-start(bf16[458752]{0:T(1024)(128)(2,1)} %pad_maximum_fusion), channel_id=1, source_target_pairs={{0,4},{8,12},{16,20},{24,28},{1,5},{9,13},{17,21},{25,29},{2,6},{1... | collective-permute-start | bytes 2752520 | tf_op jit(solution)/shard_map/ppermute | solution.py:105
  68.2 0.9 %copy-start.3 = (bf16[458752]{0:T(1024)(128)(2,1)}, bf16[458752]{0:T(1024)(128)(2,1)S(1)}, u32[]{:S(2)}) copy-start(bf16[458752]{0:T(1024)(128)(2,1)S(1)} %collective-permute-done.3) | copy-start | bytes 2752516
  71.0 6.2 %copy-start.5 = (bf16[128,512]{1,0:T(8,128)(2,1)S(1)}, bf16[128,512]{1,0:T(8,128)(2,1)}, u32[]{:S(2)}) copy-start(bf16[128,512]{1,0:T(8,128)(2,1)} %copy-done.4) | copy-start | bytes 393220
  71.0 17.6 %collective-permute-start.6 = (f32[128]{0:T(128)S(1)}, f32[128]{0:T(128)S(1)}, u32[]{:S(2)}, u32[]{:S(2)}) collective-permute-start(f32[128]{0:T(128)S(1)} %get-tuple-element.25), channel_id=1, source_target_pairs={{0,3},{1,0},{2,1},{3,2},{4,7},{5,4},{6,5},{7,6},{8,11},{9,8},{10,9... | collective-permute-start | bytes 1544 | tf_op jit(solution)/shard_map/ppermute | solution.py:21
  74.7 14.0 %collective-permute-start.5 = (f32[128]{0:T(128)S(1)}, f32[128]{0:T(128)S(1)}, u32[]{:S(2)}, u32[]{:S(2)}) collective-permute-start(f32[128]{0:T(128)S(1)} %get-tuple-element.25), channel_id=1, source_target_pairs={{0,2},{1,3},{2,0},{3,1},{4,6},{5,7},{6,4},{7,5},{8,10},{9,11},{10,... | collective-permute-start | bytes 1544 | tf_op jit(solution)/shard_map/ppermute | solution.py:21
  74.7 14.0 %collective-permute-start.4 = (f32[128]{0:T(128)S(1)}, f32[128]{0:T(128)S(1)}, u32[]{:S(2)}, u32[]{:S(2)}) collective-permute-start(f32[128]{0:T(128)S(1)} %get-tuple-element.25), channel_id=1, source_target_pairs={{0,1},{1,2},{2,3},{3,0},{4,5},{5,6},{6,7},{7,4},{8,9},{9,10},{10,1... | collective-permute-start | bytes 1544 | tf_op jit(solution)/shard_map/ppermute | solution.py:21
  86.2 3.1 %copy-start.6 = (bf16[128,2048]{1,0:T(8,128)(2,1)S(1)}, bf16[128,2048]{1,0:T(8,128)(2,1)}, u32[]{:S(2)}) copy-start(bf16[128,2048]{1,0:T(8,128)(2,1)} %param.15) | copy-start | bytes 1572868
  86.2 3.1 %copy-start.8 = (f32[2048]{0:T(1024)S(1)}, f32[2048]{0:T(1024)}, u32[]{:S(2)}) copy-start(f32[2048]{0:T(1024)} %param.16) | copy-start | bytes 24580

commit v3 on v1

--- a/solution.py
+++ b/solution.py
@@ -62,21 +62,64 @@
     inner, level, carried, shrinkage_multiplier, state = block_terms(
         query, lookup_array, values, log_decay, docs, before
     )
-    kv_width = soft_k.shape[1]
-    pair = jnp.concatenate([soft_k, soft_v], axis=1)
-    state_b = state.astype(jnp.bfloat16)
-    key_blocks = [soft_k]
-    value_blocks = [soft_v]
-    incoming = jnp.zeros((heads_here, DH, DH), jnp.float32)
-    running = jnp.ones((heads_here,), jnp.float32)
-    for step in range(1, SPAN + 1):
-        far_pair, far_factor, far_state = from_behind((pair, shrinkage_multiplier, state_b), "ctx", step)
-        key_blocks.append(far_pair[:, :kv_width])
-        value_blocks.append(far_pair[:, kv_width:])
-        incoming = incoming + running[:, None, None] * far_state.astype(jnp.float32)
-        running = running * far_factor
+    count = lax.axis_size("ctx")
+    odd = (shard % 2) == 1
+    pair = jnp.concatenate(
+        [soft_k.reshape(rows, kv_here, DH).transpose(1, 0, 2),
+         soft_v.reshape(rows, kv_here, DH).transpose(1, 0, 2)],
+        axis=0,
+    ).reshape(-1, DH)
+    n_pair = pair.shape[0]
+    n_state = heads_here * DH
+    state_rows = state.reshape(n_state, DH)
+    factor_rows = jnp.pad(shrinkage_multiplier[None, :], ((0, 7), (0, DH - heads_here)))
+    first = jnp.concatenate([state_rows, factor_rows, pair.astype(jnp.float32)], axis=0)
+    got = lax.ppermute(first, "ctx", [(i, i ^ 1) for i in range(count)])
+    state_mate = got[:n_state]
+    factor_mate = got[n_state, :heads_here]
+    pair_mate = got[n_state + 8 :].astype(jnp.bfloat16)
+    state_lo = jnp.where(odd, state_mate, state_rows).reshape(state.shape)
+    state_hi = jnp.where(odd, state_rows, state_mate).reshape(state.shape)
+    factor_lo = jnp.where(odd, factor_mate, shrinkage_multiplier)
+    factor_hi = jnp.where(odd, shrinkage_multiplier, factor_mate)
+    pair_lo = jnp.where(odd, pair_mate, pair)
+    pair_hi = jnp.where(odd, pair, pair_mate)
+    chip_state = factor_hi[:, None, None] * state_lo + state_hi
+    chip_factor = factor_hi * factor_lo
+    chip_top = chip_factor.astype(jnp.bfloat16)
+    chip_rest = (chip_factor - chip_top.astype(jnp.float32)).astype(jnp.bfloat16)
+    chip_rows = jnp.pad(jnp.stack([chip_top, chip_rest]), ((0, 14), (0, DH - heads_here)))
+    packet = jnp.concatenate(
+        [chip_state.astype(jnp.bfloat16).reshape(n_state, DH), chip_rows, pair_lo, pair_hi], axis=0
+    )
+    near = lax.ppermute(packet, "ctx", [(i, i + 1) for i in range(1, count - 1, 2)])
+    far = lax.ppermute(packet, "ctx", [(i, i + 4) for i in range(0, count - 4, 2)])
+
+    def unpack(got_packet):
+        chip = got_packet[:n_state].reshape(state.shape).astype(jnp.float32)
+        mult = got_packet[n_state, :heads_here].astype(jnp.float32) + got_packet[
+            n_state + 1, :heads_here
+        ].astype(jnp.float32)
+        low = got_packet[n_state + 16 : n_state + 16 + n_pair]
+        high = got_packet[n_state + 16 + n_pair :]
+        return chip, mult, low, high
+
+    state_near, factor_near, near_lo, near_hi = unpack(near)
+    state_far, _, far_lo, far_hi = unpack(far)
+    incoming_even = state_near + factor_near[:, None, None] * state_far
+    onward = shrinkage_multiplier[:, None, None] * incoming_even + state
+    fourth = jnp.concatenate(
+        [onward.astype(jnp.bfloat16).reshape(n_state, DH), far_hi, near_lo, near_hi], axis=0
+    )
+    back = lax.ppermute(fourth, "ctx", [(i, i + 1) for i in range(0, count, 2)])
+    incoming_odd = back[:n_state].reshape(state.shape)
+    incoming_b = jnp.where(odd, incoming_odd, incoming_even.astype(jnp.bfloat16))
+    window_even = jnp.concatenate([far_lo, far_hi, near_lo, near_hi], axis=0)
+    window_odd = jnp.concatenate([back[n_state:], pair_mate], axis=0)
+    window = jnp.concatenate([jnp.where(odd, window_odd, window_even), pair], axis=0)
+    window = window.reshape(SPAN + 1, 2 * kv_here, rows, DH)
     outer = jnp.einsum(
-        "thd,hde->the", query, incoming.astype(jnp.bfloat16), preferred_element_type=jnp.float32
+        "thd,hde->the", query, incoming_b, preferred_element_type=jnp.float32
     )
     outer = outer * (jnp.exp(level).T * carried[:, None].astype(jnp.float32))[:, :, None]
     mixed = inner + outer
@@ -92,20 +135,21 @@
     )
     lin_out = normed.astype(jnp.bfloat16)
     span_rows = (SPAN + 1) * rows
-    all_keys = jnp.concatenate(key_blocks[::-1], axis=0).reshape(span_rows, kv_here, DH)
-    all_values = jnp.concatenate(value_blocks[::-1], axis=0).reshape(span_rows, kv_here, DH)
     key_pos = shard * rows - SPAN * rows + jnp.arange(span_rows, dtype=jnp.int32)
     key_docs = jnp.where(key_pos >= 0, document_of(key_pos, doc_lengths), -1)
     allowed = (key_docs[None, :] == docs[:, None]) & (key_pos[None, :] <= positions[:, None])
     soft_query = soft_q.reshape(rows, kv_here, group, DH)
     scores = jnp.einsum(
-        "tkgd,skd->kgts", soft_query, all_keys, preferred_element_type=jnp.float32
-    ) * DH ** (-0.5)
+        "tkgd,bksd->kgtbs", soft_query, window[:, :kv_here], preferred_element_type=jnp.float32
+    ).reshape(kv_here, group, rows, span_rows) * DH ** (-0.5)
     top = jnp.max(jnp.where(allowed, scores, -1e30), axis=-1, keepdims=True)
     expd = jnp.where(allowed, jnp.exp(jnp.minimum(scores - top, 0.0)), 0.0)
     total = jnp.sum(expd, axis=-1)
     attended = jnp.einsum(
-        "kgts,skd->tkgd", expd.astype(jnp.bfloat16), all_values, preferred_element_type=jnp.float32
+        "kgtbs,bksd->tkgd",
+        expd.astype(jnp.bfloat16).reshape(kv_here, group, rows, SPAN + 1, rows),
+        window[:, kv_here:],
+        preferred_element_type=jnp.float32,
     )
     attended = attended / total.transpose(2, 0, 1)[..., None]
     soft_out = attended.reshape(rows, kv_here * group * DH).astype(jnp.bfloat16)

time: 86.3 us -> 70.2 us (0.81)
  the two profiles are of different devices: /device:TPU:1 before, /device:TPU:0 now
where the time goes in v3:
time: 70.2 us; the launch traced here: 69.2 us
  waiting for transfers between devices  17.4 us (25%)
  other arithmetic  16.7 us (24%)
  starting transfers between devices  13.6 us (19%)
  local copies, waits for them, and re-layouts  12.6 us (18%)
  matrix products  6.51 us (9%)
  between operations  2.39 us (3%)
    ppermute x1, waiting for transfers between devices, local(): lax.ppermute(packet, 'ctx', [(i, i + 4) for i in range(0, count - 4, 2)])  14.6 us
    unnamed x53, local copies, waits for them, and re-layouts  5.72 us
    ppermute x1, starting transfers between devices, local(): lax.ppermute(packet, 'ctx', [(i, i + 4) for i in range(0, count - 4, 2)])  5.42 us
    ppermute x3, starting transfers between devices, all_sum(): lax.ppermute(x, axis, [(i, (i + by) % count) for i in range(count)])  4.66 us
    ppermute x1, waiting for transfers between devices, local(): got = lax.ppermute(first, 'ctx', [(i, i ^ 1) for i in range(count)])  2.8 us
    dot_general x1, matrix products, block_terms(): jnp.einsum('hts,shd->thd', weights, values, preferred_element_type=jnp.fl...  2.43 us
    ppermute x1, starting transfers between devices, local(): back = lax.ppermute(fourth, 'ctx', [(i, i + 1) for i in range(0, count, 2)])  2.27 us
    dot_general x1, matrix products, local(): jnp.einsum('kgtbs,bksd->tkgd', expd.astype(jnp.bfloat16).reshape(kv_here,...  2.18 us
  transfers between devices with their start and end apart: 7, of which 2 were waited for; matrix products, arithmetic and copies ran while one was open for 22% of the time, Pallas kernels for 0%

profile of v3, /device:TPU:0, one launch (start us, length us, event | category | flops | bytes accessed | tf_op | source)
XLA Modules:
  0.0 69.2 jit_solution(16555090875570489461)
XLA Ops:
  0.7 0.9 %reduce-window.4 = s32[6,1]{0,1:T(1,128)S(1)} reduce-window(s32[6,1]{0,1:T(1,128)} %bitcast.167, s32[]{:T(128)} %constant.61.clone.1), window={size=6x1 pad=5_0x0_0}, to_apply=%region_0.0 | reduce-window | flops 30 | bytes 52 | tf_op jit(solution)/shard_map/reduce-window
  1.6 0.6 fusion.56
  2.4 0.6 slice.63
  3.6 0.7 fusion.64
  4.3 0.6 slice.62
  5.5 0.9 %bitcast_bitcast_fusion = (bf16[2,128,128]{2,1,0:T(8,128)(2,1)S(1)}, bf16[2,128,128]{2,1,0:T(8,128)(2,1)S(1)}) fusion(bf16[128,256]{1,0:T(8,128)(2,1)} %param.18, bf16[128,256]{1,0:T(8,128)(2,1)} %param.19), kind=kLoop, calls=%fused_computation.66 | loop fusion | bytes 262144 | tf_op jit(solution)/shard_map/transpose | solution.py:69
  6.4 0.7 %bitcast_convert_fusion = f32[512,128]{1,0:T(8,128)} fusion(bf16[4,128,128]{2,1,0:T(8,128)(2,1)S(1)} %pad_maximum_fusion.3), kind=kLoop, calls=%fused_computation.112 | loop fusion | flops 65536 | bytes 393216 | tf_op jit(solution)/shard_map/convert_element_type | solution.py:76
  7.2 1.3 %copy.63 = bf16[128,2048]{0,1:T(8,128)(2,1)S(1)} copy(bf16[128,2048]{1,0:T(8,128)(2,1)} %param.12) | data formatting | bytes 1048576 | tf_op jit(solution)/shard_map/reshape | solution.py:60
  8.5 0.3 reduce_window_sum.20
  8.8 0.2 slice_reduce_fusion
  9.0 0.6 multiply_bitcast_fusion
  9.6 0.3 fusion.27
  10.0 0.5 collective-permute-start
  10.5 2.8 %collective-permute-done = f32[2568,128]{1,0:T(8,128)} collective-permute-done((f32[2568,128]{1,0:T(8,128)S(1)}, f32[2568,128]{1,0:T(8,128)}, u32[]{:S(2)}, u32[]{:S(2)}) %collective-permute-start) | collective-permute-done | bytes 1314848 | tf_op jit(solution)/shard_map/ppermute | solution.py:77
  13.3 0.7 fusion.65
  14.0 1.3 %broadcast_select_fusion.4 = (f32[16]{0:T(128)S(1)}, f32[16]{0:T(128)}) fusion(pred[]{:T(512)S(6)} %eq.61, f32[2568,128]{1,0:T(8,128)} %collective-permute-done, f32[]{:T(128)} %bitcast.4, f32[16]{0:T(128)S(1)} %get-tuple-element.8), kind=kLoop, calls=%fused_computation.98 | loop fusion | flops 32 | bytes 261 | tf_op jit(solution)/shard_map/jit(_where)/select_n | solution.py:84
  15.4 1.0 %broadcast_select_fusion.1 = (bf16[512,128]{1,0:T(8,128)(2,1)S(1)}, bf16[512,128]{1,0:T(8,128)(2,1)S(1)}) fusion(pred[]{:T(512)S(6)} %eq.61, bf16[4,128,128]{2,1,0:T(8,128)(2,1)S(1)} %pad_maximum_fusion.3, f32[2568,128]{1,0:T(8,128)} %collective-permute-done), kind=kLoop, calls=%fused_computation.65 | loop fusion | flops 65536 | bytes 524289 | tf_op jit(solution)/shard_map/jit(_where)/select_n | solution.py:85
  16.4 0.6 copy-done.6
  17.0 1.6 %add_convert_fusion.1 = bf16[2048,128]{1,0:T(8,128)(2,1)S(1)} fusion(f32[2568,128]{1,0:T(8,128)} %collective-permute-done, f32[2048]{0:T(1024)S(1)} %broadcast_bitcast_fusion, pred[]{:T(512)S(6)} %eq.61, f32[16,128,128]{2,1,0:T(8,128)S(1)} %fusion.27), kind=kLoop, calls=%fused_computation.30 | loop fusion | flops 1310720 | bytes 2629633 | tf_op jit(solution)/shard_map/convert_element_type | solution.py:93
  18.6 1.0 %pad_maximum_fusion.1 = bf16[3088,128]{1,0:T(8,128)(2,1)} fusion(bf16[512,128]{1,0:T(8,128)(2,1)S(1)} %broadcast_select_fusion, bf16[512,128]{1,0:T(8,128)(2,1)S(1)} %get-tuple-element.16, bf16[16,128]{1,0:T(8,128)(2,1)S(1)} %fusion.54, bf16[2048,128]{1,0:T(8,128)(2,1)S(1)} %add_convert_fusion.1), kind=kLoop, calls=%fused_computation.37 | loop fusion | flops 3162112 | bytes 1581056 | tf_op jit(solution)/shard_map/concatenate | solution.py:92
  19.6 0.7 %collective-permute-start.1 = (bf16[3088,128]{1,0:T(8,128)(2,1)}, bf16[3088,128]{1,0:T(8,128)(2,1)S(1)}, u32[]{:S(2)}, u32[]{:S(2)}) collective-permute-start(bf16[3088,128]{1,0:T(8,128)(2,1)} %pad_maximum_fusion.1), channel_id=1, source_target_pairs={{4,8},{12,16},{20,24},{5,9},{13,17},{21,25},{6,10},{14,18},{22,26}... | collective-permute-start | bytes 2371592 | tf_op jit(solution)/shard_map/ppermute | solution.py:95
  20.3 5.4 %collective-permute-start.2 = (bf16[3088,128]{1,0:T(8,128)(2,1)}, bf16[3088,128]{1,0:T(8,128)(2,1)S(1)}, u32[]{:S(2)}, u32[]{:S(2)}) collective-permute-start(bf16[3088,128]{1,0:T(8,128)(2,1)} %pad_maximum_fusion.1), channel_id=1, source_target_pairs={{0,16},{8,24},{1,17},{9,25},{2,18},{10,26},{3,19},{11,27}} | collective-permute-start | bytes 2371592 | tf_op jit(solution)/shard_map/ppermute | solution.py:96
  25.7 2.0 %copy.68 = bf16[16,8,16,128]{3,2,1,0:T(8,128)(2,1)} copy(bf16[16,8,16,128]{3,1,2,0:T(8,128)(2,1)} %bitcast.156) | data formatting | bytes 1048576
  27.7 0.6 pad_clamp_fusion
  28.4 14.6 %collective-permute-done.2 = bf16[3088,128]{1,0:T(8,128)(2,1)S(1)} collective-permute-done((bf16[3088,128]{1,0:T(8,128)(2,1)}, bf16[3088,128]{1,0:T(8,128)(2,1)S(1)}, u32[]{:S(2)}, u32[]{:S(2)}) %collective-permute-start.2) | collective-permute-done | bytes 790560 | tf_op jit(solution)/shard_map/ppermute | solution.py:96
  43.0 1.1 %add_convert_fusion = bf16[16,128,128]{2,1,0:T(8,128)(2,1)S(1)} fusion(f32[16,128,128]{2,1,0:T(8,128)S(1)} %fusion.27, f32[16]{0:T(128)S(1)} %fusion.60, f32[16]{0:T(128)} %get-tuple-element.13, bf16[3088,128]{1,0:T(8,128)(2,1)S(1)} %collective-permute-done.2, bf16[3088,128]{1,0:T(8,128)(2,1)S(1)} %collective-permute-done.1), kind=kLoop, calls=%fused_computation.29 | loop fusion | flops 1835008 | bytes 2621568 | tf_op jit(solution)/shard_map/convert_element_type | solution.py:112
  44.2 1.0 %pad_maximum_fusion = bf16[3584,128]{1,0:T(8,128)(2,1)} fusion(bf16[1024,128]{1,0:T(8,128)(2,1)S(1)} %slice.89, bf16[512,128]{1,0:T(8,128)(2,1)S(1)} %slice.88, bf16[2048,128]{1,0:T(8,128)(2,1)S(1)} %bitcast.150), kind=kLoop, calls=%fused_computation.36 | loop fusion | flops 2752512 | bytes 1835008 | tf_op jit(solution)/shard_map/concatenate | solution.py:111
  45.2 2.3 %collective-permute-start.3 = (bf16[3584,128]{1,0:T(8,128)(2,1)}, bf16[3584,128]{1,0:T(8,128)(2,1)}, u32[]{:S(2)}, u32[]{:S(2)}) collective-permute-start(bf16[3584,128]{1,0:T(8,128)(2,1)} %pad_maximum_fusion), channel_id=1, source_target_pairs={{0,4},{8,12},{16,20},{24,28},{1,5},{9,13},{17,21},{25,29},{2,6},{1... | collective-permute-start | bytes 2752520 | tf_op jit(solution)/shard_map/ppermute | solution.py:114
  47.4 0.7 fusion.48
  48.1 0.9 %compare_and_fusion = pred[128,5,128]{0,2,1:T(8,128)(4,1)} fusion(s32[128]{0:T(128)S(1)} %copy-done.22, s32[5,128]{1,0:T(8,128)S(1)} %get-tuple-element.30, s32[128]{0:T(128)S(1)} %copy-done.16, s32[5,128]{1,0:T(8,128)S(1)} %get-tuple-element.29), kind=kLoop, calls=%fused_computation.61 | loop fusion | flops 245760 | bytes 88064 | tf_op jit(solution)/shard_map/and | solution.py:140
  49.0 2.4 %convolution_bitcast_fusion.1 = f32[128,16,128]{0,2,1:T(8,128)} fusion(bf16[128,16,128]{0,2,1:T(8,128)(2,1)S(1)} %bitcast.155, f32[16,128]{1,0:T(8,128)S(1)} %reduce_window_sum.20, pred[128,128]{1,0:T(8,128)(4,1)} %fusion.48, bf16[128,2048]{1,0:T(8,128)(2,1)S(1)} %copy-done.12, bf16[128,2048]{1,0:T(8,128)(2,1)S(1)} %copy-done), kind=kOutput, calls=%fused_computation.17 | convolution fusion | flops 135528448 | bytes 2646016 | tf_op jit(solution)/shard_map/hts,shd->thd/dot_general | solution.py:40
  51.5 1.2 %slice.90 = bf16[2048,128]{1,0:T(8,128)(2,1)S(1)} slice(bf16[3584,128]{1,0:T(8,128)(2,1)} %collective-permute-done.3), slice={[0:2048], [0:128]} | slice | bytes 1048576 | tf_op jit(solution)/shard_map/slice | solution.py:115
  52.7 0.1 copy-done.8
  52.8 0.1 slice-done.1
  53.0 0.7 multiply_reduce_fusion
  53.7 3.6 %collective-permute-start.6 = (f32[128]{0:T(128)S(1)}, f32[128]{0:T(128)S(1)}, u32[]{:S(2)}, u32[]{:S(2)}) collective-permute-start(f32[128]{0:T(128)S(1)} %get-tuple-element.23), channel_id=1, source_target_pairs={{0,3},{1,0},{2,1},{3,2},{4,7},{5,4},{6,5},{7,6},{8,11},{9,8},{10,9... | collective-permute-start | bytes 1544 | tf_op jit(solution)/shard_map/ppermute | solution.py:21
  57.3 1.0 %collective-permute-start.4 = (f32[128]{0:T(128)S(1)}, f32[128]{0:T(128)S(1)}, u32[]{:S(2)}, u32[]{:S(2)}) collective-permute-start(f32[128]{0:T(128)S(1)} %get-tuple-element.23), channel_id=1, source_target_pairs={{0,1},{1,2},{2,3},{3,0},{4,5},{5,6},{6,7},{7,4},{8,9},{9,10},{10,1... | collective-permute-start | bytes 1544 | tf_op jit(solution)/shard_map/ppermute | solution.py:21
  58.3 1.0 %slice.91 = bf16[1536,128]{1,0:T(8,128)(2,1)S(1)} slice(bf16[3584,128]{1,0:T(8,128)(2,1)} %collective-permute-done.3), slice={[2048:3584], [0:128]} | slice | bytes 786432 | tf_op jit(solution)/shard_map/slice | solution.py:118
  59.4 0.2 maximum_select_fusion
  59.7 0.2 copy.61
  59.9 0.7 copy-done.2
  60.6 0.9 %fusion = (f32[2,8,128]{2,1,0:T(8,128)S(1)}, f32[2,5,128,128,8]{3,2,4,1,0:T(8,128)S(1)}) fusion(pred[128,5,128]{0,2,1:T(8,128)(4,1)S(1)} %copy-done.5, bf16[128,2,8,128,1]{3,2,1,0,4:T(8,128)(2,1)S(1)} %bitcast.151, bf16[5,2,128,128]{3,2,1,0:T(8,128)(2,1)S(1)} %get-tuple-element.19), kind=kOutput, calls=%fused_computation.3 | convolution fusion | flops 339474432 | bytes 6184960 | tf_op jit(solution)/shard_map/tkgd,bksd->kgtbs/dot_general | solution.py:142
  61.5 1.2 %fusion.4 = f32[2,8,128]{2,1,0:T(8,128)S(1)} fusion(f32[2,5,128,128,8]{3,2,4,1,0:T(8,128)S(1)} %get-tuple-element.26, f32[2,8,128]{2,1,0:T(8,128)S(1)} %get-tuple-element.25, pred[128,5,128]{0,2,1:T(8,128)(4,1)S(1)} %copy-done.5), kind=kLoop, calls=%fused_computation.7 | loop fusion | flops 6551552 | bytes 5341184 | tf_op jit(solution)/shard_map/reduce_sum | solution.py:147
  62.7 2.2 %divide_convert_fusion = bf16[128,2,8,128]{0,3,2,1:T(8,128)(2,1)} fusion(f32[2,5,128,128,8]{3,2,4,1,0:T(8,128)S(1)} %get-tuple-element.26, f32[2,8,128]{2,1,0:T(8,128)S(1)} %get-tuple-element.25, pred[128,5,128]{0,2,1:T(8,128)(4,1)S(1)} %copy-done.5, f32[128,2,8]{0,2,1:T(8,128)S(1)} %bitcast.158, bf16[5,2,128,128]{2,3,0,1:T(8,128)(2,1)S(1)} %copy.61), kind=kOutput, calls=%fused_computation.26 | convolution fusion | flops 342622208 | bytes 6193152 | tf_op jit(solution)/shard_map/kgtbs,bksd->tkgd/dot_general | solution.py:148
  64.9 0.3 copy.46
  65.3 2.0 %copy.51 = bf16[128,2048]{1,0:T(8,128)(2,1)} copy(bf16[128,2048]{0,1:T(8,128)(2,1)} %bitcast.157) | data formatting | bytes 1048576
  67.3 0.7 gather_fusion
  68.1 1.1 %multiply_convert_fusion = bf16[128,2048]{1,0:T(8,128)(2,1)} fusion(bf16[128,2048]{1,0:T(8,128)(2,1)S(1)} %copy-done.10, f32[128,2048]{1,0:T(8,128)S(1)} %copy.46, f32[2048]{0:T(1024)S(1)} %copy-done.14, f32[128]{0:T(128)S(1)} %add_rsqrt_fusion), kind=kLoop, calls=%fused_computation.27 | loop fusion | flops 2097152 | bytes 2105856 | tf_op jit(solution)/shard_map/convert_element_type | solution.py:136
  (77 shorter events, 0.8 us)
Async XLA Ops:
  0.6 48.4 %copy-start = (bf16[128,2048]{1,0:T(8,128)(2,1)S(1)}, bf16[128,2048]{1,0:T(8,128)(2,1)}, u32[]{:S(2)}) copy-start(bf16[128,2048]{1,0:T(8,128)(2,1)} %param.11) | copy-start | bytes 1572868
  0.6 7.8 %copy-start.17 = (f32[16,128]{1,0:T(8,128)S(1)}, f32[16,128]{1,0:T(8,128)}, u32[]{:S(2)}) copy-start(f32[16,128]{1,0:T(8,128)} %param.14) | copy-start | bytes 24580
  0.7 8.9 %copy-start.11 = (bf16[128,2048]{1,0:T(8,128)(2,1)S(1)}, bf16[128,2048]{1,0:T(8,128)(2,1)}, u32[]{:S(2)}) copy-start(bf16[128,2048]{1,0:T(8,128)(2,1)} %param.13) | copy-start | bytes 1572868
  0.7 8.9 %copy-start.21 = (s32[128]{0:T(128)}, s32[128]{0:T(128)S(1)}, u32[]{:S(2)}) copy-start(s32[128]{0:T(128)S(1)} %iota_add_fusion.1) | copy-start | bytes 1540
  1.6 8.0 %copy-start.23 = (s32[6,1]{0,1:T(1,128)}, s32[6,1]{0,1:T(1,128)S(1)}, u32[]{:S(2)}) copy-start(s32[6,1]{0,1:T(1,128)S(1)} %reduce-window.4) | copy-start | bytes 76
  2.4 7.2 %copy-start.15 = (s32[128]{0:T(128)}, s32[128]{0:T(128)S(1)}, u32[]{:S(2)}) copy-start(s32[128]{0:T(128)S(1)} %convert_reduce_fusion.1) | copy-start | bytes 1540
  8.5 1.5 %copy-start.3 = (bf16[128,2048]{0,1:T(8,128)(2,1)}, bf16[128,2048]{0,1:T(8,128)(2,1)S(1)}, u32[]{:S(2)}) copy-start(bf16[128,2048]{0,1:T(8,128)(2,1)S(1)} %copy.63) | copy-start | bytes 1572868
  8.8 1.1 %copy-start.9 = (f32[512,128]{1,0:T(8,128)S(1)}, f32[512,128]{1,0:T(8,128)}, u32[]{:S(2)}) copy-start(f32[512,128]{1,0:T(8,128)} %bitcast_convert_fusion) | copy-start | bytes 786436
  9.0 1.1 %copy-start.18 = (f32[16]{0:T(128)}, f32[16]{0:T(128)S(1)}, u32[]{:S(2)}) copy-start(f32[16]{0:T(128)S(1)} %get-tuple-element.9) | copy-start | bytes 196
  10.0 3.3 %collective-permute-start = (f32[2568,128]{1,0:T(8,128)S(1)}, f32[2568,128]{1,0:T(8,128)}, u32[]{:S(2)}, u32[]{:S(2)}) collective-permute-start(f32[2568,128]{1,0:T(8,128)S(1)} %fusion.15), channel_id=1, source_target_pairs={{0,4},{4,0},{8,12},{12,8},{16,20},{20,16},{24,28},{28,24},{1,5},{5... | collective-permute-start | bytes 3944456 | tf_op jit(solution)/shard_map/ppermute | solution.py:77
  16.4 0.6 copy-start.6
  18.6 9.7 %copy-start.24 = (s32[6,1]{0,1:T(1,128)S(1)}, s32[6,1]{0,1:T(1,128)}, u32[]{:S(2)}) copy-start(s32[6,1]{0,1:T(1,128)} %copy-done.23) | copy-start | bytes 76
  19.6 8.8 %collective-permute-start.1 = (bf16[3088,128]{1,0:T(8,128)(2,1)}, bf16[3088,128]{1,0:T(8,128)(2,1)S(1)}, u32[]{:S(2)}, u32[]{:S(2)}) collective-permute-start(bf16[3088,128]{1,0:T(8,128)(2,1)} %pad_maximum_fusion.1), channel_id=1, source_target_pairs={{4,8},{12,16},{20,24},{5,9},{13,17},{21,25},{6,10},{14,18},{22,26}... | collective-permute-start | bytes 2371592 | tf_op jit(solution)/shard_map/ppermute | solution.py:95
  20.3 22.7 %collective-permute-start.2 = (bf16[3088,128]{1,0:T(8,128)(2,1)}, bf16[3088,128]{1,0:T(8,128)(2,1)S(1)}, u32[]{:S(2)}, u32[]{:S(2)}) collective-permute-start(bf16[3088,128]{1,0:T(8,128)(2,1)} %pad_maximum_fusion.1), channel_id=1, source_target_pairs={{0,16},{8,24},{1,17},{9,25},{2,18},{10,26},{3,19},{11,27}} | collective-permute-start | bytes 2371592 | tf_op jit(solution)/shard_map/ppermute | solution.py:96
  28.4 16.8 %copy-start.19 = (f32[16]{0:T(128)}, f32[16]{0:T(128)S(1)}, u32[]{:S(2)}) copy-start(f32[16]{0:T(128)S(1)} %fusion.60) | copy-start | bytes 196
  43.0 8.5 %copy-start.1 = (bf16[3088,128]{1,0:T(8,128)(2,1)}, bf16[3088,128]{1,0:T(8,128)(2,1)S(1)}, u32[]{:S(2)}) copy-start(bf16[3088,128]{1,0:T(8,128)(2,1)S(1)} %collective-permute-done.2) | copy-start | bytes 2371588
  43.0 4.4 %copy-start.16 = (s32[128]{0:T(128)S(1)}, s32[128]{0:T(128)}, u32[]{:S(2)}) copy-start(s32[128]{0:T(128)} %copy-done.15) | copy-start | bytes 1540
  43.0 5.1 %copy-start.22 = (s32[128]{0:T(128)S(1)}, s32[128]{0:T(128)}, u32[]{:S(2)}) copy-start(s32[128]{0:T(128)} %copy-done.21) | copy-start | bytes 1540
  44.1 4.9 %copy-start.4 = (bf16[128,2048]{0,1:T(8,128)(2,1)S(1)}, bf16[128,2048]{0,1:T(8,128)(2,1)}, u32[]{:S(2)}) copy-start(bf16[128,2048]{0,1:T(8,128)(2,1)} %copy-done.3) | copy-start | bytes 1572868
  44.1 4.9 %copy-start.12 = (bf16[128,2048]{1,0:T(8,128)(2,1)S(1)}, bf16[128,2048]{1,0:T(8,128)(2,1)}, u32[]{:S(2)}) copy-start(bf16[128,2048]{1,0:T(8,128)(2,1)} %param.13) | copy-start | bytes 1572868
  45.2 6.3 %collective-permute-start.3 = (bf16[3584,128]{1,0:T(8,128)(2,1)}, bf16[3584,128]{1,0:T(8,128)(2,1)}, u32[]{:S(2)}, u32[]{:S(2)}) collective-permute-start(bf16[3584,128]{1,0:T(8,128)(2,1)} %pad_maximum_fusion), channel_id=1, source_target_pairs={{0,4},{8,12},{16,20},{24,28},{1,5},{9,13},{17,21},{25,29},{2,6},{1... | collective-permute-start | bytes 2752520 | tf_op jit(solution)/shard_map/ppermute | solution.py:114
  51.4 1.4 %copy-start.8 = (f32[128,16,128]{0,2,1:T(8,128)S(1)}, f32[128,16,128]{0,2,1:T(8,128)}, u32[]{:S(2)}) copy-start(f32[128,16,128]{0,2,1:T(8,128)} %convolution_bitcast_fusion.1) | copy-start | bytes 3145732
  51.4 1.4 %copy-start.13 = (f32[128,16]{0,1:T(8,128)S(1)}, f32[128,16]{0,1:T(8,128)}, u32[]{:S(2)}) copy-start(f32[128,16]{0,1:T(8,128)} %get-tuple-element.20) | copy-start | bytes 24580
  51.5 1.4 %copy-start.20 = (f32[16]{0:T(128)S(1)}, f32[16]{0:T(128)}, u32[]{:S(2)}) copy-start(f32[16]{0:T(128)} %copy-done.19) | copy-start | bytes 196
  51.5 1.5 %slice-start.1 = ((bf16[3088,128]{1,0:T(8,128)(2,1)}), bf16[2048,128]{1,0:T(8,128)(2,1)S(1)}, s32[]{:S(2)}) async-start(bf16[3088,128]{1,0:T(8,128)(2,1)} %copy-done.1), calls=%async_computation.1 | async-start | bytes 1048576 | tf_op jit(solution)/shard_map/slice | solution.py:99
  53.0 6.4 %slice-start = ((bf16[3088,128]{1,0:T(8,128)(2,1)}), bf16[1024,128]{1,0:T(8,128)(2,1)S(1)}, s32[]{:S(2)}) async-start(bf16[3088,128]{1,0:T(8,128)(2,1)} %copy-done.1), calls=%async_computation | async-start | bytes 524288 | tf_op jit(solution)/shard_map/slice | solution.py:103
  53.0 6.4 %copy-start.7 = (bf16[512,128]{1,0:T(8,128)(2,1)S(1)}, bf16[512,128]{1,0:T(8,128)(2,1)}, u32[]{:S(2)}) copy-start(bf16[512,128]{1,0:T(8,128)(2,1)} %copy-done.6) | copy-start | bytes 393220
  53.7 13.6 %collective-permute-start.6 = (f32[128]{0:T(128)S(1)}, f32[128]{0:T(128)S(1)}, u32[]{:S(2)}, u32[]{:S(2)}) collective-permute-start(f32[128]{0:T(128)S(1)} %get-tuple-element.23), channel_id=1, source_target_pairs={{0,3},{1,0},{2,1},{3,2},{4,7},{5,4},{6,5},{7,6},{8,11},{9,8},{10,9... | collective-permute-start | bytes 1544 | tf_op jit(solution)/shard_map/ppermute | solution.py:21
  57.3 10.0 %collective-permute-start.5 = (f32[128]{0:T(128)S(1)}, f32[128]{0:T(128)S(1)}, u32[]{:S(2)}, u32[]{:S(2)}) collective-permute-start(f32[128]{0:T(128)S(1)} %get-tuple-element.23), channel_id=1, source_target_pairs={{0,2},{1,3},{2,0},{3,1},{4,6},{5,7},{6,4},{7,5},{8,10},{9,11},{10,... | collective-permute-start | bytes 1544 | tf_op jit(solution)/shard_map/ppermute | solution.py:21
  57.3 10.0 %collective-permute-start.4 = (f32[128]{0:T(128)S(1)}, f32[128]{0:T(128)S(1)}, u32[]{:S(2)}, u32[]{:S(2)}) collective-permute-start(f32[128]{0:T(128)S(1)} %get-tuple-element.23), channel_id=1, source_target_pairs={{0,1},{1,2},{2,3},{3,0},{4,5},{5,6},{6,7},{7,4},{8,9},{9,10},{10,1... | collective-permute-start | bytes 1544 | tf_op jit(solution)/shard_map/ppermute | solution.py:21
  59.5 1.0 %copy-start.2 = (bf16[16,8,16,128]{3,2,1,0:T(8,128)(2,1)S(1)}, bf16[16,8,16,128]{3,2,1,0:T(8,128)(2,1)}, u32[]{:S(2)}) copy-start(bf16[16,8,16,128]{3,2,1,0:T(8,128)(2,1)} %copy.68) | copy-start | bytes 1572868
  59.5 1.0 %copy-start.5 = (pred[128,5,128]{0,2,1:T(8,128)(4,1)S(1)}, pred[128,5,128]{0,2,1:T(8,128)(4,1)}, u32[]{:S(2)}) copy-start(pred[128,5,128]{0,2,1:T(8,128)(4,1)} %compare_and_fusion) | copy-start | bytes 245764
  64.9 3.1 %copy-start.10 = (bf16[128,2048]{1,0:T(8,128)(2,1)S(1)}, bf16[128,2048]{1,0:T(8,128)(2,1)}, u32[]{:S(2)}) copy-start(bf16[128,2048]{1,0:T(8,128)(2,1)} %param.15) | copy-start | bytes 1572868
  64.9 3.1 %copy-start.14 = (f32[2048]{0:T(1024)S(1)}, f32[2048]{0:T(1024)}, u32[]{:S(2)}) copy-start(f32[2048]{0:T(1024)} %param.16) | copy-start | bytes 24580

commit v4 on v3

--- a/solution.py
+++ b/solution.py
@@ -124,7 +124,7 @@
     outer = outer * (jnp.exp(level).T * carried[:, None].astype(jnp.float32))[:, :, None]
     mixed = inner + outer
     local_sq = jnp.sum(mixed * mixed, axis=(1, 2))
-    total_sq = all_sum(local_sq, "head")
+    total_sq = lax.psum(local_sq, "head")
     mean_sq = total_sq / (lax.axis_size("head") * heads_here * DH)
     flat = mixed.reshape(rows, heads_here * DH)
     normed = (

time: 70.2 us -> 75.9 us (1.081)
  blocking collectives: 0 us -> 12.1 us
  starting transfers between devices: 13.6 us -> 8.85 us
  local copies, waits for them, and re-layouts: 12.6 us -> 14.4 us
  matrix products: 6.51 us -> 4.99 us
  waiting for transfers between devices: 17.4 us -> 16.5 us
    psum x0 -> x1, blocking collectives: none -> 12.1 us  [local(): total_sq = lax.psum(local_sq, 'head')]
    ppermute x3 -> x0, starting transfers between devices: 4.66 us -> none  [all_sum(): lax.ppermute(x, axis, [(i, (i + by) % count) for i in range(count)])]
    ppermute x1, waiting for transfers between devices: 14.6 us -> 13.5 us  [local(): lax.ppermute(packet, 'ctx', [(i, i + 4) for i in range(0, count - 4, 2)])]
    concatenate x1, other arithmetic: 0.09 us -> 1.16 us  [local(): jnp.concatenate([state_rows, factor_rows, pair.astype(jnp.float32)], axis=0)]
    slice x3, local copies, waits for them, and re-layouts: 0.18 us -> 1.2 us  [unpack(): chip = got_packet[:n_state].reshape(state.shape).astype(jnp.float32)]
    slice x3, local copies, waits for them, and re-layouts: 0.02 us -> 0.97 us  [unpack(): low = got_packet[n_state + 16:n_state + 16 + n_pair]]
    ppermute x1, starting transfers between devices: 0.7 us -> 1.54 us  [local(): lax.ppermute(packet, 'ctx', [(i, i + 1) for i in range(1, count - 1, 2)])]
    ppermute x1, starting transfers between devices: 5.42 us -> 4.59 us  [local(): lax.ppermute(packet, 'ctx', [(i, i + 4) for i in range(0, count - 4, 2)])]
  transfers between devices with their start and end apart: 7 -> 4, of which waited for: 2 -> 2; matrix products, arithmetic and copies ran while one was open for 22% -> 10% of each run, Pallas kernels for 0% -> 0%
where the time goes in v4:
time: 75.9 us; the launch traced here: 75.2 us
  waiting for transfers between devices  16.5 us (22%)
  other arithmetic  16 us (21%)
  local copies, waits for them, and re-layouts  14.4 us (19%)
  blocking collectives  12.1 us (16%)
  starting transfers between devices  8.85 us (12%)
  matrix products  4.99 us (7%)
  between operations  2.35 us (3%)
    ppermute x1, waiting for transfers between devices, local(): lax.ppermute(packet, 'ctx', [(i, i + 4) for i in range(0, count - 4, 2)])  13.5 us
    psum x1, blocking collectives, local(): total_sq = lax.psum(local_sq, 'head')  12.1 us
    unnamed x37, local copies, waits for them, and re-layouts  5.51 us
    ppermute x1, starting transfers between devices, local(): lax.ppermute(packet, 'ctx', [(i, i + 4) for i in range(0, count - 4, 2)])  4.59 us
    ppermute x1, waiting for transfers between devices, local(): got = lax.ppermute(first, 'ctx', [(i, i ^ 1) for i in range(count)])  3.01 us
    ppermute x1, starting transfers between devices, local(): back = lax.ppermute(fourth, 'ctx', [(i, i + 1) for i in range(0, count, 2)])  2.27 us
    convert_element_type x1, other arithmetic, local(): onward.astype(jnp.bfloat16).reshape(n_state, DH)  1.75 us
    dot_general x1, matrix products, block_terms(): jnp.einsum('hts,shd->thd', weights, values, preferred_element_type=jnp.fl...  1.7 us
  transfers between devices with their start and end apart: 4, of which 2 were waited for; matrix products, arithmetic and copies ran while one was open for 10% of the time, Pallas kernels for 0%

profile of v4, /device:TPU:0, one launch (start us, length us, event | category | flops | bytes accessed | tf_op | source)
XLA Modules:
  0.0 75.2 jit_solution(17974479454466055723)
XLA Ops:
  0.7 0.9 %reduce-window.4 = s32[6,1]{0,1:T(1,128)S(1)} reduce-window(s32[6,1]{0,1:T(1,128)} %bitcast.157, s32[]{:T(128)} %constant.24.clone.1), window={size=6x1 pad=5_0x0_0}, to_apply=%region_0.0 | reduce-window | flops 30 | bytes 52 | tf_op jit(solution)/shard_map/reduce-window
  1.6 0.6 fusion.56
  2.3 0.1 convert_reduce_fusion.1
  2.4 0.6 slice.63
  3.6 0.7 fusion.62
  4.2 0.6 slice.62
  5.5 0.9 %bitcast_bitcast_fusion = (bf16[2,128,128]{2,1,0:T(8,128)(2,1)S(1)}, bf16[2,128,128]{2,1,0:T(8,128)(2,1)S(1)}) fusion(bf16[128,256]{1,0:T(8,128)(2,1)} %param.18, bf16[128,256]{1,0:T(8,128)(2,1)} %param.19), kind=kLoop, calls=%fused_computation.65 | loop fusion | bytes 262144 | tf_op jit(solution)/shard_map/transpose | solution.py:69
  6.4 1.3 %copy.63 = bf16[128,2048]{0,1:T(8,128)(2,1)S(1)} copy(bf16[128,2048]{1,0:T(8,128)(2,1)} %param.12) | data formatting | bytes 1048576 | tf_op jit(solution)/shard_map/reshape | solution.py:60
  7.8 0.3 reduce_window_sum.20
  8.1 0.2 slice_reduce_fusion
  8.3 0.1 multiply_bitcast_fusion
  8.3 0.3 fusion.27
  8.7 1.2 %fusion.15 = f32[2568,128]{1,0:T(8,128)} fusion(f32[1,16]{1,0:T(1,128)S(1)} %bitcast.153, f32[512,128]{1,0:T(8,128)S(1)} %bitcast_convert_fusion, f32[2048,128]{1,0:T(8,128)S(1)} %bitcast.139), kind=kLoop, calls=%fused_computation.20 | loop fusion | flops 1972224 | bytes 2625600 | tf_op jit(solution)/shard_map/concatenate | solution.py:76
  9.8 0.5 collective-permute-start
  10.3 3.0 %collective-permute-done = f32[2568,128]{1,0:T(8,128)} collective-permute-done((f32[2568,128]{1,0:T(8,128)}, f32[2568,128]{1,0:T(8,128)}, u32[]{:S(2)}, u32[]{:S(2)}) %collective-permute-start) | collective-permute-done | bytes 1314848 | tf_op jit(solution)/shard_map/ppermute | solution.py:77
  13.3 0.7 fusion.63
  14.0 0.7 broadcast_select_fusion.4
  14.7 1.0 %broadcast_select_fusion.1 = (bf16[512,128]{1,0:T(8,128)(2,1)S(1)}, bf16[512,128]{1,0:T(8,128)(2,1)S(1)}) fusion(pred[]{:T(512)S(6)} %eq.59, bf16[4,128,128]{2,1,0:T(8,128)(2,1)S(1)} %pad_maximum_fusion.3, f32[2568,128]{1,0:T(8,128)} %collective-permute-done), kind=kLoop, calls=%fused_computation.64 | loop fusion | flops 65536 | bytes 524289 | tf_op jit(solution)/shard_map/jit(_where)/select_n | solution.py:85
  15.8 0.6 copy-done.8
  16.4 1.6 %add_convert_fusion.1 = bf16[2048,128]{1,0:T(8,128)(2,1)S(1)} fusion(f32[2568,128]{1,0:T(8,128)} %collective-permute-done, f32[2048]{0:T(1024)S(1)} %broadcast_bitcast_fusion, pred[]{:T(512)S(6)} %eq.59, f32[16,128,128]{2,1,0:T(8,128)S(1)} %fusion.27), kind=kLoop, calls=%fused_computation.29 | loop fusion | flops 1310720 | bytes 2629633 | tf_op jit(solution)/shard_map/convert_element_type | solution.py:93
  17.9 0.9 %pad_maximum_fusion.1 = bf16[3088,128]{1,0:T(8,128)(2,1)} fusion(bf16[512,128]{1,0:T(8,128)(2,1)S(1)} %broadcast_select_fusion, bf16[512,128]{1,0:T(8,128)(2,1)S(1)} %get-tuple-element.16, bf16[16,128]{1,0:T(8,128)(2,1)S(1)} %fusion.54, bf16[2048,128]{1,0:T(8,128)(2,1)S(1)} %add_convert_fusion.1), kind=kLoop, calls=%fused_computation.36 | loop fusion | flops 3162112 | bytes 1581056 | tf_op jit(solution)/shard_map/concatenate | solution.py:92
  18.9 1.5 %collective-permute-start.1 = (bf16[3088,128]{1,0:T(8,128)(2,1)}, bf16[3088,128]{1,0:T(8,128)(2,1)}, u32[]{:S(2)}, u32[]{:S(2)}) collective-permute-start(bf16[3088,128]{1,0:T(8,128)(2,1)} %pad_maximum_fusion.1), channel_id=1, source_target_pairs={{4,8},{12,16},{20,24},{5,9},{13,17},{21,25},{6,10},{14,18},{22,26}... | collective-permute-start | bytes 2371592 | tf_op jit(solution)/shard_map/ppermute | solution.py:95
  20.4 4.6 %collective-permute-start.2 = (bf16[3088,128]{1,0:T(8,128)(2,1)}, bf16[3088,128]{1,0:T(8,128)(2,1)S(1)}, u32[]{:S(2)}, u32[]{:S(2)}) collective-permute-start(bf16[3088,128]{1,0:T(8,128)(2,1)} %pad_maximum_fusion.1), channel_id=1, source_target_pairs={{0,16},{8,24},{1,17},{9,25},{2,18},{10,26},{3,19},{11,27}} | collective-permute-start | bytes 2371592 | tf_op jit(solution)/shard_map/ppermute | solution.py:96
  25.0 2.0 %copy.68 = bf16[16,8,16,128]{3,2,1,0:T(8,128)(2,1)} copy(bf16[16,8,16,128]{3,1,2,0:T(8,128)(2,1)} %bitcast.150) | data formatting | bytes 1048576
  27.0 0.1 convert_reduce_fusion
  27.1 1.0 %slice.87 = bf16[1024,128]{1,0:T(8,128)(2,1)S(1)} slice(bf16[3088,128]{1,0:T(8,128)(2,1)} %collective-permute-done.1), slice={[2064:3088], [0:128]} | slice | bytes 524288 | tf_op jit(solution)/shard_map/slice | solution.py:103
  28.1 0.8 %fusion.58 = f32[16]{0:T(128)S(1)} fusion(bf16[3088,128]{1,0:T(8,128)(2,1)} %collective-permute-done.1), kind=kLoop, calls=%fused_computation.96 | loop fusion | flops 48 | bytes 128 | tf_op jit(solution)/shard_map/add | solution.py:100
  28.8 13.5 %collective-permute-done.2 = bf16[3088,128]{1,0:T(8,128)(2,1)S(1)} collective-permute-done((bf16[3088,128]{1,0:T(8,128)(2,1)}, bf16[3088,128]{1,0:T(8,128)(2,1)S(1)}, u32[]{:S(2)}, u32[]{:S(2)}) %collective-permute-start.2) | collective-permute-done | bytes 790560 | tf_op jit(solution)/shard_map/ppermute | solution.py:96
  42.3 1.8 %add_convert_fusion = bf16[16,128,128]{2,1,0:T(8,128)(2,1)S(1)} fusion(f32[16,128,128]{2,1,0:T(8,128)S(1)} %fusion.27, f32[16]{0:T(128)S(1)} %fusion.58, f32[16]{0:T(128)S(1)} %get-tuple-element.13, bf16[3088,128]{1,0:T(8,128)(2,1)S(1)} %collective-permute-done.2, bf16[3088,128]{1,0:T(8,128)(2,1)} %collective-permute-done.1), kind=kLoop, calls=%fused_computation.28 | loop fusion | flops 1835008 | bytes 2621568 | tf_op jit(solution)/shard_map/convert_element_type | solution.py:112
  44.1 1.0 %pad_maximum_fusion = bf16[3584,128]{1,0:T(8,128)(2,1)} fusion(bf16[1024,128]{1,0:T(8,128)(2,1)S(1)} %slice.87, bf16[512,128]{1,0:T(8,128)(2,1)S(1)} %slice.86, bf16[2048,128]{1,0:T(8,128)(2,1)S(1)} %bitcast.144), kind=kLoop, calls=%fused_computation.35 | loop fusion | flops 2752512 | bytes 1835008 | tf_op jit(solution)/shard_map/concatenate | solution.py:111
  45.1 2.3 %collective-permute-start.3 = (bf16[3584,128]{1,0:T(8,128)(2,1)}, bf16[3584,128]{1,0:T(8,128)(2,1)}, u32[]{:S(2)}, u32[]{:S(2)}) collective-permute-start(bf16[3584,128]{1,0:T(8,128)(2,1)} %pad_maximum_fusion), channel_id=1, source_target_pairs={{0,4},{8,12},{16,20},{24,28},{1,5},{9,13},{17,21},{25,29},{2,6},{1... | collective-permute-start | bytes 2752520 | tf_op jit(solution)/shard_map/ppermute | solution.py:114
  47.4 0.1 fusion.48
  47.5 0.9 %compare_and_fusion = pred[128,5,128]{0,2,1:T(8,128)(4,1)} fusion(s32[128]{0:T(128)S(1)} %iota_add_fusion.1, s32[5,128]{1,0:T(8,128)S(1)} %get-tuple-element.30, s32[128]{0:T(128)S(1)} %convert_reduce_fusion.1, s32[5,128]{1,0:T(8,128)S(1)} %get-tuple-element.29), kind=kLoop, calls=%fused_computation.60 | loop fusion | flops 245760 | bytes 88064 | tf_op jit(solution)/shard_map/and | solution.py:140
  48.4 1.7 %convolution_bitcast_fusion.1 = f32[128,16,128]{0,2,1:T(8,128)} fusion(bf16[128,16,128]{0,2,1:T(8,128)(2,1)S(1)} %bitcast.149, f32[16,128]{1,0:T(8,128)S(1)} %reduce_window_sum.20, pred[128,128]{1,0:T(8,128)(4,1)S(1)} %fusion.48, bf16[128,2048]{1,0:T(8,128)(2,1)S(1)} %copy-done.13, bf16[128,2048]{1,0:T(8,128)(2,1)S(1)} %copy-done), kind=kOutput, calls=%fused_computation.16 | convolution fusion | flops 135528448 | bytes 2646016 | tf_op jit(solution)/shard_map/hts,shd->thd/dot_general | solution.py:40
  50.1 1.2 %slice.82 = bf16[2048,128]{1,0:T(8,128)(2,1)S(1)} slice(bf16[3088,128]{1,0:T(8,128)(2,1)} %collective-permute-done.1), slice={[0:2048], [0:128]} | slice | bytes 1048576 | tf_op jit(solution)/shard_map/slice | solution.py:99
  51.3 1.1 %slice.88 = bf16[2048,128]{1,0:T(8,128)(2,1)S(1)} slice(bf16[3584,128]{1,0:T(8,128)(2,1)} %collective-permute-done.3), slice={[0:2048], [0:128]} | slice | bytes 1048576 | tf_op jit(solution)/shard_map/slice | solution.py:115
  52.4 0.7 multiply_reduce_fusion
  53.1 12.1 %psum.7 = f32[128]{0:T(128)S(1)} all-reduce(f32[128]{0:T(128)S(1)} %get-tuple-element.23), channel_id=1, replica_groups=mesh['ctx'=8,'head'=4] {'head'}, use_global_device_ids=true, to_apply=%region_5.6 | all-reduce | flops 128 | bytes 1024 | tf_op jit(solution)/shard_map/psum | solution.py:127
  65.2 0.3 copy.46
  65.5 1.0 %slice.89 = bf16[1536,128]{1,0:T(8,128)(2,1)S(1)} slice(bf16[3584,128]{1,0:T(8,128)(2,1)} %collective-permute-done.3), slice={[2048:3584], [0:128]} | slice | bytes 786432 | tf_op jit(solution)/shard_map/slice | solution.py:118
  66.6 0.1 maximum_select_fusion
  66.8 0.8 %fusion.65 = (bf16[5,2,128,128]{3,2,1,0:T(8,128)(2,1)}, bf16[5,2,128,128]{3,2,1,0:T(8,128)(2,1)S(1)}) fusion(bf16[5,4,128,128]{3,2,1,0:T(8,128)(2,1)S(1)} %bitcast.143), kind=kLoop, calls=%fused_computation.109 | loop fusion | bytes 1310720 | tf_op jit(solution)/shard_map/slice | solution.py:151
  67.6 1.9 %copy.61 = bf16[5,2,128,128]{2,3,0,1:T(8,128)(2,1)} copy(bf16[5,2,128,128]{3,2,1,0:T(8,128)(2,1)} %get-tuple-element.18) | data formatting | bytes 655360
  69.4 0.9 %fusion = (f32[2,8,128]{2,1,0:T(8,128)S(1)}, f32[2,5,128,128,8]{3,2,4,1,0:T(8,128)S(1)}) fusion(pred[128,5,128]{0,2,1:T(8,128)(4,1)S(1)} %copy-done.7, bf16[128,2,8,128,1]{3,2,1,0,4:T(8,128)(2,1)S(1)} %bitcast.145, bf16[5,2,128,128]{3,2,1,0:T(8,128)(2,1)S(1)} %get-tuple-element.19), kind=kOutput, calls=%fused_computation.2 | convolution fusion | flops 339474432 | bytes 6184960 | tf_op jit(solution)/shard_map/tkgd,bksd->kgtbs/dot_general | solution.py:142
  70.4 1.2 %fusion.4 = f32[2,8,128]{2,1,0:T(8,128)S(1)} fusion(f32[2,5,128,128,8]{3,2,4,1,0:T(8,128)S(1)} %get-tuple-element.26, f32[2,8,128]{2,1,0:T(8,128)S(1)} %get-tuple-element.25, pred[128,5,128]{0,2,1:T(8,128)(4,1)S(1)} %copy-done.7), kind=kLoop, calls=%fused_computation.6 | loop fusion | flops 6551552 | bytes 5341184 | tf_op jit(solution)/shard_map/reduce_sum | solution.py:147
  71.6 1.4 %divide_convert_fusion = bf16[128,2,8,128]{0,3,2,1:T(8,128)(2,1)S(1)} fusion(f32[2,5,128,128,8]{3,2,4,1,0:T(8,128)S(1)} %get-tuple-element.26, f32[2,8,128]{2,1,0:T(8,128)S(1)} %get-tuple-element.25, pred[128,5,128]{0,2,1:T(8,128)(4,1)S(1)} %copy-done.7, f32[128,2,8]{0,2,1:T(8,128)S(1)} %bitcast.152, bf16[5,2,128,128]{2,3,0,1:T(8,128)(2,1)S(1)} %copy-done.14), kind=kOutput, calls=%fused_computation.25 | convolution fusion | flops 342622208 | bytes 6193152 | tf_op jit(solution)/shard_map/kgtbs,bksd->tkgd/dot_general | solution.py:148
  73.0 1.0 %copy.51 = bf16[128,2048]{1,0:T(8,128)(2,1)} copy(bf16[128,2048]{0,1:T(8,128)(2,1)S(1)} %bitcast.151) | data formatting | bytes 1048576
  74.0 1.1 %multiply_convert_fusion = bf16[128,2048]{1,0:T(8,128)(2,1)} fusion(bf16[128,2048]{1,0:T(8,128)(2,1)S(1)} %copy-done.11, f32[128,2048]{1,0:T(8,128)S(1)} %copy.46, f32[2048]{0:T(1024)S(1)} %copy-done.15, f32[128]{0:T(128)S(1)} %add_rsqrt_fusion), kind=kLoop, calls=%fused_computation.26 | loop fusion | flops 2097152 | bytes 2105856 | tf_op jit(solution)/shard_map/convert_element_type | solution.py:136
  (51 shorter events, 0.3 us)
Async XLA Ops:
  0.6 47.7 %copy-start = (bf16[128,2048]{1,0:T(8,128)(2,1)S(1)}, bf16[128,2048]{1,0:T(8,128)(2,1)}, u32[]{:S(2)}) copy-start(bf16[128,2048]{1,0:T(8,128)(2,1)} %param.11) | copy-start | bytes 1572868
  0.6 7.1 %copy-start.16 = (f32[16,128]{1,0:T(8,128)S(1)}, f32[16,128]{1,0:T(8,128)}, u32[]{:S(2)}) copy-start(f32[16,128]{1,0:T(8,128)} %param.14) | copy-start | bytes 24580
  0.7 7.7 %copy-start.12 = (bf16[128,2048]{1,0:T(8,128)(2,1)S(1)}, bf16[128,2048]{1,0:T(8,128)(2,1)}, u32[]{:S(2)}) copy-start(bf16[128,2048]{1,0:T(8,128)(2,1)} %param.13) | copy-start | bytes 1572868
  7.8 2.0 %copy-start.5 = (bf16[128,2048]{0,1:T(8,128)(2,1)}, bf16[128,2048]{0,1:T(8,128)(2,1)S(1)}, u32[]{:S(2)}) copy-start(bf16[128,2048]{0,1:T(8,128)(2,1)S(1)} %copy.63) | copy-start | bytes 1572868
  9.8 3.5 %collective-permute-start = (f32[2568,128]{1,0:T(8,128)}, f32[2568,128]{1,0:T(8,128)}, u32[]{:S(2)}, u32[]{:S(2)}) collective-permute-start(f32[2568,128]{1,0:T(8,128)} %fusion.15), channel_id=1, source_target_pairs={{0,4},{4,0},{8,12},{12,8},{16,20},{20,16},{24,28},{28,24},{1,5},{5... | collective-permute-start | bytes 3944456 | tf_op jit(solution)/shard_map/ppermute | solution.py:77
  15.7 0.6 copy-start.8
  18.9 8.2 %collective-permute-start.1 = (bf16[3088,128]{1,0:T(8,128)(2,1)}, bf16[3088,128]{1,0:T(8,128)(2,1)}, u32[]{:S(2)}, u32[]{:S(2)}) collective-permute-start(bf16[3088,128]{1,0:T(8,128)(2,1)} %pad_maximum_fusion.1), channel_id=1, source_target_pairs={{4,8},{12,16},{20,24},{5,9},{13,17},{21,25},{6,10},{14,18},{22,26}... | collective-permute-start | bytes 2371592 | tf_op jit(solution)/shard_map/ppermute | solution.py:95
  20.4 21.9 %collective-permute-start.2 = (bf16[3088,128]{1,0:T(8,128)(2,1)}, bf16[3088,128]{1,0:T(8,128)(2,1)S(1)}, u32[]{:S(2)}, u32[]{:S(2)}) collective-permute-start(bf16[3088,128]{1,0:T(8,128)(2,1)} %pad_maximum_fusion.1), channel_id=1, source_target_pairs={{0,16},{8,24},{1,17},{9,25},{2,18},{10,26},{3,19},{11,27}} | collective-permute-start | bytes 2371592 | tf_op jit(solution)/shard_map/ppermute | solution.py:96
  28.0 17.1 %copy-start.2 = (bf16[1024,128]{1,0:T(8,128)(2,1)}, bf16[1024,128]{1,0:T(8,128)(2,1)S(1)}, u32[]{:S(2)}) copy-start(bf16[1024,128]{1,0:T(8,128)(2,1)S(1)} %slice.87) | copy-start | bytes 786436
  42.3 7.7 %copy-start.1 = (bf16[3088,128]{1,0:T(8,128)(2,1)}, bf16[3088,128]{1,0:T(8,128)(2,1)S(1)}, u32[]{:S(2)}) copy-start(bf16[3088,128]{1,0:T(8,128)(2,1)S(1)} %collective-permute-done.2) | copy-start | bytes 2371588
  44.1 4.3 %copy-start.6 = (bf16[128,2048]{0,1:T(8,128)(2,1)S(1)}, bf16[128,2048]{0,1:T(8,128)(2,1)}, u32[]{:S(2)}) copy-start(bf16[128,2048]{0,1:T(8,128)(2,1)} %copy-done.5) | copy-start | bytes 1572868
  44.1 4.3 %copy-start.13 = (bf16[128,2048]{1,0:T(8,128)(2,1)S(1)}, bf16[128,2048]{1,0:T(8,128)(2,1)}, u32[]{:S(2)}) copy-start(bf16[128,2048]{1,0:T(8,128)(2,1)} %param.13) | copy-start | bytes 1572868
  45.1 6.1 %collective-permute-start.3 = (bf16[3584,128]{1,0:T(8,128)(2,1)}, bf16[3584,128]{1,0:T(8,128)(2,1)}, u32[]{:S(2)}, u32[]{:S(2)}) collective-permute-start(bf16[3584,128]{1,0:T(8,128)(2,1)} %pad_maximum_fusion), channel_id=1, source_target_pairs={{0,4},{8,12},{16,20},{24,28},{1,5},{9,13},{17,21},{25,29},{2,6},{1... | collective-permute-start | bytes 2752520 | tf_op jit(solution)/shard_map/ppermute | solution.py:114
  50.1 2.3 %copy-start.10 = (f32[128,16,128]{0,2,1:T(8,128)S(1)}, f32[128,16,128]{0,2,1:T(8,128)}, u32[]{:S(2)}) copy-start(f32[128,16,128]{0,2,1:T(8,128)} %convolution_bitcast_fusion.1) | copy-start | bytes 3145732
  50.1 2.3 %slice-start.1 = ((bf16[3088,128]{1,0:T(8,128)(2,1)}), bf16[2048,128]{1,0:T(8,128)(2,1)S(1)}, s32[]{:S(2)}) async-start(bf16[3088,128]{1,0:T(8,128)(2,1)} %copy-done.1), calls=%async_computation.1 | async-start | bytes 1048576 | tf_op jit(solution)/shard_map/slice | solution.py:99
  53.1 13.5 %slice-start = ((bf16[3088,128]{1,0:T(8,128)(2,1)}), bf16[1024,128]{1,0:T(8,128)(2,1)S(1)}, s32[]{:S(2)}) async-start(bf16[3088,128]{1,0:T(8,128)(2,1)} %copy-done.1), calls=%async_computation | async-start | bytes 524288 | tf_op jit(solution)/shard_map/slice | solution.py:103
  53.1 13.5 %copy-start.3 = (bf16[1024,128]{1,0:T(8,128)(2,1)S(1)}, bf16[1024,128]{1,0:T(8,128)(2,1)}, u32[]{:S(2)}) copy-start(bf16[1024,128]{1,0:T(8,128)(2,1)} %copy-done.2) | copy-start | bytes 786436
  53.1 13.5 %copy-start.9 = (bf16[512,128]{1,0:T(8,128)(2,1)S(1)}, bf16[512,128]{1,0:T(8,128)(2,1)}, u32[]{:S(2)}) copy-start(bf16[512,128]{1,0:T(8,128)(2,1)} %copy-done.8) | copy-start | bytes 393220
  66.7 2.7 %copy-start.4 = (bf16[16,8,16,128]{3,2,1,0:T(8,128)(2,1)S(1)}, bf16[16,8,16,128]{3,2,1,0:T(8,128)(2,1)}, u32[]{:S(2)}) copy-start(bf16[16,8,16,128]{3,2,1,0:T(8,128)(2,1)} %copy.68) | copy-start | bytes 1572868
  66.7 2.7 %copy-start.7 = (pred[128,5,128]{0,2,1:T(8,128)(4,1)S(1)}, pred[128,5,128]{0,2,1:T(8,128)(4,1)}, u32[]{:S(2)}) copy-start(pred[128,5,128]{0,2,1:T(8,128)(4,1)} %compare_and_fusion) | copy-start | bytes 245764
  70.4 1.2 %copy-start.14 = (bf16[5,2,128,128]{2,3,0,1:T(8,128)(2,1)S(1)}, bf16[5,2,128,128]{2,3,0,1:T(8,128)(2,1)}, u32[]{:S(2)}) copy-start(bf16[5,2,128,128]{2,3,0,1:T(8,128)(2,1)} %copy.61) | copy-start | bytes 983044
  71.6 2.4 %copy-start.11 = (bf16[128,2048]{1,0:T(8,128)(2,1)S(1)}, bf16[128,2048]{1,0:T(8,128)(2,1)}, u32[]{:S(2)}) copy-start(bf16[128,2048]{1,0:T(8,128)(2,1)} %param.15) | copy-start | bytes 1572868
  71.6 2.4 %copy-start.15 = (f32[2048]{0:T(1024)S(1)}, f32[2048]{0:T(1024)}, u32[]{:S(2)}) copy-start(f32[2048]{0:T(1024)} %param.16) | copy-start | bytes 24580

commit v5 on v3

--- a/solution.py
+++ b/solution.py
@@ -78,22 +78,27 @@
     state_mate = got[:n_state]
     factor_mate = got[n_state, :heads_here]
     pair_mate = got[n_state + 8 :].astype(jnp.bfloat16)
-    state_lo = jnp.where(odd, state_mate, state_rows).reshape(state.shape)
-    state_hi = jnp.where(odd, state_rows, state_mate).reshape(state.shape)
-    factor_lo = jnp.where(odd, factor_mate, shrinkage_multiplier)
-    factor_hi = jnp.where(odd, shrinkage_multiplier, factor_mate)
+    state_cube = state_rows.reshape(state.shape)
+    mate_cube = state_mate.reshape(state.shape)
+    chip_state = jnp.where(
+        odd,
+        shrinkage_multiplier[:, None, None] * mate_cube + state_cube,
+        factor_mate[:, None, None] * state_cube + mate_cube,
+    )
+    chip_factor = shrinkage_multiplier * factor_mate
     pair_lo = jnp.where(odd, pair_mate, pair)
     pair_hi = jnp.where(odd, pair, pair_mate)
-    chip_state = factor_hi[:, None, None] * state_lo + state_hi
-    chip_factor = factor_hi * factor_lo
     chip_top = chip_factor.astype(jnp.bfloat16)
     chip_rest = (chip_factor - chip_top.astype(jnp.float32)).astype(jnp.bfloat16)
     chip_rows = jnp.pad(jnp.stack([chip_top, chip_rest]), ((0, 14), (0, DH - heads_here)))
     packet = jnp.concatenate(
         [chip_state.astype(jnp.bfloat16).reshape(n_state, DH), chip_rows, pair_lo, pair_hi], axis=0
     )
-    near = lax.ppermute(packet, "ctx", [(i, i + 1) for i in range(1, count - 1, 2)])
-    far = lax.ppermute(packet, "ctx", [(i, i + 4) for i in range(0, count - 4, 2)])
+    routes = [(i, i + 1) for i in range(1, count - 1, 2)] + [(i, i + 5) for i in range(0, count - 5, 2)]
+    received = lax.ppermute(packet, "ctx", routes)
+    mate_packet = lax.ppermute(received, "ctx", [(i, i ^ 1) for i in range(count)])
+    near = jnp.where(odd, mate_packet, received)
+    far = jnp.where(odd, received, mate_packet)
 
     def unpack(got_packet):
         chip = got_packet[:n_state].reshape(state.shape).astype(jnp.float32)
@@ -107,15 +112,10 @@
     state_near, factor_near, near_lo, near_hi = unpack(near)
     state_far, _, far_lo, far_hi = unpack(far)
     incoming_even = state_near + factor_near[:, None, None] * state_far
-    onward = shrinkage_multiplier[:, None, None] * incoming_even + state
-    fourth = jnp.concatenate(
-        [onward.astype(jnp.bfloat16).reshape(n_state, DH), far_hi, near_lo, near_hi], axis=0
-    )
-    back = lax.ppermute(fourth, "ctx", [(i, i + 1) for i in range(0, count, 2)])
-    incoming_odd = back[:n_state].reshape(state.shape)
-    incoming_b = jnp.where(odd, incoming_odd, incoming_even.astype(jnp.bfloat16))
+    incoming = jnp.where(odd, factor_mate[:, None, None] * incoming_even + mate_cube, incoming_even)
+    incoming_b = incoming.astype(jnp.bfloat16)
     window_even = jnp.concatenate([far_lo, far_hi, near_lo, near_hi], axis=0)
-    window_odd = jnp.concatenate([back[n_state:], pair_mate], axis=0)
+    window_odd = jnp.concatenate([far_hi, near_lo, near_hi, pair_mate], axis=0)
     window = jnp.concatenate([jnp.where(odd, window_odd, window_even), pair], axis=0)
     window = window.reshape(SPAN + 1, 2 * kv_here, rows, DH)
     outer = jnp.einsum(

time: 70.2 us -> 63.4 us (0.903)
  other arithmetic: 16.7 us -> 12.8 us
  local copies, waits for them, and re-layouts: 12.6 us -> 8.98 us
  starting transfers between devices: 13.6 us -> 10.5 us
  waiting for transfers between devices: 17.4 us -> 20.2 us
  matrix products: 6.51 us -> 7.84 us
    ppermute x3 -> x2, starting transfers between devices: 8.39 us -> 5.42 us  [the longest x1 5.42 us: local(): received = lax.ppermute(packet, 'ctx', routes)]
    ppermute x3 -> x2, waiting for transfers between devices: 14.6 us -> 17.3 us  [the longest x1 17.3 us: local(): received = lax.ppermute(packet, 'ctx', routes)]
    unnamed x53 -> x37, local copies, waits for them, and re-layouts: 5.72 us -> 3.39 us
    convert_element_type x1, other arithmetic: 1.56 us -> 0.28 us  [local(): chip_state.astype(jnp.bfloat16).reshape(n_state, DH)]
    slice x2, local copies, waits for them, and re-layouts: 2.2 us -> 1.03 us  [local(): state_mate = got[:n_state]]
    convert_element_type x2 -> x0, other arithmetic: 1.11 us -> none  [the longest x1 1.11 us: local(): onward.astype(jnp.bfloat16).reshape(n_state, DH)]
    concatenate x1, other arithmetic: 0.09 us -> 1.15 us  [local(): jnp.concatenate([state_rows, factor_rows, pair.astype(jnp.float32)], axis=0)]
    concatenate x1 -> x0, other arithmetic: 1.01 us -> none  [local(): jnp.concatenate([onward.astype(jnp.bfloat16).reshape(n_state, DH), far_hi...]
  transfers between devices with their start and end apart: 7 -> 6, of which waited for: 2 -> 2; matrix products, arithmetic and copies ran while one was open for 22% -> 21% of each run, Pallas kernels for 0% -> 0%
where the time goes in v5:
time: 63.4 us; the launch traced here: 62.7 us
  waiting for transfers between devices  20.2 us (32%)
  other arithmetic  12.8 us (20%)
  starting transfers between devices  10.5 us (17%)
  local copies, waits for them, and re-layouts  8.98 us (14%)
  matrix products  7.84 us (12%)
  between operations  2.36 us (4%)
    ppermute x1, waiting for transfers between devices, local(): received = lax.ppermute(packet, 'ctx', routes)  17.3 us
    ppermute x1, starting transfers between devices, local(): received = lax.ppermute(packet, 'ctx', routes)  5.42 us
    ppermute x3, starting transfers between devices, all_sum(): lax.ppermute(x, axis, [(i, (i + by) % count) for i in range(count)])  4.67 us
    unnamed x37, local copies, waits for them, and re-layouts  3.39 us
    ppermute x1, waiting for transfers between devices, local(): got = lax.ppermute(first, 'ctx', [(i, i ^ 1) for i in range(count)])  2.87 us
    dot_general x1, matrix products, block_terms(): jnp.einsum('hts,shd->thd', weights, values, preferred_element_type=jnp.fl...  2.74 us
    dot_general x1, matrix products, local(): jnp.einsum('kgtbs,bksd->tkgd', expd.astype(jnp.bfloat16).reshape(kv_here,...  2.18 us
    dot_general x1, matrix products, local(): jnp.einsum('tkgd,bksd->kgtbs', soft_query, window[:, :kv_here], preferred...  1.87 us
  transfers between devices with their start and end apart: 6, of which 2 were waited for; matrix products, arithmetic and copies ran while one was open for 21% of the time, Pallas kernels for 0%

profile of v5, /device:TPU:0, one launch (start us, length us, event | category | flops | bytes accessed | tf_op | source)
XLA Modules:
  0.0 62.7 jit_solution(15216432347909965182)
XLA Ops:
  0.6 0.0 copy-start
  0.7 0.0 copy-start.10
  0.7 0.9 %reduce-window.4 = s32[6,1]{0,1:T(1,128)S(1)} reduce-window(s32[6,1]{0,1:T(1,128)} %bitcast.165, s32[]{:T(128)} %constant.61.clone.1), window={size=6x1 pad=5_0x0_0}, to_apply=%region_0.0 | reduce-window | flops 30 | bytes 52 | tf_op jit(solution)/shard_map/reduce-window
  1.6 0.6 %fusion.53 = s32[]{:T(128)} fusion(s32[6,1]{0,1:T(1,128)S(1)} %reduce-window.4, s32[]{:T(128)} %bitcast.6), kind=kLoop, calls=%fused_computation.95 | loop fusion | flops 17 | bytes 32 | tf_op jit(solution)/shard_map/reduce_sum | solution.py:29
  2.3 0.1 convert_reduce_fusion.1
  2.4 0.6 slice.55
  3.6 0.7 %fusion.62 = (f32[128]{0:T(128)S(1)}, pred[128]{0:T(512)(128)(4,1)S(1)}, f32[128]{0:T(128)S(1)}) fusion(s32[128]{0:T(128)S(1)} %convert_reduce_fusion.1, s32[]{:T(128)S(6)} %select_n.104, s32[]{:T(128)} %bitcast.3), kind=kLoop, calls=%fused_computation.114 | loop fusion | flops 512 | bytes 1672 | tf_op jit(solution)/shard_map/convert_element_type | solution.py:124
  4.3 0.6 slice.57
  5.5 0.9 %bitcast_bitcast_fusion = (bf16[2,128,128]{2,1,0:T(8,128)(2,1)S(1)}, bf16[2,128,128]{2,1,0:T(8,128)(2,1)S(1)}) fusion(bf16[128,256]{1,0:T(8,128)(2,1)} %param.18, bf16[128,256]{1,0:T(8,128)(2,1)} %param.19), kind=kLoop, calls=%fused_computation.66 | loop fusion | bytes 262144 | tf_op jit(solution)/shard_map/transpose | solution.py:69
  6.5 1.3 %copy.63 = bf16[128,2048]{0,1:T(8,128)(2,1)S(1)} copy(bf16[128,2048]{1,0:T(8,128)(2,1)} %param.12) | data formatting | bytes 1048576 | tf_op jit(solution)/shard_map/reshape | solution.py:60
  7.8 0.0 copy-start.2
  7.8 0.3 reduce_window_sum.20
  8.1 0.2 slice_reduce_fusion
  8.3 0.6 multiply_bitcast_fusion
  8.9 0.3 fusion.24
  9.2 1.1 %fusion.15 = f32[2568,128]{1,0:T(8,128)} fusion(f32[1,16]{1,0:T(1,128)S(1)} %bitcast.158, f32[512,128]{1,0:T(8,128)S(1)} %bitcast_convert_fusion, f32[2048,128]{1,0:T(8,128)S(1)} %bitcast.144), kind=kLoop, calls=%fused_computation.21 | loop fusion | flops 1972224 | bytes 2625600 | tf_op jit(solution)/shard_map/concatenate | solution.py:76
  10.4 0.5 collective-permute-start
  10.8 2.9 %collective-permute-done = f32[2568,128]{1,0:T(8,128)S(1)} collective-permute-done((f32[2568,128]{1,0:T(8,128)}, f32[2568,128]{1,0:T(8,128)S(1)}, u32[]{:S(2)}, u32[]{:S(2)}) %collective-permute-start) | collective-permute-done | bytes 1314848 | tf_op jit(solution)/shard_map/ppermute | solution.py:77
  13.7 0.0 copy-start.5
  13.8 0.6 copy-done.5
  14.4 0.3 select_convert_fusion.1
  14.7 0.0 copy-start.9
  14.7 0.9 %pad_maximum_fusion = bf16[3088,128]{1,0:T(8,128)(2,1)} fusion(bf16[512,128]{1,0:T(8,128)(2,1)S(1)} %broadcast_select_fusion.2, bf16[512,128]{1,0:T(8,128)(2,1)S(1)} %get-tuple-element.12, bf16[16,128]{1,0:T(8,128)(2,1)S(1)} %fusion.52, bf16[2048,128]{1,0:T(8,128)(2,1)S(1)} %bitcast.152), kind=kLoop, calls=%fused_computation.35 | loop fusion | flops 3162112 | bytes 1581056 | tf_op jit(solution)/shard_map/concatenate | solution.py:94
  15.7 5.4 %collective-permute-start.1 = (bf16[3088,128]{1,0:T(8,128)(2,1)}, bf16[3088,128]{1,0:T(8,128)(2,1)}, u32[]{:S(2)}, u32[]{:S(2)}) collective-permute-start(bf16[3088,128]{1,0:T(8,128)(2,1)} %pad_maximum_fusion), channel_id=1, source_target_pairs={{4,8},{12,16},{20,24},{0,20},{8,28},{5,9},{13,17},{21,25},{1,21},{... | collective-permute-start | bytes 2371592 | tf_op jit(solution)/shard_map/ppermute | solution.py:98
  21.1 0.1 convert_reduce_fusion
  21.2 17.3 %collective-permute-done.1 = bf16[3088,128]{1,0:T(8,128)(2,1)} collective-permute-done((bf16[3088,128]{1,0:T(8,128)(2,1)}, bf16[3088,128]{1,0:T(8,128)(2,1)}, u32[]{:S(2)}, u32[]{:S(2)}) %collective-permute-start.1) | collective-permute-done | bytes 790560 | tf_op jit(solution)/shard_map/ppermute | solution.py:98
  38.6 0.6 pad_clamp_fusion
  39.1 0.1 copy.68
  39.3 0.1 fusion.46
  39.4 1.5 %compare_and_fusion = pred[128,5,128]{0,2,1:T(8,128)(4,1)} fusion(s32[128]{0:T(128)} %copy-done.16, s32[5,128]{1,0:T(8,128)S(1)} %get-tuple-element.31, s32[128]{0:T(128)S(1)} %convert_reduce_fusion.1, s32[5,128]{1,0:T(8,128)S(1)} %get-tuple-element.30), kind=kLoop, calls=%fused_computation.61 | loop fusion | flops 245760 | bytes 88064 | tf_op jit(solution)/shard_map/and | solution.py:140
  40.8 2.7 %convolution_bitcast_fusion.1 = f32[128,16,128]{0,2,1:T(8,128)} fusion(bf16[128,16,128]{0,2,1:T(8,128)(2,1)S(1)} %bitcast.154, f32[16,128]{1,0:T(8,128)S(1)} %reduce_window_sum.20, pred[128,128]{1,0:T(8,128)(4,1)S(1)} %fusion.46, bf16[128,2048]{1,0:T(8,128)(2,1)} %param.13, bf16[128,2048]{1,0:T(8,128)(2,1)S(1)} %copy-done), kind=kOutput, calls=%fused_computation.17 | convolution fusion | flops 135528448 | bytes 2646016 | tf_op jit(solution)/shard_map/hts,shd->thd/dot_general | solution.py:40
  43.6 1.5 %broadcast_select_fusion.1 = (bf16[3088,128]{1,0:T(8,128)(2,1)S(1)}, bf16[3088,128]{1,0:T(8,128)(2,1)S(1)}) fusion(bf16[3088,128]{1,0:T(8,128)(2,1)} %collective-permute-done.2, bf16[3088,128]{1,0:T(8,128)(2,1)} %collective-permute-done.1, pred[]{:T(512)S(6)} %eq.61), kind=kLoop, calls=%fused_computation.37 | loop fusion | flops 790528 | bytes 3162113 | tf_op jit(solution)/shard_map/jit(_where)/select_n | solution.py:100
  45.3 1.0 %slice-done = f32[2048,128]{1,0:T(8,128)S(1)} async-done(((f32[2568,128]{1,0:T(8,128)}), f32[2048,128]{1,0:T(8,128)S(1)}, s32[]{:S(2)}) %slice-start) | async-done | bytes 1048600 | tf_op jit(solution)/shard_map/slice | solution.py:78
  46.3 0.3 copy-done.7
  46.6 0.7 %multiply_reduce_fusion = (f32[128]{0:T(128)S(1)}, f32[128,16,128]{0,2,1:T(8,128)S(1)}) fusion(f32[128,16,128]{0,2,1:T(8,128)S(1)} %copy-done.7, f32[128,16]{0,1:T(8,128)S(1)} %copy-done.11, f32[16,128,128]{2,1,0:T(8,128)S(1)} %bitcast.146, bf16[16,128,128]{2,1,0:T(8,128)(2,1)S(1)} %bitcast.151, bf16[16,128,128]{2,1,0:T(8,128)(2,1)S(1)} %bitcast.150, ...), kind=kOutput, calls=%fused_computation.28 | convolution fusion | flops 70254464 | bytes 4727425 | tf_op jit(solution)/shard_map/thd,hde->the/dot_general | solution.py:121
  47.4 3.7 %collective-permute-start.5 = (f32[128]{0:T(128)S(1)}, f32[128]{0:T(128)S(1)}, u32[]{:S(2)}, u32[]{:S(2)}) collective-permute-start(f32[128]{0:T(128)S(1)} %get-tuple-element.24), channel_id=1, source_target_pairs={{0,3},{1,0},{2,1},{3,2},{4,7},{5,4},{6,5},{7,6},{8,11},{9,8},{10,9... | collective-permute-start | bytes 1544 | tf_op jit(solution)/shard_map/ppermute | solution.py:21
  51.0 1.0 %collective-permute-start.3 = (f32[128]{0:T(128)S(1)}, f32[128]{0:T(128)}, u32[]{:S(2)}, u32[]{:S(2)}) collective-permute-start(f32[128]{0:T(128)S(1)} %get-tuple-element.24), channel_id=1, source_target_pairs={{0,1},{1,2},{2,3},{3,0},{4,5},{5,6},{6,7},{7,4},{8,9},{9,10},{10,1... | collective-permute-start | bytes 1544 | tf_op jit(solution)/shard_map/ppermute | solution.py:21
  52.0 0.1 maximum_select_fusion
  52.2 0.1 fusion.63
  52.3 0.2 copy.61
  52.5 1.9 %fusion = (f32[2,8,128]{2,1,0:T(8,128)S(1)}, f32[2,5,128,128,8]{3,2,4,1,0:T(8,128)S(1)}) fusion(pred[128,5,128]{0,2,1:T(8,128)(4,1)} %compare_and_fusion, bf16[128,2,8,128,1]{3,2,1,0,4:T(8,128)(2,1)S(1)} %bitcast.149, bf16[5,2,128,128]{3,2,1,0:T(8,128)(2,1)S(1)} %get-tuple-element.20), kind=kOutput, calls=%fused_computation.3 | convolution fusion | flops 339474432 | bytes 6184960 | tf_op jit(solution)/shard_map/tkgd,bksd->kgtbs/dot_general | solution.py:142
  54.4 1.2 %fusion.4 = f32[2,8,128]{2,1,0:T(8,128)S(1)} fusion(f32[2,5,128,128,8]{3,2,4,1,0:T(8,128)S(1)} %get-tuple-element.27, f32[2,8,128]{2,1,0:T(8,128)S(1)} %get-tuple-element.26, pred[128,5,128]{0,2,1:T(8,128)(4,1)S(1)} %copy-done.4), kind=kLoop, calls=%fused_computation.7 | loop fusion | flops 6551552 | bytes 5341184 | tf_op jit(solution)/shard_map/reduce_sum | solution.py:147
  55.7 2.2 %divide_convert_fusion = bf16[128,2,8,128]{0,3,2,1:T(8,128)(2,1)} fusion(f32[2,5,128,128,8]{3,2,4,1,0:T(8,128)S(1)} %get-tuple-element.27, f32[2,8,128]{2,1,0:T(8,128)S(1)} %get-tuple-element.26, pred[128,5,128]{0,2,1:T(8,128)(4,1)S(1)} %copy-done.4, f32[128,2,8]{0,2,1:T(8,128)S(1)} %bitcast.157, bf16[5,2,128,128]{2,3,0,1:T(8,128)(2,1)S(1)} %copy.61), kind=kOutput, calls=%fused_computation.26 | convolution fusion | flops 342622208 | bytes 6193152 | tf_op jit(solution)/shard_map/kgtbs,bksd->tkgd/dot_general | solution.py:148
  57.8 0.3 copy.46
  58.2 2.0 %copy.51 = bf16[128,2048]{1,0:T(8,128)(2,1)} copy(bf16[128,2048]{0,1:T(8,128)(2,1)} %bitcast.156) | data formatting | bytes 1048576
  60.2 0.7 %pad_maximum_fusion.3 = f32[4,128]{1,0:T(4,128)S(1)} fusion(f32[1,128]{1,0:T(1,128)S(1)} %bitcast.163, f32[1,128]{1,0:T(1,128)S(1)} %bitcast.164, f32[1,128]{1,0:T(1,128)} %bitcast.21, f32[1,128]{1,0:T(1,128)S(1)} %bitcast.159), kind=kLoop, calls=%fused_computation.91 | loop fusion | flops 1536 | bytes 4096 | tf_op jit(solution)/shard_map/stack | solution.py:22
  60.9 0.7 %gather_fusion = f32[4,128]{1,0:T(4,128)S(1)} fusion(f32[4,128]{1,0:T(4,128)S(1)} %pad_maximum_fusion.3, s32[1024]{0:T(1024)} %pad_clamp_fusion), kind=kCustom, calls=%fused_computation | custom fusion | bytes 4112 | tf_op jit(solution)/shard_map/gather | solution.py:24
  61.6 1.1 %multiply_convert_fusion = bf16[128,2048]{1,0:T(8,128)(2,1)} fusion(bf16[128,2048]{1,0:T(8,128)(2,1)S(1)} %copy-done.8, f32[128,2048]{1,0:T(8,128)S(1)} %copy.46, f32[2048]{0:T(1024)S(1)} %copy-done.12, f32[128]{0:T(128)S(1)} %add_rsqrt_fusion), kind=kLoop, calls=%fused_computation.27 | loop fusion | flops 2097152 | bytes 2105856 | tf_op jit(solution)/shard_map/convert_element_type | solution.py:136
  (54 shorter events, 0.4 us)
Async XLA Ops:
  0.6 40.2 %copy-start = (bf16[128,2048]{1,0:T(8,128)(2,1)S(1)}, bf16[128,2048]{1,0:T(8,128)(2,1)}, u32[]{:S(2)}) copy-start(bf16[128,2048]{1,0:T(8,128)(2,1)} %param.11) | copy-start | bytes 1572868
  0.6 7.1 %copy-start.13 = (f32[16,128]{1,0:T(8,128)S(1)}, f32[16,128]{1,0:T(8,128)}, u32[]{:S(2)}) copy-start(f32[16,128]{1,0:T(8,128)} %param.14) | copy-start | bytes 24580
  0.7 8.2 %copy-start.10 = (bf16[128,2048]{1,0:T(8,128)(2,1)S(1)}, bf16[128,2048]{1,0:T(8,128)(2,1)}, u32[]{:S(2)}) copy-start(bf16[128,2048]{1,0:T(8,128)(2,1)} %param.13) | copy-start | bytes 1572868
  0.7 2.9 %copy-start.16 = (s32[128]{0:T(128)}, s32[128]{0:T(128)S(1)}, u32[]{:S(2)}) copy-start(s32[128]{0:T(128)S(1)} %iota_add_fusion.1) | copy-start | bytes 1540
  7.8 1.4 %copy-start.2 = (bf16[128,2048]{0,1:T(8,128)(2,1)}, bf16[128,2048]{0,1:T(8,128)(2,1)S(1)}, u32[]{:S(2)}) copy-start(bf16[128,2048]{0,1:T(8,128)(2,1)S(1)} %copy.63) | copy-start | bytes 1572868
  10.4 3.3 %collective-permute-start = (f32[2568,128]{1,0:T(8,128)}, f32[2568,128]{1,0:T(8,128)S(1)}, u32[]{:S(2)}, u32[]{:S(2)}) collective-permute-start(f32[2568,128]{1,0:T(8,128)} %fusion.15), channel_id=1, source_target_pairs={{0,4},{4,0},{8,12},{12,8},{16,20},{20,16},{24,28},{28,24},{1,5},{5... | collective-permute-start | bytes 3944456 | tf_op jit(solution)/shard_map/ppermute | solution.py:77
  13.7 29.9 %copy-start.1 = (f32[2568,128]{1,0:T(8,128)}, f32[2568,128]{1,0:T(8,128)S(1)}, u32[]{:S(2)}) copy-start(f32[2568,128]{1,0:T(8,128)S(1)} %collective-permute-done) | copy-start | bytes 3944452
  13.7 0.7 %copy-start.5 = (bf16[512,128]{1,0:T(8,128)(2,1)}, bf16[512,128]{1,0:T(8,128)(2,1)S(1)}, u32[]{:S(2)}) copy-start(bf16[512,128]{1,0:T(8,128)(2,1)S(1)} %get-tuple-element.13) | copy-start | bytes 393220
  13.8 1.9 %copy-start.14 = (f32[16]{0:T(128)}, f32[16]{0:T(128)S(1)}, u32[]{:S(2)}) copy-start(f32[16]{0:T(128)S(1)} %get-tuple-element.18) | copy-start | bytes 196
  14.7 24.4 %copy-start.9 = (bf16[128,2048]{1,0:T(8,128)(2,1)S(1)}, bf16[128,2048]{1,0:T(8,128)(2,1)}, u32[]{:S(2)}) copy-start(bf16[128,2048]{1,0:T(8,128)(2,1)} %param.17) | copy-start | bytes 1572868
  14.7 26.1 %copy-start.3 = (bf16[128,2048]{0,1:T(8,128)(2,1)S(1)}, bf16[128,2048]{0,1:T(8,128)(2,1)}, u32[]{:S(2)}) copy-start(bf16[128,2048]{0,1:T(8,128)(2,1)} %copy-done.2) | copy-start | bytes 1572868
  15.7 22.9 %collective-permute-start.1 = (bf16[3088,128]{1,0:T(8,128)(2,1)}, bf16[3088,128]{1,0:T(8,128)(2,1)}, u32[]{:S(2)}, u32[]{:S(2)}) collective-permute-start(bf16[3088,128]{1,0:T(8,128)(2,1)} %pad_maximum_fusion), channel_id=1, source_target_pairs={{4,8},{12,16},{20,24},{0,20},{8,28},{5,9},{13,17},{21,25},{1,21},{... | collective-permute-start | bytes 2371592 | tf_op jit(solution)/shard_map/ppermute | solution.py:98
  38.5 5.0 %collective-permute-start.2 = (bf16[3088,128]{1,0:T(8,128)(2,1)}, bf16[3088,128]{1,0:T(8,128)(2,1)}, u32[]{:S(2)}, u32[]{:S(2)}) collective-permute-start(bf16[3088,128]{1,0:T(8,128)(2,1)} %collective-permute-done.1), channel_id=1, source_target_pairs={{0,4},{4,0},{8,12},{12,8},{16,20},{20,16},{24,28},{28,24},{1,5},{5... | collective-permute-start | bytes 2371592 | tf_op jit(solution)/shard_map/ppermute | solution.py:99
  45.1 1.2 %slice-start = ((f32[2568,128]{1,0:T(8,128)}), f32[2048,128]{1,0:T(8,128)S(1)}, s32[]{:S(2)}) async-start(f32[2568,128]{1,0:T(8,128)} %copy-done.1), calls=%async_computation | async-start | bytes 2097152 | tf_op jit(solution)/shard_map/slice | solution.py:78
  45.1 1.5 %copy-start.7 = (f32[128,16,128]{0,2,1:T(8,128)S(1)}, f32[128,16,128]{0,2,1:T(8,128)}, u32[]{:S(2)}) copy-start(f32[128,16,128]{0,2,1:T(8,128)} %convolution_bitcast_fusion.1) | copy-start | bytes 3145732
  45.1 1.5 %copy-start.11 = (f32[128,16]{0,1:T(8,128)S(1)}, f32[128,16]{0,1:T(8,128)}, u32[]{:S(2)}) copy-start(f32[128,16]{0,1:T(8,128)} %get-tuple-element.21) | copy-start | bytes 24580
  45.1 1.5 %copy-start.15 = (f32[16]{0:T(128)S(1)}, f32[16]{0:T(128)}, u32[]{:S(2)}) copy-start(f32[16]{0:T(128)} %copy-done.14) | copy-start | bytes 196
  46.6 5.4 %copy-start.6 = (bf16[512,128]{1,0:T(8,128)(2,1)S(1)}, bf16[512,128]{1,0:T(8,128)(2,1)}, u32[]{:S(2)}) copy-start(bf16[512,128]{1,0:T(8,128)(2,1)} %copy-done.5) | copy-start | bytes 393220
  47.4 12.9 %collective-permute-start.5 = (f32[128]{0:T(128)S(1)}, f32[128]{0:T(128)S(1)}, u32[]{:S(2)}, u32[]{:S(2)}) collective-permute-start(f32[128]{0:T(128)S(1)} %get-tuple-element.24), channel_id=1, source_target_pairs={{0,3},{1,0},{2,1},{3,2},{4,7},{5,4},{6,5},{7,6},{8,11},{9,8},{10,9... | collective-permute-start | bytes 1544 | tf_op jit(solution)/shard_map/ppermute | solution.py:21
  51.0 9.2 %collective-permute-start.4 = (f32[128]{0:T(128)S(1)}, f32[128]{0:T(128)S(1)}, u32[]{:S(2)}, u32[]{:S(2)}) collective-permute-start(f32[128]{0:T(128)S(1)} %get-tuple-element.24), channel_id=1, source_target_pairs={{0,2},{1,3},{2,0},{3,1},{4,6},{5,7},{6,4},{7,5},{8,10},{9,11},{10,... | collective-permute-start | bytes 1544 | tf_op jit(solution)/shard_map/ppermute | solution.py:21
  51.0 9.2 %collective-permute-start.3 = (f32[128]{0:T(128)S(1)}, f32[128]{0:T(128)}, u32[]{:S(2)}, u32[]{:S(2)}) collective-permute-start(f32[128]{0:T(128)S(1)} %get-tuple-element.24), channel_id=1, source_target_pairs={{0,1},{1,2},{2,3},{3,0},{4,5},{5,6},{6,7},{7,4},{8,9},{9,10},{10,1... | collective-permute-start | bytes 1544 | tf_op jit(solution)/shard_map/ppermute | solution.py:21
  52.5 1.9 %copy-start.4 = (pred[128,5,128]{0,2,1:T(8,128)(4,1)S(1)}, pred[128,5,128]{0,2,1:T(8,128)(4,1)}, u32[]{:S(2)}) copy-start(pred[128,5,128]{0,2,1:T(8,128)(4,1)} %compare_and_fusion) | copy-start | bytes 245764
  57.8 3.8 %copy-start.8 = (bf16[128,2048]{1,0:T(8,128)(2,1)S(1)}, bf16[128,2048]{1,0:T(8,128)(2,1)}, u32[]{:S(2)}) copy-start(bf16[128,2048]{1,0:T(8,128)(2,1)} %param.15) | copy-start | bytes 1572868
  57.8 3.8 %copy-start.12 = (f32[2048]{0:T(1024)S(1)}, f32[2048]{0:T(1024)}, u32[]{:S(2)}) copy-start(f32[2048]{0:T(1024)} %param.16) | copy-start | bytes 24580

commit v6 on v5

--- a/solution.py
+++ b/solution.py
@@ -15,13 +15,19 @@
 
 def all_sum(x, axis):
     count = lax.axis_size(axis)
-    me = lax.axis_index(axis)
-    parts = [x]
-    for by in range(1, count):
-        parts.append(lax.ppermute(x, axis, [(i, (i + by) % count) for i in range(count)]))
-    stacked = jnp.stack(parts)
-    order = (me - jnp.arange(count)) % count
-    return jnp.sum(stacked[order], axis=0)
+    if count & (count - 1):
+        me = lax.axis_index(axis)
+        parts = [x]
+        for by in range(1, count):
+            parts.append(lax.ppermute(x, axis, [(i, (i + by) % count) for i in range(count)]))
+        stacked = jnp.stack(parts)
+        order = (me - jnp.arange(count)) % count
+        return jnp.sum(stacked[order], axis=0)
+    bit = 1
+    while bit < count:
+        x = x + lax.ppermute(x, axis, [(i, i ^ bit) for i in range(count)])
+        bit *= 2
+    return x
 
 
 def document_of(positions, doc_lengths):

time: 63.4 us -> 63.9 us (level)
  local copies, waits for them, and re-layouts: 8.98 us -> 10.8 us
  matrix products: 7.84 us -> 9.37 us
  other arithmetic: 12.8 us -> 11.4 us
  waiting for transfers between devices: 20.2 us -> 19.3 us
    dot_general x1, matrix products: 2.18 us -> 4.66 us  [local(): jnp.einsum('kgtbs,bksd->tkgd', expd.astype(jnp.bfloat16).reshape(kv_here,...]
    unnamed x37 -> x43, local copies, waits for them, and re-layouts: 3.39 us -> 5.85 us
    dot_general x1, matrix products: 1.87 us -> 0.92 us  [local(): jnp.einsum('tkgd,bksd->kgtbs', soft_query, window[:, :kv_here], preferred...]
    concatenate x1, other arithmetic: 0.95 us -> 0.05 us  [local(): jnp.concatenate([chip_state.astype(jnp.bfloat16).reshape(n_state, DH), ch...]
    gather x1 -> x0, local copies, waits for them, and re-layouts: 0.68 us -> none  [all_sum(): return jnp.sum(stacked[order], axis=0)]
    convert_element_type x1, other arithmetic: 0.01 us -> 0.67 us  [local(): chip_top = chip_factor.astype(jnp.bfloat16)]
    another operation x2 -> x1, other arithmetic: 1.57 us -> 0.91 us
    mul x1, other arithmetic: 0.01 us -> 0.66 us  [block_terms(): jnp.exp(level[:, -1]) * carried[-1].astype(jnp.float32)]
  transfers between devices with their start and end apart: 6 -> 5, of which waited for: 2 -> 2; matrix products, arithmetic and copies ran while one was open for 21% -> 24% of each run, Pallas kernels for 0% -> 0%
where the time goes in v6:
time: 63.9 us; the launch traced here: 63.4 us
  waiting for transfers between devices  19.3 us (30%)
  other arithmetic  11.4 us (18%)
  local copies, waits for them, and re-layouts  10.8 us (17%)
  starting transfers between devices  10.2 us (16%)
  matrix products  9.37 us (15%)
  between operations  2.37 us (4%)
    ppermute x1, waiting for transfers between devices, local(): received = lax.ppermute(packet, 'ctx', routes)  17 us
    unnamed x43, local copies, waits for them, and re-layouts  5.85 us
    ppermute x1, starting transfers between devices, local(): received = lax.ppermute(packet, 'ctx', routes)  5.42 us
    dot_general x1, matrix products, local(): jnp.einsum('kgtbs,bksd->tkgd', expd.astype(jnp.bfloat16).reshape(kv_here,...  4.66 us
    ppermute x2, starting transfers between devices, all_sum(): x = x + lax.ppermute(x, axis, [(i, i ^ bit) for i in range(count)])  4.3 us
    dot_general x1, matrix products, block_terms(): jnp.einsum('hts,shd->thd', weights, values, preferred_element_type=jnp.fl...  2.75 us
    ppermute x1, waiting for transfers between devices, local(): got = lax.ppermute(first, 'ctx', [(i, i ^ 1) for i in range(count)])  2.22 us
    select_n x1, other arithmetic, local(): near = jnp.where(odd, mate_packet, received)  1.48 us
  transfers between devices with their start and end apart: 5, of which 2 were waited for; matrix products, arithmetic and copies ran while one was open for 24% of the time, Pallas kernels for 0%

profile of v6, /device:TPU:0, one launch (start us, length us, event | category | flops | bytes accessed | tf_op | source)
XLA Modules:
  0.0 63.4 jit_solution(214368057556065557)
XLA Ops:
  0.6 0.0 copy-start
  0.7 0.0 copy-start.8
  0.7 0.9 %reduce-window.4 = s32[6,1]{0,1:T(1,128)S(1)} reduce-window(s32[6,1]{0,1:T(1,128)} %bitcast.156, s32[]{:T(128)} %constant.24.clone.1), window={size=6x1 pad=5_0x0_0}, to_apply=%region_0.0 | reduce-window | flops 30 | bytes 52 | tf_op jit(solution)/shard_map/reduce-window
  1.6 0.6 fusion.53
  2.3 0.1 convert_reduce_fusion.1
  2.4 0.6 slice.55
  3.6 0.7 %fusion.60 = (f32[128]{0:T(128)S(1)}, pred[128]{0:T(512)(128)(4,1)S(1)}, f32[128]{0:T(128)S(1)}) fusion(s32[128]{0:T(128)S(1)} %convert_reduce_fusion.1, s32[]{:T(128)S(6)} %select_n.81, s32[]{:T(128)} %bitcast.3), kind=kLoop, calls=%fused_computation.105 | loop fusion | flops 512 | bytes 1672 | tf_op jit(solution)/shard_map/convert_element_type | solution.py:130
  4.3 0.6 slice.57
  5.5 0.9 %bitcast_bitcast_fusion = (bf16[2,128,128]{2,1,0:T(8,128)(2,1)S(1)}, bf16[2,128,128]{2,1,0:T(8,128)(2,1)S(1)}) fusion(bf16[128,256]{1,0:T(8,128)(2,1)} %param.18, bf16[128,256]{1,0:T(8,128)(2,1)} %param.19), kind=kLoop, calls=%fused_computation.65 | loop fusion | bytes 262144 | tf_op jit(solution)/shard_map/transpose | solution.py:75
  6.5 1.3 %copy.63 = bf16[128,2048]{0,1:T(8,128)(2,1)S(1)} copy(bf16[128,2048]{1,0:T(8,128)(2,1)} %param.12) | data formatting | bytes 1048576 | tf_op jit(solution)/shard_map/reshape | solution.py:66
  7.8 0.3 reduce_window_sum.20
  8.1 0.2 slice_reduce_fusion
  8.3 0.0 copy-start.15
  8.3 0.6 multiply_bitcast_fusion
  8.9 0.3 fusion.24
  9.2 1.2 %fusion.15 = f32[2568,128]{1,0:T(8,128)} fusion(f32[1,16]{1,0:T(1,128)S(1)} %bitcast.152, f32[512,128]{1,0:T(8,128)S(1)} %bitcast_convert_fusion, f32[2048,128]{1,0:T(8,128)S(1)} %bitcast.138), kind=kLoop, calls=%fused_computation.20 | loop fusion | flops 1972224 | bytes 2625600 | tf_op jit(solution)/shard_map/concatenate | solution.py:82
  10.4 0.5 collective-permute-start
  10.9 0.7 %exponential_multiply_fusion = f32[16]{0:T(128)S(1)} fusion(f32[16]{0:T(128)} %copy-done.15, f32[]{:T(128)} %bitcast.7), kind=kLoop, calls=%fused_computation.95 | loop fusion | flops 16 | bytes 132 | tf_op jit(solution)/shard_map/mul | solution.py:52
  11.5 2.2 %collective-permute-done = f32[2568,128]{1,0:T(8,128)S(1)} collective-permute-done((f32[2568,128]{1,0:T(8,128)}, f32[2568,128]{1,0:T(8,128)S(1)}, u32[]{:S(2)}, u32[]{:S(2)}) %collective-permute-start) | collective-permute-done | bytes 1314848 | tf_op jit(solution)/shard_map/ppermute | solution.py:83
  13.8 0.7 %fusion.59 = (bf16[1,16]{1,0:T(2,128)(2,1)S(1)}, bf16[1,16]{1,0:T(2,128)(2,1)S(1)}, f32[16]{0:T(128)S(1)}) fusion(f32[2568,128]{1,0:T(8,128)S(1)} %collective-permute-done, f32[16]{0:T(128)} %copy-done.14), kind=kLoop, calls=%fused_computation.104 | loop fusion | flops 80 | bytes 256 | tf_op jit(solution)/shard_map/convert_element_type | solution.py:97
  14.5 0.3 select_convert_fusion.1
  14.8 0.3 copy-done.12
  15.1 0.1 pad_maximum_fusion
  15.1 5.4 %collective-permute-start.1 = (bf16[3088,128]{1,0:T(8,128)(2,1)S(1)}, bf16[3088,128]{1,0:T(8,128)(2,1)}, u32[]{:S(2)}, u32[]{:S(2)}) collective-permute-start(bf16[3088,128]{1,0:T(8,128)(2,1)S(1)} %pad_maximum_fusion), channel_id=1, source_target_pairs={{4,8},{12,16},{20,24},{0,20},{8,28},{5,9},{13,17},{21,25},{1,21},{... | collective-permute-start | bytes 2371592 | tf_op jit(solution)/shard_map/ppermute | solution.py:104
  20.6 0.1 convert_reduce_fusion
  20.6 17.0 %collective-permute-done.1 = bf16[3088,128]{1,0:T(8,128)(2,1)} collective-permute-done((bf16[3088,128]{1,0:T(8,128)(2,1)S(1)}, bf16[3088,128]{1,0:T(8,128)(2,1)}, u32[]{:S(2)}, u32[]{:S(2)}) %collective-permute-start.1) | collective-permute-done | bytes 790560 | tf_op jit(solution)/shard_map/ppermute | solution.py:104
  37.7 1.1 %copy.68 = bf16[16,8,16,128]{3,2,1,0:T(8,128)(2,1)S(1)} copy(bf16[16,8,16,128]{3,1,2,0:T(8,128)(2,1)} %bitcast.149) | data formatting | bytes 1048576
  38.9 0.1 fusion.46
  39.0 0.9 %compare_and_fusion = pred[128,5,128]{0,2,1:T(8,128)(4,1)} fusion(s32[128]{0:T(128)S(1)} %copy-done.17, s32[5,128]{1,0:T(8,128)S(1)} %get-tuple-element.31, s32[128]{0:T(128)S(1)} %convert_reduce_fusion.1, s32[5,128]{1,0:T(8,128)S(1)} %get-tuple-element.30), kind=kLoop, calls=%fused_computation.60 | loop fusion | flops 245760 | bytes 88064 | tf_op jit(solution)/shard_map/and | solution.py:146
  39.8 2.7 %convolution_bitcast_fusion.1 = f32[128,16,128]{0,2,1:T(8,128)} fusion(bf16[128,16,128]{0,2,1:T(8,128)(2,1)S(1)} %bitcast.148, f32[16,128]{1,0:T(8,128)S(1)} %reduce_window_sum.20, pred[128,128]{1,0:T(8,128)(4,1)S(1)} %fusion.46, bf16[128,2048]{1,0:T(8,128)(2,1)} %param.13, bf16[128,2048]{1,0:T(8,128)(2,1)S(1)} %copy-done), kind=kOutput, calls=%fused_computation.16 | convolution fusion | flops 135528448 | bytes 2646016 | tf_op jit(solution)/shard_map/hts,shd->thd/dot_general | solution.py:46
  42.6 1.5 %broadcast_select_fusion.1 = (bf16[3088,128]{1,0:T(8,128)(2,1)S(1)}, bf16[3088,128]{1,0:T(8,128)(2,1)S(1)}) fusion(bf16[3088,128]{1,0:T(8,128)(2,1)} %collective-permute-done.2, bf16[3088,128]{1,0:T(8,128)(2,1)} %collective-permute-done.1, pred[]{:T(512)S(6)} %eq.59), kind=kLoop, calls=%fused_computation.36 | loop fusion | flops 790528 | bytes 3162113 | tf_op jit(solution)/shard_map/jit(_where)/select_n | solution.py:106
  44.1 0.0 copy-start.5
  44.3 0.7 %copy-done.5 = bf16[512,128]{1,0:T(8,128)(2,1)S(1)} copy-done((bf16[512,128]{1,0:T(8,128)(2,1)S(1)}, bf16[512,128]{1,0:T(8,128)(2,1)}, u32[]{:S(2)}) %copy-start.5) | copy-done | bytes 131096
  45.0 0.1 maximum_select_fusion
  45.2 0.1 fusion.61
  45.3 1.1 %slice-done = f32[2048,128]{1,0:T(8,128)S(1)} async-done(((f32[2568,128]{1,0:T(8,128)}), f32[2048,128]{1,0:T(8,128)S(1)}, s32[]{:S(2)}) %slice-start) | async-done | bytes 1048600 | tf_op jit(solution)/shard_map/slice | solution.py:84
  46.4 0.3 copy-done.6
  46.7 0.7 %multiply_reduce_fusion = (f32[128]{0:T(128)S(1)}, f32[128,16,128]{0,2,1:T(8,128)S(1)}) fusion(f32[128,16,128]{0,2,1:T(8,128)S(1)} %copy-done.6, f32[128,16]{0,1:T(8,128)S(1)} %copy-done.9, f32[16,128,128]{2,1,0:T(8,128)S(1)} %bitcast.140, bf16[16,128,128]{2,1,0:T(8,128)(2,1)S(1)} %bitcast.145, bf16[16,128,128]{2,1,0:T(8,128)(2,1)S(1)} %bitcast.144, ...), kind=kOutput, calls=%fused_computation.27 | convolution fusion | flops 70254464 | bytes 4727425 | tf_op jit(solution)/shard_map/thd,hde->the/dot_general | solution.py:127
  47.4 1.6 %collective-permute-start.3 = (f32[128]{0:T(128)S(1)}, f32[128]{0:T(128)S(1)}, u32[]{:S(2)}, u32[]{:S(2)}) collective-permute-start(f32[128]{0:T(128)S(1)} %get-tuple-element.24), channel_id=1, source_target_pairs={{0,1},{1,0},{2,3},{3,2},{4,5},{5,4},{6,7},{7,6},{8,9},{9,8},{10,11... | collective-permute-start | bytes 1544 | tf_op jit(solution)/shard_map/ppermute | solution.py:28
  49.1 0.9 %fusion = (f32[2,8,128]{2,1,0:T(8,128)S(1)}, f32[2,5,128,128,8]{3,2,4,1,0:T(8,128)S(1)}) fusion(pred[128,5,128]{0,2,1:T(8,128)(4,1)S(1)} %copy-done.3, bf16[128,2,8,128,1]{3,2,1,0,4:T(8,128)(2,1)S(1)} %bitcast.143, bf16[5,2,128,128]{3,2,1,0:T(8,128)(2,1)S(1)} %get-tuple-element.20), kind=kOutput, calls=%fused_computation.2 | convolution fusion | flops 339474432 | bytes 6184960 | tf_op jit(solution)/shard_map/tkgd,bksd->kgtbs/dot_general | solution.py:148
  50.0 1.2 %fusion.4 = f32[2,8,128]{2,1,0:T(8,128)S(1)} fusion(f32[2,5,128,128,8]{3,2,4,1,0:T(8,128)S(1)} %get-tuple-element.27, f32[2,8,128]{2,1,0:T(8,128)S(1)} %get-tuple-element.26, pred[128,5,128]{0,2,1:T(8,128)(4,1)S(1)} %copy-done.3), kind=kLoop, calls=%fused_computation.6 | loop fusion | flops 6551552 | bytes 5341184 | tf_op jit(solution)/shard_map/reduce_sum | solution.py:153
  51.2 1.1 %copy-done.1 = f32[2,5,128,128,8]{3,2,4,1,0:T(8,128)} copy-done((f32[2,5,128,128,8]{3,2,4,1,0:T(8,128)}, f32[2,5,128,128,8]{3,2,4,1,0:T(8,128)S(1)}, u32[]{:S(2)}) %copy-start.1) | copy-done | bytes 5242904
  52.3 0.2 copy.61
  52.5 2.7 %collective-permute-start.4 = (f32[128]{0:T(128)S(1)}, f32[128]{0:T(128)S(1)}, u32[]{:S(2)}, u32[]{:S(2)}) collective-permute-start(f32[128]{0:T(128)S(1)} %add.95), channel_id=1, source_target_pairs={{0,2},{1,3},{2,0},{3,1},{4,6},{5,7},{6,4},{7,5},{8,10},{9,11},{10,... | collective-permute-start | bytes 1544 | tf_op jit(solution)/shard_map/ppermute | solution.py:28
  55.2 4.7 %divide_convert_fusion = bf16[128,2,8,128]{0,3,2,1:T(8,128)(2,1)} fusion(f32[2,5,128,128,8]{3,2,4,1,0:T(8,128)} %copy-done.1, f32[2,8,128]{2,1,0:T(8,128)S(1)} %get-tuple-element.26, pred[128,5,128]{0,2,1:T(8,128)(4,1)S(1)} %copy-done.3, f32[128,2,8]{0,2,1:T(8,128)S(1)} %bitcast.151, bf16[5,2,128,128]{2,3,0,1:T(8,128)(2,1)S(1)} %copy.61), kind=kOutput, calls=%fused_computation.25 | convolution fusion | flops 342622208 | bytes 6193152 | tf_op jit(solution)/shard_map/kgtbs,bksd->tkgd/dot_general | solution.py:154
  59.9 0.3 copy.46
  60.2 2.0 %copy.51 = bf16[128,2048]{1,0:T(8,128)(2,1)} copy(bf16[128,2048]{0,1:T(8,128)(2,1)} %bitcast.150) | data formatting | bytes 1048576
  62.3 1.1 %multiply_convert_fusion = bf16[128,2048]{1,0:T(8,128)(2,1)} fusion(bf16[128,2048]{1,0:T(8,128)(2,1)S(1)} %copy-done.7, f32[128,2048]{1,0:T(8,128)S(1)} %copy.46, f32[2048]{0:T(1024)S(1)} %copy-done.10, f32[128]{0:T(128)S(1)} %add_rsqrt_fusion), kind=kLoop, calls=%fused_computation.26 | loop fusion | flops 2097152 | bytes 2105856 | tf_op jit(solution)/shard_map/convert_element_type | solution.py:142
  (54 shorter events, 0.4 us)
Async XLA Ops:
  0.6 39.2 %copy-start = (bf16[128,2048]{1,0:T(8,128)(2,1)S(1)}, bf16[128,2048]{1,0:T(8,128)(2,1)}, u32[]{:S(2)}) copy-start(bf16[128,2048]{1,0:T(8,128)(2,1)} %param.11) | copy-start | bytes 1572868
  0.6 7.2 %copy-start.11 = (f32[16,128]{1,0:T(8,128)S(1)}, f32[16,128]{1,0:T(8,128)}, u32[]{:S(2)}) copy-start(f32[16,128]{1,0:T(8,128)} %param.14) | copy-start | bytes 24580
  0.7 8.3 %copy-start.8 = (bf16[128,2048]{1,0:T(8,128)(2,1)S(1)}, bf16[128,2048]{1,0:T(8,128)(2,1)}, u32[]{:S(2)}) copy-start(bf16[128,2048]{1,0:T(8,128)(2,1)} %param.13) | copy-start | bytes 1572868
  0.7 4.2 %copy-start.16 = (s32[128]{0:T(128)}, s32[128]{0:T(128)S(1)}, u32[]{:S(2)}) copy-start(s32[128]{0:T(128)S(1)} %iota_add_fusion.1) | copy-start | bytes 1540
  1.6 3.2 %copy-start.18 = (s32[6,1]{0,1:T(1,128)}, s32[6,1]{0,1:T(1,128)S(1)}, u32[]{:S(2)}) copy-start(s32[6,1]{0,1:T(1,128)S(1)} %reduce-window.4) | copy-start | bytes 76
  8.3 0.9 %copy-start.14 = (f32[16]{0:T(128)}, f32[16]{0:T(128)S(1)}, u32[]{:S(2)}) copy-start(f32[16]{0:T(128)S(1)} %get-tuple-element.9) | copy-start | bytes 196
  8.3 0.9 %copy-start.15 = (f32[16]{0:T(128)}, f32[16]{0:T(128)S(1)}, u32[]{:S(2)}) copy-start(f32[16]{0:T(128)S(1)} %get-tuple-element.8) | copy-start | bytes 196
  10.4 3.3 %collective-permute-start = (f32[2568,128]{1,0:T(8,128)}, f32[2568,128]{1,0:T(8,128)S(1)}, u32[]{:S(2)}, u32[]{:S(2)}) collective-permute-start(f32[2568,128]{1,0:T(8,128)} %fusion.15), channel_id=1, source_target_pairs={{0,4},{4,0},{8,12},{12,8},{16,20},{20,16},{24,28},{28,24},{1,5},{5... | collective-permute-start | bytes 3944456 | tf_op jit(solution)/shard_map/ppermute | solution.py:83
  13.7 28.8 %copy-start.2 = (f32[2568,128]{1,0:T(8,128)}, f32[2568,128]{1,0:T(8,128)S(1)}, u32[]{:S(2)}) copy-start(f32[2568,128]{1,0:T(8,128)S(1)} %collective-permute-done) | copy-start | bytes 3944452
  13.8 0.7 %copy-start.4 = (bf16[512,128]{1,0:T(8,128)(2,1)}, bf16[512,128]{1,0:T(8,128)(2,1)S(1)}, u32[]{:S(2)}) copy-start(bf16[512,128]{1,0:T(8,128)(2,1)S(1)} %get-tuple-element.13) | copy-start | bytes 393220
  14.5 0.6 copy-start.12
  14.8 5.7 %copy-start.19 = (s32[6,1]{0,1:T(1,128)S(1)}, s32[6,1]{0,1:T(1,128)}, u32[]{:S(2)}) copy-start(s32[6,1]{0,1:T(1,128)} %copy-done.18) | copy-start | bytes 76
  14.8 24.1 %copy-start.17 = (s32[128]{0:T(128)S(1)}, s32[128]{0:T(128)}, u32[]{:S(2)}) copy-start(s32[128]{0:T(128)} %copy-done.16) | copy-start | bytes 1540
  15.1 22.5 %collective-permute-start.1 = (bf16[3088,128]{1,0:T(8,128)(2,1)S(1)}, bf16[3088,128]{1,0:T(8,128)(2,1)}, u32[]{:S(2)}, u32[]{:S(2)}) collective-permute-start(bf16[3088,128]{1,0:T(8,128)(2,1)S(1)} %pad_maximum_fusion), channel_id=1, source_target_pairs={{4,8},{12,16},{20,24},{0,20},{8,28},{5,9},{13,17},{21,25},{1,21},{... | collective-permute-start | bytes 2371592 | tf_op jit(solution)/shard_map/ppermute | solution.py:104
  37.7 4.9 %collective-permute-start.2 = (bf16[3088,128]{1,0:T(8,128)(2,1)}, bf16[3088,128]{1,0:T(8,128)(2,1)}, u32[]{:S(2)}, u32[]{:S(2)}) collective-permute-start(bf16[3088,128]{1,0:T(8,128)(2,1)} %collective-permute-done.1), channel_id=1, source_target_pairs={{0,4},{4,0},{8,12},{12,8},{16,20},{20,16},{24,28},{28,24},{1,5},{5... | collective-permute-start | bytes 2371592 | tf_op jit(solution)/shard_map/ppermute | solution.py:105
  44.1 0.9 %copy-start.5 = (bf16[512,128]{1,0:T(8,128)(2,1)S(1)}, bf16[512,128]{1,0:T(8,128)(2,1)}, u32[]{:S(2)}) copy-start(bf16[512,128]{1,0:T(8,128)(2,1)} %copy-done.4) | copy-start | bytes 393220
  45.1 1.2 %slice-start = ((f32[2568,128]{1,0:T(8,128)}), f32[2048,128]{1,0:T(8,128)S(1)}, s32[]{:S(2)}) async-start(f32[2568,128]{1,0:T(8,128)} %copy-done.2), calls=%async_computation | async-start | bytes 2097152 | tf_op jit(solution)/shard_map/slice | solution.py:84
  45.1 1.5 %copy-start.6 = (f32[128,16,128]{0,2,1:T(8,128)S(1)}, f32[128,16,128]{0,2,1:T(8,128)}, u32[]{:S(2)}) copy-start(f32[128,16,128]{0,2,1:T(8,128)} %convolution_bitcast_fusion.1) | copy-start | bytes 3145732
  45.2 1.5 %copy-start.9 = (f32[128,16]{0,1:T(8,128)S(1)}, f32[128,16]{0,1:T(8,128)}, u32[]{:S(2)}) copy-start(f32[128,16]{0,1:T(8,128)} %get-tuple-element.21) | copy-start | bytes 24580
  45.2 1.5 %copy-start.13 = (f32[16]{0:T(128)S(1)}, f32[16]{0:T(128)}, u32[]{:S(2)}) copy-start(f32[16]{0:T(128)} %copy-done.12) | copy-start | bytes 196
  46.7 2.4 %copy-start.3 = (pred[128,5,128]{0,2,1:T(8,128)(4,1)S(1)}, pred[128,5,128]{0,2,1:T(8,128)(4,1)}, u32[]{:S(2)}) copy-start(pred[128,5,128]{0,2,1:T(8,128)(4,1)} %compare_and_fusion) | copy-start | bytes 245764
  47.4 5.1 %collective-permute-start.3 = (f32[128]{0:T(128)S(1)}, f32[128]{0:T(128)S(1)}, u32[]{:S(2)}, u32[]{:S(2)}) collective-permute-start(f32[128]{0:T(128)S(1)} %get-tuple-element.24), channel_id=1, source_target_pairs={{0,1},{1,0},{2,3},{3,2},{4,5},{5,4},{6,7},{7,6},{8,9},{9,8},{10,11... | collective-permute-start | bytes 1544 | tf_op jit(solution)/shard_map/ppermute | solution.py:28
  50.0 2.3 %copy-start.1 = (f32[2,5,128,128,8]{3,2,4,1,0:T(8,128)}, f32[2,5,128,128,8]{3,2,4,1,0:T(8,128)S(1)}, u32[]{:S(2)}) copy-start(f32[2,5,128,128,8]{3,2,4,1,0:T(8,128)S(1)} %get-tuple-element.27) | copy-start | bytes 15728644
  52.5 9.7 %collective-permute-start.4 = (f32[128]{0:T(128)S(1)}, f32[128]{0:T(128)S(1)}, u32[]{:S(2)}, u32[]{:S(2)}) collective-permute-start(f32[128]{0:T(128)S(1)} %add.95), channel_id=1, source_target_pairs={{0,2},{1,3},{2,0},{3,1},{4,6},{5,7},{6,4},{7,5},{8,10},{9,11},{10,... | collective-permute-start | bytes 1544 | tf_op jit(solution)/shard_map/ppermute | solution.py:28
  59.9 2.4 %copy-start.7 = (bf16[128,2048]{1,0:T(8,128)(2,1)S(1)}, bf16[128,2048]{1,0:T(8,128)(2,1)}, u32[]{:S(2)}) copy-start(bf16[128,2048]{1,0:T(8,128)(2,1)} %param.15) | copy-start | bytes 1572868
  59.9 2.4 %copy-start.10 = (f32[2048]{0:T(1024)S(1)}, f32[2048]{0:T(1024)}, u32[]{:S(2)}) copy-start(f32[2048]{0:T(1024)} %param.16) | copy-start | bytes 24580

commit v7 on v6

--- a/solution.py
+++ b/solution.py
@@ -79,11 +79,13 @@
     n_state = heads_here * DH
     state_rows = state.reshape(n_state, DH)
     factor_rows = jnp.pad(shrinkage_multiplier[None, :], ((0, 7), (0, DH - heads_here)))
-    first = jnp.concatenate([state_rows, factor_rows, pair.astype(jnp.float32)], axis=0)
+    window = jnp.concatenate(
+        [from_behind(pair, "ctx", step) for step in range(SPAN, 0, -1)] + [pair], axis=0
+    ).reshape(SPAN + 1, 2 * kv_here, rows, DH)
+    first = jnp.concatenate([state_rows, factor_rows], axis=0)
     got = lax.ppermute(first, "ctx", [(i, i ^ 1) for i in range(count)])
     state_mate = got[:n_state]
     factor_mate = got[n_state, :heads_here]
-    pair_mate = got[n_state + 8 :].astype(jnp.bfloat16)
     state_cube = state_rows.reshape(state.shape)
     mate_cube = state_mate.reshape(state.shape)
     chip_state = jnp.where(
@@ -92,13 +94,11 @@
         factor_mate[:, None, None] * state_cube + mate_cube,
     )
     chip_factor = shrinkage_multiplier * factor_mate
-    pair_lo = jnp.where(odd, pair_mate, pair)
-    pair_hi = jnp.where(odd, pair, pair_mate)
     chip_top = chip_factor.astype(jnp.bfloat16)
     chip_rest = (chip_factor - chip_top.astype(jnp.float32)).astype(jnp.bfloat16)
     chip_rows = jnp.pad(jnp.stack([chip_top, chip_rest]), ((0, 14), (0, DH - heads_here)))
     packet = jnp.concatenate(
-        [chip_state.astype(jnp.bfloat16).reshape(n_state, DH), chip_rows, pair_lo, pair_hi], axis=0
+        [chip_state.astype(jnp.bfloat16).reshape(n_state, DH), chip_rows], axis=0
     )
     routes = [(i, i + 1) for i in range(1, count - 1, 2)] + [(i, i + 5) for i in range(0, count - 5, 2)]
     received = lax.ppermute(packet, "ctx", routes)
@@ -111,19 +111,13 @@
         mult = got_packet[n_state, :heads_here].astype(jnp.float32) + got_packet[
             n_state + 1, :heads_here
         ].astype(jnp.float32)
-        low = got_packet[n_state + 16 : n_state + 16 + n_pair]
-        high = got_packet[n_state + 16 + n_pair :]
-        return chip, mult, low, high
+        return chip, mult
 
-    state_near, factor_near, near_lo, near_hi = unpack(near)
-    state_far, _, far_lo, far_hi = unpack(far)
+    state_near, factor_near = unpack(near)
+    state_far, _ = unpack(far)
     incoming_even = state_near + factor_near[:, None, None] * state_far
     incoming = jnp.where(odd, factor_mate[:, None, None] * incoming_even + mate_cube, incoming_even)
     incoming_b = incoming.astype(jnp.bfloat16)
-    window_even = jnp.concatenate([far_lo, far_hi, near_lo, near_hi], axis=0)
-    window_odd = jnp.concatenate([far_hi, near_lo, near_hi, pair_mate], axis=0)
-    window = jnp.concatenate([jnp.where(odd, window_odd, window_even), pair], axis=0)
-    window = window.reshape(SPAN + 1, 2 * kv_here, rows, DH)
     outer = jnp.einsum(
         "thd,hde->the", query, incoming_b, preferred_element_type=jnp.float32
     )

time: 63.9 us -> 59.3 us (0.928)
  waiting for transfers between devices: 19.3 us -> 9.97 us
  starting transfers between devices: 10.2 us -> 18.5 us
  other arithmetic: 11.4 us -> 7.82 us
    ppermute x0 -> x4, starting transfers between devices: none -> 12.8 us  [from_behind(): return lax.ppermute(shard, axis, pairs)]
    ppermute x1, waiting for transfers between devices: 17 us -> 8.64 us  [local(): received = lax.ppermute(packet, 'ctx', routes)]
    ppermute x1, starting transfers between devices: 5.42 us -> 1.32 us  [local(): received = lax.ppermute(packet, 'ctx', routes)]
    ppermute x1, waiting for transfers between devices: 2.22 us -> 0.01 us  [local(): got = lax.ppermute(first, 'ctx', [(i, i ^ 1) for i in range(count)])]
    select_n x1, other arithmetic: 1.48 us -> 0.06 us  [local(): near = jnp.where(odd, mate_packet, received)]
    unnamed x43 -> x21, local copies, waits for them, and re-layouts: 5.85 us -> 7.17 us
    dot_general x1, matrix products: 0.3 us -> 1.35 us  [block_terms(): jnp.einsum('shd,she->hde', weighted, values, preferred_element_type=jnp.f...]
    slice x2 -> x1, local copies, waits for them, and re-layouts: 1.08 us -> 0.07 us  [local(): state_mate = got[:n_state]]
  transfers between devices with their start and end apart: 5 -> 9, of which waited for: 2 -> 3; matrix products, arithmetic and copies ran while one was open for 24% -> 40% of each run, Pallas kernels for 0% -> 0%
where the time goes in v7:
time: 59.3 us; the launch traced here: 58.8 us
  starting transfers between devices  18.5 us (31%)
  local copies, waits for them, and re-layouts  10.3 us (17%)
  waiting for transfers between devices  9.97 us (17%)
  matrix products  9.89 us (17%)
  other arithmetic  7.82 us (13%)
  between operations  2.33 us (4%)
    ppermute x4, starting transfers between devices, from_behind(): return lax.ppermute(shard, axis, pairs)  12.8 us
    ppermute x1, waiting for transfers between devices, local(): received = lax.ppermute(packet, 'ctx', routes)  8.64 us
    unnamed x21, local copies, waits for them, and re-layouts  7.17 us
    ppermute x2, starting transfers between devices, all_sum(): x = x + lax.ppermute(x, axis, [(i, i ^ bit) for i in range(count)])  4.23 us
    dot_general x1, matrix products, local(): jnp.einsum('kgtbs,bksd->tkgd', expd.astype(jnp.bfloat16).reshape(kv_here,...  3.94 us
    dot_general x1, matrix products, block_terms(): jnp.einsum('hts,shd->thd', weights, values, preferred_element_type=jnp.fl...  2.94 us
    dot_general x1, matrix products, block_terms(): jnp.einsum('shd,she->hde', weighted, values, preferred_element_type=jnp.f...  1.35 us
    ppermute x1, starting transfers between devices, local(): received = lax.ppermute(packet, 'ctx', routes)  1.32 us
  transfers between devices with their start and end apart: 9, of which 3 were waited for; matrix products, arithmetic and copies ran while one was open for 40% of the time, Pallas kernels for 0%

profile of v7, /device:TPU:0, one launch (start us, length us, event | category | flops | bytes accessed | tf_op | source)
XLA Modules:
  0.0 58.8 jit_solution(10884657219100749674)
XLA Ops:
  0.6 0.0 copy-start
  0.6 1.0 %copy.57 = bf16[128,256]{0,1:T(8,128)(2,1)S(1)} copy(bf16[128,256]{1,0:T(8,128)(2,1)} %param.18) | data formatting | bytes 131072 | tf_op args[8]
  1.7 1.0 %copy.58 = bf16[128,256]{0,1:T(8,128)(2,1)S(1)} copy(bf16[128,256]{1,0:T(8,128)(2,1)} %param.19) | data formatting | bytes 131072 | tf_op args[9]
  2.6 0.1 copy.59
  2.8 5.5 %collective-permute-start.5 = (bf16[512,128]{1,0:T(8,128)(2,1)S(1)}, bf16[512,128]{1,0:T(8,128)(2,1)}, u32[]{:S(2)}, u32[]{:S(2)}) collective-permute-start(bf16[512,128]{1,0:T(8,128)(2,1)S(1)} %bitcast.139), channel_id=1, source_target_pairs={{0,16},{4,20},{8,24},{12,28},{1,17},{5,21},{9,25},{13,29},{2,18},{... | collective-permute-start | bytes 393224 | tf_op jit(solution)/shard_map/ppermute | solution.py:13
  8.3 3.2 %collective-permute-start.6 = (bf16[512,128]{1,0:T(8,128)(2,1)S(1)}, bf16[512,128]{1,0:T(8,128)(2,1)}, u32[]{:S(2)}, u32[]{:S(2)}) collective-permute-start(bf16[512,128]{1,0:T(8,128)(2,1)S(1)} %bitcast.140), channel_id=1, source_target_pairs={{0,12},{4,16},{8,20},{12,24},{16,28},{1,13},{5,17},{9,21},{13,25},... | collective-permute-start | bytes 393224 | tf_op jit(solution)/shard_map/ppermute | solution.py:13
  11.5 2.8 %collective-permute-start.7 = (bf16[512,128]{1,0:T(8,128)(2,1)S(1)}, bf16[512,128]{1,0:T(8,128)(2,1)}, u32[]{:S(2)}, u32[]{:S(2)}) collective-permute-start(bf16[512,128]{1,0:T(8,128)(2,1)S(1)} %bitcast.141), channel_id=1, source_target_pairs={{0,8},{4,12},{8,16},{12,20},{16,24},{20,28},{1,9},{5,13},{9,17},{1... | collective-permute-start | bytes 393224 | tf_op jit(solution)/shard_map/ppermute | solution.py:13
  14.3 1.3 %collective-permute-start.8 = (bf16[512,128]{1,0:T(8,128)(2,1)S(1)}, bf16[512,128]{1,0:T(8,128)(2,1)S(1)}, u32[]{:S(2)}, u32[]{:S(2)}) collective-permute-start(bf16[512,128]{1,0:T(8,128)(2,1)S(1)} %bitcast.142), channel_id=1, source_target_pairs={{0,4},{4,8},{8,12},{12,16},{16,20},{20,24},{24,28},{1,5},{5,9},{9,... | collective-permute-start | bytes 393224 | tf_op jit(solution)/shard_map/ppermute | solution.py:13
  15.6 0.8 %reduce-window.4 = s32[6,1]{0,1:T(1,128)S(1)} reduce-window(s32[6,1]{0,1:T(1,128)} %bitcast.151, s32[]{:T(128)} %constant.24.clone.1), window={size=6x1 pad=5_0x0_0}, to_apply=%region_0.0 | reduce-window | flops 30 | bytes 52 | tf_op jit(solution)/shard_map/reduce-window
  16.4 0.1 convert_reduce_fusion.1
  16.6 0.6 %fusion.51 = s32[]{:T(128)} fusion(s32[6,1]{0,1:T(1,128)S(1)} %reduce-window.4, s32[]{:T(128)} %bitcast.6), kind=kLoop, calls=%fused_computation.83 | loop fusion | flops 17 | bytes 32 | tf_op jit(solution)/shard_map/reduce_sum | solution.py:35
  17.2 0.6 slice.38
  18.4 0.7 %fusion.58 = (f32[128]{0:T(128)S(1)}, pred[128]{0:T(512)(128)(4,1)S(1)}, f32[128]{0:T(128)S(1)}) fusion(s32[128]{0:T(128)S(1)} %convert_reduce_fusion.1, s32[]{:T(128)S(6)} %select_n.61, s32[]{:T(128)} %bitcast.3), kind=kLoop, calls=%fused_computation.99 | loop fusion | flops 512 | bytes 1672 | tf_op jit(solution)/shard_map/convert_element_type | solution.py:124
  19.1 0.6 slice.40
  20.3 1.3 %copy.76 = bf16[128,2048]{0,1:T(8,128)(2,1)S(1)} copy(bf16[128,2048]{1,0:T(8,128)(2,1)} %param.12) | data formatting | bytes 1048576 | tf_op jit(solution)/shard_map/reshape | solution.py:66
  21.6 0.0 copy-start.2
  21.7 1.0 %reduce_window_sum.20 = f32[16,128]{1,0:T(8,128)S(1)} reduce-window(f32[16,128]{1,0:T(8,128)} %param.14, f32[]{:T(128)} %constant.49.clone.1), window={size=1x128 pad=0_0x127_0}, to_apply=%region_2.3 | reduce-window | flops 260096 | bytes 16388 | tf_op jit(solution)/shard_map/jit(cumsum)/reduce_window_sum | solution.py:40
  22.7 0.2 slice_reduce_fusion
  22.9 0.1 multiply_bitcast_fusion
  22.9 1.4 %fusion.22 = f32[16,128,128]{2,1,0:T(8,128)S(1)} fusion(bf16[128,16,128]{0,2,1:T(8,128)(2,1)S(1)} %bitcast.133, f32[128,16]{0,1:T(8,128)S(1)} %get-tuple-element.20, bf16[128,2048]{1,0:T(8,128)(2,1)} %param.13), kind=kOutput, calls=%fused_computation.33 | convolution fusion | flops 67895296 | bytes 2105344 | tf_op jit(solution)/shard_map/shd,she->hde/dot_general | solution.py:51
  24.3 1.1 %select_maximum_fusion = f32[2056,128]{1,0:T(8,128)} fusion(f32[1,16]{1,0:T(1,128)S(1)} %bitcast.147, f32[2048,128]{1,0:T(8,128)S(1)} %bitcast.127), kind=kLoop, calls=%fused_computation.18 | loop fusion | flops 789504 | bytes 2101312 | tf_op jit(solution)/shard_map/concatenate | solution.py:85
  25.4 0.1 collective-permute-start
  25.5 1.1 %copy.79 = bf16[16,8,16,128]{3,2,1,0:T(8,128)(2,1)S(1)} copy(bf16[16,8,16,128]{3,1,2,0:T(8,128)(2,1)} %bitcast.137) | data formatting | bytes 1048576
  26.6 0.1 convert_reduce_fusion
  26.7 0.1 fusion.44
  26.8 0.2 compare_and_fusion
  27.1 2.9 %convolution_bitcast_fusion.1 = f32[128,16,128]{0,2,1:T(8,128)} fusion(bf16[128,16,128]{0,2,1:T(8,128)(2,1)} %bitcast.134, f32[16,128]{1,0:T(8,128)S(1)} %reduce_window_sum.20, pred[128,128]{1,0:T(8,128)(4,1)S(1)} %fusion.44, bf16[128,2048]{1,0:T(8,128)(2,1)} %param.13, bf16[128,2048]{1,0:T(8,128)(2,1)S(1)} %copy-done), kind=kOutput, calls=%fused_computation.14 | convolution fusion | flops 135528448 | bytes 2646016 | tf_op jit(solution)/shard_map/hts,shd->thd/dot_general | solution.py:46
  30.0 0.3 select_convert_fusion.1
  30.4 1.3 %collective-permute-start.1 = (bf16[2064,128]{1,0:T(8,128)(2,1)S(1)}, bf16[2064,128]{1,0:T(8,128)(2,1)S(1)}, u32[]{:S(2)}, u32[]{:S(2)}) collective-permute-start(bf16[2064,128]{1,0:T(8,128)(2,1)S(1)} %pad_maximum_fusion), channel_id=1, source_target_pairs={{4,8},{12,16},{20,24},{0,20},{8,28},{5,9},{13,17},{21,25},{1,21},{... | collective-permute-start | bytes 1585160 | tf_op jit(solution)/shard_map/ppermute | solution.py:104
  31.7 0.9 %constant_dynamic-update-slice_fusion.4 = bf16[2560,128]{1,0:T(8,128)(2,1)S(1)} fusion(bf16[512,128]{1,0:T(8,128)(2,1)} %collective-permute-done.5), kind=kLoop, calls=%fused_computation.64 | loop fusion | bytes 262144
  32.7 0.9 %constant_dynamic-update-slice_fusion.3 = bf16[2560,128]{1,0:T(8,128)(2,1)S(1)} fusion(bf16[2560,128]{1,0:T(8,128)(2,1)S(1)} %constant_dynamic-update-slice_fusion.4, bf16[512,128]{1,0:T(8,128)(2,1)} %collective-permute-done.6), kind=kLoop, calls=%fused_computation.63 | loop fusion | bytes 262144
  33.6 0.9 %constant_dynamic-update-slice_fusion.2 = bf16[2560,128]{1,0:T(8,128)(2,1)S(1)} fusion(bf16[2560,128]{1,0:T(8,128)(2,1)S(1)} %constant_dynamic-update-slice_fusion.3, bf16[512,128]{1,0:T(8,128)(2,1)} %collective-permute-done.7), kind=kLoop, calls=%fused_computation.62 | loop fusion | bytes 262144
  34.6 8.6 %collective-permute-done.1 = bf16[2064,128]{1,0:T(8,128)(2,1)S(1)} collective-permute-done((bf16[2064,128]{1,0:T(8,128)(2,1)S(1)}, bf16[2064,128]{1,0:T(8,128)(2,1)S(1)}, u32[]{:S(2)}, u32[]{:S(2)}) %collective-permute-start.1) | collective-permute-done | bytes 528416 | tf_op jit(solution)/shard_map/ppermute | solution.py:104
  43.3 0.9 %fusion = (f32[2,8,128]{2,1,0:T(8,128)S(1)}, f32[2,5,128,128,8]{3,2,4,1,0:T(8,128)S(1)}) fusion(pred[128,5,128]{0,2,1:T(8,128)(4,1)S(1)} %compare_and_fusion, bf16[128,2,8,128,1]{3,2,1,0,4:T(8,128)(2,1)S(1)} %bitcast.130, bf16[5,2,128,128]{3,2,1,0:T(8,128)(2,1)S(1)} %get-tuple-element.18), kind=kOutput, calls=%fused_computation.2 | convolution fusion | flops 339474432 | bytes 6184960 | tf_op jit(solution)/shard_map/tkgd,bksd->kgtbs/dot_general | solution.py:142
  44.2 0.1 slice.51
  44.3 0.8 %collective-permute-done.2 = bf16[2064,128]{1,0:T(8,128)(2,1)S(1)} collective-permute-done((bf16[2064,128]{1,0:T(8,128)(2,1)S(1)}, bf16[2064,128]{1,0:T(8,128)(2,1)S(1)}, u32[]{:S(2)}, u32[]{:S(2)}) %collective-permute-start.2) | collective-permute-done | bytes 528416 | tf_op jit(solution)/shard_map/ppermute | solution.py:105
  45.2 0.1 broadcast_select_fusion
  45.3 0.1 slice_select_fusion
  45.4 0.7 %multiply_reduce_fusion = (f32[128]{0:T(128)S(1)}, f32[128,16,128]{0,2,1:T(8,128)S(1)}) fusion(f32[128,16,128]{0,2,1:T(8,128)S(1)} %copy-done.3, f32[128,16]{0,1:T(8,128)S(1)} %get-tuple-element.19, f32[16,128,128]{2,1,0:T(8,128)S(1)} %bitcast.129, bf16[16,128,128]{2,1,0:T(8,128)(2,1)S(1)} %bitcast.132, bf16[16,128,128]{2,1,0:T(8,128)(2,1)S(1)} %bitcast.131, ...), kind=kOutput, calls=%fused_computation.24 | convolution fusion | flops 70254464 | bytes 4727425 | tf_op jit(solution)/shard_map/thd,hde->the/dot_general | solution.py:121
  46.1 1.6 %collective-permute-start.3 = (f32[128]{0:T(128)S(1)}, f32[128]{0:T(128)S(1)}, u32[]{:S(2)}, u32[]{:S(2)}) collective-permute-start(f32[128]{0:T(128)S(1)} %get-tuple-element.22), channel_id=1, source_target_pairs={{0,1},{1,0},{2,3},{3,2},{4,5},{5,4},{6,7},{7,6},{8,9},{9,8},{10,11... | collective-permute-start | bytes 1544 | tf_op jit(solution)/shard_map/ppermute | solution.py:28
  47.7 1.2 %fusion.4 = f32[2,8,128]{2,1,0:T(8,128)S(1)} fusion(f32[2,5,128,128,8]{3,2,4,1,0:T(8,128)S(1)} %get-tuple-element.25, f32[2,8,128]{2,1,0:T(8,128)S(1)} %get-tuple-element.24, pred[128,5,128]{0,2,1:T(8,128)(4,1)S(1)} %compare_and_fusion), kind=kLoop, calls=%fused_computation.6 | loop fusion | flops 6551552 | bytes 5341184 | tf_op jit(solution)/shard_map/reduce_sum | solution.py:147
  49.0 0.2 copy.74
  49.2 0.5 collective-permute-done.3
  49.7 2.6 %collective-permute-start.4 = (f32[128]{0:T(128)S(1)}, f32[128]{0:T(128)S(1)}, u32[]{:S(2)}, u32[]{:S(2)}) collective-permute-start(f32[128]{0:T(128)S(1)} %add.95), channel_id=1, source_target_pairs={{0,2},{1,3},{2,0},{3,1},{4,6},{5,7},{6,4},{7,5},{8,10},{9,11},{10,... | collective-permute-start | bytes 1544 | tf_op jit(solution)/shard_map/ppermute | solution.py:28
  52.3 3.9 %divide_convert_fusion = bf16[128,2,8,128]{0,3,2,1:T(8,128)(2,1)S(1)} fusion(f32[2,5,128,128,8]{3,2,4,1,0:T(8,128)} %copy-done.1, f32[2,8,128]{2,1,0:T(8,128)S(1)} %get-tuple-element.24, pred[128,5,128]{0,2,1:T(8,128)(4,1)S(1)} %compare_and_fusion, f32[128,2,8]{0,2,1:T(8,128)S(1)} %bitcast.146, bf16[5,2,128,128]{2,3,0,1:T(8,128)(2,1)S(1)} %copy.74), kind=kOutput, calls=%fused_computation.22 | convolution fusion | flops 342622208 | bytes 6193152 | tf_op jit(solution)/shard_map/kgtbs,bksd->tkgd/dot_general | solution.py:148
  56.2 1.0 %copy.64 = bf16[128,2048]{1,0:T(8,128)(2,1)} copy(bf16[128,2048]{0,1:T(8,128)(2,1)S(1)} %bitcast.138) | data formatting | bytes 1048576
  57.3 0.3 copy.56
  57.6 1.1 %multiply_convert_fusion = bf16[128,2048]{1,0:T(8,128)(2,1)} fusion(bf16[128,2048]{1,0:T(8,128)(2,1)S(1)} %copy-done.4, f32[128,2048]{1,0:T(8,128)S(1)} %copy.56, f32[2048]{0:T(1024)S(1)} %copy-done.5, f32[128]{0:T(128)S(1)} %add_rsqrt_fusion), kind=kLoop, calls=%fused_computation.23 | loop fusion | flops 2097152 | bytes 2105856 | tf_op jit(solution)/shard_map/convert_element_type | solution.py:136
  (32 shorter events, 0.3 us)
Async XLA Ops:
  0.6 26.4 %copy-start = (bf16[128,2048]{1,0:T(8,128)(2,1)S(1)}, bf16[128,2048]{1,0:T(8,128)(2,1)}, u32[]{:S(2)}) copy-start(bf16[128,2048]{1,0:T(8,128)(2,1)} %param.11) | copy-start | bytes 1572868
  2.8 28.9 %collective-permute-start.5 = (bf16[512,128]{1,0:T(8,128)(2,1)S(1)}, bf16[512,128]{1,0:T(8,128)(2,1)}, u32[]{:S(2)}, u32[]{:S(2)}) collective-permute-start(bf16[512,128]{1,0:T(8,128)(2,1)S(1)} %bitcast.139), channel_id=1, source_target_pairs={{0,16},{4,20},{8,24},{12,28},{1,17},{5,21},{9,25},{13,29},{2,18},{... | collective-permute-start | bytes 393224 | tf_op jit(solution)/shard_map/ppermute | solution.py:13
  8.3 24.3 %collective-permute-start.6 = (bf16[512,128]{1,0:T(8,128)(2,1)S(1)}, bf16[512,128]{1,0:T(8,128)(2,1)}, u32[]{:S(2)}, u32[]{:S(2)}) collective-permute-start(bf16[512,128]{1,0:T(8,128)(2,1)S(1)} %bitcast.140), channel_id=1, source_target_pairs={{0,12},{4,16},{8,20},{12,24},{16,28},{1,13},{5,17},{9,21},{13,25},... | collective-permute-start | bytes 393224 | tf_op jit(solution)/shard_map/ppermute | solution.py:13
  11.5 22.1 %collective-permute-start.7 = (bf16[512,128]{1,0:T(8,128)(2,1)S(1)}, bf16[512,128]{1,0:T(8,128)(2,1)}, u32[]{:S(2)}, u32[]{:S(2)}) collective-permute-start(bf16[512,128]{1,0:T(8,128)(2,1)S(1)} %bitcast.141), channel_id=1, source_target_pairs={{0,8},{4,12},{8,16},{12,20},{16,24},{20,28},{1,9},{5,13},{9,17},{1... | collective-permute-start | bytes 393224 | tf_op jit(solution)/shard_map/ppermute | solution.py:13
  14.3 20.2 %collective-permute-start.8 = (bf16[512,128]{1,0:T(8,128)(2,1)S(1)}, bf16[512,128]{1,0:T(8,128)(2,1)S(1)}, u32[]{:S(2)}, u32[]{:S(2)}) collective-permute-start(bf16[512,128]{1,0:T(8,128)(2,1)S(1)} %bitcast.142), channel_id=1, source_target_pairs={{0,4},{4,8},{8,12},{12,16},{16,20},{20,24},{24,28},{1,5},{5,9},{9,... | collective-permute-start | bytes 393224 | tf_op jit(solution)/shard_map/ppermute | solution.py:13
  21.6 2.6 %copy-start.2 = (bf16[128,2048]{0,1:T(8,128)(2,1)}, bf16[128,2048]{0,1:T(8,128)(2,1)S(1)}, u32[]{:S(2)}) copy-start(bf16[128,2048]{0,1:T(8,128)(2,1)S(1)} %copy.76) | copy-start | bytes 1572868
  25.4 4.7 %collective-permute-start = (f32[2056,128]{1,0:T(8,128)}, f32[2056,128]{1,0:T(8,128)S(1)}, u32[]{:S(2)}, u32[]{:S(2)}) collective-permute-start(f32[2056,128]{1,0:T(8,128)} %select_maximum_fusion), channel_id=1, source_target_pairs={{0,4},{4,0},{8,12},{12,8},{16,20},{20,16},{24,28},{28,24},{1,5},{5... | collective-permute-start | bytes 3158024 | tf_op jit(solution)/shard_map/ppermute | solution.py:86
  30.4 12.8 %collective-permute-start.1 = (bf16[2064,128]{1,0:T(8,128)(2,1)S(1)}, bf16[2064,128]{1,0:T(8,128)(2,1)S(1)}, u32[]{:S(2)}, u32[]{:S(2)}) collective-permute-start(bf16[2064,128]{1,0:T(8,128)(2,1)S(1)} %pad_maximum_fusion), channel_id=1, source_target_pairs={{4,8},{12,16},{20,24},{0,20},{8,28},{5,9},{13,17},{21,25},{1,21},{... | collective-permute-start | bytes 1585160 | tf_op jit(solution)/shard_map/ppermute | solution.py:104
  43.2 1.9 %collective-permute-start.2 = (bf16[2064,128]{1,0:T(8,128)(2,1)S(1)}, bf16[2064,128]{1,0:T(8,128)(2,1)S(1)}, u32[]{:S(2)}, u32[]{:S(2)}) collective-permute-start(bf16[2064,128]{1,0:T(8,128)(2,1)S(1)} %collective-permute-done.1), channel_id=1, source_target_pairs={{0,4},{4,0},{8,12},{12,8},{16,20},{20,16},{24,28},{28,24},{1,5},{5... | collective-permute-start | bytes 1585160 | tf_op jit(solution)/shard_map/ppermute | solution.py:105
  43.3 2.1 %copy-start.3 = (f32[128,16,128]{0,2,1:T(8,128)S(1)}, f32[128,16,128]{0,2,1:T(8,128)}, u32[]{:S(2)}) copy-start(f32[128,16,128]{0,2,1:T(8,128)} %convolution_bitcast_fusion.1) | copy-start | bytes 3145732
  44.2 3.5 %copy-start.1 = (f32[2,5,128,128,8]{3,2,4,1,0:T(8,128)}, f32[2,5,128,128,8]{3,2,4,1,0:T(8,128)S(1)}, u32[]{:S(2)}) copy-start(f32[2,5,128,128,8]{3,2,4,1,0:T(8,128)S(1)} %get-tuple-element.25) | copy-start | bytes 15728644
  46.1 3.6 %collective-permute-start.3 = (f32[128]{0:T(128)S(1)}, f32[128]{0:T(128)S(1)}, u32[]{:S(2)}, u32[]{:S(2)}) collective-permute-start(f32[128]{0:T(128)S(1)} %get-tuple-element.22), channel_id=1, source_target_pairs={{0,1},{1,0},{2,3},{3,2},{4,5},{5,4},{6,7},{7,6},{8,9},{9,8},{10,11... | collective-permute-start | bytes 1544 | tf_op jit(solution)/shard_map/ppermute | solution.py:28
  49.7 7.9 %collective-permute-start.4 = (f32[128]{0:T(128)S(1)}, f32[128]{0:T(128)S(1)}, u32[]{:S(2)}, u32[]{:S(2)}) collective-permute-start(f32[128]{0:T(128)S(1)} %add.95), channel_id=1, source_target_pairs={{0,2},{1,3},{2,0},{3,1},{4,6},{5,7},{6,4},{7,5},{8,10},{9,11},{10,... | collective-permute-start | bytes 1544 | tf_op jit(solution)/shard_map/ppermute | solution.py:28
  52.3 5.3 %copy-start.4 = (bf16[128,2048]{1,0:T(8,128)(2,1)S(1)}, bf16[128,2048]{1,0:T(8,128)(2,1)}, u32[]{:S(2)}) copy-start(bf16[128,2048]{1,0:T(8,128)(2,1)} %param.15) | copy-start | bytes 1572868
  52.3 5.3 %copy-start.5 = (f32[2048]{0:T(1024)S(1)}, f32[2048]{0:T(1024)}, u32[]{:S(2)}) copy-start(f32[2048]{0:T(1024)} %param.16) | copy-start | bytes 24580

commit v8 on v7

--- a/solution.py
+++ b/solution.py
@@ -79,9 +79,6 @@
     n_state = heads_here * DH
     state_rows = state.reshape(n_state, DH)
     factor_rows = jnp.pad(shrinkage_multiplier[None, :], ((0, 7), (0, DH - heads_here)))
-    window = jnp.concatenate(
-        [from_behind(pair, "ctx", step) for step in range(SPAN, 0, -1)] + [pair], axis=0
-    ).reshape(SPAN + 1, 2 * kv_here, rows, DH)
     first = jnp.concatenate([state_rows, factor_rows], axis=0)
     got = lax.ppermute(first, "ctx", [(i, i ^ 1) for i in range(count)])
     state_mate = got[:n_state]
@@ -102,7 +99,11 @@
     )
     routes = [(i, i + 1) for i in range(1, count - 1, 2)] + [(i, i + 5) for i in range(0, count - 5, 2)]
     received = lax.ppermute(packet, "ctx", routes)
+    pair_late, received = lax.optimization_barrier((pair, received))
     mate_packet = lax.ppermute(received, "ctx", [(i, i ^ 1) for i in range(count)])
+    window = jnp.concatenate(
+        [from_behind(pair_late, "ctx", step) for step in range(SPAN, 0, -1)] + [pair], axis=0
+    ).reshape(SPAN + 1, 2 * kv_here, rows, DH)
     near = jnp.where(odd, mate_packet, received)
     far = jnp.where(odd, received, mate_packet)
 

time: 59.3 us -> 62.2 us (1.049)
  waiting for transfers between devices: 9.97 us -> 14.9 us
  local copies, waits for them, and re-layouts: 10.3 us -> 6.14 us
  starting transfers between devices: 18.5 us -> 19.9 us
  other arithmetic: 7.82 us -> 8.69 us
    unnamed x21 -> x25, local copies, waits for them, and re-layouts: 7.17 us -> 3.02 us
    ppermute x1, starting transfers between devices: 1.32 us -> 4.55 us  [local(): received = lax.ppermute(packet, 'ctx', routes)]
    ppermute x4, waiting for transfers between devices: 0.01 us -> 2.63 us  [from_behind(): return lax.ppermute(shard, axis, pairs)]
    ppermute x4, starting transfers between devices: 12.8 us -> 10.6 us  [from_behind(): return lax.ppermute(shard, axis, pairs)]
    ppermute x1, waiting for transfers between devices: 0.01 us -> 2.13 us  [local(): got = lax.ppermute(first, 'ctx', [(i, i ^ 1) for i in range(count)])]
    ppermute x1, waiting for transfers between devices: 8.64 us -> 9.65 us  [local(): received = lax.ppermute(packet, 'ctx', routes)]
    ppermute x1, waiting for transfers between devices: 0.83 us -> 0.01 us  [local(): lax.ppermute(received, 'ctx', [(i, i ^ 1) for i in range(count)])]
    concatenate x1, other arithmetic: 0.04 us -> 0.87 us  [local(): jnp.concatenate([chip_state.astype(jnp.bfloat16).reshape(n_state, DH), ch...]
  transfers between devices with their start and end apart: 9 -> 9, of which waited for: 3 -> 4; matrix products, arithmetic and copies ran while one was open for 40% -> 20% of each run, Pallas kernels for 0% -> 0%
where the time goes in v8:
time: 62.2 us; the launch traced here: 61.7 us
  starting transfers between devices  19.9 us (32%)
  waiting for transfers between devices  14.9 us (24%)
  matrix products  9.74 us (16%)
  other arithmetic  8.69 us (14%)
  local copies, waits for them, and re-layouts  6.14 us (10%)
  between operations  2.38 us (4%)
    ppermute x4, starting transfers between devices, from_behind(): return lax.ppermute(shard, axis, pairs)  10.6 us
    ppermute x1, waiting for transfers between devices, local(): received = lax.ppermute(packet, 'ctx', routes)  9.65 us
    ppermute x1, starting transfers between devices, local(): received = lax.ppermute(packet, 'ctx', routes)  4.55 us
    ppermute x2, starting transfers between devices, all_sum(): x = x + lax.ppermute(x, axis, [(i, i ^ bit) for i in range(count)])  4.23 us
    dot_general x1, matrix products, local(): jnp.einsum('kgtbs,bksd->tkgd', expd.astype(jnp.bfloat16).reshape(kv_here,...  3.94 us
    unnamed x25, local copies, waits for them, and re-layouts  3.02 us
    dot_general x1, matrix products, block_terms(): jnp.einsum('hts,shd->thd', weights, values, preferred_element_type=jnp.fl...  2.78 us
    ppermute x4, waiting for transfers between devices, from_behind(): return lax.ppermute(shard, axis, pairs)  2.63 us
  transfers between devices with their start and end apart: 9, of which 4 were waited for; matrix products, arithmetic and copies ran while one was open for 20% of the time, Pallas kernels for 0%

profile of v8, /device:TPU:0, one launch (start us, length us, event | category | flops | bytes accessed | tf_op | source)
XLA Modules:
  0.0 61.7 jit_solution(11046206300294120934)
XLA Ops:
  0.6 0.0 copy-start
  0.7 0.9 %reduce-window.4 = s32[6,1]{0,1:T(1,128)S(1)} reduce-window(s32[6,1]{0,1:T(1,128)} %bitcast.151, s32[]{:T(128)} %constant.24.clone.1), window={size=6x1 pad=5_0x0_0}, to_apply=%region_0.0 | reduce-window | flops 30 | bytes 52 | tf_op jit(solution)/shard_map/reduce-window
  1.6 0.6 %fusion.51 = s32[]{:T(128)} fusion(s32[6,1]{0,1:T(1,128)S(1)} %reduce-window.4, s32[]{:T(128)} %bitcast.6), kind=kLoop, calls=%fused_computation.83 | loop fusion | flops 17 | bytes 32 | tf_op jit(solution)/shard_map/reduce_sum | solution.py:35
  2.2 0.1 convert_reduce_fusion.1
  2.3 0.6 slice.38
  3.6 0.7 %fusion.58 = (f32[128]{0:T(128)S(1)}, pred[128]{0:T(512)(128)(4,1)S(1)}, f32[128]{0:T(128)S(1)}) fusion(s32[128]{0:T(128)S(1)} %convert_reduce_fusion.1, s32[]{:T(128)S(6)} %select_n.61, s32[]{:T(128)} %bitcast.3), kind=kLoop, calls=%fused_computation.99 | loop fusion | flops 512 | bytes 1672 | tf_op jit(solution)/shard_map/convert_element_type | solution.py:125
  4.2 0.6 slice.40
  5.5 1.3 %copy.76 = bf16[128,2048]{0,1:T(8,128)(2,1)S(1)} copy(bf16[128,2048]{1,0:T(8,128)(2,1)} %param.12) | data formatting | bytes 1048576 | tf_op jit(solution)/shard_map/reshape | solution.py:66
  6.8 1.0 %reduce_window_sum.20 = f32[16,128]{1,0:T(8,128)S(1)} reduce-window(f32[16,128]{1,0:T(8,128)} %param.14, f32[]{:T(128)} %constant.49.clone.1), window={size=1x128 pad=0_0x127_0}, to_apply=%region_2.3 | reduce-window | flops 260096 | bytes 16388 | tf_op jit(solution)/shard_map/jit(cumsum)/reduce_window_sum | solution.py:40
  7.8 0.2 slice_reduce_fusion
  8.0 0.1 multiply_bitcast_fusion
  8.0 1.4 %fusion.22 = f32[16,128,128]{2,1,0:T(8,128)S(1)} fusion(bf16[128,16,128]{0,2,1:T(8,128)(2,1)S(1)} %bitcast.133, f32[128,16]{0,1:T(8,128)S(1)} %get-tuple-element.24, bf16[128,2048]{1,0:T(8,128)(2,1)} %param.13), kind=kOutput, calls=%fused_computation.33 | convolution fusion | flops 67895296 | bytes 2105344 | tf_op jit(solution)/shard_map/shd,she->hde/dot_general | solution.py:51
  9.4 1.1 %select_maximum_fusion = f32[2056,128]{1,0:T(8,128)} fusion(f32[1,16]{1,0:T(1,128)S(1)} %bitcast.147, f32[2048,128]{1,0:T(8,128)S(1)} %bitcast.127), kind=kLoop, calls=%fused_computation.18 | loop fusion | flops 789504 | bytes 2101312 | tf_op jit(solution)/shard_map/concatenate | solution.py:82
  10.5 0.5 collective-permute-start
  10.9 0.1 copy.54
  11.1 0.1 copy.55
  11.2 0.1 convert_reduce_fusion
  11.3 2.1 %collective-permute-done = f32[2056,128]{1,0:T(8,128)S(1)} collective-permute-done((f32[2056,128]{1,0:T(8,128)}, f32[2056,128]{1,0:T(8,128)S(1)}, u32[]{:S(2)}, u32[]{:S(2)}) %collective-permute-start) | collective-permute-done | bytes 1052704 | tf_op jit(solution)/shard_map/ppermute | solution.py:83
  13.4 0.3 select_convert_fusion.1
  13.7 0.9 %pad_maximum_fusion = bf16[2064,128]{1,0:T(8,128)(2,1)} fusion(bf16[16,128]{1,0:T(8,128)(2,1)S(1)} %fusion.50, bf16[2048,128]{1,0:T(8,128)(2,1)S(1)} %bitcast.135), kind=kLoop, calls=%fused_computation.31 | loop fusion | flops 1056768 | bytes 1056768 | tf_op jit(solution)/shard_map/concatenate | solution.py:97
  14.6 4.6 %collective-permute-start.1 = (bf16[2064,128]{1,0:T(8,128)(2,1)}, bf16[2064,128]{1,0:T(8,128)(2,1)S(1)}, u32[]{:S(2)}, u32[]{:S(2)}) collective-permute-start(bf16[2064,128]{1,0:T(8,128)(2,1)} %pad_maximum_fusion), channel_id=1, source_target_pairs={{4,8},{12,16},{20,24},{0,20},{8,28},{5,9},{13,17},{21,25},{1,21},{... | collective-permute-start | bytes 1585160 | tf_op jit(solution)/shard_map/ppermute | solution.py:101
  19.2 0.1 copy.56
  19.3 0.1 fusion.44
  19.4 2.8 %convolution_bitcast_fusion.1 = f32[128,16,128]{0,2,1:T(8,128)} fusion(bf16[128,16,128]{0,2,1:T(8,128)(2,1)S(1)} %bitcast.134, f32[16,128]{1,0:T(8,128)S(1)} %reduce_window_sum.20, pred[128,128]{1,0:T(8,128)(4,1)S(1)} %fusion.44, bf16[128,2048]{1,0:T(8,128)(2,1)} %param.13, bf16[128,2048]{1,0:T(8,128)(2,1)S(1)} %copy-done), kind=kOutput, calls=%fused_computation.14 | convolution fusion | flops 135528448 | bytes 2646016 | tf_op jit(solution)/shard_map/hts,shd->thd/dot_general | solution.py:46
  22.2 9.7 %collective-permute-done.1 = bf16[2064,128]{1,0:T(8,128)(2,1)S(1)} collective-permute-done((bf16[2064,128]{1,0:T(8,128)(2,1)}, bf16[2064,128]{1,0:T(8,128)(2,1)S(1)}, u32[]{:S(2)}, u32[]{:S(2)}) %collective-permute-start.1) | collective-permute-done | bytes 528416 | tf_op jit(solution)/shard_map/ppermute | solution.py:101
  31.9 1.3 %collective-permute-start.6 = (bf16[512,128]{1,0:T(8,128)(2,1)S(1)}, bf16[512,128]{1,0:T(8,128)(2,1)S(1)}, u32[]{:S(2)}, u32[]{:S(2)}) collective-permute-start(bf16[512,128]{1,0:T(8,128)(2,1)S(1)} %bitcast.139), channel_id=1, source_target_pairs={{0,12},{4,16},{8,20},{12,24},{16,28},{1,13},{5,17},{9,21},{13,25},... | collective-permute-start | bytes 393224 | tf_op jit(solution)/shard_map/ppermute | solution.py:13
  33.2 1.3 %collective-permute-start.5 = (bf16[512,128]{1,0:T(8,128)(2,1)S(1)}, bf16[512,128]{1,0:T(8,128)(2,1)S(1)}, u32[]{:S(2)}, u32[]{:S(2)}) collective-permute-start(bf16[512,128]{1,0:T(8,128)(2,1)S(1)} %bitcast.140), channel_id=1, source_target_pairs={{0,16},{4,20},{8,24},{12,28},{1,17},{5,21},{9,25},{13,29},{2,18},{... | collective-permute-start | bytes 393224 | tf_op jit(solution)/shard_map/ppermute | solution.py:13
  34.5 0.2 compare_and_fusion
  34.7 1.1 %copy.79 = bf16[16,8,16,128]{3,2,1,0:T(8,128)(2,1)S(1)} copy(bf16[16,8,16,128]{3,1,2,0:T(8,128)(2,1)} %bitcast.137) | data formatting | bytes 1048576
  35.9 4.7 %collective-permute-start.8 = (bf16[512,128]{1,0:T(8,128)(2,1)S(1)}, bf16[512,128]{1,0:T(8,128)(2,1)S(1)}, u32[]{:S(2)}, u32[]{:S(2)}) collective-permute-start(bf16[512,128]{1,0:T(8,128)(2,1)S(1)} %bitcast.141), channel_id=1, source_target_pairs={{0,4},{4,8},{8,12},{12,16},{16,20},{20,24},{24,28},{1,5},{5,9},{9,... | collective-permute-start | bytes 393224 | tf_op jit(solution)/shard_map/ppermute | solution.py:13
  40.6 3.3 %collective-permute-start.7 = (bf16[512,128]{1,0:T(8,128)(2,1)S(1)}, bf16[512,128]{1,0:T(8,128)(2,1)S(1)}, u32[]{:S(2)}, u32[]{:S(2)}) collective-permute-start(bf16[512,128]{1,0:T(8,128)(2,1)S(1)} %bitcast.142), channel_id=1, source_target_pairs={{0,8},{4,12},{8,16},{12,20},{16,24},{20,28},{1,9},{5,13},{9,17},{1... | collective-permute-start | bytes 393224 | tf_op jit(solution)/shard_map/ppermute | solution.py:13
  43.9 0.1 collective-permute-start.2
  44.0 2.6 %collective-permute-done.7 = bf16[512,128]{1,0:T(8,128)(2,1)S(1)} collective-permute-done((bf16[512,128]{1,0:T(8,128)(2,1)S(1)}, bf16[512,128]{1,0:T(8,128)(2,1)S(1)}, u32[]{:S(2)}, u32[]{:S(2)}) %collective-permute-start.7) | collective-permute-done | bytes 131104 | tf_op jit(solution)/shard_map/ppermute | solution.py:13
  46.8 0.9 %fusion = (f32[2,8,128]{2,1,0:T(8,128)S(1)}, f32[2,5,128,128,8]{3,2,4,1,0:T(8,128)S(1)}) fusion(pred[128,5,128]{0,2,1:T(8,128)(4,1)S(1)} %compare_and_fusion, bf16[128,2,8,128,1]{3,2,1,0,4:T(8,128)(2,1)S(1)} %bitcast.130, bf16[5,2,128,128]{3,2,1,0:T(8,128)(2,1)S(1)} %get-tuple-element.22), kind=kOutput, calls=%fused_computation.2 | convolution fusion | flops 339474432 | bytes 6184960 | tf_op jit(solution)/shard_map/tkgd,bksd->kgtbs/dot_general | solution.py:143
  47.8 0.1 broadcast_select_fusion
  47.9 0.1 slice_select_fusion
  48.0 0.1 slice-done
  48.0 0.3 copy-done.3
  48.3 0.7 %multiply_reduce_fusion = (f32[128]{0:T(128)S(1)}, f32[128,16,128]{0,2,1:T(8,128)S(1)}) fusion(f32[128,16,128]{0,2,1:T(8,128)S(1)} %copy-done.3, f32[128,16]{0,1:T(8,128)S(1)} %get-tuple-element.23, f32[16,128,128]{2,1,0:T(8,128)S(1)} %bitcast.128, bf16[16,128,128]{2,1,0:T(8,128)(2,1)S(1)} %bitcast.132, bf16[16,128,128]{2,1,0:T(8,128)(2,1)S(1)} %bitcast.131, ...), kind=kOutput, calls=%fused_computation.24 | convolution fusion | flops 70254464 | bytes 4727425 | tf_op jit(solution)/shard_map/thd,hde->the/dot_general | solution.py:122
  49.1 1.6 %collective-permute-start.3 = (f32[128]{0:T(128)S(1)}, f32[128]{0:T(128)S(1)}, u32[]{:S(2)}, u32[]{:S(2)}) collective-permute-start(f32[128]{0:T(128)S(1)} %get-tuple-element.26), channel_id=1, source_target_pairs={{0,1},{1,0},{2,3},{3,2},{4,5},{5,4},{6,7},{7,6},{8,9},{9,8},{10,11... | collective-permute-start | bytes 1544 | tf_op jit(solution)/shard_map/ppermute | solution.py:28
  50.7 1.2 %fusion.4 = f32[2,8,128]{2,1,0:T(8,128)S(1)} fusion(f32[2,5,128,128,8]{3,2,4,1,0:T(8,128)S(1)} %get-tuple-element.29, f32[2,8,128]{2,1,0:T(8,128)S(1)} %get-tuple-element.28, pred[128,5,128]{0,2,1:T(8,128)(4,1)S(1)} %compare_and_fusion), kind=kLoop, calls=%fused_computation.6 | loop fusion | flops 6551552 | bytes 5341184 | tf_op jit(solution)/shard_map/reduce_sum | solution.py:148
  52.0 0.2 copy.74
  52.2 0.5 collective-permute-done.3
  52.7 2.6 %collective-permute-start.4 = (f32[128]{0:T(128)S(1)}, f32[128]{0:T(128)S(1)}, u32[]{:S(2)}, u32[]{:S(2)}) collective-permute-start(f32[128]{0:T(128)S(1)} %add.95), channel_id=1, source_target_pairs={{0,2},{1,3},{2,0},{3,1},{4,6},{5,7},{6,4},{7,5},{8,10},{9,11},{10,... | collective-permute-start | bytes 1544 | tf_op jit(solution)/shard_map/ppermute | solution.py:28
  55.3 3.9 %divide_convert_fusion = bf16[128,2,8,128]{0,3,2,1:T(8,128)(2,1)S(1)} fusion(f32[2,5,128,128,8]{3,2,4,1,0:T(8,128)} %copy-done.1, f32[2,8,128]{2,1,0:T(8,128)S(1)} %get-tuple-element.28, pred[128,5,128]{0,2,1:T(8,128)(4,1)S(1)} %compare_and_fusion, f32[128,2,8]{0,2,1:T(8,128)S(1)} %bitcast.146, bf16[5,2,128,128]{2,3,0,1:T(8,128)(2,1)S(1)} %copy.74), kind=kOutput, calls=%fused_computation.22 | convolution fusion | flops 342622208 | bytes 6193152 | tf_op jit(solution)/shard_map/kgtbs,bksd->tkgd/dot_general | solution.py:149
  59.2 1.0 %copy.64 = bf16[128,2048]{1,0:T(8,128)(2,1)} copy(bf16[128,2048]{0,1:T(8,128)(2,1)S(1)} %bitcast.138) | data formatting | bytes 1048576
  60.2 0.3 copy.59
  60.6 1.1 %multiply_convert_fusion = bf16[128,2048]{1,0:T(8,128)(2,1)} fusion(bf16[128,2048]{1,0:T(8,128)(2,1)S(1)} %copy-done.4, f32[128,2048]{1,0:T(8,128)S(1)} %copy.59, f32[2048]{0:T(1024)S(1)} %copy-done.7, f32[128]{0:T(128)S(1)} %add_rsqrt_fusion), kind=kLoop, calls=%fused_computation.23 | loop fusion | flops 2097152 | bytes 2105856 | tf_op jit(solution)/shard_map/convert_element_type | solution.py:137
  (37 shorter events, 0.3 us)
Async XLA Ops:
  0.6 18.8 %copy-start = (bf16[128,2048]{1,0:T(8,128)(2,1)S(1)}, bf16[128,2048]{1,0:T(8,128)(2,1)}, u32[]{:S(2)}) copy-start(bf16[128,2048]{1,0:T(8,128)(2,1)} %param.11) | copy-start | bytes 1572868
  0.6 10.3 %copy-start.5 = (bf16[128,256]{1,0:T(8,128)(2,1)S(1)}, bf16[128,256]{1,0:T(8,128)(2,1)}, u32[]{:S(2)}) copy-start(bf16[128,256]{1,0:T(8,128)(2,1)} %param.18) | copy-start | bytes 196612
  0.7 10.4 %copy-start.6 = (bf16[128,256]{1,0:T(8,128)(2,1)S(1)}, bf16[128,256]{1,0:T(8,128)(2,1)}, u32[]{:S(2)}) copy-start(bf16[128,256]{1,0:T(8,128)(2,1)} %param.19) | copy-start | bytes 196612
  10.5 3.0 %collective-permute-start = (f32[2056,128]{1,0:T(8,128)}, f32[2056,128]{1,0:T(8,128)S(1)}, u32[]{:S(2)}, u32[]{:S(2)}) collective-permute-start(f32[2056,128]{1,0:T(8,128)} %select_maximum_fusion), channel_id=1, source_target_pairs={{0,4},{4,0},{8,12},{12,8},{16,20},{20,16},{24,28},{28,24},{1,5},{5... | collective-permute-start | bytes 3158024 | tf_op jit(solution)/shard_map/ppermute | solution.py:83
  13.4 22.4 %copy-start.2 = (f32[2056,128]{1,0:T(8,128)}, f32[2056,128]{1,0:T(8,128)S(1)}, u32[]{:S(2)}) copy-start(f32[2056,128]{1,0:T(8,128)S(1)} %collective-permute-done) | copy-start | bytes 3158020
  14.6 17.3 %collective-permute-start.1 = (bf16[2064,128]{1,0:T(8,128)(2,1)}, bf16[2064,128]{1,0:T(8,128)(2,1)S(1)}, u32[]{:S(2)}, u32[]{:S(2)}) collective-permute-start(bf16[2064,128]{1,0:T(8,128)(2,1)} %pad_maximum_fusion), channel_id=1, source_target_pairs={{4,8},{12,16},{20,24},{0,20},{8,28},{5,9},{13,17},{21,25},{1,21},{... | collective-permute-start | bytes 1585160 | tf_op jit(solution)/shard_map/ppermute | solution.py:101
  31.9 12.1 %collective-permute-start.6 = (bf16[512,128]{1,0:T(8,128)(2,1)S(1)}, bf16[512,128]{1,0:T(8,128)(2,1)S(1)}, u32[]{:S(2)}, u32[]{:S(2)}) collective-permute-start(bf16[512,128]{1,0:T(8,128)(2,1)S(1)} %bitcast.139), channel_id=1, source_target_pairs={{0,12},{4,16},{8,20},{12,24},{16,28},{1,13},{5,17},{9,21},{13,25},... | collective-permute-start | bytes 393224 | tf_op jit(solution)/shard_map/ppermute | solution.py:13
  33.2 10.8 %collective-permute-start.5 = (bf16[512,128]{1,0:T(8,128)(2,1)S(1)}, bf16[512,128]{1,0:T(8,128)(2,1)S(1)}, u32[]{:S(2)}, u32[]{:S(2)}) collective-permute-start(bf16[512,128]{1,0:T(8,128)(2,1)S(1)} %bitcast.140), channel_id=1, source_target_pairs={{0,16},{4,20},{8,24},{12,28},{1,17},{5,21},{9,25},{13,29},{2,18},{... | collective-permute-start | bytes 393224 | tf_op jit(solution)/shard_map/ppermute | solution.py:13
  35.9 10.8 %collective-permute-start.8 = (bf16[512,128]{1,0:T(8,128)(2,1)S(1)}, bf16[512,128]{1,0:T(8,128)(2,1)S(1)}, u32[]{:S(2)}, u32[]{:S(2)}) collective-permute-start(bf16[512,128]{1,0:T(8,128)(2,1)S(1)} %bitcast.141), channel_id=1, source_target_pairs={{0,4},{4,8},{8,12},{12,16},{16,20},{20,24},{24,28},{1,5},{5,9},{9,... | collective-permute-start | bytes 393224 | tf_op jit(solution)/shard_map/ppermute | solution.py:13
  40.6 6.0 %collective-permute-start.7 = (bf16[512,128]{1,0:T(8,128)(2,1)S(1)}, bf16[512,128]{1,0:T(8,128)(2,1)S(1)}, u32[]{:S(2)}, u32[]{:S(2)}) collective-permute-start(bf16[512,128]{1,0:T(8,128)(2,1)S(1)} %bitcast.142), channel_id=1, source_target_pairs={{0,8},{4,12},{8,16},{12,20},{16,24},{20,28},{1,9},{5,13},{9,17},{1... | collective-permute-start | bytes 393224 | tf_op jit(solution)/shard_map/ppermute | solution.py:13
  43.9 3.9 %collective-permute-start.2 = (bf16[2064,128]{1,0:T(8,128)(2,1)S(1)}, bf16[2064,128]{1,0:T(8,128)(2,1)S(1)}, u32[]{:S(2)}, u32[]{:S(2)}) collective-permute-start(bf16[2064,128]{1,0:T(8,128)(2,1)S(1)} %collective-permute-done.1), channel_id=1, source_target_pairs={{0,4},{4,0},{8,12},{12,8},{16,20},{20,16},{24,28},{28,24},{1,5},{5... | collective-permute-start | bytes 1585160 | tf_op jit(solution)/shard_map/ppermute | solution.py:103
  46.8 1.2 %slice-start = ((f32[2056,128]{1,0:T(8,128)}), f32[2048,128]{1,0:T(8,128)S(1)}, s32[]{:S(2)}) async-start(f32[2056,128]{1,0:T(8,128)} %copy-done.2), calls=%async_computation | async-start | bytes 2097152 | tf_op jit(solution)/shard_map/slice | solution.py:84
  46.8 1.5 %copy-start.3 = (f32[128,16,128]{0,2,1:T(8,128)S(1)}, f32[128,16,128]{0,2,1:T(8,128)}, u32[]{:S(2)}) copy-start(f32[128,16,128]{0,2,1:T(8,128)} %convolution_bitcast_fusion.1) | copy-start | bytes 3145732
  47.8 4.2 %copy-start.1 = (f32[2,5,128,128,8]{3,2,4,1,0:T(8,128)}, f32[2,5,128,128,8]{3,2,4,1,0:T(8,128)S(1)}, u32[]{:S(2)}) copy-start(f32[2,5,128,128,8]{3,2,4,1,0:T(8,128)S(1)} %get-tuple-element.29) | copy-start | bytes 15728644
  49.1 3.6 %collective-permute-start.3 = (f32[128]{0:T(128)S(1)}, f32[128]{0:T(128)S(1)}, u32[]{:S(2)}, u32[]{:S(2)}) collective-permute-start(f32[128]{0:T(128)S(1)} %get-tuple-element.26), channel_id=1, source_target_pairs={{0,1},{1,0},{2,3},{3,2},{4,5},{5,4},{6,7},{7,6},{8,9},{9,8},{10,11... | collective-permute-start | bytes 1544 | tf_op jit(solution)/shard_map/ppermute | solution.py:28
  52.7 7.9 %collective-permute-start.4 = (f32[128]{0:T(128)S(1)}, f32[128]{0:T(128)S(1)}, u32[]{:S(2)}, u32[]{:S(2)}) collective-permute-start(f32[128]{0:T(128)S(1)} %add.95), channel_id=1, source_target_pairs={{0,2},{1,3},{2,0},{3,1},{4,6},{5,7},{6,4},{7,5},{8,10},{9,11},{10,... | collective-permute-start | bytes 1544 | tf_op jit(solution)/shard_map/ppermute | solution.py:28
  55.3 5.3 %copy-start.4 = (bf16[128,2048]{1,0:T(8,128)(2,1)S(1)}, bf16[128,2048]{1,0:T(8,128)(2,1)}, u32[]{:S(2)}) copy-start(bf16[128,2048]{1,0:T(8,128)(2,1)} %param.15) | copy-start | bytes 1572868
  55.3 5.3 %copy-start.7 = (f32[2048]{0:T(1024)S(1)}, f32[2048]{0:T(1024)}, u32[]{:S(2)}) copy-start(f32[2048]{0:T(1024)} %param.16) | copy-start | bytes 24580

commit v9 on v7

--- a/solution.py
+++ b/solution.py
@@ -79,11 +79,22 @@
     n_state = heads_here * DH
     state_rows = state.reshape(n_state, DH)
     factor_rows = jnp.pad(shrinkage_multiplier[None, :], ((0, 7), (0, DH - heads_here)))
-    window = jnp.concatenate(
-        [from_behind(pair, "ctx", step) for step in range(SPAN, 0, -1)] + [pair], axis=0
-    ).reshape(SPAN + 1, 2 * kv_here, rows, DH)
+    swap = [(i, i ^ 1) for i in range(count)]
+    routes = [(i, i + 1) for i in range(1, count - 1, 2)] + [(i, i + 5) for i in range(0, count - 5, 2)]
+    pair_mate = lax.ppermute(pair, "ctx", swap)
+    chip_pair = jnp.concatenate(
+        [jnp.where(odd, pair_mate, pair), jnp.where(odd, pair, pair_mate)], axis=0
+    )
+    pairs_got = lax.ppermute(chip_pair, "ctx", routes)
+    pairs_other = lax.ppermute(pairs_got, "ctx", swap)
+    pairs_near = jnp.where(odd, pairs_other, pairs_got)
+    pairs_far = jnp.where(odd, pairs_got, pairs_other)
+    window_even = jnp.concatenate([pairs_far, pairs_near], axis=0)
+    window_odd = jnp.concatenate([pairs_far[n_pair:], pairs_near, pair_mate], axis=0)
+    window = jnp.concatenate([jnp.where(odd, window_odd, window_even), pair], axis=0)
+    window = window.reshape(SPAN + 1, 2 * kv_here, rows, DH)
     first = jnp.concatenate([state_rows, factor_rows], axis=0)
-    got = lax.ppermute(first, "ctx", [(i, i ^ 1) for i in range(count)])
+    got = lax.ppermute(first, "ctx", swap)
     state_mate = got[:n_state]
     factor_mate = got[n_state, :heads_here]
     state_cube = state_rows.reshape(state.shape)
@@ -100,9 +111,8 @@
     packet = jnp.concatenate(
         [chip_state.astype(jnp.bfloat16).reshape(n_state, DH), chip_rows], axis=0
     )
-    routes = [(i, i + 1) for i in range(1, count - 1, 2)] + [(i, i + 5) for i in range(0, count - 5, 2)]
     received = lax.ppermute(packet, "ctx", routes)
-    mate_packet = lax.ppermute(received, "ctx", [(i, i ^ 1) for i in range(count)])
+    mate_packet = lax.ppermute(received, "ctx", swap)
     near = jnp.where(odd, mate_packet, received)
     far = jnp.where(odd, received, mate_packet)
 

time: 59.3 us -> 61.4 us (1.035)
  waiting for transfers between devices: 9.97 us -> 17.4 us
  starting transfers between devices: 18.5 us -> 14 us
  local copies, waits for them, and re-layouts: 10.3 us -> 7.48 us
  other arithmetic: 7.82 us -> 9.79 us
    ppermute x6 -> x5, starting transfers between devices: 12.9 us -> 5.79 us  [the longest x1 5.21 us: local(): pairs_got = lax.ppermute(chip_pair, 'ctx', routes)]
    ppermute x6 -> x5, waiting for transfers between devices: 0.85 us -> 4.77 us  [the longest x1 3.94 us: local(): pairs_got = lax.ppermute(chip_pair, 'ctx', routes)]
    ppermute x1, waiting for transfers between devices: 8.64 us -> 12.2 us  [local(): received = lax.ppermute(packet, 'ctx', routes)]
    unnamed x21, local copies, waits for them, and re-layouts: 7.17 us -> 4.38 us
    ppermute x1, starting transfers between devices: 1.32 us -> 3.95 us  [local(): received = lax.ppermute(packet, 'ctx', routes)]
    select_n x0 -> x3, other arithmetic: none -> 1.28 us  [the longest x1 1.1 us: local(): pairs_far = jnp.where(odd, pairs_got, pairs_other)]
    and x1, other arithmetic: 0.24 us -> 0.87 us  [local(): (key_docs[None, :] == docs[:, None]) & (key_pos[None, :] <= positions[:,...]
  transfers between devices with their start and end apart: 9 -> 8, of which waited for: 3 -> 4; matrix products, arithmetic and copies ran while one was open for 40% -> 37% of each run, Pallas kernels for 0% -> 0%
where the time goes in v9:
time: 61.4 us; the launch traced here: 60.9 us
  waiting for transfers between devices  17.4 us (28%)
  starting transfers between devices  14 us (23%)
  matrix products  9.85 us (16%)
  other arithmetic  9.79 us (16%)
  local copies, waits for them, and re-layouts  7.48 us (12%)
  between operations  2.33 us (4%)
    ppermute x1, waiting for transfers between devices, local(): received = lax.ppermute(packet, 'ctx', routes)  12.2 us
    ppermute x1, starting transfers between devices, local(): pairs_got = lax.ppermute(chip_pair, 'ctx', routes)  5.21 us
    unnamed x21, local copies, waits for them, and re-layouts  4.38 us
    ppermute x2, starting transfers between devices, all_sum(): x = x + lax.ppermute(x, axis, [(i, i ^ bit) for i in range(count)])  4.23 us
    ppermute x1, starting transfers between devices, local(): received = lax.ppermute(packet, 'ctx', routes)  3.95 us
    ppermute x1, waiting for transfers between devices, local(): pairs_got = lax.ppermute(chip_pair, 'ctx', routes)  3.94 us
    dot_general x1, matrix products, local(): jnp.einsum('kgtbs,bksd->tkgd', expd.astype(jnp.bfloat16).reshape(kv_here,...  3.92 us
    dot_general x1, matrix products, block_terms(): jnp.einsum('hts,shd->thd', weights, values, preferred_element_type=jnp.fl...  2.94 us
  transfers between devices with their start and end apart: 8, of which 4 were waited for; matrix products, arithmetic and copies ran while one was open for 37% of the time, Pallas kernels for 0%

profile of v9, /device:TPU:0, one launch (start us, length us, event | category | flops | bytes accessed | tf_op | source)
XLA Modules:
  0.0 60.9 jit_solution(4057364405811271075)
XLA Ops:
  0.6 0.0 copy-start
  0.6 1.0 %copy.57 = bf16[128,256]{0,1:T(8,128)(2,1)S(1)} copy(bf16[128,256]{1,0:T(8,128)(2,1)} %param.18) | data formatting | bytes 131072 | tf_op args[8]
  1.7 1.0 %copy.58 = bf16[128,256]{0,1:T(8,128)(2,1)S(1)} copy(bf16[128,256]{1,0:T(8,128)(2,1)} %param.19) | data formatting | bytes 131072 | tf_op args[9]
  2.6 0.1 copy.59
  2.8 0.5 collective-permute-start.5
  3.3 0.8 %reduce-window.4 = s32[6,1]{0,1:T(1,128)S(1)} reduce-window(s32[6,1]{0,1:T(1,128)} %bitcast.150, s32[]{:T(128)} %constant.24.clone.1), window={size=6x1 pad=5_0x0_0}, to_apply=%region_0.0 | reduce-window | flops 30 | bytes 52 | tf_op jit(solution)/shard_map/reduce-window
  4.1 0.1 convert_reduce_fusion.1
  4.3 0.6 %fusion.51 = s32[]{:T(128)} fusion(s32[6,1]{0,1:T(1,128)S(1)} %reduce-window.4, s32[]{:T(128)} %bitcast.6), kind=kLoop, calls=%fused_computation.85 | loop fusion | flops 17 | bytes 32 | tf_op jit(solution)/shard_map/reduce_sum | solution.py:35
  4.9 0.6 slice.41
  6.1 0.7 %fusion.58 = (f32[128]{0:T(128)S(1)}, pred[128]{0:T(512)(128)(4,1)S(1)}, f32[128]{0:T(128)S(1)}) fusion(s32[128]{0:T(128)S(1)} %convert_reduce_fusion.1, s32[]{:T(128)S(6)} %select_n.93, s32[]{:T(128)} %bitcast.3), kind=kLoop, calls=%fused_computation.101 | loop fusion | flops 512 | bytes 1672 | tf_op jit(solution)/shard_map/convert_element_type | solution.py:134
  6.8 0.6 slice.43
  8.0 1.3 %copy.76 = bf16[128,2048]{0,1:T(8,128)(2,1)S(1)} copy(bf16[128,2048]{1,0:T(8,128)(2,1)} %param.12) | data formatting | bytes 1048576 | tf_op jit(solution)/shard_map/reshape | solution.py:66
  9.3 0.0 copy-start.2
  9.3 1.0 %reduce_window_sum.20 = f32[16,128]{1,0:T(8,128)S(1)} reduce-window(f32[16,128]{1,0:T(8,128)} %param.14, f32[]{:T(128)} %constant.49.clone.1), window={size=1x128 pad=0_0x127_0}, to_apply=%region_2.3 | reduce-window | flops 260096 | bytes 16388 | tf_op jit(solution)/shard_map/jit(cumsum)/reduce_window_sum | solution.py:40
  10.4 0.2 slice_reduce_fusion
  10.5 0.1 multiply_bitcast_fusion
  10.6 1.4 %fusion.22 = f32[16,128,128]{2,1,0:T(8,128)S(1)} fusion(bf16[128,16,128]{0,2,1:T(8,128)(2,1)S(1)} %bitcast.136, f32[128,16]{0,1:T(8,128)S(1)} %get-tuple-element.24, bf16[128,2048]{1,0:T(8,128)(2,1)} %param.13), kind=kOutput, calls=%fused_computation.34 | convolution fusion | flops 67895296 | bytes 2105344 | tf_op jit(solution)/shard_map/shd,she->hde/dot_general | solution.py:51
  12.0 1.1 %select_maximum_fusion = f32[2056,128]{1,0:T(8,128)} fusion(f32[1,16]{1,0:T(1,128)S(1)} %bitcast.146, f32[2048,128]{1,0:T(8,128)S(1)} %bitcast.129), kind=kLoop, calls=%fused_computation.18 | loop fusion | flops 789504 | bytes 2101312 | tf_op jit(solution)/shard_map/concatenate | solution.py:96
  13.0 0.1 collective-permute-start
  13.1 0.1 fusion.44
  13.2 0.1 convert_reduce_fusion
  13.4 5.2 %collective-permute-start.6 = (bf16[1024,128]{1,0:T(8,128)(2,1)S(1)}, bf16[1024,128]{1,0:T(8,128)(2,1)}, u32[]{:S(2)}, u32[]{:S(2)}) collective-permute-start(bf16[1024,128]{1,0:T(8,128)(2,1)S(1)} %pad_maximum_fusion.2), channel_id=1, source_target_pairs={{4,8},{12,16},{20,24},{0,20},{8,28},{5,9},{13,17},{21,25},{1,21},{... | collective-permute-start | bytes 786440 | tf_op jit(solution)/shard_map/ppermute | solution.py:88
  18.6 1.1 %copy.79 = bf16[16,8,16,128]{3,2,1,0:T(8,128)(2,1)S(1)} copy(bf16[16,8,16,128]{3,1,2,0:T(8,128)(2,1)} %bitcast.141) | data formatting | bytes 1048576
  19.8 0.9 %compare_and_fusion = pred[128,5,128]{0,2,1:T(8,128)(4,1)} fusion(s32[128]{0:T(128)S(1)} %iota_add_fusion.1, s32[5,128]{1,0:T(8,128)S(1)} %get-tuple-element.31, s32[128]{0:T(128)S(1)} %convert_reduce_fusion.1, s32[5,128]{1,0:T(8,128)S(1)} %get-tuple-element.30), kind=kLoop, calls=%fused_computation.57 | loop fusion | flops 245760 | bytes 88064 | tf_op jit(solution)/shard_map/and | solution.py:150
  20.6 3.9 %collective-permute-done.6 = bf16[1024,128]{1,0:T(8,128)(2,1)} collective-permute-done((bf16[1024,128]{1,0:T(8,128)(2,1)S(1)}, bf16[1024,128]{1,0:T(8,128)(2,1)}, u32[]{:S(2)}, u32[]{:S(2)}) %collective-permute-start.6) | collective-permute-done | bytes 262176 | tf_op jit(solution)/shard_map/ppermute | solution.py:88
  24.6 2.9 %convolution_bitcast_fusion.1 = f32[128,16,128]{0,2,1:T(8,128)} fusion(bf16[128,16,128]{0,2,1:T(8,128)(2,1)} %bitcast.137, f32[16,128]{1,0:T(8,128)S(1)} %reduce_window_sum.20, pred[128,128]{1,0:T(8,128)(4,1)S(1)} %fusion.44, bf16[128,2048]{1,0:T(8,128)(2,1)} %param.13, bf16[128,2048]{1,0:T(8,128)(2,1)S(1)} %copy-done), kind=kOutput, calls=%fused_computation.14 | convolution fusion | flops 135528448 | bytes 2646016 | tf_op jit(solution)/shard_map/hts,shd->thd/dot_general | solution.py:46
  27.5 1.1 %broadcast_select_fusion.2 = (bf16[1024,128]{1,0:T(8,128)(2,1)S(1)}, bf16[1024,128]{1,0:T(8,128)(2,1)S(1)}) fusion(bf16[1024,128]{1,0:T(8,128)(2,1)} %collective-permute-done.6, bf16[1024,128]{1,0:T(8,128)(2,1)} %collective-permute-done.7, pred[]{:T(512)S(6)} %eq.59), kind=kLoop, calls=%fused_computation.60 | loop fusion | flops 262144 | bytes 1048577 | tf_op jit(solution)/shard_map/jit(_where)/select_n | solution.py:91
  28.7 0.3 select_convert_fusion.1
  29.1 3.9 %collective-permute-start.1 = (bf16[2064,128]{1,0:T(8,128)(2,1)S(1)}, bf16[2064,128]{1,0:T(8,128)(2,1)S(1)}, u32[]{:S(2)}, u32[]{:S(2)}) collective-permute-start(bf16[2064,128]{1,0:T(8,128)(2,1)S(1)} %pad_maximum_fusion.1), channel_id=1, source_target_pairs={{4,8},{12,16},{20,24},{0,20},{8,28},{5,9},{13,17},{21,25},{1,21},{... | collective-permute-start | bytes 1585160 | tf_op jit(solution)/shard_map/ppermute | solution.py:114
  33.0 0.1 maximum_select_fusion
  33.2 12.2 %collective-permute-done.1 = bf16[2064,128]{1,0:T(8,128)(2,1)S(1)} collective-permute-done((bf16[2064,128]{1,0:T(8,128)(2,1)S(1)}, bf16[2064,128]{1,0:T(8,128)(2,1)S(1)}, u32[]{:S(2)}, u32[]{:S(2)}) %collective-permute-start.1) | collective-permute-done | bytes 528416 | tf_op jit(solution)/shard_map/ppermute | solution.py:114
  45.4 0.1 fusion.59
  45.4 0.9 %fusion = (f32[2,8,128]{2,1,0:T(8,128)S(1)}, f32[2,5,128,128,8]{3,2,4,1,0:T(8,128)S(1)}) fusion(pred[128,5,128]{0,2,1:T(8,128)(4,1)S(1)} %copy-done.3, bf16[128,2,8,128,1]{3,2,1,0,4:T(8,128)(2,1)S(1)} %bitcast.133, bf16[5,2,128,128]{3,2,1,0:T(8,128)(2,1)S(1)} %get-tuple-element.18), kind=kOutput, calls=%fused_computation.2 | convolution fusion | flops 339474432 | bytes 6184960 | tf_op jit(solution)/shard_map/tkgd,bksd->kgtbs/dot_general | solution.py:152
  46.4 0.1 slice.55
  46.5 0.8 %collective-permute-done.2 = bf16[2064,128]{1,0:T(8,128)(2,1)S(1)} collective-permute-done((bf16[2064,128]{1,0:T(8,128)(2,1)S(1)}, bf16[2064,128]{1,0:T(8,128)(2,1)S(1)}, u32[]{:S(2)}, u32[]{:S(2)}) %collective-permute-start.2) | collective-permute-done | bytes 528416 | tf_op jit(solution)/shard_map/ppermute | solution.py:115
  47.3 0.1 broadcast_select_fusion
  47.4 0.1 slice_select_fusion
  47.5 0.0 copy-start.4
  47.5 0.7 %multiply_reduce_fusion = (f32[128]{0:T(128)S(1)}, f32[128,16,128]{0,2,1:T(8,128)S(1)}) fusion(f32[128,16,128]{0,2,1:T(8,128)S(1)} %copy-done.5, f32[128,16]{0,1:T(8,128)S(1)} %get-tuple-element.23, f32[16,128,128]{2,1,0:T(8,128)S(1)} %bitcast.131, bf16[16,128,128]{2,1,0:T(8,128)(2,1)S(1)} %bitcast.135, bf16[16,128,128]{2,1,0:T(8,128)(2,1)S(1)} %bitcast.134, ...), kind=kOutput, calls=%fused_computation.24 | convolution fusion | flops 70254464 | bytes 4727425 | tf_op jit(solution)/shard_map/thd,hde->the/dot_general | solution.py:131
  48.2 1.6 %collective-permute-start.3 = (f32[128]{0:T(128)S(1)}, f32[128]{0:T(128)S(1)}, u32[]{:S(2)}, u32[]{:S(2)}) collective-permute-start(f32[128]{0:T(128)S(1)} %get-tuple-element.26), channel_id=1, source_target_pairs={{0,1},{1,0},{2,3},{3,2},{4,5},{5,4},{6,7},{7,6},{8,9},{9,8},{10,11... | collective-permute-start | bytes 1544 | tf_op jit(solution)/shard_map/ppermute | solution.py:28
  49.9 1.2 %fusion.4 = f32[2,8,128]{2,1,0:T(8,128)S(1)} fusion(f32[2,5,128,128,8]{3,2,4,1,0:T(8,128)S(1)} %get-tuple-element.29, f32[2,8,128]{2,1,0:T(8,128)S(1)} %get-tuple-element.28, pred[128,5,128]{0,2,1:T(8,128)(4,1)S(1)} %copy-done.3), kind=kLoop, calls=%fused_computation.6 | loop fusion | flops 6551552 | bytes 5341184 | tf_op jit(solution)/shard_map/reduce_sum | solution.py:157
  51.1 0.2 copy.74
  51.3 0.5 collective-permute-done.3
  51.8 2.6 %collective-permute-start.4 = (f32[128]{0:T(128)S(1)}, f32[128]{0:T(128)S(1)}, u32[]{:S(2)}, u32[]{:S(2)}) collective-permute-start(f32[128]{0:T(128)S(1)} %add.95), channel_id=1, source_target_pairs={{0,2},{1,3},{2,0},{3,1},{4,6},{5,7},{6,4},{7,5},{8,10},{9,11},{10,... | collective-permute-start | bytes 1544 | tf_op jit(solution)/shard_map/ppermute | solution.py:28
  54.4 3.9 %divide_convert_fusion = bf16[128,2,8,128]{0,3,2,1:T(8,128)(2,1)S(1)} fusion(f32[2,5,128,128,8]{3,2,4,1,0:T(8,128)} %copy-done.1, f32[2,8,128]{2,1,0:T(8,128)S(1)} %get-tuple-element.28, pred[128,5,128]{0,2,1:T(8,128)(4,1)S(1)} %copy-done.4, f32[128,2,8]{0,2,1:T(8,128)S(1)} %bitcast.145, bf16[5,2,128,128]{2,3,0,1:T(8,128)(2,1)S(1)} %copy.74), kind=kOutput, calls=%fused_computation.22 | convolution fusion | flops 342622208 | bytes 6193152 | tf_op jit(solution)/shard_map/kgtbs,bksd->tkgd/dot_general | solution.py:158
  58.4 1.0 %copy.64 = bf16[128,2048]{1,0:T(8,128)(2,1)} copy(bf16[128,2048]{0,1:T(8,128)(2,1)S(1)} %bitcast.142) | data formatting | bytes 1048576
  59.4 0.3 copy.56
  59.8 1.1 %multiply_convert_fusion = bf16[128,2048]{1,0:T(8,128)(2,1)} fusion(bf16[128,2048]{1,0:T(8,128)(2,1)S(1)} %copy-done.6, f32[128,2048]{1,0:T(8,128)S(1)} %copy.56, f32[2048]{0:T(1024)S(1)} %copy-done.7, f32[128]{0:T(128)S(1)} %add_rsqrt_fusion), kind=kLoop, calls=%fused_computation.23 | loop fusion | flops 2097152 | bytes 2105856 | tf_op jit(solution)/shard_map/convert_element_type | solution.py:146
  (35 shorter events, 0.3 us)
Async XLA Ops:
  0.6 24.0 %copy-start = (bf16[128,2048]{1,0:T(8,128)(2,1)S(1)}, bf16[128,2048]{1,0:T(8,128)(2,1)}, u32[]{:S(2)}) copy-start(bf16[128,2048]{1,0:T(8,128)(2,1)} %param.11) | copy-start | bytes 1572868
  2.8 10.5 %collective-permute-start.5 = (bf16[512,128]{1,0:T(8,128)(2,1)S(1)}, bf16[512,128]{1,0:T(8,128)(2,1)S(1)}, u32[]{:S(2)}, u32[]{:S(2)}) collective-permute-start(bf16[512,128]{1,0:T(8,128)(2,1)S(1)} %bitcast.139), channel_id=1, source_target_pairs={{0,4},{4,0},{8,12},{12,8},{16,20},{20,16},{24,28},{28,24},{1,5},{5... | collective-permute-start | bytes 393224 | tf_op jit(solution)/shard_map/ppermute | solution.py:84
  9.3 2.6 %copy-start.2 = (bf16[128,2048]{0,1:T(8,128)(2,1)}, bf16[128,2048]{0,1:T(8,128)(2,1)S(1)}, u32[]{:S(2)}) copy-start(bf16[128,2048]{0,1:T(8,128)(2,1)S(1)} %copy.76) | copy-start | bytes 1572868
  13.0 15.6 %collective-permute-start = (f32[2056,128]{1,0:T(8,128)}, f32[2056,128]{1,0:T(8,128)S(1)}, u32[]{:S(2)}, u32[]{:S(2)}) collective-permute-start(f32[2056,128]{1,0:T(8,128)} %select_maximum_fusion), channel_id=1, source_target_pairs={{0,4},{4,0},{8,12},{12,8},{16,20},{20,16},{24,28},{28,24},{1,5},{5... | collective-permute-start | bytes 3158024 | tf_op jit(solution)/shard_map/ppermute | solution.py:97
  13.4 11.2 %collective-permute-start.6 = (bf16[1024,128]{1,0:T(8,128)(2,1)S(1)}, bf16[1024,128]{1,0:T(8,128)(2,1)}, u32[]{:S(2)}, u32[]{:S(2)}) collective-permute-start(bf16[1024,128]{1,0:T(8,128)(2,1)S(1)} %pad_maximum_fusion.2), channel_id=1, source_target_pairs={{4,8},{12,16},{20,24},{0,20},{8,28},{5,9},{13,17},{21,25},{1,21},{... | collective-permute-start | bytes 786440 | tf_op jit(solution)/shard_map/ppermute | solution.py:88
  24.6 3.0 %collective-permute-start.7 = (bf16[1024,128]{1,0:T(8,128)(2,1)}, bf16[1024,128]{1,0:T(8,128)(2,1)}, u32[]{:S(2)}, u32[]{:S(2)}) collective-permute-start(bf16[1024,128]{1,0:T(8,128)(2,1)} %collective-permute-done.6), channel_id=1, source_target_pairs={{0,4},{4,0},{8,12},{12,8},{16,20},{20,16},{24,28},{28,24},{1,5},{5... | collective-permute-start | bytes 786440 | tf_op jit(solution)/shard_map/ppermute | solution.py:89
  27.5 17.9 %copy-start.3 = (pred[128,5,128]{0,2,1:T(8,128)(4,1)S(1)}, pred[128,5,128]{0,2,1:T(8,128)(4,1)}, u32[]{:S(2)}) copy-start(pred[128,5,128]{0,2,1:T(8,128)(4,1)} %compare_and_fusion) | copy-start | bytes 245764
  29.1 16.3 %collective-permute-start.1 = (bf16[2064,128]{1,0:T(8,128)(2,1)S(1)}, bf16[2064,128]{1,0:T(8,128)(2,1)S(1)}, u32[]{:S(2)}, u32[]{:S(2)}) collective-permute-start(bf16[2064,128]{1,0:T(8,128)(2,1)S(1)} %pad_maximum_fusion.1), channel_id=1, source_target_pairs={{4,8},{12,16},{20,24},{0,20},{8,28},{5,9},{13,17},{21,25},{1,21},{... | collective-permute-start | bytes 1585160 | tf_op jit(solution)/shard_map/ppermute | solution.py:114
  45.4 1.9 %collective-permute-start.2 = (bf16[2064,128]{1,0:T(8,128)(2,1)S(1)}, bf16[2064,128]{1,0:T(8,128)(2,1)S(1)}, u32[]{:S(2)}, u32[]{:S(2)}) collective-permute-start(bf16[2064,128]{1,0:T(8,128)(2,1)S(1)} %collective-permute-done.1), channel_id=1, source_target_pairs={{0,4},{4,0},{8,12},{12,8},{16,20},{20,16},{24,28},{28,24},{1,5},{5... | collective-permute-start | bytes 1585160 | tf_op jit(solution)/shard_map/ppermute | solution.py:115
  45.4 2.0 %copy-start.5 = (f32[128,16,128]{0,2,1:T(8,128)S(1)}, f32[128,16,128]{0,2,1:T(8,128)}, u32[]{:S(2)}) copy-start(f32[128,16,128]{0,2,1:T(8,128)} %convolution_bitcast_fusion.1) | copy-start | bytes 3145732
  46.4 3.5 %copy-start.1 = (f32[2,5,128,128,8]{3,2,4,1,0:T(8,128)}, f32[2,5,128,128,8]{3,2,4,1,0:T(8,128)S(1)}, u32[]{:S(2)}) copy-start(f32[2,5,128,128,8]{3,2,4,1,0:T(8,128)S(1)} %get-tuple-element.29) | copy-start | bytes 15728644
  47.5 6.9 %copy-start.4 = (pred[128,5,128]{0,2,1:T(8,128)(4,1)S(1)}, pred[128,5,128]{0,2,1:T(8,128)(4,1)}, u32[]{:S(2)}) copy-start(pred[128,5,128]{0,2,1:T(8,128)(4,1)} %compare_and_fusion) | copy-start | bytes 245764
  48.2 3.6 %collective-permute-start.3 = (f32[128]{0:T(128)S(1)}, f32[128]{0:T(128)S(1)}, u32[]{:S(2)}, u32[]{:S(2)}) collective-permute-start(f32[128]{0:T(128)S(1)} %get-tuple-element.26), channel_id=1, source_target_pairs={{0,1},{1,0},{2,3},{3,2},{4,5},{5,4},{6,7},{7,6},{8,9},{9,8},{10,11... | collective-permute-start | bytes 1544 | tf_op jit(solution)/shard_map/ppermute | solution.py:28
  51.8 7.9 %collective-permute-start.4 = (f32[128]{0:T(128)S(1)}, f32[128]{0:T(128)S(1)}, u32[]{:S(2)}, u32[]{:S(2)}) collective-permute-start(f32[128]{0:T(128)S(1)} %add.95), channel_id=1, source_target_pairs={{0,2},{1,3},{2,0},{3,1},{4,6},{5,7},{6,4},{7,5},{8,10},{9,11},{10,... | collective-permute-start | bytes 1544 | tf_op jit(solution)/shard_map/ppermute | solution.py:28
  54.4 5.3 %copy-start.6 = (bf16[128,2048]{1,0:T(8,128)(2,1)S(1)}, bf16[128,2048]{1,0:T(8,128)(2,1)}, u32[]{:S(2)}) copy-start(bf16[128,2048]{1,0:T(8,128)(2,1)} %param.15) | copy-start | bytes 1572868
  54.4 5.3 %copy-start.7 = (f32[2048]{0:T(1024)S(1)}, f32[2048]{0:T(1024)}, u32[]{:S(2)}) copy-start(f32[2048]{0:T(1024)} %param.16) | copy-start | bytes 24580

commit v10 on v7

--- a/solution.py
+++ b/solution.py
@@ -70,18 +70,16 @@
     )
     count = lax.axis_size("ctx")
     odd = (shard % 2) == 1
-    pair = jnp.concatenate(
-        [soft_k.reshape(rows, kv_here, DH).transpose(1, 0, 2),
-         soft_v.reshape(rows, kv_here, DH).transpose(1, 0, 2)],
-        axis=0,
-    ).reshape(-1, DH)
-    n_pair = pair.shape[0]
+    pair = jnp.concatenate([soft_k, soft_v], axis=1)
+    kv_width = soft_k.shape[1]
     n_state = heads_here * DH
     state_rows = state.reshape(n_state, DH)
     factor_rows = jnp.pad(shrinkage_multiplier[None, :], ((0, 7), (0, DH - heads_here)))
     window = jnp.concatenate(
         [from_behind(pair, "ctx", step) for step in range(SPAN, 0, -1)] + [pair], axis=0
-    ).reshape(SPAN + 1, 2 * kv_here, rows, DH)
+    )
+    all_keys = window[:, :kv_width].reshape(-1, kv_here, DH)
+    all_values = window[:, kv_width:].reshape(-1, kv_here, DH)
     first = jnp.concatenate([state_rows, factor_rows], axis=0)
     got = lax.ppermute(first, "ctx", [(i, i ^ 1) for i in range(count)])
     state_mate = got[:n_state]
@@ -140,16 +138,13 @@
     allowed = (key_docs[None, :] == docs[:, None]) & (key_pos[None, :] <= positions[:, None])
     soft_query = soft_q.reshape(rows, kv_here, group, DH)
     scores = jnp.einsum(
-        "tkgd,bksd->kgtbs", soft_query, window[:, :kv_here], preferred_element_type=jnp.float32
-    ).reshape(kv_here, group, rows, span_rows) * DH ** (-0.5)
+        "tkgd,skd->kgts", soft_query, all_keys, preferred_element_type=jnp.float32
+    ) * DH ** (-0.5)
     top = jnp.max(jnp.where(allowed, scores, -1e30), axis=-1, keepdims=True)
     expd = jnp.where(allowed, jnp.exp(jnp.minimum(scores - top, 0.0)), 0.0)
     total = jnp.sum(expd, axis=-1)
     attended = jnp.einsum(
-        "kgtbs,bksd->tkgd",
-        expd.astype(jnp.bfloat16).reshape(kv_here, group, rows, SPAN + 1, rows),
-        window[:, kv_here:],
-        preferred_element_type=jnp.float32,
+        "kgts,skd->tkgd", expd.astype(jnp.bfloat16), all_values, preferred_element_type=jnp.float32
     )
     attended = attended / total.transpose(2, 0, 1)[..., None]
     soft_out = attended.reshape(rows, kv_here * group * DH).astype(jnp.bfloat16)

time: 59.3 us -> 67.1 us (1.13)
  other arithmetic: 7.82 us -> 13.7 us
  matrix products: 9.89 us -> 13.2 us
  waiting for transfers between devices: 9.97 us -> 7.97 us
    sub x0 -> x1, matrix products: none -> 5.37 us  [local(): expd = jnp.where(allowed, jnp.exp(jnp.minimum(scores - top, 0.0)), 0.0)]
    dot_general x2 -> x1, matrix products: 4.86 us -> 2.31 us  [local(): jnp.einsum('kgts,skd->tkgd', expd.astype(jnp.bfloat16), all_values, prefe...]
    unnamed x21 -> x46, local copies, waits for them, and re-layouts: 7.17 us -> 5.86 us
    and x1, other arithmetic: 0.08 us -> 1.36 us  [block_terms(): same = (docs[:, None] == docs[None, :]) & (order[None, :] <= order[:, None])]
    reduce_sum x3, other arithmetic: 0.8 us -> 2.06 us  [document_of(): jnp.sum((ends[None, :] <= positions[:, None]).astype(jnp.int32), axis=1)]
    mul x1, other arithmetic: 0.01 us -> 1.25 us  [block_terms(): jnp.exp(level[:, -1]) * carried[-1].astype(jnp.float32)]
    reduce_sum x1 -> x0, other arithmetic: 1.23 us -> none  [local(): total = jnp.sum(expd, axis=-1)]
    slice x1 -> x2, local copies, waits for them, and re-layouts: 0.07 us -> 0.92 us  [local(): state_mate = got[:n_state]]
  transfers between devices with their start and end apart: 9 -> 9, of which waited for: 3 -> 2; matrix products, arithmetic and copies ran while one was open for 40% -> 35% of each run, Pallas kernels for 0% -> 0%
where the time goes in v10:
time: 67.1 us; the launch traced here: 66.5 us
  starting transfers between devices  18.9 us (28%)
  other arithmetic  13.7 us (20%)
  matrix products  13.2 us (20%)
  local copies, waits for them, and re-layouts  10.5 us (16%)
  waiting for transfers between devices  7.97 us (12%)
  between operations  2.34 us (3%)
    ppermute x4, starting transfers between devices, from_behind(): return lax.ppermute(shard, axis, pairs)  12.9 us
    ppermute x1, waiting for transfers between devices, local(): received = lax.ppermute(packet, 'ctx', routes)  7.87 us
    unnamed x46, local copies, waits for them, and re-layouts  5.86 us
    sub x1, matrix products, local(): expd = jnp.where(allowed, jnp.exp(jnp.minimum(scores - top, 0.0)), 0.0)  5.37 us
    ppermute x2, starting transfers between devices, all_sum(): x = x + lax.ppermute(x, axis, [(i, i ^ bit) for i in range(count)])  4.17 us
    dot_general x1, matrix products, block_terms(): jnp.einsum('hts,shd->thd', weights, values, preferred_element_type=jnp.fl...  2.83 us
    dot_general x1, matrix products, local(): jnp.einsum('kgts,skd->tkgd', expd.astype(jnp.bfloat16), all_values, prefe...  2.31 us
    reduce_sum x3, other arithmetic, document_of(): jnp.sum((ends[None, :] <= positions[:, None]).astype(jnp.int32), axis=1)  2.06 us
  transfers between devices with their start and end apart: 9, of which 2 were waited for; matrix products, arithmetic and copies ran while one was open for 35% of the time, Pallas kernels for 0%

profile of v10, /device:TPU:0, one launch (start us, length us, event | category | flops | bytes accessed | tf_op | source)
XLA Modules:
  0.0 66.5 jit_solution(3709440332206615093)
XLA Ops:
  0.7 0.9 %reduce-window.4 = s32[6,1]{0,1:T(1,128)S(1)} reduce-window(s32[6,1]{0,1:T(1,128)} %bitcast.125, s32[]{:T(128)} %constant.21.clone.1), window={size=6x1 pad=5_0x0_0}, to_apply=%region_0.0 | reduce-window | flops 30 | bytes 52 | tf_op jit(solution)/shard_map/reduce-window
  1.5 0.1 convert_reduce_fusion.1
  1.6 0.5 copy-done.16
  2.2 0.6 fusion.63
  2.8 0.6 slice.38
  4.0 0.7 fusion.70
  4.7 0.6 slice.40
  5.9 1.4 %copy.54 = bf16[128,2048]{0,1:T(8,128)(2,1)S(1)} copy(bf16[128,2048]{1,0:T(8,128)(2,1)} %param.12) | data formatting | bytes 1048576 | tf_op jit(solution)/shard_map/reshape | solution.py:66
  7.3 1.0 %reduce_window_sum.20 = f32[16,128]{1,0:T(8,128)S(1)} reduce-window(f32[16,128]{1,0:T(8,128)} %param.14, f32[]{:T(128)} %constant.47.clone.1), window={size=1x128 pad=0_0x127_0}, to_apply=%region_2.3 | reduce-window | flops 260096 | bytes 16388 | tf_op jit(solution)/shard_map/jit(cumsum)/reduce_window_sum | solution.py:40
  8.3 0.2 slice_reduce_fusion
  8.5 0.6 multiply_bitcast_fusion
  9.1 1.3 %fusion.30 = f32[16,128,128]{2,1,0:T(8,128)S(1)} fusion(bf16[128,16,128]{0,2,1:T(8,128)(2,1)S(1)} %bitcast.113, f32[128,16]{0,1:T(8,128)S(1)} %get-tuple-element.18, bf16[128,2048]{1,0:T(8,128)(2,1)} %param.13), kind=kOutput, calls=%fused_computation.38 | convolution fusion | flops 67895296 | bytes 2105344 | tf_op jit(solution)/shard_map/shd,she->hde/dot_general | solution.py:51
  10.5 1.0 %select_maximum_fusion = f32[2056,128]{1,0:T(8,128)} fusion(f32[1,16]{1,0:T(1,128)S(1)} %bitcast.121, f32[2048,128]{1,0:T(8,128)S(1)} %bitcast.108), kind=kLoop, calls=%fused_computation.23 | loop fusion | flops 789504 | bytes 2101312 | tf_op jit(solution)/shard_map/concatenate | solution.py:83
  11.5 0.5 collective-permute-start
  12.0 0.1 copy.42
  12.1 0.1 copy.43
  12.3 5.1 %collective-permute-start.5 = (bf16[128,512]{0,1:T(8,128)(2,1)S(1)}, bf16[128,512]{0,1:T(8,128)(2,1)}, u32[]{:S(2)}, u32[]{:S(2)}) collective-permute-start(bf16[128,512]{0,1:T(8,128)(2,1)S(1)} %pad_maximum_fusion.1), channel_id=1, source_target_pairs={{0,16},{4,20},{8,24},{12,28},{1,17},{5,21},{9,25},{13,29},{2,18},{... | collective-permute-start | bytes 393224 | tf_op jit(solution)/shard_map/ppermute | solution.py:13
  17.3 3.9 %collective-permute-start.6 = (bf16[128,512]{0,1:T(8,128)(2,1)S(1)}, bf16[128,512]{0,1:T(8,128)(2,1)}, u32[]{:S(2)}, u32[]{:S(2)}) collective-permute-start(bf16[128,512]{0,1:T(8,128)(2,1)S(1)} %pad_maximum_fusion.1), channel_id=1, source_target_pairs={{0,12},{4,16},{8,20},{12,24},{16,28},{1,13},{5,17},{9,21},{13,25},... | collective-permute-start | bytes 393224 | tf_op jit(solution)/shard_map/ppermute | solution.py:13
  21.2 2.1 %collective-permute-start.7 = (bf16[128,512]{0,1:T(8,128)(2,1)S(1)}, bf16[128,512]{0,1:T(8,128)(2,1)}, u32[]{:S(2)}, u32[]{:S(2)}) collective-permute-start(bf16[128,512]{0,1:T(8,128)(2,1)S(1)} %pad_maximum_fusion.1), channel_id=1, source_target_pairs={{0,8},{4,12},{8,16},{12,20},{16,24},{20,28},{1,9},{5,13},{9,17},{1... | collective-permute-start | bytes 393224 | tf_op jit(solution)/shard_map/ppermute | solution.py:13
  23.3 1.8 %collective-permute-start.8 = (bf16[128,512]{0,1:T(8,128)(2,1)S(1)}, bf16[128,512]{0,1:T(8,128)(2,1)S(1)}, u32[]{:S(2)}, u32[]{:S(2)}) collective-permute-start(bf16[128,512]{0,1:T(8,128)(2,1)S(1)} %pad_maximum_fusion.1), channel_id=1, source_target_pairs={{0,4},{4,8},{8,12},{12,16},{16,20},{20,24},{24,28},{1,5},{5,9},{9,... | collective-permute-start | bytes 393224 | tf_op jit(solution)/shard_map/ppermute | solution.py:13
  25.2 1.3 %convert_reduce_fusion = s32[640]{0:T(1024)} fusion(s32[640]{0:T(1024)S(1)} %iota_add_fusion, s32[6]{0:T(128)} %bitcast.124), kind=kLoop, calls=%fused_computation.63 | loop fusion | flops 10880 | bytes 5144 | tf_op jit(solution)/shard_map/reduce_sum | solution.py:35
  26.5 1.3 %exponential_multiply_fusion = f32[16]{0:T(128)} fusion(f32[16]{0:T(128)} %copy-done.15, f32[]{:T(128)} %bitcast.7), kind=kLoop, calls=%fused_computation.93 | loop fusion | flops 16 | bytes 132 | tf_op jit(solution)/shard_map/mul | solution.py:52
  27.8 1.4 %fusion.56 = pred[128,128]{1,0:T(8,128)(4,1)} fusion(s32[128]{0:T(128)} %copy-done.12), kind=kLoop, calls=%fused_computation.62 | loop fusion | flops 49152 | bytes 16896 | tf_op jit(solution)/shard_map/and | solution.py:42
  29.2 2.8 %convolution_bitcast_fusion.1 = f32[128,16,128]{0,2,1:T(8,128)} fusion(bf16[128,16,128]{0,2,1:T(8,128)(2,1)S(1)} %bitcast.114, f32[16,128]{1,0:T(8,128)S(1)} %reduce_window_sum.20, pred[128,128]{1,0:T(8,128)(4,1)} %fusion.56, bf16[128,2048]{1,0:T(8,128)(2,1)} %param.13, bf16[128,2048]{1,0:T(8,128)(2,1)S(1)} %copy-done), kind=kOutput, calls=%fused_computation.16 | convolution fusion | flops 135528448 | bytes 2646016 | tf_op jit(solution)/shard_map/hts,shd->thd/dot_general | solution.py:46
  32.0 0.8 %fusion.69 = (bf16[1,16]{1,0:T(2,128)(2,1)S(1)}, bf16[1,16]{1,0:T(2,128)(2,1)S(1)}, f32[16]{0:T(128)S(1)}) fusion(f32[2056,128]{1,0:T(8,128)S(1)} %collective-permute-done, f32[16]{0:T(128)} %copy-done.14), kind=kLoop, calls=%fused_computation.101 | loop fusion | flops 80 | bytes 256 | tf_op jit(solution)/shard_map/convert_element_type | solution.py:95
  32.8 1.0 %select_convert_fusion.1 = bf16[16,128,128]{2,1,0:T(8,128)(2,1)S(1)} fusion(f32[16,128,128]{2,1,0:T(8,128)S(1)} %fusion.30, f32[16]{0:T(128)} %exponential_multiply_fusion, f32[16]{0:T(128)S(1)} %get-tuple-element.14, pred[]{:T(512)S(6)} %eq.58, f32[2056,128]{1,0:T(8,128)S(1)} %collective-permute-done), kind=kLoop, calls=%fused_computation.30 | loop fusion | flops 1572864 | bytes 2621569 | tf_op jit(solution)/shard_map/convert_element_type | solution.py:99
  33.8 1.3 %collective-permute-start.1 = (bf16[2064,128]{1,0:T(8,128)(2,1)S(1)}, bf16[2064,128]{1,0:T(8,128)(2,1)S(1)}, u32[]{:S(2)}, u32[]{:S(2)}) collective-permute-start(bf16[2064,128]{1,0:T(8,128)(2,1)S(1)} %pad_maximum_fusion), channel_id=1, source_target_pairs={{4,8},{12,16},{20,24},{0,20},{8,28},{5,9},{13,17},{21,25},{1,21},{... | collective-permute-start | bytes 1585160 | tf_op jit(solution)/shard_map/ppermute | solution.py:102
  35.2 0.9 %compare_and_fusion = pred[128,640]{0,1:T(8,128)(4,1)} fusion(s32[128]{0:T(128)S(1)} %copy-done.17, s32[128]{0:T(128)S(1)} %copy-done.13, s32[640]{0:T(1024)S(1)} %iota_add_fusion, s32[640]{0:T(1024)S(1)} %compare_select_fusion), kind=kLoop, calls=%fused_computation.59 | loop fusion | flops 245760 | bytes 88064 | tf_op jit(solution)/shard_map/and | solution.py:138
  36.1 0.9 %copy.57 = bf16[16,8,16,128]{3,2,1,0:T(8,128)(2,1)} copy(bf16[16,8,16,128]{3,1,2,0:T(8,128)(2,1)S(1)} %bitcast.116) | data formatting | bytes 1048576
  37.0 0.9 %constant_dynamic-update-slice_fusion.4 = bf16[640,512]{0,1:T(8,128)(2,1)S(1)} fusion(bf16[128,512]{0,1:T(8,128)(2,1)} %collective-permute-done.5), kind=kLoop, calls=%fused_computation.68 | loop fusion | bytes 262144
  37.9 0.9 %constant_dynamic-update-slice_fusion.3 = bf16[640,512]{0,1:T(8,128)(2,1)S(1)} fusion(bf16[640,512]{0,1:T(8,128)(2,1)S(1)} %constant_dynamic-update-slice_fusion.4, bf16[128,512]{0,1:T(8,128)(2,1)} %collective-permute-done.6), kind=kLoop, calls=%fused_computation.67 | loop fusion | bytes 262144
  38.9 7.9 %collective-permute-done.1 = bf16[2064,128]{1,0:T(8,128)(2,1)S(1)} collective-permute-done((bf16[2064,128]{1,0:T(8,128)(2,1)S(1)}, bf16[2064,128]{1,0:T(8,128)(2,1)S(1)}, u32[]{:S(2)}, u32[]{:S(2)}) %collective-permute-start.1) | collective-permute-done | bytes 528416 | tf_op jit(solution)/shard_map/ppermute | solution.py:102
  46.8 0.9 %constant_dynamic-update-slice_fusion.2 = bf16[640,512]{0,1:T(8,128)(2,1)S(1)} fusion(bf16[640,512]{0,1:T(8,128)(2,1)S(1)} %constant_dynamic-update-slice_fusion.3, bf16[128,512]{0,1:T(8,128)(2,1)} %collective-permute-done.7), kind=kLoop, calls=%fused_computation.66 | loop fusion | bytes 262144
  47.8 0.8 %fusion.71 = (bf16[640,256]{0,1:T(8,128)(2,1)}, bf16[640,256]{0,1:T(8,128)(2,1)S(1)}) fusion(bf16[640,512]{0,1:T(8,128)(2,1)S(1)} %constant_dynamic-update-slice_fusion), kind=kLoop, calls=%fused_computation.103 | loop fusion | bytes 1310720 | tf_op jit(solution)/shard_map/slice | solution.py:81
  48.6 0.1 collective-permute-done.2
  48.7 0.1 broadcast_select_fusion
  48.8 0.1 slice_select_fusion
  48.9 0.9 %slice-done = f32[2048,128]{1,0:T(8,128)S(1)} async-done(((f32[2056,128]{1,0:T(8,128)}), f32[2048,128]{1,0:T(8,128)S(1)}, s32[]{:S(2)}) %slice-start) | async-done | bytes 1048600 | tf_op jit(solution)/shard_map/slice | solution.py:85
  49.8 0.3 copy-done.2
  50.1 1.3 %multiply_reduce_fusion = (f32[128]{0:T(128)}, f32[128,16,128]{0,2,1:T(8,128)S(1)}) fusion(f32[128,16,128]{0,2,1:T(8,128)S(1)} %copy-done.2, f32[128,16]{0,1:T(8,128)S(1)} %copy-done.9, f32[16,128,128]{2,1,0:T(8,128)S(1)} %bitcast.110, bf16[16,128,128]{2,1,0:T(8,128)(2,1)S(1)} %bitcast.112, bf16[16,128,128]{2,1,0:T(8,128)(2,1)S(1)} %bitcast.111, ...), kind=kOutput, calls=%fused_computation.28 | convolution fusion | flops 70254464 | bytes 4727425 | tf_op jit(solution)/shard_map/thd,hde->the/dot_general | solution.py:119
  51.4 1.6 %collective-permute-start.3 = (f32[128]{0:T(128)}, f32[128]{0:T(128)S(1)}, u32[]{:S(2)}, u32[]{:S(2)}) collective-permute-start(f32[128]{0:T(128)} %get-tuple-element.20), channel_id=1, source_target_pairs={{0,1},{1,0},{2,3},{3,2},{4,5},{5,4},{6,7},{7,6},{8,9},{9,8},{10,11... | collective-permute-start | bytes 1544 | tf_op jit(solution)/shard_map/ppermute | solution.py:28
  53.0 5.4 %fusion.72 = (f32[2,8,128]{2,1,0:T(8,128)S(1)}, bf16[2,8,128,640]{2,3,1,0:T(8,128)(2,1)}) fusion(pred[128,640]{0,1:T(8,128)(4,1)S(1)} %copy-done.6, bf16[640,2,128,1]{0,2,3,1:T(8,128)(2,1)} %bitcast.120, bf16[128,2,8,128]{3,2,1,0:T(8,128)(2,1)S(1)} %bitcast.117), kind=kOutput, calls=%fused_computation.104 | convolution fusion | flops 681575040 | bytes 3563520 | tf_op jit(solution)/shard_map/sub | solution.py:144
  58.4 0.7 %add.87 = f32[128]{0:T(128)S(1)} add(f32[128]{0:T(128)} %get-tuple-element.20, f32[128]{0:T(128)S(1)} %collective-permute-done.3) | non-fusion elementwise | flops 128 | bytes 1536 | tf_op jit(solution)/shard_map/add | solution.py:28
  59.1 2.6 %collective-permute-start.4 = (f32[128]{0:T(128)S(1)}, f32[128]{0:T(128)S(1)}, u32[]{:S(2)}, u32[]{:S(2)}) collective-permute-start(f32[128]{0:T(128)S(1)} %add.87), channel_id=1, source_target_pairs={{0,2},{1,3},{2,0},{3,1},{4,6},{5,7},{6,4},{7,5},{8,10},{9,11},{10,... | collective-permute-start | bytes 1544 | tf_op jit(solution)/shard_map/ppermute | solution.py:28
  61.7 2.3 %fusion.20 = bf16[128,2,8,128]{0,3,2,1:T(8,128)(2,1)S(1)} fusion(bf16[640,2,128,1]{0,2,3,1:T(8,128)(2,1)S(1)} %bitcast.119, bf16[2,8,128,640]{2,3,1,0:T(8,128)(2,1)} %get-tuple-element.23, f32[128,2,8]{0,2,1:T(8,128)S(1)} %bitcast.126), kind=kOutput, calls=%fused_computation.21 | convolution fusion | flops 336068608 | bytes 3481600 | tf_op jit(solution)/shard_map/kgts,skd->tkgd/dot_general | solution.py:146
  64.0 1.0 %copy.47 = bf16[128,2048]{1,0:T(8,128)(2,1)} copy(bf16[128,2048]{0,1:T(8,128)(2,1)S(1)} %bitcast.118) | data formatting | bytes 1048576
  65.0 0.3 copy.41
  65.4 1.1 %multiply_convert_fusion = bf16[128,2048]{1,0:T(8,128)(2,1)} fusion(bf16[128,2048]{1,0:T(8,128)(2,1)S(1)} %copy-done.3, f32[128,2048]{1,0:T(8,128)S(1)} %copy.41, f32[2048]{0:T(1024)S(1)} %copy-done.11, f32[128]{0:T(128)S(1)} %add_rsqrt_fusion), kind=kLoop, calls=%fused_computation.27 | loop fusion | flops 2097152 | bytes 2105856 | tf_op jit(solution)/shard_map/convert_element_type | solution.py:134
  (56 shorter events, 0.3 us)
Async XLA Ops:
  0.6 28.5 %copy-start = (bf16[128,2048]{1,0:T(8,128)(2,1)S(1)}, bf16[128,2048]{1,0:T(8,128)(2,1)}, u32[]{:S(2)}) copy-start(bf16[128,2048]{1,0:T(8,128)(2,1)} %param.11) | copy-start | bytes 1572868
  1.5 7.6 %copy-start.18 = (s32[6,1]{0,1:T(1,128)}, s32[6,1]{0,1:T(1,128)S(1)}, u32[]{:S(2)}) copy-start(s32[6,1]{0,1:T(1,128)S(1)} %reduce-window.4) | copy-start | bytes 76
  1.5 0.6 copy-start.16
  1.6 7.5 %copy-start.12 = (s32[128]{0:T(128)}, s32[128]{0:T(128)S(1)}, u32[]{:S(2)}) copy-start(s32[128]{0:T(128)S(1)} %convert_reduce_fusion.1) | copy-start | bytes 1540
  5.9 6.1 %copy-start.7 = (bf16[128,256]{1,0:T(8,128)(2,1)S(1)}, bf16[128,256]{1,0:T(8,128)(2,1)}, u32[]{:S(2)}) copy-start(bf16[128,256]{1,0:T(8,128)(2,1)} %param.18) | copy-start | bytes 196612
  5.9 6.2 %copy-start.8 = (bf16[128,256]{1,0:T(8,128)(2,1)S(1)}, bf16[128,256]{1,0:T(8,128)(2,1)}, u32[]{:S(2)}) copy-start(bf16[128,256]{1,0:T(8,128)(2,1)} %param.19) | copy-start | bytes 196612
  8.5 3.0 %copy-start.14 = (f32[16]{0:T(128)}, f32[16]{0:T(128)S(1)}, u32[]{:S(2)}) copy-start(f32[16]{0:T(128)S(1)} %get-tuple-element.9) | copy-start | bytes 196
  8.5 3.0 %copy-start.15 = (f32[16]{0:T(128)}, f32[16]{0:T(128)S(1)}, u32[]{:S(2)}) copy-start(f32[16]{0:T(128)S(1)} %get-tuple-element.8) | copy-start | bytes 196
  11.5 20.5 %collective-permute-start = (f32[2056,128]{1,0:T(8,128)}, f32[2056,128]{1,0:T(8,128)S(1)}, u32[]{:S(2)}, u32[]{:S(2)}) collective-permute-start(f32[2056,128]{1,0:T(8,128)} %select_maximum_fusion), channel_id=1, source_target_pairs={{0,4},{4,0},{8,12},{12,8},{16,20},{20,16},{24,28},{28,24},{1,5},{5... | collective-permute-start | bytes 3158024 | tf_op jit(solution)/shard_map/ppermute | solution.py:84
  12.3 24.7 %collective-permute-start.5 = (bf16[128,512]{0,1:T(8,128)(2,1)S(1)}, bf16[128,512]{0,1:T(8,128)(2,1)}, u32[]{:S(2)}, u32[]{:S(2)}) collective-permute-start(bf16[128,512]{0,1:T(8,128)(2,1)S(1)} %pad_maximum_fusion.1), channel_id=1, source_target_pairs={{0,16},{4,20},{8,24},{12,28},{1,17},{5,21},{9,25},{13,29},{2,18},{... | collective-permute-start | bytes 393224 | tf_op jit(solution)/shard_map/ppermute | solution.py:13
  17.3 20.6 %collective-permute-start.6 = (bf16[128,512]{0,1:T(8,128)(2,1)S(1)}, bf16[128,512]{0,1:T(8,128)(2,1)}, u32[]{:S(2)}, u32[]{:S(2)}) collective-permute-start(bf16[128,512]{0,1:T(8,128)(2,1)S(1)} %pad_maximum_fusion.1), channel_id=1, source_target_pairs={{0,12},{4,16},{8,20},{12,24},{16,28},{1,13},{5,17},{9,21},{13,25},... | collective-permute-start | bytes 393224 | tf_op jit(solution)/shard_map/ppermute | solution.py:13
  21.2 25.5 %collective-permute-start.7 = (bf16[128,512]{0,1:T(8,128)(2,1)S(1)}, bf16[128,512]{0,1:T(8,128)(2,1)}, u32[]{:S(2)}, u32[]{:S(2)}) collective-permute-start(bf16[128,512]{0,1:T(8,128)(2,1)S(1)} %pad_maximum_fusion.1), channel_id=1, source_target_pairs={{0,8},{4,12},{8,16},{12,20},{16,24},{20,28},{1,9},{5,13},{9,17},{1... | collective-permute-start | bytes 393224 | tf_op jit(solution)/shard_map/ppermute | solution.py:13
  23.3 24.4 %collective-permute-start.8 = (bf16[128,512]{0,1:T(8,128)(2,1)S(1)}, bf16[128,512]{0,1:T(8,128)(2,1)S(1)}, u32[]{:S(2)}, u32[]{:S(2)}) collective-permute-start(bf16[128,512]{0,1:T(8,128)(2,1)S(1)} %pad_maximum_fusion.1), channel_id=1, source_target_pairs={{0,4},{4,8},{8,12},{12,16},{16,20},{20,24},{24,28},{1,5},{5,9},{9,... | collective-permute-start | bytes 393224 | tf_op jit(solution)/shard_map/ppermute | solution.py:13
  32.0 3.2 %copy-start.10 = (s32[640]{0:T(1024)S(1)}, s32[640]{0:T(1024)}, u32[]{:S(2)}) copy-start(s32[640]{0:T(1024)} %convert_reduce_fusion) | copy-start | bytes 7684
  32.0 3.2 %copy-start.13 = (s32[128]{0:T(128)S(1)}, s32[128]{0:T(128)}, u32[]{:S(2)}) copy-start(s32[128]{0:T(128)} %copy-done.12) | copy-start | bytes 1540
  32.0 3.2 %copy-start.17 = (s32[128]{0:T(128)S(1)}, s32[128]{0:T(128)}, u32[]{:S(2)}) copy-start(s32[128]{0:T(128)} %copy-done.16) | copy-start | bytes 1540
  32.0 4.1 %copy-start.4 = (bf16[128,2048]{1,0:T(8,128)(2,1)S(1)}, bf16[128,2048]{1,0:T(8,128)(2,1)}, u32[]{:S(2)}) copy-start(bf16[128,2048]{1,0:T(8,128)(2,1)} %param.17) | copy-start | bytes 1572868
  32.0 16.6 %copy-start.1 = (f32[2056,128]{1,0:T(8,128)}, f32[2056,128]{1,0:T(8,128)S(1)}, u32[]{:S(2)}) copy-start(f32[2056,128]{1,0:T(8,128)S(1)} %collective-permute-done) | copy-start | bytes 3158020
  33.8 12.9 %collective-permute-start.1 = (bf16[2064,128]{1,0:T(8,128)(2,1)S(1)}, bf16[2064,128]{1,0:T(8,128)(2,1)S(1)}, u32[]{:S(2)}, u32[]{:S(2)}) collective-permute-start(bf16[2064,128]{1,0:T(8,128)(2,1)S(1)} %pad_maximum_fusion), channel_id=1, source_target_pairs={{4,8},{12,16},{20,24},{0,20},{8,28},{5,9},{13,17},{21,25},{1,21},{... | collective-permute-start | bytes 1585160 | tf_op jit(solution)/shard_map/ppermute | solution.py:102
  46.7 1.9 %collective-permute-start.2 = (bf16[2064,128]{1,0:T(8,128)(2,1)S(1)}, bf16[2064,128]{1,0:T(8,128)(2,1)S(1)}, u32[]{:S(2)}, u32[]{:S(2)}) collective-permute-start(bf16[2064,128]{1,0:T(8,128)(2,1)S(1)} %collective-permute-done.1), channel_id=1, source_target_pairs={{0,4},{4,0},{8,12},{12,8},{16,20},{20,16},{24,28},{28,24},{1,5},{5... | collective-permute-start | bytes 1585160 | tf_op jit(solution)/shard_map/ppermute | solution.py:103
  48.6 1.2 %slice-start = ((f32[2056,128]{1,0:T(8,128)}), f32[2048,128]{1,0:T(8,128)S(1)}, s32[]{:S(2)}) async-start(f32[2056,128]{1,0:T(8,128)} %copy-done.1), calls=%async_computation | async-start | bytes 2097152 | tf_op jit(solution)/shard_map/slice | solution.py:85
  48.6 1.5 %copy-start.2 = (f32[128,16,128]{0,2,1:T(8,128)S(1)}, f32[128,16,128]{0,2,1:T(8,128)}, u32[]{:S(2)}) copy-start(f32[128,16,128]{0,2,1:T(8,128)} %convolution_bitcast_fusion.1) | copy-start | bytes 3145732
  48.6 1.5 %copy-start.9 = (f32[128,16]{0,1:T(8,128)S(1)}, f32[128,16]{0,1:T(8,128)}, u32[]{:S(2)}) copy-start(f32[128,16]{0,1:T(8,128)} %get-tuple-element.17) | copy-start | bytes 24580
  48.9 4.2 %copy-start.5 = (bf16[16,8,16,128]{3,2,1,0:T(8,128)(2,1)S(1)}, bf16[16,8,16,128]{3,2,1,0:T(8,128)(2,1)}, u32[]{:S(2)}) copy-start(bf16[16,8,16,128]{3,2,1,0:T(8,128)(2,1)} %copy.57) | copy-start | bytes 1572868
  48.9 4.1 %copy-start.6 = (pred[128,640]{0,1:T(8,128)(4,1)S(1)}, pred[128,640]{0,1:T(8,128)(4,1)}, u32[]{:S(2)}) copy-start(pred[128,640]{0,1:T(8,128)(4,1)} %compare_and_fusion) | copy-start | bytes 245764
  51.4 7.0 %collective-permute-start.3 = (f32[128]{0:T(128)}, f32[128]{0:T(128)S(1)}, u32[]{:S(2)}, u32[]{:S(2)}) collective-permute-start(f32[128]{0:T(128)} %get-tuple-element.20), channel_id=1, source_target_pairs={{0,1},{1,0},{2,3},{3,2},{4,5},{5,4},{6,7},{7,6},{8,9},{9,8},{10,11... | collective-permute-start | bytes 1544 | tf_op jit(solution)/shard_map/ppermute | solution.py:28
  59.1 6.3 %collective-permute-start.4 = (f32[128]{0:T(128)S(1)}, f32[128]{0:T(128)S(1)}, u32[]{:S(2)}, u32[]{:S(2)}) collective-permute-start(f32[128]{0:T(128)S(1)} %add.87), channel_id=1, source_target_pairs={{0,2},{1,3},{2,0},{3,1},{4,6},{5,7},{6,4},{7,5},{8,10},{9,11},{10,... | collective-permute-start | bytes 1544 | tf_op jit(solution)/shard_map/ppermute | solution.py:28
  64.0 1.4 %copy-start.3 = (bf16[128,2048]{1,0:T(8,128)(2,1)S(1)}, bf16[128,2048]{1,0:T(8,128)(2,1)}, u32[]{:S(2)}) copy-start(bf16[128,2048]{1,0:T(8,128)(2,1)} %param.15) | copy-start | bytes 1572868
  64.0 1.4 %copy-start.11 = (f32[2048]{0:T(1024)S(1)}, f32[2048]{0:T(1024)}, u32[]{:S(2)}) copy-start(f32[2048]{0:T(1024)} %param.16) | copy-start | bytes 24580

commit v11 on v7

--- a/solution.py
+++ b/solution.py
@@ -31,7 +31,9 @@
 
 
 def document_of(positions, doc_lengths):
-    ends = jnp.cumsum(doc_lengths)
+    count = doc_lengths.shape[0]
+    upto = jnp.arange(count)[:, None] <= jnp.arange(count)[None, :]
+    ends = jnp.sum(jnp.where(upto, doc_lengths[:, None], 0), axis=0)
     return jnp.sum((ends[None, :] <= positions[:, None]).astype(jnp.int32), axis=1)
 
 
@@ -78,14 +80,16 @@
     n_pair = pair.shape[0]
     n_state = heads_here * DH
     state_rows = state.reshape(n_state, DH)
-    factor_rows = jnp.pad(shrinkage_multiplier[None, :], ((0, 7), (0, DH - heads_here)))
+    swap = [(i, i ^ 1) for i in range(count)]
+    decay_mate = lax.ppermute(log_decay, "ctx", swap)
+    mate_start = (shard ^ 1) * rows
+    mate_ends = document_of(jnp.stack([mate_start - 1, mate_start + rows - 1]), doc_lengths)
+    mate_carried = (mate_ends[1] == jnp.where(mate_start > 0, mate_ends[0], -1)).astype(jnp.float32)
+    factor_mate = jnp.exp(jnp.cumsum(decay_mate, axis=1)[:, -1]) * mate_carried
     window = jnp.concatenate(
         [from_behind(pair, "ctx", step) for step in range(SPAN, 0, -1)] + [pair], axis=0
     ).reshape(SPAN + 1, 2 * kv_here, rows, DH)
-    first = jnp.concatenate([state_rows, factor_rows], axis=0)
-    got = lax.ppermute(first, "ctx", [(i, i ^ 1) for i in range(count)])
-    state_mate = got[:n_state]
-    factor_mate = got[n_state, :heads_here]
+    state_mate = lax.ppermute(state_rows, "ctx", swap)
     state_cube = state_rows.reshape(state.shape)
     mate_cube = state_mate.reshape(state.shape)
     chip_state = jnp.where(
@@ -102,7 +106,7 @@
     )
     routes = [(i, i + 1) for i in range(1, count - 1, 2)] + [(i, i + 5) for i in range(0, count - 5, 2)]
     received = lax.ppermute(packet, "ctx", routes)
-    mate_packet = lax.ppermute(received, "ctx", [(i, i ^ 1) for i in range(count)])
+    mate_packet = lax.ppermute(received, "ctx", swap)
     near = jnp.where(odd, mate_packet, received)
     far = jnp.where(odd, received, mate_packet)
 

time: 59.3 us -> 63 us (1.062)
  between operations: 2.33 us -> 3.65 us
  starting transfers between devices: 18.5 us -> 19.5 us
  matrix products: 9.89 us -> 10.8 us
    concatenate x1 -> x0, other arithmetic: 1.06 us -> none  [local(): first = jnp.concatenate([state_rows, factor_rows], axis=0)]
    dot_general x1, matrix products: 0.74 us -> 1.73 us  [local(): jnp.einsum('thd,hde->the', query, incoming_b, preferred_element_type=jnp....]
    mul x1 -> x2, other arithmetic: 0.01 us -> 0.77 us  [block_terms(): jnp.exp(level[:, -1]) * carried[-1].astype(jnp.float32)]
    another operation x1, other arithmetic: 0.83 us -> 0.08 us  [local(): jnp.stack([mate_start - 1, mate_start + rows - 1])]
    reduce_sum x0 -> x1, other arithmetic: none -> 0.74 us  [document_of(): ends = jnp.sum(jnp.where(upto, doc_lengths[:, None], 0), axis=0)]
    ppermute x1, waiting for transfers between devices: 8.64 us -> 7.97 us  [local(): received = lax.ppermute(packet, 'ctx', routes)]
    convert_element_type x1, other arithmetic: 0.3 us -> 0.95 us  [local(): chip_state.astype(jnp.bfloat16).reshape(n_state, DH)]
  transfers between devices with their start and end apart: 9 -> 10, of which waited for: 3 -> 3; matrix products, arithmetic and copies ran while one was open for 40% -> 39% of each run, Pallas kernels for 0% -> 0%
where the time goes in v11:
time: 63 us; the launch traced here: 62.4 us
  starting transfers between devices  19.5 us (31%)
  local copies, waits for them, and re-layouts  10.8 us (17%)
  matrix products  10.8 us (17%)
  waiting for transfers between devices  9.4 us (15%)
  other arithmetic  8.25 us (13%)
  between operations  3.65 us (6%)
    ppermute x4, starting transfers between devices, from_behind(): return lax.ppermute(shard, axis, pairs)  13.4 us
    ppermute x1, waiting for transfers between devices, local(): received = lax.ppermute(packet, 'ctx', routes)  7.97 us
    unnamed x21, local copies, waits for them, and re-layouts  7.14 us
    ppermute x2, starting transfers between devices, all_sum(): x = x + lax.ppermute(x, axis, [(i, i ^ bit) for i in range(count)])  4.15 us
    dot_general x1, matrix products, local(): jnp.einsum('kgtbs,bksd->tkgd', expd.astype(jnp.bfloat16).reshape(kv_here,...  3.98 us
    dot_general x1, matrix products, block_terms(): jnp.einsum('hts,shd->thd', weights, values, preferred_element_type=jnp.fl...  2.79 us
    dot_general x1, matrix products, local(): jnp.einsum('thd,hde->the', query, incoming_b, preferred_element_type=jnp....  1.73 us
    dot_general x1, matrix products, block_terms(): jnp.einsum('shd,she->hde', weighted, values, preferred_element_type=jnp.f...  1.35 us
  transfers between devices with their start and end apart: 10, of which 3 were waited for; matrix products, arithmetic and copies ran while one was open for 39% of the time, Pallas kernels for 0%

profile of v11, /device:TPU:0, one launch (start us, length us, event | category | flops | bytes accessed | tf_op | source)
XLA Modules:
  0.0 62.4 jit_solution(18413815617811649641)
XLA Ops:
  0.6 1.0 %copy.57 = bf16[128,256]{0,1:T(8,128)(2,1)S(1)} copy(bf16[128,256]{1,0:T(8,128)(2,1)} %param.18) | data formatting | bytes 131072 | tf_op args[8]
  1.7 1.0 %copy.58 = bf16[128,256]{0,1:T(8,128)(2,1)S(1)} copy(bf16[128,256]{1,0:T(8,128)(2,1)} %param.19) | data formatting | bytes 131072 | tf_op args[9]
  2.6 0.1 copy.59
  2.8 5.5 %collective-permute-start.6 = (bf16[512,128]{1,0:T(8,128)(2,1)S(1)}, bf16[512,128]{1,0:T(8,128)(2,1)}, u32[]{:S(2)}, u32[]{:S(2)}) collective-permute-start(bf16[512,128]{1,0:T(8,128)(2,1)S(1)} %bitcast.145), channel_id=1, source_target_pairs={{0,16},{4,20},{8,24},{12,28},{1,17},{5,21},{9,25},{13,29},{2,18},{... | collective-permute-start | bytes 393224 | tf_op jit(solution)/shard_map/ppermute | solution.py:13
  8.3 3.2 %collective-permute-start.7 = (bf16[512,128]{1,0:T(8,128)(2,1)S(1)}, bf16[512,128]{1,0:T(8,128)(2,1)}, u32[]{:S(2)}, u32[]{:S(2)}) collective-permute-start(bf16[512,128]{1,0:T(8,128)(2,1)S(1)} %bitcast.146), channel_id=1, source_target_pairs={{0,12},{4,16},{8,20},{12,24},{16,28},{1,13},{5,17},{9,21},{13,25},... | collective-permute-start | bytes 393224 | tf_op jit(solution)/shard_map/ppermute | solution.py:13
  11.5 2.1 %collective-permute-start.8 = (bf16[512,128]{1,0:T(8,128)(2,1)S(1)}, bf16[512,128]{1,0:T(8,128)(2,1)S(1)}, u32[]{:S(2)}, u32[]{:S(2)}) collective-permute-start(bf16[512,128]{1,0:T(8,128)(2,1)S(1)} %bitcast.147), channel_id=1, source_target_pairs={{0,8},{4,12},{8,16},{12,20},{16,24},{20,28},{1,9},{5,13},{9,17},{1... | collective-permute-start | bytes 393224 | tf_op jit(solution)/shard_map/ppermute | solution.py:13
  13.7 0.7 %select_reduce_fusion = s32[6]{0:T(128)S(1)} fusion(s32[6]{0:T(128)} %param.10), kind=kLoop, calls=%fused_computation.79 | loop fusion | flops 102 | bytes 48 | tf_op jit(solution)/shard_map/reduce_sum | solution.py:36
  14.5 0.1 convert_reduce_fusion.1
  14.6 0.6 %fusion.52 = s32[]{:T(128)} fusion(s32[6]{0:T(128)S(1)} %select_reduce_fusion, s32[]{:T(128)} %bitcast.5), kind=kLoop, calls=%fused_computation.85 | loop fusion | flops 17 | bytes 32 | tf_op jit(solution)/shard_map/reduce_sum | solution.py:37
  15.2 0.6 slice.48
  16.5 0.7 %fusion.59 = (f32[128]{0:T(128)S(1)}, pred[128]{0:T(512)(128)(4,1)S(1)}, f32[128]{0:T(128)S(1)}) fusion(s32[128]{0:T(128)S(1)} %convert_reduce_fusion.1, s32[]{:T(128)S(6)} %select_n.74, s32[]{:T(128)} %bitcast.7), kind=kLoop, calls=%fused_computation.102 | loop fusion | flops 512 | bytes 1672 | tf_op jit(solution)/shard_map/convert_element_type | solution.py:128
  17.1 0.6 slice.47
  18.4 1.0 %reduce_window_sum.13 = f32[16,128]{1,0:T(8,128)S(1)} reduce-window(f32[16,128]{1,0:T(8,128)} %param.14, f32[]{:T(128)} %constant.47.clone.1), window={size=1x128 pad=0_0x127_0}, to_apply=%region_2.3 | reduce-window | flops 260096 | bytes 16388 | tf_op jit(solution)/shard_map/jit(cumsum)/reduce_window_sum | solution.py:42
  19.3 1.3 %copy.76 = bf16[128,2048]{0,1:T(8,128)(2,1)S(1)} copy(bf16[128,2048]{1,0:T(8,128)(2,1)} %param.12) | data formatting | bytes 1048576 | tf_op jit(solution)/shard_map/reshape | solution.py:68
  20.7 0.2 multiply_reduce_fusion.1
  20.8 0.1 multiply_bitcast_fusion
  20.9 1.4 %fusion.22 = f32[16,128,128]{2,1,0:T(8,128)S(1)} fusion(bf16[128,16,128]{0,2,1:T(8,128)(2,1)S(1)} %bitcast.139, f32[128,16]{0,1:T(8,128)S(1)} %get-tuple-element.19, bf16[128,2048]{1,0:T(8,128)(2,1)} %param.13), kind=kOutput, calls=%fused_computation.31 | convolution fusion | flops 67895296 | bytes 2105344 | tf_op jit(solution)/shard_map/shd,she->hde/dot_general | solution.py:53
  22.3 0.6 collective-permute-start.1
  22.8 0.6 exponential_multiply_fusion
  23.4 0.1 fusion.44
  23.5 0.1 convert_reduce_fusion
  23.6 0.2 compare_and_fusion
  23.9 0.1 pad_add_fusion
  23.9 0.2 fusion.51
  24.1 2.8 %convolution_bitcast_fusion.1 = f32[128,16,128]{0,2,1:T(8,128)} fusion(bf16[128,16,128]{0,2,1:T(8,128)(2,1)S(1)} %bitcast.140, f32[16,128]{1,0:T(8,128)S(1)} %reduce_window_sum.13, pred[128,128]{1,0:T(8,128)(4,1)S(1)} %fusion.44, bf16[128,2048]{1,0:T(8,128)(2,1)} %param.13, bf16[128,2048]{1,0:T(8,128)(2,1)S(1)} %copy-done), kind=kOutput, calls=%fused_computation.14 | convolution fusion | flops 135528448 | bytes 2646016 | tf_op jit(solution)/shard_map/hts,shd->thd/dot_general | solution.py:48
  26.9 0.6 fusion.61
  27.5 1.1 %copy.79 = bf16[16,8,16,128]{3,2,1,0:T(8,128)(2,1)S(1)} copy(bf16[16,8,16,128]{3,1,2,0:T(8,128)(2,1)} %bitcast.143) | data formatting | bytes 1048576
  30.0 2.6 %collective-permute-start.9 = (bf16[512,128]{1,0:T(8,128)(2,1)S(1)}, bf16[512,128]{1,0:T(8,128)(2,1)}, u32[]{:S(2)}, u32[]{:S(2)}) collective-permute-start(bf16[512,128]{1,0:T(8,128)(2,1)S(1)} %bitcast.148), channel_id=1, source_target_pairs={{0,4},{4,8},{8,12},{12,16},{16,20},{20,24},{24,28},{1,5},{5,9},{9,... | collective-permute-start | bytes 393224 | tf_op jit(solution)/shard_map/ppermute | solution.py:13
  32.6 0.1 slice.42
  32.7 1.0 %select_convert_fusion.1 = bf16[16,128,128]{2,1,0:T(8,128)(2,1)S(1)} fusion(f32[16,128,128]{2,1,0:T(8,128)S(1)} %fusion.22, f32[16]{0:T(128)} %exponential_multiply_fusion, f32[16]{0:T(128)S(1)} %get-tuple-element.15, pred[]{:T(512)S(6)} %eq.62, f32[2048,128]{1,0:T(8,128)S(1)} %collective-permute-done.1), kind=kLoop, calls=%fused_computation.24 | loop fusion | flops 1572864 | bytes 2621569 | tf_op jit(solution)/shard_map/convert_element_type | solution.py:105
  33.7 1.3 %collective-permute-start.2 = (bf16[2064,128]{1,0:T(8,128)(2,1)S(1)}, bf16[2064,128]{1,0:T(8,128)(2,1)S(1)}, u32[]{:S(2)}, u32[]{:S(2)}) collective-permute-start(bf16[2064,128]{1,0:T(8,128)(2,1)S(1)} %pad_maximum_fusion), channel_id=1, source_target_pairs={{4,8},{12,16},{20,24},{0,20},{8,28},{5,9},{13,17},{21,25},{1,21},{... | collective-permute-start | bytes 1585160 | tf_op jit(solution)/shard_map/ppermute | solution.py:108
  35.1 0.9 %constant_dynamic-update-slice_fusion.4 = bf16[2560,128]{1,0:T(8,128)(2,1)S(1)} fusion(bf16[512,128]{1,0:T(8,128)(2,1)} %collective-permute-done.6), kind=kLoop, calls=%fused_computation.62 | loop fusion | bytes 262144
  36.0 0.9 %constant_dynamic-update-slice_fusion.3 = bf16[2560,128]{1,0:T(8,128)(2,1)S(1)} fusion(bf16[2560,128]{1,0:T(8,128)(2,1)S(1)} %constant_dynamic-update-slice_fusion.4, bf16[512,128]{1,0:T(8,128)(2,1)} %collective-permute-done.7), kind=kLoop, calls=%fused_computation.61 | loop fusion | bytes 262144
  37.0 0.9 %constant_dynamic-update-slice_fusion.1 = bf16[2560,128]{1,0:T(8,128)(2,1)S(1)} fusion(bf16[2560,128]{1,0:T(8,128)(2,1)S(1)} %constant_dynamic-update-slice_fusion.2, bf16[512,128]{1,0:T(8,128)(2,1)} %collective-permute-done.9), kind=kLoop, calls=%fused_computation.59 | loop fusion | bytes 262144
  37.9 8.0 %collective-permute-done.2 = bf16[2064,128]{1,0:T(8,128)(2,1)S(1)} collective-permute-done((bf16[2064,128]{1,0:T(8,128)(2,1)S(1)}, bf16[2064,128]{1,0:T(8,128)(2,1)S(1)}, u32[]{:S(2)}, u32[]{:S(2)}) %collective-permute-start.2) | collective-permute-done | bytes 528416 | tf_op jit(solution)/shard_map/ppermute | solution.py:108
  46.0 0.9 %fusion = (f32[2,8,128]{2,1,0:T(8,128)S(1)}, f32[2,5,128,128,8]{3,2,4,1,0:T(8,128)S(1)}) fusion(pred[128,5,128]{0,2,1:T(8,128)(4,1)S(1)} %compare_and_fusion, bf16[128,2,8,128,1]{3,2,1,0,4:T(8,128)(2,1)S(1)} %bitcast.136, bf16[5,2,128,128]{3,2,1,0:T(8,128)(2,1)S(1)} %get-tuple-element.17), kind=kOutput, calls=%fused_computation.2 | convolution fusion | flops 339474432 | bytes 6184960 | tf_op jit(solution)/shard_map/tkgd,bksd->kgtbs/dot_general | solution.py:146
  46.9 0.9 %collective-permute-done.3 = bf16[2064,128]{1,0:T(8,128)(2,1)S(1)} collective-permute-done((bf16[2064,128]{1,0:T(8,128)(2,1)S(1)}, bf16[2064,128]{1,0:T(8,128)(2,1)S(1)}, u32[]{:S(2)}, u32[]{:S(2)}) %collective-permute-start.3) | collective-permute-done | bytes 528416 | tf_op jit(solution)/shard_map/ppermute | solution.py:109
  47.9 0.1 slice_select_fusion
  48.0 1.7 %multiply_reduce_fusion = (f32[128]{0:T(128)S(1)}, f32[128,16,128]{0,2,1:T(8,128)}) fusion(f32[128,16,128]{0,2,1:T(8,128)S(1)} %copy-done.3, f32[128,16]{0,1:T(8,128)S(1)} %get-tuple-element.18, f32[16,128,128]{2,1,0:T(8,128)S(1)} %bitcast.134, bf16[16,128,128]{2,1,0:T(8,128)(2,1)S(1)} %bitcast.138, bf16[16,128,128]{2,1,0:T(8,128)(2,1)S(1)} %bitcast.137, ...), kind=kOutput, calls=%fused_computation.22 | convolution fusion | flops 70254464 | bytes 4727425 | tf_op jit(solution)/shard_map/thd,hde->the/dot_general | solution.py:125
  49.8 1.6 %collective-permute-start.4 = (f32[128]{0:T(128)S(1)}, f32[128]{0:T(128)S(1)}, u32[]{:S(2)}, u32[]{:S(2)}) collective-permute-start(f32[128]{0:T(128)S(1)} %get-tuple-element.23), channel_id=1, source_target_pairs={{0,1},{1,0},{2,3},{3,2},{4,5},{5,4},{6,7},{7,6},{8,9},{9,8},{10,11... | collective-permute-start | bytes 1544 | tf_op jit(solution)/shard_map/ppermute | solution.py:28
  51.3 1.2 %fusion.4 = f32[2,8,128]{2,1,0:T(8,128)S(1)} fusion(f32[2,5,128,128,8]{3,2,4,1,0:T(8,128)S(1)} %get-tuple-element.26, f32[2,8,128]{2,1,0:T(8,128)S(1)} %get-tuple-element.25, pred[128,5,128]{0,2,1:T(8,128)(4,1)S(1)} %compare_and_fusion), kind=kLoop, calls=%fused_computation.6 | loop fusion | flops 6551552 | bytes 5341184 | tf_op jit(solution)/shard_map/reduce_sum | solution.py:151
  52.6 0.2 copy.74
  52.8 0.5 collective-permute-done.4
  53.3 2.6 %collective-permute-start.5 = (f32[128]{0:T(128)S(1)}, f32[128]{0:T(128)S(1)}, u32[]{:S(2)}, u32[]{:S(2)}) collective-permute-start(f32[128]{0:T(128)S(1)} %add.98), channel_id=1, source_target_pairs={{0,2},{1,3},{2,0},{3,1},{4,6},{5,7},{6,4},{7,5},{8,10},{9,11},{10,... | collective-permute-start | bytes 1544 | tf_op jit(solution)/shard_map/ppermute | solution.py:28
  55.9 4.0 %divide_convert_fusion = bf16[128,2,8,128]{0,3,2,1:T(8,128)(2,1)S(1)} fusion(f32[2,5,128,128,8]{3,2,4,1,0:T(8,128)} %copy-done.1, f32[2,8,128]{2,1,0:T(8,128)S(1)} %get-tuple-element.25, pred[128,5,128]{0,2,1:T(8,128)(4,1)S(1)} %compare_and_fusion, f32[128,2,8]{0,2,1:T(8,128)S(1)} %bitcast.152, bf16[5,2,128,128]{2,3,0,1:T(8,128)(2,1)S(1)} %copy.74), kind=kOutput, calls=%fused_computation.20 | convolution fusion | flops 342622208 | bytes 6193152 | tf_op jit(solution)/shard_map/kgtbs,bksd->tkgd/dot_general | solution.py:152
  59.9 1.0 %copy.64 = bf16[128,2048]{1,0:T(8,128)(2,1)} copy(bf16[128,2048]{0,1:T(8,128)(2,1)S(1)} %bitcast.144) | data formatting | bytes 1048576
  60.9 0.3 copy.56
  61.3 1.1 %multiply_convert_fusion = bf16[128,2048]{1,0:T(8,128)(2,1)} fusion(bf16[128,2048]{1,0:T(8,128)(2,1)S(1)} %copy-done.4, f32[128,2048]{1,0:T(8,128)S(1)} %copy.56, f32[2048]{0:T(1024)S(1)} %copy-done.5, f32[128]{0:T(128)S(1)} %add_rsqrt_fusion), kind=kLoop, calls=%fused_computation.21 | loop fusion | flops 2097152 | bytes 2105856 | tf_op jit(solution)/shard_map/convert_element_type | solution.py:140
  (37 shorter events, 0.4 us)
Async XLA Ops:
  0.6 23.5 %copy-start = (bf16[128,2048]{1,0:T(8,128)(2,1)S(1)}, bf16[128,2048]{1,0:T(8,128)(2,1)}, u32[]{:S(2)}) copy-start(bf16[128,2048]{1,0:T(8,128)(2,1)} %param.11) | copy-start | bytes 1572868
  2.8 32.3 %collective-permute-start.6 = (bf16[512,128]{1,0:T(8,128)(2,1)S(1)}, bf16[512,128]{1,0:T(8,128)(2,1)}, u32[]{:S(2)}, u32[]{:S(2)}) collective-permute-start(bf16[512,128]{1,0:T(8,128)(2,1)S(1)} %bitcast.145), channel_id=1, source_target_pairs={{0,16},{4,20},{8,24},{12,28},{1,17},{5,21},{9,25},{13,29},{2,18},{... | collective-permute-start | bytes 393224 | tf_op jit(solution)/shard_map/ppermute | solution.py:13
  8.3 27.7 %collective-permute-start.7 = (bf16[512,128]{1,0:T(8,128)(2,1)S(1)}, bf16[512,128]{1,0:T(8,128)(2,1)}, u32[]{:S(2)}, u32[]{:S(2)}) collective-permute-start(bf16[512,128]{1,0:T(8,128)(2,1)S(1)} %bitcast.146), channel_id=1, source_target_pairs={{0,12},{4,16},{8,20},{12,24},{16,28},{1,13},{5,17},{9,21},{13,25},... | collective-permute-start | bytes 393224 | tf_op jit(solution)/shard_map/ppermute | solution.py:13
  11.5 25.4 %collective-permute-start.8 = (bf16[512,128]{1,0:T(8,128)(2,1)S(1)}, bf16[512,128]{1,0:T(8,128)(2,1)S(1)}, u32[]{:S(2)}, u32[]{:S(2)}) collective-permute-start(bf16[512,128]{1,0:T(8,128)(2,1)S(1)} %bitcast.147), channel_id=1, source_target_pairs={{0,8},{4,12},{8,16},{12,20},{16,24},{20,28},{1,9},{5,13},{9,17},{1... | collective-permute-start | bytes 393224 | tf_op jit(solution)/shard_map/ppermute | solution.py:13
  13.6 16.3 %collective-permute-start = (f32[16,128]{1,0:T(8,128)}, f32[16,128]{1,0:T(8,128)S(1)}, u32[]{:S(2)}, u32[]{:S(2)}) collective-permute-start(f32[16,128]{1,0:T(8,128)} %param.14), channel_id=1, source_target_pairs={{0,4},{4,0},{8,12},{12,8},{16,20},{20,16},{24,28},{28,24},{1,5},{5... | collective-permute-start | bytes 24584 | tf_op jit(solution)/shard_map/ppermute | solution.py:84
  22.3 10.4 %collective-permute-start.1 = (f32[2048,128]{1,0:T(8,128)S(1)}, f32[2048,128]{1,0:T(8,128)S(1)}, u32[]{:S(2)}, u32[]{:S(2)}) collective-permute-start(f32[2048,128]{1,0:T(8,128)S(1)} %bitcast.133), channel_id=1, source_target_pairs={{0,4},{4,0},{8,12},{12,8},{16,20},{20,16},{24,28},{28,24},{1,5},{5... | collective-permute-start | bytes 3145736 | tf_op jit(solution)/shard_map/ppermute | solution.py:92
  30.0 7.0 %collective-permute-start.9 = (bf16[512,128]{1,0:T(8,128)(2,1)S(1)}, bf16[512,128]{1,0:T(8,128)(2,1)}, u32[]{:S(2)}, u32[]{:S(2)}) collective-permute-start(bf16[512,128]{1,0:T(8,128)(2,1)S(1)} %bitcast.148), channel_id=1, source_target_pairs={{0,4},{4,8},{8,12},{12,16},{16,20},{20,24},{24,28},{1,5},{5,9},{9,... | collective-permute-start | bytes 393224 | tf_op jit(solution)/shard_map/ppermute | solution.py:13
  33.7 12.2 %collective-permute-start.2 = (bf16[2064,128]{1,0:T(8,128)(2,1)S(1)}, bf16[2064,128]{1,0:T(8,128)(2,1)S(1)}, u32[]{:S(2)}, u32[]{:S(2)}) collective-permute-start(bf16[2064,128]{1,0:T(8,128)(2,1)S(1)} %pad_maximum_fusion), channel_id=1, source_target_pairs={{4,8},{12,16},{20,24},{0,20},{8,28},{5,9},{13,17},{21,25},{1,21},{... | collective-permute-start | bytes 1585160 | tf_op jit(solution)/shard_map/ppermute | solution.py:108
  45.9 1.9 %collective-permute-start.3 = (bf16[2064,128]{1,0:T(8,128)(2,1)S(1)}, bf16[2064,128]{1,0:T(8,128)(2,1)S(1)}, u32[]{:S(2)}, u32[]{:S(2)}) collective-permute-start(bf16[2064,128]{1,0:T(8,128)(2,1)S(1)} %collective-permute-done.2), channel_id=1, source_target_pairs={{0,4},{4,0},{8,12},{12,8},{16,20},{20,16},{24,28},{28,24},{1,5},{5... | collective-permute-start | bytes 1585160 | tf_op jit(solution)/shard_map/ppermute | solution.py:109
  46.0 2.0 %copy-start.3 = (f32[128,16,128]{0,2,1:T(8,128)S(1)}, f32[128,16,128]{0,2,1:T(8,128)}, u32[]{:S(2)}) copy-start(f32[128,16,128]{0,2,1:T(8,128)} %convolution_bitcast_fusion.1) | copy-start | bytes 3145732
  46.9 5.7 %copy-start.1 = (f32[2,5,128,128,8]{3,2,4,1,0:T(8,128)}, f32[2,5,128,128,8]{3,2,4,1,0:T(8,128)S(1)}, u32[]{:S(2)}) copy-start(f32[2,5,128,128,8]{3,2,4,1,0:T(8,128)S(1)} %get-tuple-element.26) | copy-start | bytes 15728644
  49.8 3.5 %collective-permute-start.4 = (f32[128]{0:T(128)S(1)}, f32[128]{0:T(128)S(1)}, u32[]{:S(2)}, u32[]{:S(2)}) collective-permute-start(f32[128]{0:T(128)S(1)} %get-tuple-element.23), channel_id=1, source_target_pairs={{0,1},{1,0},{2,3},{3,2},{4,5},{5,4},{6,7},{7,6},{8,9},{9,8},{10,11... | collective-permute-start | bytes 1544 | tf_op jit(solution)/shard_map/ppermute | solution.py:28
  53.3 7.9 %collective-permute-start.5 = (f32[128]{0:T(128)S(1)}, f32[128]{0:T(128)S(1)}, u32[]{:S(2)}, u32[]{:S(2)}) collective-permute-start(f32[128]{0:T(128)S(1)} %add.98), channel_id=1, source_target_pairs={{0,2},{1,3},{2,0},{3,1},{4,6},{5,7},{6,4},{7,5},{8,10},{9,11},{10,... | collective-permute-start | bytes 1544 | tf_op jit(solution)/shard_map/ppermute | solution.py:28
  55.9 5.0 %copy-start.2 = (f32[128,16,128]{0,2,1:T(8,128)S(1)}, f32[128,16,128]{0,2,1:T(8,128)}, u32[]{:S(2)}) copy-start(f32[128,16,128]{0,2,1:T(8,128)} %get-tuple-element.24) | copy-start | bytes 3145732
  55.9 5.4 %copy-start.4 = (bf16[128,2048]{1,0:T(8,128)(2,1)S(1)}, bf16[128,2048]{1,0:T(8,128)(2,1)}, u32[]{:S(2)}) copy-start(bf16[128,2048]{1,0:T(8,128)(2,1)} %param.15) | copy-start | bytes 1572868
  55.9 5.4 %copy-start.5 = (f32[2048]{0:T(1024)S(1)}, f32[2048]{0:T(1024)}, u32[]{:S(2)}) copy-start(f32[2048]{0:T(1024)} %param.16) | copy-start | bytes 24580

commit v12 on v7

--- a/solution.py
+++ b/solution.py
@@ -102,6 +102,26 @@
     )
     routes = [(i, i + 1) for i in range(1, count - 1, 2)] + [(i, i + 5) for i in range(0, count - 5, 2)]
     received = lax.ppermute(packet, "ctx", routes)
+    span_rows = (SPAN + 1) * rows
+    key_pos = shard * rows - SPAN * rows + jnp.arange(span_rows, dtype=jnp.int32)
+    key_docs = jnp.where(key_pos >= 0, document_of(key_pos, doc_lengths), -1)
+    allowed = (key_docs[None, :] == docs[:, None]) & (key_pos[None, :] <= positions[:, None])
+    soft_query = soft_q.reshape(rows, kv_here, group, DH)
+    scores = jnp.einsum(
+        "tkgd,bksd->kgtbs", soft_query, window[:, :kv_here], preferred_element_type=jnp.float32
+    ).reshape(kv_here, group, rows, span_rows) * DH ** (-0.5)
+    top = jnp.max(jnp.where(allowed, scores, -1e30), axis=-1, keepdims=True)
+    expd = jnp.where(allowed, jnp.exp(jnp.minimum(scores - top, 0.0)), 0.0)
+    total = jnp.sum(expd, axis=-1)
+    attended = jnp.einsum(
+        "kgtbs,bksd->tkgd",
+        expd.astype(jnp.bfloat16).reshape(kv_here, group, rows, SPAN + 1, rows),
+        window[:, kv_here:],
+        preferred_element_type=jnp.float32,
+    )
+    attended = attended / total.transpose(2, 0, 1)[..., None]
+    soft_out = attended.reshape(rows, kv_here * group * DH).astype(jnp.bfloat16)
+    soft_out, received = lax.optimization_barrier((soft_out, received))
     mate_packet = lax.ppermute(received, "ctx", [(i, i ^ 1) for i in range(count)])
     near = jnp.where(odd, mate_packet, received)
     far = jnp.where(odd, received, mate_packet)
@@ -134,25 +154,6 @@
         * jax.nn.sigmoid(out_gate.astype(jnp.float32))
     )
     lin_out = normed.astype(jnp.bfloat16)
-    span_rows = (SPAN + 1) * rows
-    key_pos = shard * rows - SPAN * rows + jnp.arange(span_rows, dtype=jnp.int32)
-    key_docs = jnp.where(key_pos >= 0, document_of(key_pos, doc_lengths), -1)
-    allowed = (key_docs[None, :] == docs[:, None]) & (key_pos[None, :] <= positions[:, None])
-    soft_query = soft_q.reshape(rows, kv_here, group, DH)
-    scores = jnp.einsum(
-        "tkgd,bksd->kgtbs", soft_query, window[:, :kv_here], preferred_element_type=jnp.float32
-    ).reshape(kv_here, group, rows, span_rows) * DH ** (-0.5)
-    top = jnp.max(jnp.where(allowed, scores, -1e30), axis=-1, keepdims=True)
-    expd = jnp.where(allowed, jnp.exp(jnp.minimum(scores - top, 0.0)), 0.0)
-    total = jnp.sum(expd, axis=-1)
-    attended = jnp.einsum(
-        "kgtbs,bksd->tkgd",
-        expd.astype(jnp.bfloat16).reshape(kv_here, group, rows, SPAN + 1, rows),
-        window[:, kv_here:],
-        preferred_element_type=jnp.float32,
-    )
-    attended = attended / total.transpose(2, 0, 1)[..., None]
-    soft_out = attended.reshape(rows, kv_here * group * DH).astype(jnp.bfloat16)
     return (lin_out, soft_out)
 
 

time: 59.3 us -> 64.7 us (1.091)
  other arithmetic: 7.82 us -> 10.7 us
  waiting for transfers between devices: 9.97 us -> 12.5 us
  matrix products: 9.89 us -> 8.11 us
  local copies, waits for them, and re-layouts: 10.3 us -> 11.8 us
    dot_general x1, matrix products: 3.94 us -> 1.4 us  [local(): jnp.einsum('kgtbs,bksd->tkgd', expd.astype(jnp.bfloat16).reshape(kv_here,...]
    ppermute x2, waiting for transfers between devices: 0.48 us -> 2.46 us  [all_sum(): x = x + lax.ppermute(x, axis, [(i, i ^ bit) for i in range(count)])]
    ppermute x1, waiting for transfers between devices: 8.64 us -> 10.1 us  [local(): received = lax.ppermute(packet, 'ctx', routes)]
    select_n x1, other arithmetic: 0.07 us -> 1.23 us  [local(): far = jnp.where(odd, received, mate_packet)]
    dot_general x1, matrix products: 0.92 us -> 1.86 us  [local(): jnp.einsum('tkgd,bksd->kgtbs', soft_query, window[:, :kv_here], preferred...]
    ppermute x1, waiting for transfers between devices: 0.83 us -> 0.01 us  [local(): lax.ppermute(received, 'ctx', [(i, i ^ 1) for i in range(count)])]
    unnamed x21 -> x33, local copies, waits for them, and re-layouts: 7.17 us -> 7.93 us
    slice x1, local copies, waits for them, and re-layouts: 0.05 us -> 0.78 us  [local(): window[:, kv_here:]]
  transfers between devices with their start and end apart: 9 -> 9, of which waited for: 3 -> 3; matrix products, arithmetic and copies ran while one was open for 40% -> 39% of each run, Pallas kernels for 0% -> 0%
where the time goes in v12:
time: 64.7 us; the launch traced here: 64 us
  starting transfers between devices  18.5 us (29%)
  waiting for transfers between devices  12.5 us (19%)
  local copies, waits for them, and re-layouts  11.8 us (18%)
  other arithmetic  10.7 us (17%)
  matrix products  8.11 us (13%)
  between operations  2.4 us (4%)
    ppermute x4, starting transfers between devices, from_behind(): return lax.ppermute(shard, axis, pairs)  12.2 us
    ppermute x1, waiting for transfers between devices, local(): received = lax.ppermute(packet, 'ctx', routes)  10.1 us
    unnamed x33, local copies, waits for them, and re-layouts  7.93 us
    ppermute x2, starting transfers between devices, all_sum(): x = x + lax.ppermute(x, axis, [(i, i ^ bit) for i in range(count)])  4.25 us
    dot_general x1, matrix products, block_terms(): jnp.einsum('hts,shd->thd', weights, values, preferred_element_type=jnp.fl...  2.77 us
    ppermute x2, waiting for transfers between devices, all_sum(): x = x + lax.ppermute(x, axis, [(i, i ^ bit) for i in range(count)])  2.46 us
    dot_general x1, matrix products, local(): jnp.einsum('tkgd,bksd->kgtbs', soft_query, window[:, :kv_here], preferred...  1.86 us
    dot_general x1, matrix products, local(): jnp.einsum('kgtbs,bksd->tkgd', expd.astype(jnp.bfloat16).reshape(kv_here,...  1.4 us
  transfers between devices with their start and end apart: 9, of which 3 were waited for; matrix products, arithmetic and copies ran while one was open for 39% of the time, Pallas kernels for 0%

profile of v12, /device:TPU:0, one launch (start us, length us, event | category | flops | bytes accessed | tf_op | source)
XLA Modules:
  0.0 64.0 jit_solution(2163645815008199252)
XLA Ops:
  0.6 0.0 copy-start
  0.6 1.0 %copy.54 = bf16[128,256]{0,1:T(8,128)(2,1)S(1)} copy(bf16[128,256]{1,0:T(8,128)(2,1)} %param.18) | data formatting | bytes 131072 | tf_op args[8]
  1.7 1.0 %copy.55 = bf16[128,256]{0,1:T(8,128)(2,1)S(1)} copy(bf16[128,256]{1,0:T(8,128)(2,1)} %param.19) | data formatting | bytes 131072 | tf_op args[9]
  2.6 0.1 copy.56
  2.8 5.5 %collective-permute-start.1 = (bf16[512,128]{1,0:T(8,128)(2,1)S(1)}, bf16[512,128]{1,0:T(8,128)(2,1)}, u32[]{:S(2)}, u32[]{:S(2)}) collective-permute-start(bf16[512,128]{1,0:T(8,128)(2,1)S(1)} %bitcast.139), channel_id=1, source_target_pairs={{0,16},{4,20},{8,24},{12,28},{1,17},{5,21},{9,25},{13,29},{2,18},{... | collective-permute-start | bytes 393224 | tf_op jit(solution)/shard_map/ppermute | solution.py:13
  8.3 3.2 %collective-permute-start.2 = (bf16[512,128]{1,0:T(8,128)(2,1)S(1)}, bf16[512,128]{1,0:T(8,128)(2,1)}, u32[]{:S(2)}, u32[]{:S(2)}) collective-permute-start(bf16[512,128]{1,0:T(8,128)(2,1)S(1)} %bitcast.140), channel_id=1, source_target_pairs={{0,12},{4,16},{8,20},{12,24},{16,28},{1,13},{5,17},{9,21},{13,25},... | collective-permute-start | bytes 393224 | tf_op jit(solution)/shard_map/ppermute | solution.py:13
  11.5 2.1 %collective-permute-start.3 = (bf16[512,128]{1,0:T(8,128)(2,1)S(1)}, bf16[512,128]{1,0:T(8,128)(2,1)S(1)}, u32[]{:S(2)}, u32[]{:S(2)}) collective-permute-start(bf16[512,128]{1,0:T(8,128)(2,1)S(1)} %bitcast.141), channel_id=1, source_target_pairs={{0,8},{4,12},{8,16},{12,20},{16,24},{20,28},{1,9},{5,13},{9,17},{1... | collective-permute-start | bytes 393224 | tf_op jit(solution)/shard_map/ppermute | solution.py:13
  13.7 1.3 %collective-permute-start.4 = (bf16[512,128]{1,0:T(8,128)(2,1)S(1)}, bf16[512,128]{1,0:T(8,128)(2,1)S(1)}, u32[]{:S(2)}, u32[]{:S(2)}) collective-permute-start(bf16[512,128]{1,0:T(8,128)(2,1)S(1)} %bitcast.142), channel_id=1, source_target_pairs={{0,4},{4,8},{8,12},{12,16},{16,20},{20,24},{24,28},{1,5},{5,9},{9,... | collective-permute-start | bytes 393224 | tf_op jit(solution)/shard_map/ppermute | solution.py:13
  15.0 0.8 %reduce-window.4 = s32[6,1]{0,1:T(1,128)S(1)} reduce-window(s32[6,1]{0,1:T(1,128)} %bitcast.151, s32[]{:T(128)} %constant.24.clone.1), window={size=6x1 pad=5_0x0_0}, to_apply=%region_0.0 | reduce-window | flops 30 | bytes 52 | tf_op jit(solution)/shard_map/reduce-window
  15.9 0.6 fusion.51
  16.5 0.1 convert_reduce_fusion.1
  16.6 0.6 slice.38
  17.8 0.7 %fusion.58 = (f32[128]{0:T(128)S(1)}, pred[128]{0:T(512)(128)(4,1)S(1)}, f32[128]{0:T(128)S(1)}) fusion(s32[128]{0:T(128)S(1)} %convert_reduce_fusion.1, s32[]{:T(128)S(6)} %select_n.61, s32[]{:T(128)} %bitcast.3), kind=kLoop, calls=%fused_computation.99 | loop fusion | flops 512 | bytes 1672 | tf_op jit(solution)/shard_map/convert_element_type | solution.py:144
  18.5 0.6 slice.40
  19.7 1.3 %copy.76 = bf16[128,2048]{0,1:T(8,128)(2,1)S(1)} copy(bf16[128,2048]{1,0:T(8,128)(2,1)} %param.12) | data formatting | bytes 1048576 | tf_op jit(solution)/shard_map/reshape | solution.py:66
  21.0 1.0 %reduce_window_sum.20 = f32[16,128]{1,0:T(8,128)S(1)} reduce-window(f32[16,128]{1,0:T(8,128)} %param.14, f32[]{:T(128)} %constant.49.clone.1), window={size=1x128 pad=0_0x127_0}, to_apply=%region_2.3 | reduce-window | flops 260096 | bytes 16388 | tf_op jit(solution)/shard_map/jit(cumsum)/reduce_window_sum | solution.py:40
  22.0 0.2 slice_reduce_fusion
  22.2 0.6 multiply_bitcast_fusion
  22.8 1.3 %fusion.22 = f32[16,128,128]{2,1,0:T(8,128)S(1)} fusion(bf16[128,16,128]{0,2,1:T(8,128)(2,1)S(1)} %bitcast.133, f32[128,16]{0,1:T(8,128)S(1)} %get-tuple-element.24, bf16[128,2048]{1,0:T(8,128)(2,1)} %param.13), kind=kOutput, calls=%fused_computation.33 | convolution fusion | flops 67895296 | bytes 2105344 | tf_op jit(solution)/shard_map/shd,she->hde/dot_general | solution.py:51
  24.2 1.1 %select_maximum_fusion = f32[2056,128]{1,0:T(8,128)} fusion(f32[1,16]{1,0:T(1,128)S(1)} %bitcast.147, f32[2048,128]{1,0:T(8,128)S(1)} %bitcast.127), kind=kLoop, calls=%fused_computation.18 | loop fusion | flops 789504 | bytes 2101312 | tf_op jit(solution)/shard_map/concatenate | solution.py:85
  25.3 0.7 %collective-permute-start = (f32[2056,128]{1,0:T(8,128)}, f32[2056,128]{1,0:T(8,128)S(1)}, u32[]{:S(2)}, u32[]{:S(2)}) collective-permute-start(f32[2056,128]{1,0:T(8,128)} %select_maximum_fusion), channel_id=1, source_target_pairs={{0,4},{4,0},{8,12},{12,8},{16,20},{20,16},{24,28},{28,24},{1,5},{5... | collective-permute-start | bytes 3158024 | tf_op jit(solution)/shard_map/ppermute | solution.py:86
  26.0 0.1 convert_reduce_fusion
  26.1 0.9 %compare_and_fusion = pred[128,5,128]{0,2,1:T(8,128)(4,1)} fusion(s32[128]{0:T(128)S(1)} %iota_add_fusion.1, s32[5,128]{1,0:T(8,128)S(1)} %get-tuple-element.31, s32[128]{0:T(128)S(1)} %convert_reduce_fusion.1, s32[5,128]{1,0:T(8,128)S(1)} %get-tuple-element.30), kind=kLoop, calls=%fused_computation.55 | loop fusion | flops 245760 | bytes 88064 | tf_op jit(solution)/shard_map/and | solution.py:108
  27.0 0.6 exponential_multiply_fusion
  27.6 1.1 %copy.79 = bf16[16,8,16,128]{3,2,1,0:T(8,128)(2,1)S(1)} copy(bf16[16,8,16,128]{3,1,2,0:T(8,128)(2,1)} %bitcast.137) | data formatting | bytes 1048576
  28.7 0.9 %constant_dynamic-update-slice_fusion.4 = bf16[2560,128]{1,0:T(8,128)(2,1)S(1)} fusion(bf16[512,128]{1,0:T(8,128)(2,1)} %collective-permute-done.1), kind=kLoop, calls=%fused_computation.64 | loop fusion | bytes 262144
  29.6 0.9 %constant_dynamic-update-slice_fusion.3 = bf16[2560,128]{1,0:T(8,128)(2,1)S(1)} fusion(bf16[2560,128]{1,0:T(8,128)(2,1)S(1)} %constant_dynamic-update-slice_fusion.4, bf16[512,128]{1,0:T(8,128)(2,1)} %collective-permute-done.2), kind=kLoop, calls=%fused_computation.63 | loop fusion | bytes 262144
  30.7 0.8 %fusion.59 = (bf16[5,2,128,128]{3,2,1,0:T(8,128)(2,1)}, bf16[5,2,128,128]{3,2,1,0:T(8,128)(2,1)S(1)}) fusion(bf16[5,4,128,128]{3,2,1,0:T(8,128)(2,1)S(1)} %bitcast.136), kind=kLoop, calls=%fused_computation.100 | loop fusion | bytes 1310720 | tf_op jit(solution)/shard_map/slice | solution.py:119
  31.5 1.9 %copy.74 = bf16[5,2,128,128]{2,3,0,1:T(8,128)(2,1)} copy(bf16[5,2,128,128]{3,2,1,0:T(8,128)(2,1)} %get-tuple-element.21) | data formatting | bytes 655360
  33.3 1.9 %fusion = (f32[2,8,128]{2,1,0:T(8,128)S(1)}, f32[2,5,128,128,8]{3,2,4,1,0:T(8,128)S(1)}) fusion(pred[128,5,128]{0,2,1:T(8,128)(4,1)} %compare_and_fusion, bf16[128,2,8,128,1]{3,2,1,0,4:T(8,128)(2,1)S(1)} %bitcast.130, bf16[5,2,128,128]{3,2,1,0:T(8,128)(2,1)S(1)} %get-tuple-element.22), kind=kOutput, calls=%fused_computation.2 | convolution fusion | flops 339474432 | bytes 6184960 | tf_op jit(solution)/shard_map/tkgd,bksd->kgtbs/dot_general | solution.py:110
  35.2 1.2 %fusion.4 = f32[2,8,128]{2,1,0:T(8,128)S(1)} fusion(f32[2,5,128,128,8]{3,2,4,1,0:T(8,128)S(1)} %get-tuple-element.27, f32[2,8,128]{2,1,0:T(8,128)S(1)} %get-tuple-element.26, pred[128,5,128]{0,2,1:T(8,128)(4,1)S(1)} %copy-done.3), kind=kLoop, calls=%fused_computation.6 | loop fusion | flops 6551552 | bytes 5341184 | tf_op jit(solution)/shard_map/reduce_sum | solution.py:115
  36.5 0.3 select_convert_fusion.1
  36.9 1.3 %collective-permute-start.5 = (bf16[2064,128]{1,0:T(8,128)(2,1)S(1)}, bf16[2064,128]{1,0:T(8,128)(2,1)S(1)}, u32[]{:S(2)}, u32[]{:S(2)}) collective-permute-start(bf16[2064,128]{1,0:T(8,128)(2,1)S(1)} %pad_maximum_fusion), channel_id=1, source_target_pairs={{4,8},{12,16},{20,24},{0,20},{8,28},{5,9},{13,17},{21,25},{1,21},{... | collective-permute-start | bytes 1585160 | tf_op jit(solution)/shard_map/ppermute | solution.py:104
  38.2 1.4 %divide_convert_fusion = bf16[128,2,8,128]{0,3,2,1:T(8,128)(2,1)S(1)} fusion(f32[2,5,128,128,8]{3,2,4,1,0:T(8,128)S(1)} %get-tuple-element.27, f32[2,8,128]{2,1,0:T(8,128)S(1)} %get-tuple-element.26, pred[128,5,128]{0,2,1:T(8,128)(4,1)S(1)} %copy-done.3, f32[128,2,8]{0,2,1:T(8,128)S(1)} %bitcast.146, bf16[5,2,128,128]{2,3,0,1:T(8,128)(2,1)S(1)} %copy-done.6), kind=kOutput, calls=%fused_computation.26 | convolution fusion | flops 342622208 | bytes 6193152 | tf_op jit(solution)/shard_map/kgtbs,bksd->tkgd/dot_general | solution.py:116
  39.6 10.1 %collective-permute-done.5 = bf16[2064,128]{1,0:T(8,128)(2,1)S(1)} collective-permute-done((bf16[2064,128]{1,0:T(8,128)(2,1)S(1)}, bf16[2064,128]{1,0:T(8,128)(2,1)S(1)}, u32[]{:S(2)}, u32[]{:S(2)}) %collective-permute-start.5) | collective-permute-done | bytes 528416 | tf_op jit(solution)/shard_map/ppermute | solution.py:104
  49.7 0.1 fusion.44
  49.8 2.8 %convolution_bitcast_fusion.1 = f32[128,16,128]{0,2,1:T(8,128)} fusion(bf16[128,16,128]{0,2,1:T(8,128)(2,1)S(1)} %bitcast.134, f32[16,128]{1,0:T(8,128)S(1)} %reduce_window_sum.20, pred[128,128]{1,0:T(8,128)(4,1)S(1)} %fusion.44, bf16[128,2048]{1,0:T(8,128)(2,1)} %param.13, bf16[128,2048]{1,0:T(8,128)(2,1)S(1)} %copy-done), kind=kOutput, calls=%fused_computation.14 | convolution fusion | flops 135528448 | bytes 2646016 | tf_op jit(solution)/shard_map/hts,shd->thd/dot_general | solution.py:46
  52.6 0.1 slice.53
  52.7 0.1 broadcast_select_fusion
  52.9 1.2 %slice_select_fusion = bf16[2048,128]{1,0:T(8,128)(2,1)S(1)} fusion(bf16[2064,128]{1,0:T(8,128)(2,1)} %collective-permute-done.6, bf16[2064,128]{1,0:T(8,128)(2,1)S(1)} %collective-permute-done.5, pred[]{:T(512)S(6)} %eq.59), kind=kLoop, calls=%fused_computation.38 | loop fusion | flops 262144 | bytes 1572865 | tf_op jit(solution)/shard_map/jit(_where)/select_n | solution.py:127
  54.1 0.7 %multiply_reduce_fusion = (f32[128]{0:T(128)S(1)}, f32[128,16,128]{0,2,1:T(8,128)S(1)}) fusion(f32[128,16,128]{0,2,1:T(8,128)S(1)} %copy-done.4, f32[128,16]{0,1:T(8,128)S(1)} %copy-done.7, f32[16,128,128]{2,1,0:T(8,128)S(1)} %bitcast.129, bf16[16,128,128]{2,1,0:T(8,128)(2,1)S(1)} %bitcast.132, bf16[16,128,128]{2,1,0:T(8,128)(2,1)S(1)} %bitcast.131, ...), kind=kOutput, calls=%fused_computation.23 | convolution fusion | flops 70254464 | bytes 4727425 | tf_op jit(solution)/shard_map/thd,hde->the/dot_general | solution.py:141
  54.8 1.6 %collective-permute-start.7 = (f32[128]{0:T(128)S(1)}, f32[128]{0:T(128)S(1)}, u32[]{:S(2)}, u32[]{:S(2)}) collective-permute-start(f32[128]{0:T(128)S(1)} %get-tuple-element.28), channel_id=1, source_target_pairs={{0,1},{1,0},{2,3},{3,2},{4,5},{5,4},{6,7},{7,6},{8,9},{9,8},{10,11... | collective-permute-start | bytes 1544 | tf_op jit(solution)/shard_map/ppermute | solution.py:28
  56.5 2.0 %collective-permute-done.7 = f32[128]{0:T(128)S(1)} collective-permute-done((f32[128]{0:T(128)S(1)}, f32[128]{0:T(128)S(1)}, u32[]{:S(2)}, u32[]{:S(2)}) %collective-permute-start.7) | collective-permute-done | bytes 544 | tf_op jit(solution)/shard_map/ppermute | solution.py:28
  58.4 2.6 %collective-permute-start.8 = (f32[128]{0:T(128)S(1)}, f32[128]{0:T(128)S(1)}, u32[]{:S(2)}, u32[]{:S(2)}) collective-permute-start(f32[128]{0:T(128)S(1)} %add.99), channel_id=1, source_target_pairs={{0,2},{1,3},{2,0},{3,1},{4,6},{5,7},{6,4},{7,5},{8,10},{9,11},{10,... | collective-permute-start | bytes 1544 | tf_op jit(solution)/shard_map/ppermute | solution.py:28
  61.1 1.0 %copy.64 = bf16[128,2048]{1,0:T(8,128)(2,1)} copy(bf16[128,2048]{0,1:T(8,128)(2,1)S(1)} %bitcast.138) | data formatting | bytes 1048576
  62.1 0.3 copy.63
  62.4 0.5 collective-permute-done.8
  62.9 1.1 %multiply_convert_fusion = bf16[128,2048]{1,0:T(8,128)(2,1)} fusion(bf16[128,2048]{1,0:T(8,128)(2,1)S(1)} %copy-done.5, f32[128,2048]{1,0:T(8,128)S(1)} %copy.63, f32[2048]{0:T(1024)S(1)} %copy-done.8, f32[128]{0:T(128)S(1)} %add_rsqrt_fusion), kind=kLoop, calls=%fused_computation.22 | loop fusion | flops 2097152 | bytes 2105856 | tf_op jit(solution)/shard_map/convert_element_type | solution.py:156
  (44 shorter events, 0.3 us)
Async XLA Ops:
  0.6 49.2 %copy-start = (bf16[128,2048]{1,0:T(8,128)(2,1)S(1)}, bf16[128,2048]{1,0:T(8,128)(2,1)}, u32[]{:S(2)}) copy-start(bf16[128,2048]{1,0:T(8,128)(2,1)} %param.11) | copy-start | bytes 1572868
  2.8 25.9 %collective-permute-start.1 = (bf16[512,128]{1,0:T(8,128)(2,1)S(1)}, bf16[512,128]{1,0:T(8,128)(2,1)}, u32[]{:S(2)}, u32[]{:S(2)}) collective-permute-start(bf16[512,128]{1,0:T(8,128)(2,1)S(1)} %bitcast.139), channel_id=1, source_target_pairs={{0,16},{4,20},{8,24},{12,28},{1,17},{5,21},{9,25},{13,29},{2,18},{... | collective-permute-start | bytes 393224 | tf_op jit(solution)/shard_map/ppermute | solution.py:13
  8.3 21.3 %collective-permute-start.2 = (bf16[512,128]{1,0:T(8,128)(2,1)S(1)}, bf16[512,128]{1,0:T(8,128)(2,1)}, u32[]{:S(2)}, u32[]{:S(2)}) collective-permute-start(bf16[512,128]{1,0:T(8,128)(2,1)S(1)} %bitcast.140), channel_id=1, source_target_pairs={{0,12},{4,16},{8,20},{12,24},{16,28},{1,13},{5,17},{9,21},{13,25},... | collective-permute-start | bytes 393224 | tf_op jit(solution)/shard_map/ppermute | solution.py:13
  11.5 19.1 %collective-permute-start.3 = (bf16[512,128]{1,0:T(8,128)(2,1)S(1)}, bf16[512,128]{1,0:T(8,128)(2,1)S(1)}, u32[]{:S(2)}, u32[]{:S(2)}) collective-permute-start(bf16[512,128]{1,0:T(8,128)(2,1)S(1)} %bitcast.141), channel_id=1, source_target_pairs={{0,8},{4,12},{8,16},{12,20},{16,24},{20,28},{1,9},{5,13},{9,17},{1... | collective-permute-start | bytes 393224 | tf_op jit(solution)/shard_map/ppermute | solution.py:13
  13.7 17.0 %collective-permute-start.4 = (bf16[512,128]{1,0:T(8,128)(2,1)S(1)}, bf16[512,128]{1,0:T(8,128)(2,1)S(1)}, u32[]{:S(2)}, u32[]{:S(2)}) collective-permute-start(bf16[512,128]{1,0:T(8,128)(2,1)S(1)} %bitcast.142), channel_id=1, source_target_pairs={{0,4},{4,8},{8,12},{12,16},{16,20},{20,24},{24,28},{1,5},{5,9},{9,... | collective-permute-start | bytes 393224 | tf_op jit(solution)/shard_map/ppermute | solution.py:13
  21.0 3.2 %copy-start.1 = (bf16[128,2048]{0,1:T(8,128)(2,1)}, bf16[128,2048]{0,1:T(8,128)(2,1)S(1)}, u32[]{:S(2)}) copy-start(bf16[128,2048]{0,1:T(8,128)(2,1)S(1)} %copy.76) | copy-start | bytes 1572868
  22.2 3.8 %copy-start.9 = (f32[16]{0:T(128)}, f32[16]{0:T(128)S(1)}, u32[]{:S(2)}) copy-start(f32[16]{0:T(128)S(1)} %get-tuple-element.15) | copy-start | bytes 196
  25.3 11.2 %collective-permute-start = (f32[2056,128]{1,0:T(8,128)}, f32[2056,128]{1,0:T(8,128)S(1)}, u32[]{:S(2)}, u32[]{:S(2)}) collective-permute-start(f32[2056,128]{1,0:T(8,128)} %select_maximum_fusion), channel_id=1, source_target_pairs={{0,4},{4,0},{8,12},{12,8},{16,20},{20,16},{24,28},{28,24},{1,5},{5... | collective-permute-start | bytes 3158024 | tf_op jit(solution)/shard_map/ppermute | solution.py:86
  33.3 1.9 %copy-start.3 = (pred[128,5,128]{0,2,1:T(8,128)(4,1)S(1)}, pred[128,5,128]{0,2,1:T(8,128)(4,1)}, u32[]{:S(2)}) copy-start(pred[128,5,128]{0,2,1:T(8,128)(4,1)} %compare_and_fusion) | copy-start | bytes 245764
  33.3 3.2 %copy-start.10 = (f32[16]{0:T(128)S(1)}, f32[16]{0:T(128)}, u32[]{:S(2)}) copy-start(f32[16]{0:T(128)} %copy-done.9) | copy-start | bytes 196
  33.3 3.2 %copy-start.11 = (f32[16]{0:T(128)S(1)}, f32[16]{0:T(128)}, u32[]{:S(2)}) copy-start(f32[16]{0:T(128)} %exponential_multiply_fusion) | copy-start | bytes 196
  35.2 3.0 %copy-start.6 = (bf16[5,2,128,128]{2,3,0,1:T(8,128)(2,1)S(1)}, bf16[5,2,128,128]{2,3,0,1:T(8,128)(2,1)}, u32[]{:S(2)}) copy-start(bf16[5,2,128,128]{2,3,0,1:T(8,128)(2,1)} %copy.74) | copy-start | bytes 983044
  36.9 12.8 %collective-permute-start.5 = (bf16[2064,128]{1,0:T(8,128)(2,1)S(1)}, bf16[2064,128]{1,0:T(8,128)(2,1)S(1)}, u32[]{:S(2)}, u32[]{:S(2)}) collective-permute-start(bf16[2064,128]{1,0:T(8,128)(2,1)S(1)} %pad_maximum_fusion), channel_id=1, source_target_pairs={{4,8},{12,16},{20,24},{0,20},{8,28},{5,9},{13,17},{21,25},{1,21},{... | collective-permute-start | bytes 1585160 | tf_op jit(solution)/shard_map/ppermute | solution.py:104
  38.2 11.6 %copy-start.2 = (bf16[128,2048]{0,1:T(8,128)(2,1)S(1)}, bf16[128,2048]{0,1:T(8,128)(2,1)}, u32[]{:S(2)}) copy-start(bf16[128,2048]{0,1:T(8,128)(2,1)} %copy-done.1) | copy-start | bytes 1572868
  39.6 14.5 %copy-start.7 = (f32[128,16]{0,1:T(8,128)S(1)}, f32[128,16]{0,1:T(8,128)}, u32[]{:S(2)}) copy-start(f32[128,16]{0,1:T(8,128)} %get-tuple-element.23) | copy-start | bytes 24580
  49.7 3.0 %collective-permute-start.6 = (bf16[2064,128]{1,0:T(8,128)(2,1)S(1)}, bf16[2064,128]{1,0:T(8,128)(2,1)}, u32[]{:S(2)}, u32[]{:S(2)}) collective-permute-start(bf16[2064,128]{1,0:T(8,128)(2,1)S(1)} %collective-permute-done.5), channel_id=1, source_target_pairs={{0,4},{4,0},{8,12},{12,8},{16,20},{20,16},{24,28},{28,24},{1,5},{5... | collective-permute-start | bytes 1585160 | tf_op jit(solution)/shard_map/ppermute | solution.py:125
  52.6 1.5 %copy-start.4 = (f32[128,16,128]{0,2,1:T(8,128)S(1)}, f32[128,16,128]{0,2,1:T(8,128)}, u32[]{:S(2)}) copy-start(f32[128,16,128]{0,2,1:T(8,128)} %convolution_bitcast_fusion.1) | copy-start | bytes 3145732
  52.8 10.1 %copy-start.5 = (bf16[128,2048]{1,0:T(8,128)(2,1)S(1)}, bf16[128,2048]{1,0:T(8,128)(2,1)}, u32[]{:S(2)}) copy-start(bf16[128,2048]{1,0:T(8,128)(2,1)} %param.15) | copy-start | bytes 1572868
  52.8 10.1 %copy-start.8 = (f32[2048]{0:T(1024)S(1)}, f32[2048]{0:T(1024)}, u32[]{:S(2)}) copy-start(f32[2048]{0:T(1024)} %param.16) | copy-start | bytes 24580
  54.8 3.6 %collective-permute-start.7 = (f32[128]{0:T(128)S(1)}, f32[128]{0:T(128)S(1)}, u32[]{:S(2)}, u32[]{:S(2)}) collective-permute-start(f32[128]{0:T(128)S(1)} %get-tuple-element.28), channel_id=1, source_target_pairs={{0,1},{1,0},{2,3},{3,2},{4,5},{5,4},{6,7},{7,6},{8,9},{9,8},{10,11... | collective-permute-start | bytes 1544 | tf_op jit(solution)/shard_map/ppermute | solution.py:28
  58.4 4.5 %collective-permute-start.8 = (f32[128]{0:T(128)S(1)}, f32[128]{0:T(128)S(1)}, u32[]{:S(2)}, u32[]{:S(2)}) collective-permute-start(f32[128]{0:T(128)S(1)} %add.99), channel_id=1, source_target_pairs={{0,2},{1,3},{2,0},{3,1},{4,6},{5,7},{6,4},{7,5},{8,10},{9,11},{10,... | collective-permute-start | bytes 1544 | tf_op jit(solution)/shard_map/ppermute | solution.py:28

commit v13 on v7

--- a/solution.py
+++ b/solution.py
@@ -78,14 +78,12 @@
     n_pair = pair.shape[0]
     n_state = heads_here * DH
     state_rows = state.reshape(n_state, DH)
-    factor_rows = jnp.pad(shrinkage_multiplier[None, :], ((0, 7), (0, DH - heads_here)))
     window = jnp.concatenate(
         [from_behind(pair, "ctx", step) for step in range(SPAN, 0, -1)] + [pair], axis=0
     ).reshape(SPAN + 1, 2 * kv_here, rows, DH)
-    first = jnp.concatenate([state_rows, factor_rows], axis=0)
-    got = lax.ppermute(first, "ctx", [(i, i ^ 1) for i in range(count)])
-    state_mate = got[:n_state]
-    factor_mate = got[n_state, :heads_here]
+    state_mate, factor_mate = lax.ppermute(
+        (state_rows, shrinkage_multiplier), "ctx", [(i, i ^ 1) for i in range(count)]
+    )
     state_cube = state_rows.reshape(state.shape)
     mate_cube = state_mate.reshape(state.shape)
     chip_state = jnp.where(

time: 59.3 us -> 60.1 us (1.013)
  matrix products: 9.89 us -> 10.9 us
  waiting for transfers between devices: 9.97 us -> 10.9 us
  local copies, waits for them, and re-layouts: 10.3 us -> 9.47 us
  other arithmetic: 7.82 us -> 7.06 us
    concatenate x1 -> x0, other arithmetic: 1.06 us -> none  [local(): first = jnp.concatenate([state_rows, factor_rows], axis=0)]
    dot_general x1, matrix products: 0.74 us -> 1.7 us  [local(): jnp.einsum('thd,hde->the', query, incoming_b, preferred_element_type=jnp....]
    unnamed x21 -> x29, local copies, waits for them, and re-layouts: 7.17 us -> 6.26 us
    ppermute x1, waiting for transfers between devices: 8.64 us -> 9.5 us  [local(): received = lax.ppermute(packet, 'ctx', routes)]
  transfers between devices with their start and end apart: 9 -> 10, of which waited for: 3 -> 3; matrix products, arithmetic and copies ran while one was open for 40% -> 37% of each run, Pallas kernels for 0% -> 0%
where the time goes in v13:
time: 60.1 us; the launch traced here: 59.5 us
  starting transfers between devices  18.9 us (31%)
  matrix products  10.9 us (18%)
  waiting for transfers between devices  10.9 us (18%)
  local copies, waits for them, and re-layouts  9.47 us (16%)
  other arithmetic  7.06 us (12%)
  between operations  2.3 us (4%)
    ppermute x4, starting transfers between devices, from_behind(): return lax.ppermute(shard, axis, pairs)  12.8 us
    ppermute x1, waiting for transfers between devices, local(): received = lax.ppermute(packet, 'ctx', routes)  9.5 us
    unnamed x29, local copies, waits for them, and re-layouts  6.26 us
    ppermute x2, starting transfers between devices, all_sum(): x = x + lax.ppermute(x, axis, [(i, i ^ bit) for i in range(count)])  4.16 us
    dot_general x1, matrix products, local(): jnp.einsum('kgtbs,bksd->tkgd', expd.astype(jnp.bfloat16).reshape(kv_here,...  3.99 us
    dot_general x1, matrix products, block_terms(): jnp.einsum('hts,shd->thd', weights, values, preferred_element_type=jnp.fl...  2.94 us
    dot_general x1, matrix products, local(): jnp.einsum('thd,hde->the', query, incoming_b, preferred_element_type=jnp....  1.7 us
    dot_general x1, matrix products, block_terms(): jnp.einsum('shd,she->hde', weighted, values, preferred_element_type=jnp.f...  1.34 us
  transfers between devices with their start and end apart: 10, of which 3 were waited for; matrix products, arithmetic and copies ran while one was open for 37% of the time, Pallas kernels for 0%

profile of v13, /device:TPU:0, one launch (start us, length us, event | category | flops | bytes accessed | tf_op | source)
XLA Modules:
  0.0 59.5 jit_solution(10698070732639750927)
XLA Ops:
  0.6 0.0 copy-start
  0.6 1.0 %copy.57 = bf16[128,256]{0,1:T(8,128)(2,1)S(1)} copy(bf16[128,256]{1,0:T(8,128)(2,1)} %param.18) | data formatting | bytes 131072 | tf_op args[8]
  1.7 1.0 %copy.58 = bf16[128,256]{0,1:T(8,128)(2,1)S(1)} copy(bf16[128,256]{1,0:T(8,128)(2,1)} %param.19) | data formatting | bytes 131072 | tf_op args[9]
  2.6 0.1 copy.59
  2.8 5.5 %collective-permute-start.6 = (bf16[512,128]{1,0:T(8,128)(2,1)S(1)}, bf16[512,128]{1,0:T(8,128)(2,1)}, u32[]{:S(2)}, u32[]{:S(2)}) collective-permute-start(bf16[512,128]{1,0:T(8,128)(2,1)S(1)} %bitcast.135), channel_id=1, source_target_pairs={{0,16},{4,20},{8,24},{12,28},{1,17},{5,21},{9,25},{13,29},{2,18},{... | collective-permute-start | bytes 393224 | tf_op jit(solution)/shard_map/ppermute | solution.py:13
  8.3 3.2 %collective-permute-start.7 = (bf16[512,128]{1,0:T(8,128)(2,1)S(1)}, bf16[512,128]{1,0:T(8,128)(2,1)}, u32[]{:S(2)}, u32[]{:S(2)}) collective-permute-start(bf16[512,128]{1,0:T(8,128)(2,1)S(1)} %bitcast.136), channel_id=1, source_target_pairs={{0,12},{4,16},{8,20},{12,24},{16,28},{1,13},{5,17},{9,21},{13,25},... | collective-permute-start | bytes 393224 | tf_op jit(solution)/shard_map/ppermute | solution.py:13
  11.5 2.1 %collective-permute-start.8 = (bf16[512,128]{1,0:T(8,128)(2,1)S(1)}, bf16[512,128]{1,0:T(8,128)(2,1)S(1)}, u32[]{:S(2)}, u32[]{:S(2)}) collective-permute-start(bf16[512,128]{1,0:T(8,128)(2,1)S(1)} %bitcast.137), channel_id=1, source_target_pairs={{0,8},{4,12},{8,16},{12,20},{16,24},{20,28},{1,9},{5,13},{9,17},{1... | collective-permute-start | bytes 393224 | tf_op jit(solution)/shard_map/ppermute | solution.py:13
  13.7 0.8 %reduce-window.4 = s32[6,1]{0,1:T(1,128)S(1)} reduce-window(s32[6,1]{0,1:T(1,128)} %bitcast.146, s32[]{:T(128)} %constant.23.clone.1), window={size=6x1 pad=5_0x0_0}, to_apply=%region_0.0 | reduce-window | flops 30 | bytes 52 | tf_op jit(solution)/shard_map/reduce-window
  14.5 0.1 convert_reduce_fusion.1
  14.6 0.6 %fusion.51 = s32[]{:T(128)} fusion(s32[6,1]{0,1:T(1,128)S(1)} %reduce-window.4, s32[]{:T(128)} %bitcast.3), kind=kLoop, calls=%fused_computation.80 | loop fusion | flops 17 | bytes 32 | tf_op jit(solution)/shard_map/reduce_sum | solution.py:35
  15.2 0.6 %slice.34 = s32[1]{0:T(128)} slice(s32[128]{0:T(128)S(1)} %convert_reduce_fusion.1), slice={[127:128]} | slice | bytes 8 | tf_op jit(solution)/shard_map/slice | solution.py:48
  15.9 1.0 %reduce_window_sum.20 = f32[16,128]{1,0:T(8,128)S(1)} reduce-window(f32[16,128]{1,0:T(8,128)} %param.14, f32[]{:T(128)} %constant.48.clone.1), window={size=1x128 pad=0_0x127_0}, to_apply=%region_2.3 | reduce-window | flops 260096 | bytes 16388 | tf_op jit(solution)/shard_map/jit(cumsum)/reduce_window_sum | solution.py:40
  16.8 0.2 slice_reduce_fusion
  17.0 1.3 %copy.76 = bf16[128,2048]{0,1:T(8,128)(2,1)S(1)} copy(bf16[128,2048]{1,0:T(8,128)(2,1)} %param.12) | data formatting | bytes 1048576 | tf_op jit(solution)/shard_map/reshape | solution.py:66
  18.3 0.0 copy-start.3
  19.0 0.6 %fusion.57 = (f32[128]{0:T(128)S(1)}, pred[128]{0:T(512)(128)(4,1)S(1)}, f32[128]{0:T(128)S(1)}) fusion(s32[128]{0:T(128)S(1)} %convert_reduce_fusion.1, s32[]{:T(128)S(6)} %select_n.61, s32[]{:T(128)} %bitcast.5), kind=kLoop, calls=%fused_computation.94 | loop fusion | flops 512 | bytes 1672 | tf_op jit(solution)/shard_map/convert_element_type | solution.py:122
  19.6 0.6 %multiply_bitcast_fusion = (f32[128,16]{0,1:T(8,128)}, f32[128,16]{0,1:T(8,128)S(1)}) fusion(f32[16,128]{1,0:T(8,128)S(1)} %reduce_window_sum.20, f32[128]{0:T(128)S(1)} %get-tuple-element.10, f32[128]{0:T(128)S(1)} %get-tuple-element.18, f32[16]{0:T(128)S(1)} %slice_reduce_fusion), kind=kLoop, calls=%fused_computation.69 | loop fusion | flops 6144 | bytes 25664 | tf_op jit(solution)/shard_map/mul | solution.py:122
  20.2 1.3 %fusion.22 = f32[16,128,128]{2,1,0:T(8,128)S(1)} fusion(bf16[128,16,128]{0,2,1:T(8,128)(2,1)S(1)} %bitcast.129, f32[128,16]{0,1:T(8,128)S(1)} %get-tuple-element.15, bf16[128,2048]{1,0:T(8,128)(2,1)} %param.13), kind=kOutput, calls=%fused_computation.31 | convolution fusion | flops 67895296 | bytes 2105344 | tf_op jit(solution)/shard_map/shd,she->hde/dot_general | solution.py:51
  21.6 0.1 collective-permute-start.1
  21.7 0.6 slice.33
  22.8 0.6 collective-permute-start
  23.4 0.1 fusion.44
  23.5 0.1 convert_reduce_fusion
  23.5 1.1 %copy.79 = bf16[16,8,16,128]{3,2,1,0:T(8,128)(2,1)S(1)} copy(bf16[16,8,16,128]{3,1,2,0:T(8,128)(2,1)} %bitcast.133) | data formatting | bytes 1048576
  24.7 0.2 compare_and_fusion
  25.0 2.9 %convolution_bitcast_fusion.1 = f32[128,16,128]{0,2,1:T(8,128)} fusion(bf16[128,16,128]{0,2,1:T(8,128)(2,1)} %bitcast.130, f32[16,128]{1,0:T(8,128)S(1)} %reduce_window_sum.20, pred[128,128]{1,0:T(8,128)(4,1)S(1)} %fusion.44, bf16[128,2048]{1,0:T(8,128)(2,1)} %param.13, bf16[128,2048]{1,0:T(8,128)(2,1)S(1)} %copy-done), kind=kOutput, calls=%fused_computation.14 | convolution fusion | flops 135528448 | bytes 2646016 | tf_op jit(solution)/shard_map/hts,shd->thd/dot_general | solution.py:46
  27.9 1.9 %collective-permute-start.9 = (bf16[512,128]{1,0:T(8,128)(2,1)S(1)}, bf16[512,128]{1,0:T(8,128)(2,1)S(1)}, u32[]{:S(2)}, u32[]{:S(2)}) collective-permute-start(bf16[512,128]{1,0:T(8,128)(2,1)S(1)} %bitcast.138), channel_id=1, source_target_pairs={{0,4},{4,8},{8,12},{12,16},{16,20},{20,24},{24,28},{1,5},{5,9},{9,... | collective-permute-start | bytes 393224 | tf_op jit(solution)/shard_map/ppermute | solution.py:13
  29.9 0.3 select_convert_fusion.1
  30.2 1.3 %collective-permute-start.2 = (bf16[2064,128]{1,0:T(8,128)(2,1)S(1)}, bf16[2064,128]{1,0:T(8,128)(2,1)S(1)}, u32[]{:S(2)}, u32[]{:S(2)}) collective-permute-start(bf16[2064,128]{1,0:T(8,128)(2,1)S(1)} %pad_maximum_fusion), channel_id=1, source_target_pairs={{4,8},{12,16},{20,24},{0,20},{8,28},{5,9},{13,17},{21,25},{1,21},{... | collective-permute-start | bytes 1585160 | tf_op jit(solution)/shard_map/ppermute | solution.py:102
  31.6 0.9 %constant_dynamic-update-slice_fusion.4 = bf16[2560,128]{1,0:T(8,128)(2,1)S(1)} fusion(bf16[512,128]{1,0:T(8,128)(2,1)} %collective-permute-done.6), kind=kLoop, calls=%fused_computation.62 | loop fusion | bytes 262144
  32.5 0.9 %constant_dynamic-update-slice_fusion.3 = bf16[2560,128]{1,0:T(8,128)(2,1)S(1)} fusion(bf16[2560,128]{1,0:T(8,128)(2,1)S(1)} %constant_dynamic-update-slice_fusion.4, bf16[512,128]{1,0:T(8,128)(2,1)} %collective-permute-done.7), kind=kLoop, calls=%fused_computation.61 | loop fusion | bytes 262144
  33.5 9.5 %collective-permute-done.2 = bf16[2064,128]{1,0:T(8,128)(2,1)S(1)} collective-permute-done((bf16[2064,128]{1,0:T(8,128)(2,1)S(1)}, bf16[2064,128]{1,0:T(8,128)(2,1)S(1)}, u32[]{:S(2)}, u32[]{:S(2)}) %collective-permute-start.2) | collective-permute-done | bytes 528416 | tf_op jit(solution)/shard_map/ppermute | solution.py:102
  43.1 0.0 copy-start.6
  43.1 0.0 copy-start.9
  43.1 0.9 %fusion = (f32[2,8,128]{2,1,0:T(8,128)S(1)}, f32[2,5,128,128,8]{3,2,4,1,0:T(8,128)S(1)}) fusion(pred[128,5,128]{0,2,1:T(8,128)(4,1)S(1)} %compare_and_fusion, bf16[128,2,8,128,1]{3,2,1,0,4:T(8,128)(2,1)S(1)} %bitcast.126, bf16[5,2,128,128]{3,2,1,0:T(8,128)(2,1)S(1)} %get-tuple-element.13), kind=kOutput, calls=%fused_computation.2 | convolution fusion | flops 339474432 | bytes 6184960 | tf_op jit(solution)/shard_map/tkgd,bksd->kgtbs/dot_general | solution.py:140
  44.1 0.9 %collective-permute-done.3 = bf16[2064,128]{1,0:T(8,128)(2,1)S(1)} collective-permute-done((bf16[2064,128]{1,0:T(8,128)(2,1)S(1)}, bf16[2064,128]{1,0:T(8,128)(2,1)S(1)}, u32[]{:S(2)}, u32[]{:S(2)}) %collective-permute-start.3) | collective-permute-done | bytes 528416 | tf_op jit(solution)/shard_map/ppermute | solution.py:103
  45.0 0.1 broadcast_select_fusion
  45.1 0.1 slice_select_fusion
  45.2 1.7 %multiply_reduce_fusion = (f32[128]{0:T(128)S(1)}, f32[128,16,128]{0,2,1:T(8,128)}) fusion(f32[128,16,128]{0,2,1:T(8,128)S(1)} %copy-done.4, f32[128,16]{0,1:T(8,128)S(1)} %copy-done.6, f32[16,128,128]{2,1,0:T(8,128)S(1)} %bitcast.124, bf16[16,128,128]{2,1,0:T(8,128)(2,1)S(1)} %bitcast.128, bf16[16,128,128]{2,1,0:T(8,128)(2,1)S(1)} %bitcast.127, ...), kind=kOutput, calls=%fused_computation.22 | convolution fusion | flops 70254464 | bytes 4727425 | tf_op jit(solution)/shard_map/thd,hde->the/dot_general | solution.py:119
  46.9 1.6 %collective-permute-start.4 = (f32[128]{0:T(128)S(1)}, f32[128]{0:T(128)S(1)}, u32[]{:S(2)}, u32[]{:S(2)}) collective-permute-start(f32[128]{0:T(128)S(1)} %get-tuple-element.19), channel_id=1, source_target_pairs={{0,1},{1,0},{2,3},{3,2},{4,5},{5,4},{6,7},{7,6},{8,9},{9,8},{10,11... | collective-permute-start | bytes 1544 | tf_op jit(solution)/shard_map/ppermute | solution.py:28
  48.5 1.2 %fusion.4 = f32[2,8,128]{2,1,0:T(8,128)S(1)} fusion(f32[2,5,128,128,8]{3,2,4,1,0:T(8,128)S(1)} %get-tuple-element.22, f32[2,8,128]{2,1,0:T(8,128)S(1)} %get-tuple-element.21, pred[128,5,128]{0,2,1:T(8,128)(4,1)S(1)} %compare_and_fusion), kind=kLoop, calls=%fused_computation.6 | loop fusion | flops 6551552 | bytes 5341184 | tf_op jit(solution)/shard_map/reduce_sum | solution.py:145
  49.7 0.2 copy.74
  49.9 0.5 collective-permute-done.4
  50.4 2.6 %collective-permute-start.5 = (f32[128]{0:T(128)S(1)}, f32[128]{0:T(128)S(1)}, u32[]{:S(2)}, u32[]{:S(2)}) collective-permute-start(f32[128]{0:T(128)S(1)} %add.93), channel_id=1, source_target_pairs={{0,2},{1,3},{2,0},{3,1},{4,6},{5,7},{6,4},{7,5},{8,10},{9,11},{10,... | collective-permute-start | bytes 1544 | tf_op jit(solution)/shard_map/ppermute | solution.py:28
  53.0 4.0 %divide_convert_fusion = bf16[128,2,8,128]{0,3,2,1:T(8,128)(2,1)S(1)} fusion(f32[2,5,128,128,8]{3,2,4,1,0:T(8,128)} %copy-done.1, f32[2,8,128]{2,1,0:T(8,128)S(1)} %get-tuple-element.21, pred[128,5,128]{0,2,1:T(8,128)(4,1)S(1)} %compare_and_fusion, f32[128,2,8]{0,2,1:T(8,128)S(1)} %bitcast.142, bf16[5,2,128,128]{2,3,0,1:T(8,128)(2,1)S(1)} %copy.74), kind=kOutput, calls=%fused_computation.20 | convolution fusion | flops 342622208 | bytes 6193152 | tf_op jit(solution)/shard_map/kgtbs,bksd->tkgd/dot_general | solution.py:146
  57.0 1.0 %copy.64 = bf16[128,2048]{1,0:T(8,128)(2,1)} copy(bf16[128,2048]{0,1:T(8,128)(2,1)S(1)} %bitcast.134) | data formatting | bytes 1048576
  58.0 0.3 copy.56
  58.4 1.1 %multiply_convert_fusion = bf16[128,2048]{1,0:T(8,128)(2,1)} fusion(bf16[128,2048]{1,0:T(8,128)(2,1)S(1)} %copy-done.5, f32[128,2048]{1,0:T(8,128)S(1)} %copy.56, f32[2048]{0:T(1024)S(1)} %copy-done.7, f32[128]{0:T(128)S(1)} %add_rsqrt_fusion), kind=kLoop, calls=%fused_computation.21 | loop fusion | flops 2097152 | bytes 2105856 | tf_op jit(solution)/shard_map/convert_element_type | solution.py:134
  (40 shorter events, 0.3 us)
Async XLA Ops:
  0.6 24.3 %copy-start = (bf16[128,2048]{1,0:T(8,128)(2,1)S(1)}, bf16[128,2048]{1,0:T(8,128)(2,1)}, u32[]{:S(2)}) copy-start(bf16[128,2048]{1,0:T(8,128)(2,1)} %param.11) | copy-start | bytes 1572868
  2.8 28.8 %collective-permute-start.6 = (bf16[512,128]{1,0:T(8,128)(2,1)S(1)}, bf16[512,128]{1,0:T(8,128)(2,1)}, u32[]{:S(2)}, u32[]{:S(2)}) collective-permute-start(bf16[512,128]{1,0:T(8,128)(2,1)S(1)} %bitcast.135), channel_id=1, source_target_pairs={{0,16},{4,20},{8,24},{12,28},{1,17},{5,21},{9,25},{13,29},{2,18},{... | collective-permute-start | bytes 393224 | tf_op jit(solution)/shard_map/ppermute | solution.py:13
  8.3 24.2 %collective-permute-start.7 = (bf16[512,128]{1,0:T(8,128)(2,1)S(1)}, bf16[512,128]{1,0:T(8,128)(2,1)}, u32[]{:S(2)}, u32[]{:S(2)}) collective-permute-start(bf16[512,128]{1,0:T(8,128)(2,1)S(1)} %bitcast.136), channel_id=1, source_target_pairs={{0,12},{4,16},{8,20},{12,24},{16,28},{1,13},{5,17},{9,21},{13,25},... | collective-permute-start | bytes 393224 | tf_op jit(solution)/shard_map/ppermute | solution.py:13
  11.5 21.9 %collective-permute-start.8 = (bf16[512,128]{1,0:T(8,128)(2,1)S(1)}, bf16[512,128]{1,0:T(8,128)(2,1)S(1)}, u32[]{:S(2)}, u32[]{:S(2)}) collective-permute-start(bf16[512,128]{1,0:T(8,128)(2,1)S(1)} %bitcast.137), channel_id=1, source_target_pairs={{0,8},{4,12},{8,16},{12,20},{16,24},{20,28},{1,9},{5,13},{9,17},{1... | collective-permute-start | bytes 393224 | tf_op jit(solution)/shard_map/ppermute | solution.py:13
  18.3 3.3 %copy-start.3 = (bf16[128,2048]{0,1:T(8,128)(2,1)}, bf16[128,2048]{0,1:T(8,128)(2,1)S(1)}, u32[]{:S(2)}) copy-start(bf16[128,2048]{0,1:T(8,128)(2,1)S(1)} %copy.76) | copy-start | bytes 1572868
  21.6 8.3 %collective-permute-start.1 = (f32[2048,128]{1,0:T(8,128)S(1)}, f32[2048,128]{1,0:T(8,128)S(1)}, u32[]{:S(2)}, u32[]{:S(2)}) collective-permute-start(f32[2048,128]{1,0:T(8,128)S(1)} %bitcast.123), channel_id=1, source_target_pairs={{0,4},{4,0},{8,12},{12,8},{16,20},{20,16},{24,28},{28,24},{1,5},{5... | collective-permute-start | bytes 3145736 | tf_op jit(solution)/shard_map/ppermute | solution.py:84
  22.8 5.1 %collective-permute-start = (f32[16]{0:T(128)S(1)}, f32[16]{0:T(128)S(1)}, u32[]{:S(2)}, u32[]{:S(2)}) collective-permute-start(f32[16]{0:T(128)S(1)} %exponential_multiply_fusion), channel_id=1, source_target_pairs={{0,4},{4,0},{8,12},{12,8},{16,20},{20,16},{24,28},{28,24},{1,5},{5... | collective-permute-start | bytes 200 | tf_op jit(solution)/shard_map/ppermute | solution.py:84
  27.9 15.1 %copy-start.8 = (f32[16]{0:T(128)}, f32[16]{0:T(128)S(1)}, u32[]{:S(2)}) copy-start(f32[16]{0:T(128)S(1)} %collective-permute-done) | copy-start | bytes 196
  27.9 5.6 %collective-permute-start.9 = (bf16[512,128]{1,0:T(8,128)(2,1)S(1)}, bf16[512,128]{1,0:T(8,128)(2,1)S(1)}, u32[]{:S(2)}, u32[]{:S(2)}) collective-permute-start(bf16[512,128]{1,0:T(8,128)(2,1)S(1)} %bitcast.138), channel_id=1, source_target_pairs={{0,4},{4,8},{8,12},{12,16},{16,20},{20,24},{24,28},{1,5},{5,9},{9,... | collective-permute-start | bytes 393224 | tf_op jit(solution)/shard_map/ppermute | solution.py:13
  30.2 12.8 %collective-permute-start.2 = (bf16[2064,128]{1,0:T(8,128)(2,1)S(1)}, bf16[2064,128]{1,0:T(8,128)(2,1)S(1)}, u32[]{:S(2)}, u32[]{:S(2)}) collective-permute-start(bf16[2064,128]{1,0:T(8,128)(2,1)S(1)} %pad_maximum_fusion), channel_id=1, source_target_pairs={{4,8},{12,16},{20,24},{0,20},{8,28},{5,9},{13,17},{21,25},{1,21},{... | collective-permute-start | bytes 1585160 | tf_op jit(solution)/shard_map/ppermute | solution.py:102
  43.0 1.9 %collective-permute-start.3 = (bf16[2064,128]{1,0:T(8,128)(2,1)S(1)}, bf16[2064,128]{1,0:T(8,128)(2,1)S(1)}, u32[]{:S(2)}, u32[]{:S(2)}) collective-permute-start(bf16[2064,128]{1,0:T(8,128)(2,1)S(1)} %collective-permute-done.2), channel_id=1, source_target_pairs={{0,4},{4,0},{8,12},{12,8},{16,20},{20,16},{24,28},{28,24},{1,5},{5... | collective-permute-start | bytes 1585160 | tf_op jit(solution)/shard_map/ppermute | solution.py:103
  43.1 2.1 %copy-start.4 = (f32[128,16,128]{0,2,1:T(8,128)S(1)}, f32[128,16,128]{0,2,1:T(8,128)}, u32[]{:S(2)}) copy-start(f32[128,16,128]{0,2,1:T(8,128)} %convolution_bitcast_fusion.1) | copy-start | bytes 3145732
  43.1 2.1 %copy-start.6 = (f32[128,16]{0,1:T(8,128)S(1)}, f32[128,16]{0,1:T(8,128)}, u32[]{:S(2)}) copy-start(f32[128,16]{0,1:T(8,128)} %get-tuple-element.14) | copy-start | bytes 24580
  43.1 2.1 %copy-start.9 = (f32[16]{0:T(128)S(1)}, f32[16]{0:T(128)}, u32[]{:S(2)}) copy-start(f32[16]{0:T(128)} %copy-done.8) | copy-start | bytes 196
  44.0 5.7 %copy-start.1 = (f32[2,5,128,128,8]{3,2,4,1,0:T(8,128)}, f32[2,5,128,128,8]{3,2,4,1,0:T(8,128)S(1)}, u32[]{:S(2)}) copy-start(f32[2,5,128,128,8]{3,2,4,1,0:T(8,128)S(1)} %get-tuple-element.22) | copy-start | bytes 15728644
  46.9 3.5 %collective-permute-start.4 = (f32[128]{0:T(128)S(1)}, f32[128]{0:T(128)S(1)}, u32[]{:S(2)}, u32[]{:S(2)}) collective-permute-start(f32[128]{0:T(128)S(1)} %get-tuple-element.19), channel_id=1, source_target_pairs={{0,1},{1,0},{2,3},{3,2},{4,5},{5,4},{6,7},{7,6},{8,9},{9,8},{10,11... | collective-permute-start | bytes 1544 | tf_op jit(solution)/shard_map/ppermute | solution.py:28
  50.4 7.9 %collective-permute-start.5 = (f32[128]{0:T(128)S(1)}, f32[128]{0:T(128)S(1)}, u32[]{:S(2)}, u32[]{:S(2)}) collective-permute-start(f32[128]{0:T(128)S(1)} %add.93), channel_id=1, source_target_pairs={{0,2},{1,3},{2,0},{3,1},{4,6},{5,7},{6,4},{7,5},{8,10},{9,11},{10,... | collective-permute-start | bytes 1544 | tf_op jit(solution)/shard_map/ppermute | solution.py:28
  53.0 5.0 %copy-start.2 = (f32[128,16,128]{0,2,1:T(8,128)S(1)}, f32[128,16,128]{0,2,1:T(8,128)}, u32[]{:S(2)}) copy-start(f32[128,16,128]{0,2,1:T(8,128)} %get-tuple-element.20) | copy-start | bytes 3145732
  53.0 5.4 %copy-start.5 = (bf16[128,2048]{1,0:T(8,128)(2,1)S(1)}, bf16[128,2048]{1,0:T(8,128)(2,1)}, u32[]{:S(2)}) copy-start(bf16[128,2048]{1,0:T(8,128)(2,1)} %param.15) | copy-start | bytes 1572868
  53.0 5.4 %copy-start.7 = (f32[2048]{0:T(1024)S(1)}, f32[2048]{0:T(1024)}, u32[]{:S(2)}) copy-start(f32[2048]{0:T(1024)} %param.16) | copy-start | bytes 24580

commit v14 on v12

--- a/solution.py
+++ b/solution.py
@@ -101,6 +101,7 @@
         [chip_state.astype(jnp.bfloat16).reshape(n_state, DH), chip_rows], axis=0
     )
     routes = [(i, i + 1) for i in range(1, count - 1, 2)] + [(i, i + 5) for i in range(0, count - 5, 2)]
+    packet, soft_q = lax.optimization_barrier((packet, soft_q))
     received = lax.ppermute(packet, "ctx", routes)
     span_rows = (SPAN + 1) * rows
     key_pos = shard * rows - SPAN * rows + jnp.arange(span_rows, dtype=jnp.int32)

time: 64.7 us -> 57.4 us (0.89)
  local copies, waits for them, and re-layouts: 11.8 us -> 8.25 us
  other arithmetic: 10.7 us -> 9.01 us
  matrix products: 8.11 us -> 7.18 us
    unnamed x33 -> x23, local copies, waits for them, and re-layouts: 7.93 us -> 5.14 us
    ppermute x1, waiting for transfers between devices: 10.1 us -> 8.5 us  [local(): received = lax.ppermute(packet, 'ctx', routes)]
    ppermute x1, waiting for transfers between devices: 0.01 us -> 1 us  [local(): got = lax.ppermute(first, 'ctx', [(i, i ^ 1) for i in range(count)])]
    dot_general x1, matrix products: 1.86 us -> 0.92 us  [local(): jnp.einsum('tkgd,bksd->kgtbs', soft_query, window[:, :kv_here], preferred...]
    ppermute x4, starting transfers between devices: 12.2 us -> 11.4 us  [from_behind(): return lax.ppermute(shard, axis, pairs)]
    slice x1, local copies, waits for them, and re-layouts: 0.78 us -> 0.04 us  [local(): window[:, kv_here:]]
  transfers between devices with their start and end apart: 9 -> 9, of which waited for: 3 -> 4; matrix products, arithmetic and copies ran while one was open for 39% -> 31% of each run, Pallas kernels for 0% -> 0%
where the time goes in v14:
time: 57.4 us; the launch traced here: 56.9 us
  starting transfers between devices  18.1 us (32%)
  waiting for transfers between devices  12 us (21%)
  other arithmetic  9.01 us (16%)
  local copies, waits for them, and re-layouts  8.25 us (14%)
  matrix products  7.18 us (13%)
  between operations  2.38 us (4%)
    ppermute x4, starting transfers between devices, from_behind(): return lax.ppermute(shard, axis, pairs)  11.4 us
    ppermute x1, waiting for transfers between devices, local(): received = lax.ppermute(packet, 'ctx', routes)  8.5 us
    unnamed x23, local copies, waits for them, and re-layouts  5.14 us
    ppermute x2, starting transfers between devices, all_sum(): x = x + lax.ppermute(x, axis, [(i, i ^ bit) for i in range(count)])  4.25 us
    dot_general x1, matrix products, block_terms(): jnp.einsum('hts,shd->thd', weights, values, preferred_element_type=jnp.fl...  2.77 us
    ppermute x2, waiting for transfers between devices, all_sum(): x = x + lax.ppermute(x, axis, [(i, i ^ bit) for i in range(count)])  2.46 us
    dot_general x1, matrix products, local(): jnp.einsum('kgtbs,bksd->tkgd', expd.astype(jnp.bfloat16).reshape(kv_here,...  1.4 us
    dot_general x1, matrix products, block_terms(): jnp.einsum('shd,she->hde', weighted, values, preferred_element_type=jnp.f...  1.35 us
  transfers between devices with their start and end apart: 9, of which 4 were waited for; matrix products, arithmetic and copies ran while one was open for 31% of the time, Pallas kernels for 0%

profile of v14, /device:TPU:0, one launch (start us, length us, event | category | flops | bytes accessed | tf_op | source)
XLA Modules:
  0.0 56.9 jit_solution(10921105738556421705)
XLA Ops:
  0.6 0.0 copy-start
  0.6 1.0 %copy.54 = bf16[128,256]{0,1:T(8,128)(2,1)S(1)} copy(bf16[128,256]{1,0:T(8,128)(2,1)} %param.18) | data formatting | bytes 131072 | tf_op args[8]
  1.7 1.0 %copy.55 = bf16[128,256]{0,1:T(8,128)(2,1)S(1)} copy(bf16[128,256]{1,0:T(8,128)(2,1)} %param.19) | data formatting | bytes 131072 | tf_op args[9]
  2.6 0.1 copy.56
  2.8 4.9 %collective-permute-start.1 = (bf16[512,128]{1,0:T(8,128)(2,1)S(1)}, bf16[512,128]{1,0:T(8,128)(2,1)S(1)}, u32[]{:S(2)}, u32[]{:S(2)}) collective-permute-start(bf16[512,128]{1,0:T(8,128)(2,1)S(1)} %bitcast.139), channel_id=1, source_target_pairs={{0,16},{4,20},{8,24},{12,28},{1,17},{5,21},{9,25},{13,29},{2,18},{... | collective-permute-start | bytes 393224 | tf_op jit(solution)/shard_map/ppermute | solution.py:13
  7.7 2.6 %collective-permute-start.2 = (bf16[512,128]{1,0:T(8,128)(2,1)S(1)}, bf16[512,128]{1,0:T(8,128)(2,1)S(1)}, u32[]{:S(2)}, u32[]{:S(2)}) collective-permute-start(bf16[512,128]{1,0:T(8,128)(2,1)S(1)} %bitcast.140), channel_id=1, source_target_pairs={{0,12},{4,16},{8,20},{12,24},{16,28},{1,13},{5,17},{9,21},{13,25},... | collective-permute-start | bytes 393224 | tf_op jit(solution)/shard_map/ppermute | solution.py:13
  10.2 2.1 %collective-permute-start.3 = (bf16[512,128]{1,0:T(8,128)(2,1)S(1)}, bf16[512,128]{1,0:T(8,128)(2,1)S(1)}, u32[]{:S(2)}, u32[]{:S(2)}) collective-permute-start(bf16[512,128]{1,0:T(8,128)(2,1)S(1)} %bitcast.141), channel_id=1, source_target_pairs={{0,8},{4,12},{8,16},{12,20},{16,24},{20,28},{1,9},{5,13},{9,17},{1... | collective-permute-start | bytes 393224 | tf_op jit(solution)/shard_map/ppermute | solution.py:13
  12.4 1.8 %collective-permute-start.4 = (bf16[512,128]{1,0:T(8,128)(2,1)S(1)}, bf16[512,128]{1,0:T(8,128)(2,1)S(1)}, u32[]{:S(2)}, u32[]{:S(2)}) collective-permute-start(bf16[512,128]{1,0:T(8,128)(2,1)S(1)} %bitcast.142), channel_id=1, source_target_pairs={{0,4},{4,8},{8,12},{12,16},{16,20},{20,24},{24,28},{1,5},{5,9},{9,... | collective-permute-start | bytes 393224 | tf_op jit(solution)/shard_map/ppermute | solution.py:13
  14.2 0.8 %reduce-window.4 = s32[6,1]{0,1:T(1,128)S(1)} reduce-window(s32[6,1]{0,1:T(1,128)} %bitcast.151, s32[]{:T(128)} %constant.24.clone.1), window={size=6x1 pad=5_0x0_0}, to_apply=%region_0.0 | reduce-window | flops 30 | bytes 52 | tf_op jit(solution)/shard_map/reduce-window
  15.1 0.6 %fusion.51 = s32[]{:T(128)} fusion(s32[6,1]{0,1:T(1,128)S(1)} %reduce-window.4, s32[]{:T(128)} %bitcast.6), kind=kLoop, calls=%fused_computation.83 | loop fusion | flops 17 | bytes 32 | tf_op jit(solution)/shard_map/reduce_sum | solution.py:35
  15.7 0.1 convert_reduce_fusion.1
  15.8 0.6 %slice.38 = s32[1]{0:T(128)} slice(s32[128]{0:T(128)S(1)} %convert_reduce_fusion.1), slice={[127:128]} | slice | bytes 8 | tf_op jit(solution)/shard_map/slice | solution.py:48
  17.0 0.7 %fusion.58 = (f32[128]{0:T(128)S(1)}, pred[128]{0:T(512)(128)(4,1)S(1)}, f32[128]{0:T(128)S(1)}) fusion(s32[128]{0:T(128)S(1)} %convert_reduce_fusion.1, s32[]{:T(128)S(6)} %select_n.61, s32[]{:T(128)} %bitcast.3), kind=kLoop, calls=%fused_computation.99 | loop fusion | flops 512 | bytes 1672 | tf_op jit(solution)/shard_map/convert_element_type | solution.py:145
  17.7 0.6 %slice.40 = pred[1]{0:T(512)(128)(4,1)} slice(pred[128]{0:T(512)(128)(4,1)S(1)} %get-tuple-element.21), slice={[127:128]} | slice | bytes 2 | tf_op jit(solution)/shard_map/slice | solution.py:52
  18.9 1.3 %copy.76 = bf16[128,2048]{0,1:T(8,128)(2,1)S(1)} copy(bf16[128,2048]{1,0:T(8,128)(2,1)} %param.12) | data formatting | bytes 1048576 | tf_op jit(solution)/shard_map/reshape | solution.py:66
  20.3 0.0 copy-start.1
  20.3 1.0 %reduce_window_sum.20 = f32[16,128]{1,0:T(8,128)S(1)} reduce-window(f32[16,128]{1,0:T(8,128)} %param.14, f32[]{:T(128)} %constant.49.clone.1), window={size=1x128 pad=0_0x127_0}, to_apply=%region_2.3 | reduce-window | flops 260096 | bytes 16388 | tf_op jit(solution)/shard_map/jit(cumsum)/reduce_window_sum | solution.py:40
  21.3 0.2 slice_reduce_fusion
  21.5 0.1 multiply_bitcast_fusion
  21.5 1.4 %fusion.22 = f32[16,128,128]{2,1,0:T(8,128)S(1)} fusion(bf16[128,16,128]{0,2,1:T(8,128)(2,1)S(1)} %bitcast.133, f32[128,16]{0,1:T(8,128)S(1)} %get-tuple-element.28, bf16[128,2048]{1,0:T(8,128)(2,1)} %param.13), kind=kOutput, calls=%fused_computation.33 | convolution fusion | flops 67895296 | bytes 2105344 | tf_op jit(solution)/shard_map/shd,she->hde/dot_general | solution.py:51
  22.9 1.1 %select_maximum_fusion = f32[2056,128]{1,0:T(8,128)} fusion(f32[1,16]{1,0:T(1,128)S(1)} %bitcast.147, f32[2048,128]{1,0:T(8,128)S(1)} %bitcast.127), kind=kLoop, calls=%fused_computation.18 | loop fusion | flops 789504 | bytes 2101312 | tf_op jit(solution)/shard_map/concatenate | solution.py:85
  24.0 1.1 %collective-permute-start = (f32[2056,128]{1,0:T(8,128)}, f32[2056,128]{1,0:T(8,128)S(1)}, u32[]{:S(2)}, u32[]{:S(2)}) collective-permute-start(f32[2056,128]{1,0:T(8,128)} %select_maximum_fusion), channel_id=1, source_target_pairs={{0,4},{4,0},{8,12},{12,8},{16,20},{20,16},{24,28},{28,24},{1,5},{5... | collective-permute-start | bytes 3158024 | tf_op jit(solution)/shard_map/ppermute | solution.py:86
  25.1 0.1 convert_reduce_fusion
  25.2 0.2 compare_and_fusion
  25.7 0.9 %copy.74 = bf16[5,2,128,128]{2,3,0,1:T(8,128)(2,1)} copy(bf16[5,2,128,128]{3,2,1,0:T(8,128)(2,1)S(1)} %get-tuple-element.25) | data formatting | bytes 655360
  26.6 1.0 %collective-permute-done = f32[2056,128]{1,0:T(8,128)S(1)} collective-permute-done((f32[2056,128]{1,0:T(8,128)}, f32[2056,128]{1,0:T(8,128)S(1)}, u32[]{:S(2)}, u32[]{:S(2)}) %collective-permute-start) | collective-permute-done | bytes 1052704 | tf_op jit(solution)/shard_map/ppermute | solution.py:86
  27.6 0.3 select_convert_fusion.1
  27.9 1.1 %copy.79 = bf16[16,8,16,128]{3,2,1,0:T(8,128)(2,1)S(1)} copy(bf16[16,8,16,128]{3,1,2,0:T(8,128)(2,1)} %bitcast.137) | data formatting | bytes 1048576
  29.1 1.3 %collective-permute-start.5 = (bf16[2064,128]{1,0:T(8,128)(2,1)S(1)}, bf16[2064,128]{1,0:T(8,128)(2,1)S(1)}, u32[]{:S(2)}, u32[]{:S(2)}) collective-permute-start(bf16[2064,128]{1,0:T(8,128)(2,1)S(1)} %pad_maximum_fusion), channel_id=1, source_target_pairs={{4,8},{12,16},{20,24},{0,20},{8,28},{5,9},{13,17},{21,25},{1,21},{... | collective-permute-start | bytes 1585160 | tf_op jit(solution)/shard_map/ppermute | solution.py:105
  30.4 0.0 copy-start.5
  30.4 0.9 %fusion = (f32[2,8,128]{2,1,0:T(8,128)S(1)}, f32[2,5,128,128,8]{3,2,4,1,0:T(8,128)S(1)}) fusion(pred[128,5,128]{0,2,1:T(8,128)(4,1)S(1)} %compare_and_fusion, bf16[128,2,8,128,1]{3,2,1,0,4:T(8,128)(2,1)S(1)} %bitcast.132, bf16[5,2,128,128]{3,2,1,0:T(8,128)(2,1)S(1)} %get-tuple-element.26), kind=kOutput, calls=%fused_computation.2 | convolution fusion | flops 339474432 | bytes 6184960 | tf_op jit(solution)/shard_map/tkgd,bksd->kgtbs/dot_general | solution.py:111
  31.4 1.2 %fusion.4 = f32[2,8,128]{2,1,0:T(8,128)S(1)} fusion(f32[2,5,128,128,8]{3,2,4,1,0:T(8,128)S(1)} %get-tuple-element.31, f32[2,8,128]{2,1,0:T(8,128)S(1)} %get-tuple-element.30, pred[128,5,128]{0,2,1:T(8,128)(4,1)S(1)} %compare_and_fusion), kind=kLoop, calls=%fused_computation.6 | loop fusion | flops 6551552 | bytes 5341184 | tf_op jit(solution)/shard_map/reduce_sum | solution.py:116
  32.6 1.4 %divide_convert_fusion = bf16[128,2,8,128]{0,3,2,1:T(8,128)(2,1)S(1)} fusion(f32[2,5,128,128,8]{3,2,4,1,0:T(8,128)S(1)} %get-tuple-element.31, f32[2,8,128]{2,1,0:T(8,128)S(1)} %get-tuple-element.30, pred[128,5,128]{0,2,1:T(8,128)(4,1)S(1)} %compare_and_fusion, f32[128,2,8]{0,2,1:T(8,128)S(1)} %bitcast.146, bf16[5,2,128,128]{2,3,0,1:T(8,128)(2,1)S(1)} %copy-done.5), kind=kOutput, calls=%fused_computation.25 | convolution fusion | flops 342622208 | bytes 6193152 | tf_op jit(solution)/shard_map/kgtbs,bksd->tkgd/dot_general | solution.py:117
  34.0 8.5 %collective-permute-done.5 = bf16[2064,128]{1,0:T(8,128)(2,1)S(1)} collective-permute-done((bf16[2064,128]{1,0:T(8,128)(2,1)S(1)}, bf16[2064,128]{1,0:T(8,128)(2,1)S(1)}, u32[]{:S(2)}, u32[]{:S(2)}) %collective-permute-start.5) | collective-permute-done | bytes 528416 | tf_op jit(solution)/shard_map/ppermute | solution.py:105
  42.5 0.1 fusion.44
  42.7 2.8 %convolution_bitcast_fusion.1 = f32[128,16,128]{0,2,1:T(8,128)} fusion(bf16[128,16,128]{0,2,1:T(8,128)(2,1)S(1)} %bitcast.134, f32[16,128]{1,0:T(8,128)S(1)} %reduce_window_sum.20, pred[128,128]{1,0:T(8,128)(4,1)S(1)} %fusion.44, bf16[128,2048]{1,0:T(8,128)(2,1)} %param.13, bf16[128,2048]{1,0:T(8,128)(2,1)S(1)} %copy-done), kind=kOutput, calls=%fused_computation.14 | convolution fusion | flops 135528448 | bytes 2646016 | tf_op jit(solution)/shard_map/hts,shd->thd/dot_general | solution.py:46
  45.4 0.1 slice.53
  45.5 0.1 broadcast_select_fusion
  45.6 0.0 copy-start.6
  45.7 1.2 %slice_select_fusion = bf16[2048,128]{1,0:T(8,128)(2,1)S(1)} fusion(bf16[2064,128]{1,0:T(8,128)(2,1)} %collective-permute-done.6, bf16[2064,128]{1,0:T(8,128)(2,1)S(1)} %collective-permute-done.5, pred[]{:T(512)S(6)} %eq.59), kind=kLoop, calls=%fused_computation.38 | loop fusion | flops 262144 | bytes 1572865 | tf_op jit(solution)/shard_map/jit(_where)/select_n | solution.py:128
  46.9 0.7 %multiply_reduce_fusion = (f32[128]{0:T(128)S(1)}, f32[128,16,128]{0,2,1:T(8,128)S(1)}) fusion(f32[128,16,128]{0,2,1:T(8,128)S(1)} %copy-done.3, f32[128,16]{0,1:T(8,128)S(1)} %get-tuple-element.27, f32[16,128,128]{2,1,0:T(8,128)S(1)} %bitcast.129, bf16[16,128,128]{2,1,0:T(8,128)(2,1)S(1)} %bitcast.131, bf16[16,128,128]{2,1,0:T(8,128)(2,1)S(1)} %bitcast.130, ...), kind=kOutput, calls=%fused_computation.23 | convolution fusion | flops 70254464 | bytes 4727425 | tf_op jit(solution)/shard_map/thd,hde->the/dot_general | solution.py:142
  47.7 1.6 %collective-permute-start.7 = (f32[128]{0:T(128)S(1)}, f32[128]{0:T(128)S(1)}, u32[]{:S(2)}, u32[]{:S(2)}) collective-permute-start(f32[128]{0:T(128)S(1)} %get-tuple-element.32), channel_id=1, source_target_pairs={{0,1},{1,0},{2,3},{3,2},{4,5},{5,4},{6,7},{7,6},{8,9},{9,8},{10,11... | collective-permute-start | bytes 1544 | tf_op jit(solution)/shard_map/ppermute | solution.py:28
  49.3 2.0 %collective-permute-done.7 = f32[128]{0:T(128)S(1)} collective-permute-done((f32[128]{0:T(128)S(1)}, f32[128]{0:T(128)S(1)}, u32[]{:S(2)}, u32[]{:S(2)}) %collective-permute-start.7) | collective-permute-done | bytes 544 | tf_op jit(solution)/shard_map/ppermute | solution.py:28
  51.3 2.6 %collective-permute-start.8 = (f32[128]{0:T(128)S(1)}, f32[128]{0:T(128)S(1)}, u32[]{:S(2)}, u32[]{:S(2)}) collective-permute-start(f32[128]{0:T(128)S(1)} %add.99), channel_id=1, source_target_pairs={{0,2},{1,3},{2,0},{3,1},{4,6},{5,7},{6,4},{7,5},{8,10},{9,11},{10,... | collective-permute-start | bytes 1544 | tf_op jit(solution)/shard_map/ppermute | solution.py:28
  53.9 1.0 %copy.64 = bf16[128,2048]{1,0:T(8,128)(2,1)} copy(bf16[128,2048]{0,1:T(8,128)(2,1)S(1)} %bitcast.138) | data formatting | bytes 1048576
  54.9 0.3 copy.63
  55.2 0.5 collective-permute-done.8
  55.8 1.1 %multiply_convert_fusion = bf16[128,2048]{1,0:T(8,128)(2,1)} fusion(bf16[128,2048]{1,0:T(8,128)(2,1)S(1)} %copy-done.4, f32[128,2048]{1,0:T(8,128)S(1)} %copy.63, f32[2048]{0:T(1024)S(1)} %copy-done.6, f32[128]{0:T(128)S(1)} %add_rsqrt_fusion), kind=kLoop, calls=%fused_computation.22 | loop fusion | flops 2097152 | bytes 2105856 | tf_op jit(solution)/shard_map/convert_element_type | solution.py:157
  (34 shorter events, 0.3 us)
Async XLA Ops:
  0.6 42.0 %copy-start = (bf16[128,2048]{1,0:T(8,128)(2,1)S(1)}, bf16[128,2048]{1,0:T(8,128)(2,1)}, u32[]{:S(2)}) copy-start(bf16[128,2048]{1,0:T(8,128)(2,1)} %param.11) | copy-start | bytes 1572868
  2.8 22.7 %collective-permute-start.1 = (bf16[512,128]{1,0:T(8,128)(2,1)S(1)}, bf16[512,128]{1,0:T(8,128)(2,1)S(1)}, u32[]{:S(2)}, u32[]{:S(2)}) collective-permute-start(bf16[512,128]{1,0:T(8,128)(2,1)S(1)} %bitcast.139), channel_id=1, source_target_pairs={{0,16},{4,20},{8,24},{12,28},{1,17},{5,21},{9,25},{13,29},{2,18},{... | collective-permute-start | bytes 393224 | tf_op jit(solution)/shard_map/ppermute | solution.py:13
  7.7 17.8 %collective-permute-start.2 = (bf16[512,128]{1,0:T(8,128)(2,1)S(1)}, bf16[512,128]{1,0:T(8,128)(2,1)S(1)}, u32[]{:S(2)}, u32[]{:S(2)}) collective-permute-start(bf16[512,128]{1,0:T(8,128)(2,1)S(1)} %bitcast.140), channel_id=1, source_target_pairs={{0,12},{4,16},{8,20},{12,24},{16,28},{1,13},{5,17},{9,21},{13,25},... | collective-permute-start | bytes 393224 | tf_op jit(solution)/shard_map/ppermute | solution.py:13
  10.2 15.3 %collective-permute-start.3 = (bf16[512,128]{1,0:T(8,128)(2,1)S(1)}, bf16[512,128]{1,0:T(8,128)(2,1)S(1)}, u32[]{:S(2)}, u32[]{:S(2)}) collective-permute-start(bf16[512,128]{1,0:T(8,128)(2,1)S(1)} %bitcast.141), channel_id=1, source_target_pairs={{0,8},{4,12},{8,16},{12,20},{16,24},{20,28},{1,9},{5,13},{9,17},{1... | collective-permute-start | bytes 393224 | tf_op jit(solution)/shard_map/ppermute | solution.py:13
  12.4 13.2 %collective-permute-start.4 = (bf16[512,128]{1,0:T(8,128)(2,1)S(1)}, bf16[512,128]{1,0:T(8,128)(2,1)S(1)}, u32[]{:S(2)}, u32[]{:S(2)}) collective-permute-start(bf16[512,128]{1,0:T(8,128)(2,1)S(1)} %bitcast.142), channel_id=1, source_target_pairs={{0,4},{4,8},{8,12},{12,16},{16,20},{20,24},{24,28},{1,5},{5,9},{9,... | collective-permute-start | bytes 393224 | tf_op jit(solution)/shard_map/ppermute | solution.py:13
  20.3 2.6 %copy-start.1 = (bf16[128,2048]{0,1:T(8,128)(2,1)}, bf16[128,2048]{0,1:T(8,128)(2,1)S(1)}, u32[]{:S(2)}) copy-start(bf16[128,2048]{0,1:T(8,128)(2,1)S(1)} %copy.76) | copy-start | bytes 1572868
  24.0 3.6 %collective-permute-start = (f32[2056,128]{1,0:T(8,128)}, f32[2056,128]{1,0:T(8,128)S(1)}, u32[]{:S(2)}, u32[]{:S(2)}) collective-permute-start(f32[2056,128]{1,0:T(8,128)} %select_maximum_fusion), channel_id=1, source_target_pairs={{0,4},{4,0},{8,12},{12,8},{16,20},{20,16},{24,28},{28,24},{1,5},{5... | collective-permute-start | bytes 3158024 | tf_op jit(solution)/shard_map/ppermute | solution.py:86
  29.1 13.4 %collective-permute-start.5 = (bf16[2064,128]{1,0:T(8,128)(2,1)S(1)}, bf16[2064,128]{1,0:T(8,128)(2,1)S(1)}, u32[]{:S(2)}, u32[]{:S(2)}) collective-permute-start(bf16[2064,128]{1,0:T(8,128)(2,1)S(1)} %pad_maximum_fusion), channel_id=1, source_target_pairs={{4,8},{12,16},{20,24},{0,20},{8,28},{5,9},{13,17},{21,25},{1,21},{... | collective-permute-start | bytes 1585160 | tf_op jit(solution)/shard_map/ppermute | solution.py:105
  30.4 2.2 %copy-start.5 = (bf16[5,2,128,128]{2,3,0,1:T(8,128)(2,1)S(1)}, bf16[5,2,128,128]{2,3,0,1:T(8,128)(2,1)}, u32[]{:S(2)}) copy-start(bf16[5,2,128,128]{2,3,0,1:T(8,128)(2,1)} %copy.74) | copy-start | bytes 983044
  32.6 10.0 %copy-start.2 = (bf16[128,2048]{0,1:T(8,128)(2,1)S(1)}, bf16[128,2048]{0,1:T(8,128)(2,1)}, u32[]{:S(2)}) copy-start(bf16[128,2048]{0,1:T(8,128)(2,1)} %copy-done.1) | copy-start | bytes 1572868
  42.5 3.0 %collective-permute-start.6 = (bf16[2064,128]{1,0:T(8,128)(2,1)S(1)}, bf16[2064,128]{1,0:T(8,128)(2,1)}, u32[]{:S(2)}, u32[]{:S(2)}) collective-permute-start(bf16[2064,128]{1,0:T(8,128)(2,1)S(1)} %collective-permute-done.5), channel_id=1, source_target_pairs={{0,4},{4,0},{8,12},{12,8},{16,20},{20,16},{24,28},{28,24},{1,5},{5... | collective-permute-start | bytes 1585160 | tf_op jit(solution)/shard_map/ppermute | solution.py:126
  45.4 1.5 %copy-start.3 = (f32[128,16,128]{0,2,1:T(8,128)S(1)}, f32[128,16,128]{0,2,1:T(8,128)}, u32[]{:S(2)}) copy-start(f32[128,16,128]{0,2,1:T(8,128)} %convolution_bitcast_fusion.1) | copy-start | bytes 3145732
  45.6 10.1 %copy-start.4 = (bf16[128,2048]{1,0:T(8,128)(2,1)S(1)}, bf16[128,2048]{1,0:T(8,128)(2,1)}, u32[]{:S(2)}) copy-start(bf16[128,2048]{1,0:T(8,128)(2,1)} %param.15) | copy-start | bytes 1572868
  45.6 10.1 %copy-start.6 = (f32[2048]{0:T(1024)S(1)}, f32[2048]{0:T(1024)}, u32[]{:S(2)}) copy-start(f32[2048]{0:T(1024)} %param.16) | copy-start | bytes 24580
  47.7 3.6 %collective-permute-start.7 = (f32[128]{0:T(128)S(1)}, f32[128]{0:T(128)S(1)}, u32[]{:S(2)}, u32[]{:S(2)}) collective-permute-start(f32[128]{0:T(128)S(1)} %get-tuple-element.32), channel_id=1, source_target_pairs={{0,1},{1,0},{2,3},{3,2},{4,5},{5,4},{6,7},{7,6},{8,9},{9,8},{10,11... | collective-permute-start | bytes 1544 | tf_op jit(solution)/shard_map/ppermute | solution.py:28
  51.3 4.5 %collective-permute-start.8 = (f32[128]{0:T(128)S(1)}, f32[128]{0:T(128)S(1)}, u32[]{:S(2)}, u32[]{:S(2)}) collective-permute-start(f32[128]{0:T(128)S(1)} %add.99), channel_id=1, source_target_pairs={{0,2},{1,3},{2,0},{3,1},{4,6},{5,7},{6,4},{7,5},{8,10},{9,11},{10,... | collective-permute-start | bytes 1544 | tf_op jit(solution)/shard_map/ppermute | solution.py:28

commit v15 on v14

--- a/solution.py
+++ b/solution.py
@@ -70,18 +70,14 @@
     )
     count = lax.axis_size("ctx")
     odd = (shard % 2) == 1
-    pair = jnp.concatenate(
-        [soft_k.reshape(rows, kv_here, DH).transpose(1, 0, 2),
-         soft_v.reshape(rows, kv_here, DH).transpose(1, 0, 2)],
-        axis=0,
-    ).reshape(-1, DH)
-    n_pair = pair.shape[0]
+    pair = jnp.concatenate([soft_k, soft_v], axis=1)
+    kv_width = soft_k.shape[1]
     n_state = heads_here * DH
     state_rows = state.reshape(n_state, DH)
     factor_rows = jnp.pad(shrinkage_multiplier[None, :], ((0, 7), (0, DH - heads_here)))
     window = jnp.concatenate(
         [from_behind(pair, "ctx", step) for step in range(SPAN, 0, -1)] + [pair], axis=0
-    ).reshape(SPAN + 1, 2 * kv_here, rows, DH)
+    )
     first = jnp.concatenate([state_rows, factor_rows], axis=0)
     got = lax.ppermute(first, "ctx", [(i, i ^ 1) for i in range(count)])
     state_mate = got[:n_state]
@@ -108,17 +104,16 @@
     key_docs = jnp.where(key_pos >= 0, document_of(key_pos, doc_lengths), -1)
     allowed = (key_docs[None, :] == docs[:, None]) & (key_pos[None, :] <= positions[:, None])
     soft_query = soft_q.reshape(rows, kv_here, group, DH)
+    all_keys = window[:, :kv_width].reshape(span_rows, kv_here, DH)
+    all_values = window[:, kv_width:].reshape(span_rows, kv_here, DH)
     scores = jnp.einsum(
-        "tkgd,bksd->kgtbs", soft_query, window[:, :kv_here], preferred_element_type=jnp.float32
-    ).reshape(kv_here, group, rows, span_rows) * DH ** (-0.5)
+        "tkgd,skd->kgts", soft_query, all_keys, preferred_element_type=jnp.float32
+    ) * DH ** (-0.5)
     top = jnp.max(jnp.where(allowed, scores, -1e30), axis=-1, keepdims=True)
     expd = jnp.where(allowed, jnp.exp(jnp.minimum(scores - top, 0.0)), 0.0)
     total = jnp.sum(expd, axis=-1)
     attended = jnp.einsum(
-        "kgtbs,bksd->tkgd",
-        expd.astype(jnp.bfloat16).reshape(kv_here, group, rows, SPAN + 1, rows),
-        window[:, kv_here:],
-        preferred_element_type=jnp.float32,
+        "kgts,skd->tkgd", expd.astype(jnp.bfloat16), all_values, preferred_element_type=jnp.float32
     )
     attended = attended / total.transpose(2, 0, 1)[..., None]
     soft_out = attended.reshape(rows, kv_here * group * DH).astype(jnp.bfloat16)

time: 57.4 us -> 57.1 us (level)
  waiting for transfers between devices: 12 us -> 6.51 us
  matrix products: 7.18 us -> 12.4 us
    sub x0 -> x1, matrix products: none -> 5.37 us  [local(): expd = jnp.where(allowed, jnp.exp(jnp.minimum(scores - top, 0.0)), 0.0)]
    ppermute x1, waiting for transfers between devices: 8.5 us -> 3.84 us  [local(): received = lax.ppermute(packet, 'ctx', routes)]
    reduce_sum x1 -> x0, other arithmetic: 1.25 us -> none  [local(): total = jnp.sum(expd, axis=-1)]
    dot_general x1, matrix products: 2.77 us -> 1.72 us  [block_terms(): jnp.einsum('hts,shd->thd', weights, values, preferred_element_type=jnp.fl...]
    dot_general x2 -> x1, matrix products: 2.32 us -> 3.21 us  [local(): jnp.einsum('kgts,skd->tkgd', expd.astype(jnp.bfloat16), all_values, prefe...]
    concatenate x1, other arithmetic: 0.04 us -> 0.85 us  [local(): jnp.concatenate([chip_state.astype(jnp.bfloat16).reshape(n_state, DH), ch...]
    unnamed x23 -> x26, local copies, waits for them, and re-layouts: 5.14 us -> 4.37 us
    slice x1, local copies, waits for them, and re-layouts: 0.04 us -> 0.78 us  [local(): all_keys = window[:, :kv_width].reshape(span_rows, kv_here, DH)]
  transfers between devices with their start and end apart: 9 -> 9, of which waited for: 4 -> 4; matrix products, arithmetic and copies ran while one was open for 31% -> 41% of each run, Pallas kernels for 0% -> 0%
where the time goes in v15:
time: 57.1 us; the launch traced here: 56.5 us
  starting transfers between devices  18.1 us (32%)
  matrix products  12.4 us (22%)
  other arithmetic  9.25 us (16%)
  local copies, waits for them, and re-layouts  8 us (14%)
  waiting for transfers between devices  6.51 us (11%)
  between operations  2.32 us (4%)
    ppermute x4, starting transfers between devices, from_behind(): return lax.ppermute(shard, axis, pairs)  11.4 us
    sub x1, matrix products, local(): expd = jnp.where(allowed, jnp.exp(jnp.minimum(scores - top, 0.0)), 0.0)  5.37 us
    unnamed x26, local copies, waits for them, and re-layouts  4.37 us
    ppermute x2, starting transfers between devices, all_sum(): x = x + lax.ppermute(x, axis, [(i, i ^ bit) for i in range(count)])  4.23 us
    ppermute x1, waiting for transfers between devices, local(): received = lax.ppermute(packet, 'ctx', routes)  3.84 us
    dot_general x1, matrix products, local(): jnp.einsum('kgts,skd->tkgd', expd.astype(jnp.bfloat16), all_values, prefe...  3.21 us
    ppermute x2, waiting for transfers between devices, all_sum(): x = x + lax.ppermute(x, axis, [(i, i ^ bit) for i in range(count)])  1.97 us
    dot_general x1, matrix products, block_terms(): jnp.einsum('hts,shd->thd', weights, values, preferred_element_type=jnp.fl...  1.72 us
  transfers between devices with their start and end apart: 9, of which 4 were waited for; matrix products, arithmetic and copies ran while one was open for 41% of the time, Pallas kernels for 0%

profile of v15, /device:TPU:0, one launch (start us, length us, event | category | flops | bytes accessed | tf_op | source)
XLA Modules:
  0.0 56.5 jit_solution(11936764152633713547)
XLA Ops:
  0.6 0.0 copy-start
  0.6 1.0 %copy.39 = bf16[128,256]{0,1:T(8,128)(2,1)S(1)} copy(bf16[128,256]{1,0:T(8,128)(2,1)} %param.18) | data formatting | bytes 131072 | tf_op args[8]
  1.7 1.0 %copy.40 = bf16[128,256]{0,1:T(8,128)(2,1)S(1)} copy(bf16[128,256]{1,0:T(8,128)(2,1)} %param.19) | data formatting | bytes 131072 | tf_op args[9]
  2.6 4.9 %collective-permute-start.1 = (bf16[128,512]{0,1:T(8,128)(2,1)S(1)}, bf16[128,512]{0,1:T(8,128)(2,1)S(1)}, u32[]{:S(2)}, u32[]{:S(2)}) collective-permute-start(bf16[128,512]{0,1:T(8,128)(2,1)S(1)} %pad_maximum_fusion.1), channel_id=1, source_target_pairs={{0,16},{4,20},{8,24},{12,28},{1,17},{5,21},{9,25},{13,29},{2,18},{... | collective-permute-start | bytes 393224 | tf_op jit(solution)/shard_map/ppermute | solution.py:13
  7.5 2.6 %collective-permute-start.2 = (bf16[128,512]{0,1:T(8,128)(2,1)S(1)}, bf16[128,512]{0,1:T(8,128)(2,1)S(1)}, u32[]{:S(2)}, u32[]{:S(2)}) collective-permute-start(bf16[128,512]{0,1:T(8,128)(2,1)S(1)} %pad_maximum_fusion.1), channel_id=1, source_target_pairs={{0,12},{4,16},{8,20},{12,24},{16,28},{1,13},{5,17},{9,21},{13,25},... | collective-permute-start | bytes 393224 | tf_op jit(solution)/shard_map/ppermute | solution.py:13
  10.1 2.1 %collective-permute-start.3 = (bf16[128,512]{0,1:T(8,128)(2,1)S(1)}, bf16[128,512]{0,1:T(8,128)(2,1)S(1)}, u32[]{:S(2)}, u32[]{:S(2)}) collective-permute-start(bf16[128,512]{0,1:T(8,128)(2,1)S(1)} %pad_maximum_fusion.1), channel_id=1, source_target_pairs={{0,8},{4,12},{8,16},{12,20},{16,24},{20,28},{1,9},{5,13},{9,17},{1... | collective-permute-start | bytes 393224 | tf_op jit(solution)/shard_map/ppermute | solution.py:13
  12.2 1.8 %collective-permute-start.4 = (bf16[128,512]{0,1:T(8,128)(2,1)S(1)}, bf16[128,512]{0,1:T(8,128)(2,1)S(1)}, u32[]{:S(2)}, u32[]{:S(2)}) collective-permute-start(bf16[128,512]{0,1:T(8,128)(2,1)S(1)} %pad_maximum_fusion.1), channel_id=1, source_target_pairs={{0,4},{4,8},{8,12},{12,16},{16,20},{20,24},{24,28},{1,5},{5,9},{9,... | collective-permute-start | bytes 393224 | tf_op jit(solution)/shard_map/ppermute | solution.py:13
  14.1 0.8 %reduce-window.4 = s32[6,1]{0,1:T(1,128)S(1)} reduce-window(s32[6,1]{0,1:T(1,128)} %bitcast.125, s32[]{:T(128)} %constant.21.clone.1), window={size=6x1 pad=5_0x0_0}, to_apply=%region_0.0 | reduce-window | flops 30 | bytes 52 | tf_op jit(solution)/shard_map/reduce-window
  15.0 0.6 %fusion.63 = s32[]{:T(128)} fusion(s32[6,1]{0,1:T(1,128)S(1)} %reduce-window.4, s32[]{:T(128)} %bitcast.6), kind=kLoop, calls=%fused_computation.86 | loop fusion | flops 17 | bytes 32 | tf_op jit(solution)/shard_map/reduce_sum | solution.py:35
  15.6 0.1 convert_reduce_fusion.1
  15.7 0.6 %slice.38 = s32[1]{0:T(128)} slice(s32[128]{0:T(128)S(1)} %convert_reduce_fusion.1), slice={[127:128]} | slice | bytes 8 | tf_op jit(solution)/shard_map/slice | solution.py:48
  16.9 0.7 %fusion.70 = (f32[128]{0:T(128)S(1)}, pred[128]{0:T(512)(128)(4,1)S(1)}, f32[128]{0:T(128)S(1)}) fusion(s32[128]{0:T(128)S(1)} %convert_reduce_fusion.1, s32[]{:T(128)S(6)} %select_n.57, s32[]{:T(128)} %bitcast.3), kind=kLoop, calls=%fused_computation.102 | loop fusion | flops 512 | bytes 1672 | tf_op jit(solution)/shard_map/convert_element_type | solution.py:140
  17.6 0.6 %slice.40 = pred[1]{0:T(512)(128)(4,1)} slice(pred[128]{0:T(512)(128)(4,1)S(1)} %get-tuple-element.19), slice={[127:128]} | slice | bytes 2 | tf_op jit(solution)/shard_map/slice | solution.py:52
  18.8 1.3 %copy.54 = bf16[128,2048]{0,1:T(8,128)(2,1)S(1)} copy(bf16[128,2048]{1,0:T(8,128)(2,1)} %param.12) | data formatting | bytes 1048576 | tf_op jit(solution)/shard_map/reshape | solution.py:66
  20.1 0.0 copy-start.2
  20.1 1.0 %reduce_window_sum.20 = f32[16,128]{1,0:T(8,128)S(1)} reduce-window(f32[16,128]{1,0:T(8,128)} %param.14, f32[]{:T(128)} %constant.47.clone.1), window={size=1x128 pad=0_0x127_0}, to_apply=%region_2.3 | reduce-window | flops 260096 | bytes 16388 | tf_op jit(solution)/shard_map/jit(cumsum)/reduce_window_sum | solution.py:40
  21.1 0.2 slice_reduce_fusion
  21.3 0.1 multiply_bitcast_fusion
  21.4 1.4 %fusion.30 = f32[16,128,128]{2,1,0:T(8,128)S(1)} fusion(bf16[128,16,128]{0,2,1:T(8,128)(2,1)S(1)} %bitcast.113, f32[128,16]{0,1:T(8,128)S(1)} %get-tuple-element.26, bf16[128,2048]{1,0:T(8,128)(2,1)} %param.13), kind=kOutput, calls=%fused_computation.38 | convolution fusion | flops 67895296 | bytes 2105344 | tf_op jit(solution)/shard_map/shd,she->hde/dot_general | solution.py:51
  22.8 1.1 %select_maximum_fusion = f32[2056,128]{1,0:T(8,128)} fusion(f32[1,16]{1,0:T(1,128)S(1)} %bitcast.121, f32[2048,128]{1,0:T(8,128)S(1)} %bitcast.108), kind=kLoop, calls=%fused_computation.23 | loop fusion | flops 789504 | bytes 2101312 | tf_op jit(solution)/shard_map/concatenate | solution.py:81
  23.8 1.1 %collective-permute-start = (f32[2056,128]{1,0:T(8,128)}, f32[2056,128]{1,0:T(8,128)S(1)}, u32[]{:S(2)}, u32[]{:S(2)}) collective-permute-start(f32[2056,128]{1,0:T(8,128)} %select_maximum_fusion), channel_id=1, source_target_pairs={{0,4},{4,0},{8,12},{12,8},{16,20},{20,16},{24,28},{28,24},{1,5},{5... | collective-permute-start | bytes 3158024 | tf_op jit(solution)/shard_map/ppermute | solution.py:82
  24.9 0.1 convert_reduce_fusion
  25.0 0.9 %compare_and_fusion = pred[128,640]{0,1:T(8,128)(4,1)} fusion(s32[128]{0:T(128)S(1)} %iota_add_fusion.1, s32[128]{0:T(128)S(1)} %convert_reduce_fusion.1, s32[640]{0:T(1024)S(1)} %iota_add_fusion, s32[640]{0:T(1024)S(1)} %compare_select_fusion), kind=kLoop, calls=%fused_computation.59 | loop fusion | flops 245760 | bytes 88064 | tf_op jit(solution)/shard_map/and | solution.py:105
  25.9 0.0 collective-permute-done.1
  26.1 0.0 copy-start.6
  26.2 0.8 %fusion.71 = (bf16[640,256]{0,1:T(8,128)(2,1)}, bf16[640,256]{0,1:T(8,128)(2,1)S(1)}) fusion(bf16[640,512]{0,1:T(8,128)(2,1)S(1)} %constant_dynamic-update-slice_fusion), kind=kLoop, calls=%fused_computation.103 | loop fusion | bytes 1310720 | tf_op jit(solution)/shard_map/slice | solution.py:107
  26.9 0.5 collective-permute-done
  27.5 0.3 select_convert_fusion.1
  27.8 0.8 %pad_maximum_fusion = bf16[2064,128]{1,0:T(8,128)(2,1)} fusion(bf16[16,128]{1,0:T(8,128)(2,1)S(1)} %fusion.62, bf16[2048,128]{1,0:T(8,128)(2,1)S(1)} %bitcast.115), kind=kLoop, calls=%fused_computation.36 | loop fusion | flops 1056768 | bytes 1056768 | tf_op jit(solution)/shard_map/concatenate | solution.py:96
  28.6 0.1 copy.57
  28.7 1.3 %collective-permute-start.5 = (bf16[2064,128]{1,0:T(8,128)(2,1)}, bf16[2064,128]{1,0:T(8,128)(2,1)S(1)}, u32[]{:S(2)}, u32[]{:S(2)}) collective-permute-start(bf16[2064,128]{1,0:T(8,128)(2,1)} %pad_maximum_fusion), channel_id=1, source_target_pairs={{4,8},{12,16},{20,24},{0,20},{8,28},{5,9},{13,17},{21,25},{1,21},{... | collective-permute-start | bytes 1585160 | tf_op jit(solution)/shard_map/ppermute | solution.py:101
  30.1 5.4 %fusion.72 = (f32[2,8,128]{2,1,0:T(8,128)S(1)}, bf16[2,8,128,640]{2,3,1,0:T(8,128)(2,1)}) fusion(pred[128,640]{0,1:T(8,128)(4,1)} %compare_and_fusion, bf16[640,2,128,1]{0,2,3,1:T(8,128)(2,1)} %bitcast.120, bf16[128,2,8,128]{3,2,1,0:T(8,128)(2,1)S(1)} %bitcast.118), kind=kOutput, calls=%fused_computation.104 | convolution fusion | flops 681575040 | bytes 3563520 | tf_op jit(solution)/shard_map/sub | solution.py:113
  35.4 3.2 %fusion.20 = bf16[128,2,8,128]{0,3,2,1:T(8,128)(2,1)} fusion(bf16[640,2,128,1]{0,2,3,1:T(8,128)(2,1)S(1)} %bitcast.119, bf16[2,8,128,640]{2,3,1,0:T(8,128)(2,1)} %get-tuple-element.29, f32[128,2,8]{0,2,1:T(8,128)S(1)} %bitcast.126), kind=kOutput, calls=%fused_computation.21 | convolution fusion | flops 336068608 | bytes 3481600 | tf_op jit(solution)/shard_map/kgts,skd->tkgd/dot_general | solution.py:115
  38.6 3.8 %collective-permute-done.5 = bf16[2064,128]{1,0:T(8,128)(2,1)S(1)} collective-permute-done((bf16[2064,128]{1,0:T(8,128)(2,1)}, bf16[2064,128]{1,0:T(8,128)(2,1)S(1)}, u32[]{:S(2)}, u32[]{:S(2)}) %collective-permute-start.5) | collective-permute-done | bytes 528416 | tf_op jit(solution)/shard_map/ppermute | solution.py:101
  42.5 0.1 fusion.56
  42.6 1.7 %convolution_bitcast_fusion.1 = f32[128,16,128]{0,2,1:T(8,128)} fusion(bf16[128,16,128]{0,2,1:T(8,128)(2,1)S(1)} %bitcast.114, f32[16,128]{1,0:T(8,128)S(1)} %reduce_window_sum.20, pred[128,128]{1,0:T(8,128)(4,1)S(1)} %fusion.56, bf16[128,2048]{1,0:T(8,128)(2,1)S(1)} %copy-done.7, bf16[128,2048]{1,0:T(8,128)(2,1)S(1)} %copy-done), kind=kOutput, calls=%fused_computation.16 | convolution fusion | flops 135528448 | bytes 2646016 | tf_op jit(solution)/shard_map/hts,shd->thd/dot_general | solution.py:46
  44.3 0.2 collective-permute-done.6
  44.5 0.1 broadcast_select_fusion
  44.7 1.3 %slice_select_fusion = bf16[2048,128]{1,0:T(8,128)(2,1)S(1)} fusion(bf16[2064,128]{1,0:T(8,128)(2,1)} %collective-permute-done.6, bf16[2064,128]{1,0:T(8,128)(2,1)S(1)} %collective-permute-done.5, pred[]{:T(512)S(6)} %eq.58), kind=kLoop, calls=%fused_computation.43 | loop fusion | flops 262144 | bytes 1572865 | tf_op jit(solution)/shard_map/jit(_where)/select_n | solution.py:123
  46.0 0.1 copy-done.4
  46.0 0.7 %multiply_reduce_fusion = (f32[128]{0:T(128)S(1)}, f32[128,16,128]{0,2,1:T(8,128)S(1)}) fusion(f32[128,16,128]{0,2,1:T(8,128)S(1)} %copy-done.4, f32[128,16]{0,1:T(8,128)S(1)} %get-tuple-element.25, f32[16,128,128]{2,1,0:T(8,128)S(1)} %bitcast.110, bf16[16,128,128]{2,1,0:T(8,128)(2,1)S(1)} %bitcast.112, bf16[16,128,128]{2,1,0:T(8,128)(2,1)S(1)} %bitcast.111, ...), kind=kOutput, calls=%fused_computation.28 | convolution fusion | flops 70254464 | bytes 4727425 | tf_op jit(solution)/shard_map/thd,hde->the/dot_general | solution.py:137
  46.8 0.0 copy-start.8
  46.8 1.6 %collective-permute-start.7 = (f32[128]{0:T(128)S(1)}, f32[128]{0:T(128)S(1)}, u32[]{:S(2)}, u32[]{:S(2)}) collective-permute-start(f32[128]{0:T(128)S(1)} %get-tuple-element.30), channel_id=1, source_target_pairs={{0,1},{1,0},{2,3},{3,2},{4,5},{5,4},{6,7},{7,6},{8,9},{9,8},{10,11... | collective-permute-start | bytes 1544 | tf_op jit(solution)/shard_map/ppermute | solution.py:28
  48.4 2.0 %collective-permute-done.7 = f32[128]{0:T(128)S(1)} collective-permute-done((f32[128]{0:T(128)S(1)}, f32[128]{0:T(128)S(1)}, u32[]{:S(2)}, u32[]{:S(2)}) %collective-permute-start.7) | collective-permute-done | bytes 544 | tf_op jit(solution)/shard_map/ppermute | solution.py:28
  50.4 2.6 %collective-permute-start.8 = (f32[128]{0:T(128)S(1)}, f32[128]{0:T(128)S(1)}, u32[]{:S(2)}, u32[]{:S(2)}) collective-permute-start(f32[128]{0:T(128)S(1)} %add.89), channel_id=1, source_target_pairs={{0,2},{1,3},{2,0},{3,1},{4,6},{5,7},{6,4},{7,5},{8,10},{9,11},{10,... | collective-permute-start | bytes 1544 | tf_op jit(solution)/shard_map/ppermute | solution.py:28
  53.0 2.0 %copy.47 = bf16[128,2048]{1,0:T(8,128)(2,1)} copy(bf16[128,2048]{0,1:T(8,128)(2,1)} %bitcast.117) | data formatting | bytes 1048576
  55.0 0.3 copy.46
  55.4 1.1 %multiply_convert_fusion = bf16[128,2048]{1,0:T(8,128)(2,1)} fusion(bf16[128,2048]{1,0:T(8,128)(2,1)S(1)} %copy-done.5, f32[128,2048]{1,0:T(8,128)S(1)} %copy.46, f32[2048]{0:T(1024)S(1)} %copy-done.8, f32[128]{0:T(128)S(1)} %add_rsqrt_fusion), kind=kLoop, calls=%fused_computation.27 | loop fusion | flops 2097152 | bytes 2105856 | tf_op jit(solution)/shard_map/convert_element_type | solution.py:152
  (36 shorter events, 0.3 us)
Async XLA Ops:
  0.6 42.0 %copy-start = (bf16[128,2048]{1,0:T(8,128)(2,1)S(1)}, bf16[128,2048]{1,0:T(8,128)(2,1)}, u32[]{:S(2)}) copy-start(bf16[128,2048]{1,0:T(8,128)(2,1)} %param.11) | copy-start | bytes 1572868
  2.6 23.3 %collective-permute-start.1 = (bf16[128,512]{0,1:T(8,128)(2,1)S(1)}, bf16[128,512]{0,1:T(8,128)(2,1)S(1)}, u32[]{:S(2)}, u32[]{:S(2)}) collective-permute-start(bf16[128,512]{0,1:T(8,128)(2,1)S(1)} %pad_maximum_fusion.1), channel_id=1, source_target_pairs={{0,16},{4,20},{8,24},{12,28},{1,17},{5,21},{9,25},{13,29},{2,18},{... | collective-permute-start | bytes 393224 | tf_op jit(solution)/shard_map/ppermute | solution.py:13
  7.5 18.4 %collective-permute-start.2 = (bf16[128,512]{0,1:T(8,128)(2,1)S(1)}, bf16[128,512]{0,1:T(8,128)(2,1)S(1)}, u32[]{:S(2)}, u32[]{:S(2)}) collective-permute-start(bf16[128,512]{0,1:T(8,128)(2,1)S(1)} %pad_maximum_fusion.1), channel_id=1, source_target_pairs={{0,12},{4,16},{8,20},{12,24},{16,28},{1,13},{5,17},{9,21},{13,25},... | collective-permute-start | bytes 393224 | tf_op jit(solution)/shard_map/ppermute | solution.py:13
  10.1 15.9 %collective-permute-start.3 = (bf16[128,512]{0,1:T(8,128)(2,1)S(1)}, bf16[128,512]{0,1:T(8,128)(2,1)S(1)}, u32[]{:S(2)}, u32[]{:S(2)}) collective-permute-start(bf16[128,512]{0,1:T(8,128)(2,1)S(1)} %pad_maximum_fusion.1), channel_id=1, source_target_pairs={{0,8},{4,12},{8,16},{12,20},{16,24},{20,28},{1,9},{5,13},{9,17},{1... | collective-permute-start | bytes 393224 | tf_op jit(solution)/shard_map/ppermute | solution.py:13
  12.2 13.8 %collective-permute-start.4 = (bf16[128,512]{0,1:T(8,128)(2,1)S(1)}, bf16[128,512]{0,1:T(8,128)(2,1)S(1)}, u32[]{:S(2)}, u32[]{:S(2)}) collective-permute-start(bf16[128,512]{0,1:T(8,128)(2,1)S(1)} %pad_maximum_fusion.1), channel_id=1, source_target_pairs={{0,4},{4,8},{8,12},{12,16},{16,20},{20,24},{24,28},{1,5},{5,9},{9,... | collective-permute-start | bytes 393224 | tf_op jit(solution)/shard_map/ppermute | solution.py:13
  20.1 2.6 %copy-start.2 = (bf16[128,2048]{0,1:T(8,128)(2,1)}, bf16[128,2048]{0,1:T(8,128)(2,1)S(1)}, u32[]{:S(2)}) copy-start(bf16[128,2048]{0,1:T(8,128)(2,1)S(1)} %copy.54) | copy-start | bytes 1572868
  23.8 3.6 %collective-permute-start = (f32[2056,128]{1,0:T(8,128)}, f32[2056,128]{1,0:T(8,128)S(1)}, u32[]{:S(2)}, u32[]{:S(2)}) collective-permute-start(f32[2056,128]{1,0:T(8,128)} %select_maximum_fusion), channel_id=1, source_target_pairs={{0,4},{4,0},{8,12},{12,8},{16,20},{20,16},{24,28},{28,24},{1,5},{5... | collective-permute-start | bytes 3158024 | tf_op jit(solution)/shard_map/ppermute | solution.py:82
  26.1 2.5 %copy-start.6 = (bf16[128,2048]{1,0:T(8,128)(2,1)S(1)}, bf16[128,2048]{1,0:T(8,128)(2,1)}, u32[]{:S(2)}) copy-start(bf16[128,2048]{1,0:T(8,128)(2,1)} %param.17) | copy-start | bytes 1572868
  27.4 16.9 %copy-start.1 = (f32[2056,128]{1,0:T(8,128)}, f32[2056,128]{1,0:T(8,128)S(1)}, u32[]{:S(2)}) copy-start(f32[2056,128]{1,0:T(8,128)S(1)} %collective-permute-done) | copy-start | bytes 3158020
  28.7 13.8 %collective-permute-start.5 = (bf16[2064,128]{1,0:T(8,128)(2,1)}, bf16[2064,128]{1,0:T(8,128)(2,1)S(1)}, u32[]{:S(2)}, u32[]{:S(2)}) collective-permute-start(bf16[2064,128]{1,0:T(8,128)(2,1)} %pad_maximum_fusion), channel_id=1, source_target_pairs={{4,8},{12,16},{20,24},{0,20},{8,28},{5,9},{13,17},{21,25},{1,21},{... | collective-permute-start | bytes 1585160 | tf_op jit(solution)/shard_map/ppermute | solution.py:101
  35.4 7.2 %copy-start.3 = (bf16[128,2048]{0,1:T(8,128)(2,1)S(1)}, bf16[128,2048]{0,1:T(8,128)(2,1)}, u32[]{:S(2)}) copy-start(bf16[128,2048]{0,1:T(8,128)(2,1)} %copy-done.2) | copy-start | bytes 1572868
  35.4 7.2 %copy-start.7 = (bf16[128,2048]{1,0:T(8,128)(2,1)S(1)}, bf16[128,2048]{1,0:T(8,128)(2,1)}, u32[]{:S(2)}) copy-start(bf16[128,2048]{1,0:T(8,128)(2,1)} %param.13) | copy-start | bytes 1572868
  42.5 2.0 %collective-permute-start.6 = (bf16[2064,128]{1,0:T(8,128)(2,1)S(1)}, bf16[2064,128]{1,0:T(8,128)(2,1)}, u32[]{:S(2)}, u32[]{:S(2)}) collective-permute-start(bf16[2064,128]{1,0:T(8,128)(2,1)S(1)} %collective-permute-done.5), channel_id=1, source_target_pairs={{0,4},{4,0},{8,12},{12,8},{16,20},{20,16},{24,28},{28,24},{1,5},{5... | collective-permute-start | bytes 1585160 | tf_op jit(solution)/shard_map/ppermute | solution.py:121
  44.3 1.6 %slice-start = ((f32[2056,128]{1,0:T(8,128)}), f32[2048,128]{1,0:T(8,128)S(1)}, s32[]{:S(2)}) async-start(f32[2056,128]{1,0:T(8,128)} %copy-done.1), calls=%async_computation | async-start | bytes 2097152 | tf_op jit(solution)/shard_map/slice | solution.py:83
  44.3 1.7 %copy-start.4 = (f32[128,16,128]{0,2,1:T(8,128)S(1)}, f32[128,16,128]{0,2,1:T(8,128)}, u32[]{:S(2)}) copy-start(f32[128,16,128]{0,2,1:T(8,128)} %convolution_bitcast_fusion.1) | copy-start | bytes 3145732
  46.8 8.6 %copy-start.5 = (bf16[128,2048]{1,0:T(8,128)(2,1)S(1)}, bf16[128,2048]{1,0:T(8,128)(2,1)}, u32[]{:S(2)}) copy-start(bf16[128,2048]{1,0:T(8,128)(2,1)} %param.15) | copy-start | bytes 1572868
  46.8 8.6 %copy-start.8 = (f32[2048]{0:T(1024)S(1)}, f32[2048]{0:T(1024)}, u32[]{:S(2)}) copy-start(f32[2048]{0:T(1024)} %param.16) | copy-start | bytes 24580
  46.8 3.6 %collective-permute-start.7 = (f32[128]{0:T(128)S(1)}, f32[128]{0:T(128)S(1)}, u32[]{:S(2)}, u32[]{:S(2)}) collective-permute-start(f32[128]{0:T(128)S(1)} %get-tuple-element.30), channel_id=1, source_target_pairs={{0,1},{1,0},{2,3},{3,2},{4,5},{5,4},{6,7},{7,6},{8,9},{9,8},{10,11... | collective-permute-start | bytes 1544 | tf_op jit(solution)/shard_map/ppermute | solution.py:28
  50.4 5.0 %collective-permute-start.8 = (f32[128]{0:T(128)S(1)}, f32[128]{0:T(128)S(1)}, u32[]{:S(2)}, u32[]{:S(2)}) collective-permute-start(f32[128]{0:T(128)S(1)} %add.89), channel_id=1, source_target_pairs={{0,2},{1,3},{2,0},{3,1},{4,6},{5,7},{6,4},{7,5},{8,10},{9,11},{10,... | collective-permute-start | bytes 1544 | tf_op jit(solution)/shard_map/ppermute | solution.py:28

commit v16 on v15

--- a/solution.py
+++ b/solution.py
@@ -15,19 +15,13 @@
 
 def all_sum(x, axis):
     count = lax.axis_size(axis)
-    if count & (count - 1):
-        me = lax.axis_index(axis)
-        parts = [x]
-        for by in range(1, count):
-            parts.append(lax.ppermute(x, axis, [(i, (i + by) % count) for i in range(count)]))
-        stacked = jnp.stack(parts)
-        order = (me - jnp.arange(count)) % count
-        return jnp.sum(stacked[order], axis=0)
-    bit = 1
-    while bit < count:
-        x = x + lax.ppermute(x, axis, [(i, i ^ bit) for i in range(count)])
-        bit *= 2
-    return x
+    me = lax.axis_index(axis)
+    parts = [x]
+    for by in range(1, count):
+        parts.append(lax.ppermute(x, axis, [(i, (i + by) % count) for i in range(count)]))
+    stacked = jnp.stack(parts)
+    order = (me - jnp.arange(count)) % count
+    return jnp.sum(stacked[order], axis=0)
 
 
 def document_of(positions, doc_lengths):

time: 57.1 us -> 57.1 us (level)
  waiting for transfers between devices: 6.51 us -> 4.55 us
  starting transfers between devices: 18.1 us -> 19.4 us
    ppermute x2 -> x3, waiting for transfers between devices: 1.97 us -> 0.01 us  [all_sum(): lax.ppermute(x, axis, [(i, (i + by) % count) for i in range(count)])]
    ppermute x2 -> x3, starting transfers between devices: 4.23 us -> 5.56 us  [all_sum(): lax.ppermute(x, axis, [(i, (i + by) % count) for i in range(count)])]
  transfers between devices with their start and end apart: 9 -> 10, of which waited for: 4 -> 3; matrix products, arithmetic and copies ran while one was open for 41% -> 41% of each run, Pallas kernels for 0% -> 0%
where the time goes in v16:
time: 57.1 us; the launch traced here: 56.5 us
  starting transfers between devices  19.4 us (34%)
  matrix products  12.4 us (22%)
  other arithmetic  9.3 us (16%)
  local copies, waits for them, and re-layouts  8.57 us (15%)
  waiting for transfers between devices  4.55 us (8%)
  between operations  2.33 us (4%)
    ppermute x4, starting transfers between devices, from_behind(): return lax.ppermute(shard, axis, pairs)  11.4 us
    ppermute x3, starting transfers between devices, all_sum(): lax.ppermute(x, axis, [(i, (i + by) % count) for i in range(count)])  5.56 us
    sub x1, matrix products, local(): expd = jnp.where(allowed, jnp.exp(jnp.minimum(scores - top, 0.0)), 0.0)  5.36 us
    unnamed x26, local copies, waits for them, and re-layouts  4.38 us
    ppermute x1, waiting for transfers between devices, local(): received = lax.ppermute(packet, 'ctx', routes)  3.85 us
    dot_general x1, matrix products, local(): jnp.einsum('kgts,skd->tkgd', expd.astype(jnp.bfloat16), all_values, prefe...  3.21 us
    dot_general x1, matrix products, block_terms(): jnp.einsum('hts,shd->thd', weights, values, preferred_element_type=jnp.fl...  1.72 us
    dot_general x1, matrix products, block_terms(): jnp.einsum('shd,she->hde', weighted, values, preferred_element_type=jnp.f...  1.35 us
  transfers between devices with their start and end apart: 10, of which 3 were waited for; matrix products, arithmetic and copies ran while one was open for 41% of the time, Pallas kernels for 0%

profile of v16, /device:TPU:0, one launch (start us, length us, event | category | flops | bytes accessed | tf_op | source)
XLA Modules:
  0.0 56.5 jit_solution(9125363898994227967)
XLA Ops:
  0.6 0.0 copy-start
  0.6 1.0 %copy.39 = bf16[128,256]{0,1:T(8,128)(2,1)S(1)} copy(bf16[128,256]{1,0:T(8,128)(2,1)} %param.18) | data formatting | bytes 131072 | tf_op args[8]
  1.7 1.0 %copy.40 = bf16[128,256]{0,1:T(8,128)(2,1)S(1)} copy(bf16[128,256]{1,0:T(8,128)(2,1)} %param.19) | data formatting | bytes 131072 | tf_op args[9]
  2.6 4.9 %collective-permute-start.1 = (bf16[128,512]{0,1:T(8,128)(2,1)S(1)}, bf16[128,512]{0,1:T(8,128)(2,1)S(1)}, u32[]{:S(2)}, u32[]{:S(2)}) collective-permute-start(bf16[128,512]{0,1:T(8,128)(2,1)S(1)} %pad_maximum_fusion.1), channel_id=1, source_target_pairs={{0,16},{4,20},{8,24},{12,28},{1,17},{5,21},{9,25},{13,29},{2,18},{... | collective-permute-start | bytes 393224 | tf_op jit(solution)/shard_map/ppermute | solution.py:13
  7.5 2.6 %collective-permute-start.2 = (bf16[128,512]{0,1:T(8,128)(2,1)S(1)}, bf16[128,512]{0,1:T(8,128)(2,1)S(1)}, u32[]{:S(2)}, u32[]{:S(2)}) collective-permute-start(bf16[128,512]{0,1:T(8,128)(2,1)S(1)} %pad_maximum_fusion.1), channel_id=1, source_target_pairs={{0,12},{4,16},{8,20},{12,24},{16,28},{1,13},{5,17},{9,21},{13,25},... | collective-permute-start | bytes 393224 | tf_op jit(solution)/shard_map/ppermute | solution.py:13
  10.1 2.1 %collective-permute-start.3 = (bf16[128,512]{0,1:T(8,128)(2,1)S(1)}, bf16[128,512]{0,1:T(8,128)(2,1)S(1)}, u32[]{:S(2)}, u32[]{:S(2)}) collective-permute-start(bf16[128,512]{0,1:T(8,128)(2,1)S(1)} %pad_maximum_fusion.1), channel_id=1, source_target_pairs={{0,8},{4,12},{8,16},{12,20},{16,24},{20,28},{1,9},{5,13},{9,17},{1... | collective-permute-start | bytes 393224 | tf_op jit(solution)/shard_map/ppermute | solution.py:13
  12.2 1.8 %collective-permute-start.4 = (bf16[128,512]{0,1:T(8,128)(2,1)S(1)}, bf16[128,512]{0,1:T(8,128)(2,1)S(1)}, u32[]{:S(2)}, u32[]{:S(2)}) collective-permute-start(bf16[128,512]{0,1:T(8,128)(2,1)S(1)} %pad_maximum_fusion.1), channel_id=1, source_target_pairs={{0,4},{4,8},{8,12},{12,16},{16,20},{20,24},{24,28},{1,5},{5,9},{9,... | collective-permute-start | bytes 393224 | tf_op jit(solution)/shard_map/ppermute | solution.py:13
  14.1 0.8 %reduce-window.4 = s32[6,1]{0,1:T(1,128)S(1)} reduce-window(s32[6,1]{0,1:T(1,128)} %bitcast.135, s32[]{:T(128)} %constant.33.clone.1), window={size=6x1 pad=5_0x0_0}, to_apply=%region_0.0 | reduce-window | flops 30 | bytes 52 | tf_op jit(solution)/shard_map/reduce-window
  15.0 0.6 %fusion.63 = s32[]{:T(128)} fusion(s32[6,1]{0,1:T(1,128)S(1)} %reduce-window.4, s32[]{:T(128)} %bitcast.6), kind=kLoop, calls=%fused_computation.93 | loop fusion | flops 17 | bytes 32 | tf_op jit(solution)/shard_map/reduce_sum | solution.py:29
  15.6 0.1 convert_reduce_fusion.1
  15.7 0.6 %slice.38 = s32[1]{0:T(128)} slice(s32[128]{0:T(128)S(1)} %convert_reduce_fusion.1), slice={[127:128]} | slice | bytes 8 | tf_op jit(solution)/shard_map/slice | solution.py:42
  16.9 0.7 %fusion.72 = (f32[128]{0:T(128)S(1)}, pred[128]{0:T(512)(128)(4,1)S(1)}, f32[128]{0:T(128)S(1)}) fusion(s32[128]{0:T(128)S(1)} %convert_reduce_fusion.1, s32[]{:T(128)S(6)} %select_n.80, s32[]{:T(128)} %bitcast.3), kind=kLoop, calls=%fused_computation.111 | loop fusion | flops 512 | bytes 1672 | tf_op jit(solution)/shard_map/convert_element_type | solution.py:134
  17.6 0.6 %slice.40 = pred[1]{0:T(512)(128)(4,1)} slice(pred[128]{0:T(512)(128)(4,1)S(1)} %get-tuple-element.19), slice={[127:128]} | slice | bytes 2 | tf_op jit(solution)/shard_map/slice | solution.py:46
  18.8 1.3 %copy.54 = bf16[128,2048]{0,1:T(8,128)(2,1)S(1)} copy(bf16[128,2048]{1,0:T(8,128)(2,1)} %param.12) | data formatting | bytes 1048576 | tf_op jit(solution)/shard_map/reshape | solution.py:60
  20.1 0.0 copy-start.2
  20.1 1.0 %reduce_window_sum.20 = f32[16,128]{1,0:T(8,128)S(1)} reduce-window(f32[16,128]{1,0:T(8,128)} %param.14, f32[]{:T(128)} %constant.63.clone.1), window={size=1x128 pad=0_0x127_0}, to_apply=%region_2.3 | reduce-window | flops 260096 | bytes 16388 | tf_op jit(solution)/shard_map/jit(cumsum)/reduce_window_sum | solution.py:34
  21.1 0.2 slice_reduce_fusion
  21.3 0.1 multiply_bitcast_fusion
  21.4 1.4 %fusion.30 = f32[16,128,128]{2,1,0:T(8,128)S(1)} fusion(bf16[128,16,128]{0,2,1:T(8,128)(2,1)S(1)} %bitcast.119, f32[128,16]{0,1:T(8,128)S(1)} %get-tuple-element.26, bf16[128,2048]{1,0:T(8,128)(2,1)} %param.13), kind=kOutput, calls=%fused_computation.39 | convolution fusion | flops 67895296 | bytes 2105344 | tf_op jit(solution)/shard_map/shd,she->hde/dot_general | solution.py:45
  22.8 1.1 %select_maximum_fusion = f32[2056,128]{1,0:T(8,128)} fusion(f32[1,16]{1,0:T(1,128)S(1)} %bitcast.127, f32[2048,128]{1,0:T(8,128)S(1)} %bitcast.114), kind=kLoop, calls=%fused_computation.24 | loop fusion | flops 789504 | bytes 2101312 | tf_op jit(solution)/shard_map/concatenate | solution.py:75
  23.8 1.1 %collective-permute-start = (f32[2056,128]{1,0:T(8,128)}, f32[2056,128]{1,0:T(8,128)S(1)}, u32[]{:S(2)}, u32[]{:S(2)}) collective-permute-start(f32[2056,128]{1,0:T(8,128)} %select_maximum_fusion), channel_id=1, source_target_pairs={{0,4},{4,0},{8,12},{12,8},{16,20},{20,16},{24,28},{28,24},{1,5},{5... | collective-permute-start | bytes 3158024 | tf_op jit(solution)/shard_map/ppermute | solution.py:76
  24.9 0.1 convert_reduce_fusion
  25.0 0.9 %compare_and_fusion = pred[128,640]{0,1:T(8,128)(4,1)} fusion(s32[128]{0:T(128)S(1)} %iota_add_fusion.1, s32[128]{0:T(128)S(1)} %convert_reduce_fusion.1, s32[640]{0:T(1024)S(1)} %iota_add_fusion, s32[640]{0:T(1024)S(1)} %compare_select_fusion), kind=kLoop, calls=%fused_computation.60 | loop fusion | flops 245760 | bytes 88064 | tf_op jit(solution)/shard_map/and | solution.py:99
  26.1 0.0 copy-start.6
  26.2 0.8 %fusion.73 = (bf16[640,256]{0,1:T(8,128)(2,1)}, bf16[640,256]{0,1:T(8,128)(2,1)S(1)}) fusion(bf16[640,512]{0,1:T(8,128)(2,1)S(1)} %constant_dynamic-update-slice_fusion), kind=kLoop, calls=%fused_computation.112 | loop fusion | bytes 1310720 | tf_op jit(solution)/shard_map/slice | solution.py:101
  26.9 0.5 collective-permute-done
  27.5 0.3 select_convert_fusion.1
  27.8 0.8 %pad_maximum_fusion = bf16[2064,128]{1,0:T(8,128)(2,1)} fusion(bf16[16,128]{1,0:T(8,128)(2,1)S(1)} %fusion.62, bf16[2048,128]{1,0:T(8,128)(2,1)S(1)} %bitcast.121), kind=kLoop, calls=%fused_computation.37 | loop fusion | flops 1056768 | bytes 1056768 | tf_op jit(solution)/shard_map/concatenate | solution.py:90
  28.6 0.1 copy.57
  28.7 1.3 %collective-permute-start.5 = (bf16[2064,128]{1,0:T(8,128)(2,1)}, bf16[2064,128]{1,0:T(8,128)(2,1)S(1)}, u32[]{:S(2)}, u32[]{:S(2)}) collective-permute-start(bf16[2064,128]{1,0:T(8,128)(2,1)} %pad_maximum_fusion), channel_id=1, source_target_pairs={{4,8},{12,16},{20,24},{0,20},{8,28},{5,9},{13,17},{21,25},{1,21},{... | collective-permute-start | bytes 1585160 | tf_op jit(solution)/shard_map/ppermute | solution.py:95
  30.1 5.4 %fusion.74 = (f32[2,8,128]{2,1,0:T(8,128)S(1)}, bf16[2,8,128,640]{2,3,1,0:T(8,128)(2,1)}) fusion(pred[128,640]{0,1:T(8,128)(4,1)} %compare_and_fusion, bf16[640,2,128,1]{0,2,3,1:T(8,128)(2,1)} %bitcast.126, bf16[128,2,8,128]{3,2,1,0:T(8,128)(2,1)S(1)} %bitcast.124), kind=kOutput, calls=%fused_computation.113 | convolution fusion | flops 681575040 | bytes 3563520 | tf_op jit(solution)/shard_map/sub | solution.py:107
  35.4 3.2 %fusion.20 = bf16[128,2,8,128]{0,3,2,1:T(8,128)(2,1)} fusion(bf16[640,2,128,1]{0,2,3,1:T(8,128)(2,1)S(1)} %bitcast.125, bf16[2,8,128,640]{2,3,1,0:T(8,128)(2,1)} %get-tuple-element.29, f32[128,2,8]{0,2,1:T(8,128)S(1)} %bitcast.136), kind=kOutput, calls=%fused_computation.22 | convolution fusion | flops 336068608 | bytes 3481600 | tf_op jit(solution)/shard_map/kgts,skd->tkgd/dot_general | solution.py:109
  38.6 3.8 %collective-permute-done.5 = bf16[2064,128]{1,0:T(8,128)(2,1)S(1)} collective-permute-done((bf16[2064,128]{1,0:T(8,128)(2,1)}, bf16[2064,128]{1,0:T(8,128)(2,1)S(1)}, u32[]{:S(2)}, u32[]{:S(2)}) %collective-permute-start.5) | collective-permute-done | bytes 528416 | tf_op jit(solution)/shard_map/ppermute | solution.py:95
  42.5 0.1 fusion.56
  42.6 1.7 %convolution_bitcast_fusion.1 = f32[128,16,128]{0,2,1:T(8,128)} fusion(bf16[128,16,128]{0,2,1:T(8,128)(2,1)S(1)} %bitcast.120, f32[16,128]{1,0:T(8,128)S(1)} %reduce_window_sum.20, pred[128,128]{1,0:T(8,128)(4,1)S(1)} %fusion.56, bf16[128,2048]{1,0:T(8,128)(2,1)S(1)} %copy-done.7, bf16[128,2048]{1,0:T(8,128)(2,1)S(1)} %copy-done), kind=kOutput, calls=%fused_computation.17 | convolution fusion | flops 135528448 | bytes 2646016 | tf_op jit(solution)/shard_map/hts,shd->thd/dot_general | solution.py:40
  44.4 0.2 collective-permute-done.6
  44.5 0.1 broadcast_select_fusion
  44.7 1.3 %slice_select_fusion = bf16[2048,128]{1,0:T(8,128)(2,1)S(1)} fusion(bf16[2064,128]{1,0:T(8,128)(2,1)} %collective-permute-done.6, bf16[2064,128]{1,0:T(8,128)(2,1)S(1)} %collective-permute-done.5, pred[]{:T(512)S(6)} %eq.60), kind=kLoop, calls=%fused_computation.44 | loop fusion | flops 262144 | bytes 1572865 | tf_op jit(solution)/shard_map/jit(_where)/select_n | solution.py:117
  46.0 0.1 copy-done.4
  46.0 0.7 %multiply_reduce_fusion = (f32[128]{0:T(128)S(1)}, f32[128,16,128]{0,2,1:T(8,128)S(1)}) fusion(f32[128,16,128]{0,2,1:T(8,128)S(1)} %copy-done.4, f32[128,16]{0,1:T(8,128)S(1)} %get-tuple-element.25, f32[16,128,128]{2,1,0:T(8,128)S(1)} %bitcast.116, bf16[16,128,128]{2,1,0:T(8,128)(2,1)S(1)} %bitcast.118, bf16[16,128,128]{2,1,0:T(8,128)(2,1)S(1)} %bitcast.117, ...), kind=kOutput, calls=%fused_computation.29 | convolution fusion | flops 70254464 | bytes 4727425 | tf_op jit(solution)/shard_map/thd,hde->the/dot_general | solution.py:131
  46.8 0.0 copy-start.8
  46.8 1.6 %collective-permute-start.7 = (f32[128]{0:T(128)S(1)}, f32[128]{0:T(128)S(1)}, u32[]{:S(2)}, u32[]{:S(2)}) collective-permute-start(f32[128]{0:T(128)S(1)} %get-tuple-element.30), channel_id=1, source_target_pairs={{0,1},{1,2},{2,3},{3,0},{4,5},{5,6},{6,7},{7,4},{8,9},{9,10},{10,1... | collective-permute-start | bytes 1544 | tf_op jit(solution)/shard_map/ppermute | solution.py:21
  48.4 2.6 %collective-permute-start.8 = (f32[128]{0:T(128)S(1)}, f32[128]{0:T(128)S(1)}, u32[]{:S(2)}, u32[]{:S(2)}) collective-permute-start(f32[128]{0:T(128)S(1)} %get-tuple-element.30), channel_id=1, source_target_pairs={{0,2},{1,3},{2,0},{3,1},{4,6},{5,7},{6,4},{7,5},{8,10},{9,11},{10,... | collective-permute-start | bytes 1544 | tf_op jit(solution)/shard_map/ppermute | solution.py:21
  51.0 1.3 %collective-permute-start.9 = (f32[128]{0:T(128)S(1)}, f32[128]{0:T(128)S(1)}, u32[]{:S(2)}, u32[]{:S(2)}) collective-permute-start(f32[128]{0:T(128)S(1)} %get-tuple-element.30), channel_id=1, source_target_pairs={{0,3},{1,0},{2,1},{3,2},{4,7},{5,4},{6,5},{7,6},{8,11},{9,8},{10,9... | collective-permute-start | bytes 1544 | tf_op jit(solution)/shard_map/ppermute | solution.py:21
  52.4 2.0 %copy.47 = bf16[128,2048]{1,0:T(8,128)(2,1)} copy(bf16[128,2048]{0,1:T(8,128)(2,1)} %bitcast.123) | data formatting | bytes 1048576
  54.4 0.3 copy.46
  54.8 0.6 gather_fusion
  55.4 1.1 %multiply_convert_fusion = bf16[128,2048]{1,0:T(8,128)(2,1)} fusion(bf16[128,2048]{1,0:T(8,128)(2,1)S(1)} %copy-done.5, f32[128,2048]{1,0:T(8,128)S(1)} %copy.46, f32[2048]{0:T(1024)S(1)} %copy-done.8, f32[128]{0:T(128)S(1)} %add_rsqrt_fusion), kind=kLoop, calls=%fused_computation.28 | loop fusion | flops 2097152 | bytes 2105856 | tf_op jit(solution)/shard_map/convert_element_type | solution.py:146
  (42 shorter events, 0.4 us)
Async XLA Ops:
  0.6 42.0 %copy-start = (bf16[128,2048]{1,0:T(8,128)(2,1)S(1)}, bf16[128,2048]{1,0:T(8,128)(2,1)}, u32[]{:S(2)}) copy-start(bf16[128,2048]{1,0:T(8,128)(2,1)} %param.11) | copy-start | bytes 1572868
  2.6 23.3 %collective-permute-start.1 = (bf16[128,512]{0,1:T(8,128)(2,1)S(1)}, bf16[128,512]{0,1:T(8,128)(2,1)S(1)}, u32[]{:S(2)}, u32[]{:S(2)}) collective-permute-start(bf16[128,512]{0,1:T(8,128)(2,1)S(1)} %pad_maximum_fusion.1), channel_id=1, source_target_pairs={{0,16},{4,20},{8,24},{12,28},{1,17},{5,21},{9,25},{13,29},{2,18},{... | collective-permute-start | bytes 393224 | tf_op jit(solution)/shard_map/ppermute | solution.py:13
  7.5 18.4 %collective-permute-start.2 = (bf16[128,512]{0,1:T(8,128)(2,1)S(1)}, bf16[128,512]{0,1:T(8,128)(2,1)S(1)}, u32[]{:S(2)}, u32[]{:S(2)}) collective-permute-start(bf16[128,512]{0,1:T(8,128)(2,1)S(1)} %pad_maximum_fusion.1), channel_id=1, source_target_pairs={{0,12},{4,16},{8,20},{12,24},{16,28},{1,13},{5,17},{9,21},{13,25},... | collective-permute-start | bytes 393224 | tf_op jit(solution)/shard_map/ppermute | solution.py:13
  10.1 15.9 %collective-permute-start.3 = (bf16[128,512]{0,1:T(8,128)(2,1)S(1)}, bf16[128,512]{0,1:T(8,128)(2,1)S(1)}, u32[]{:S(2)}, u32[]{:S(2)}) collective-permute-start(bf16[128,512]{0,1:T(8,128)(2,1)S(1)} %pad_maximum_fusion.1), channel_id=1, source_target_pairs={{0,8},{4,12},{8,16},{12,20},{16,24},{20,28},{1,9},{5,13},{9,17},{1... | collective-permute-start | bytes 393224 | tf_op jit(solution)/shard_map/ppermute | solution.py:13
  12.2 13.8 %collective-permute-start.4 = (bf16[128,512]{0,1:T(8,128)(2,1)S(1)}, bf16[128,512]{0,1:T(8,128)(2,1)S(1)}, u32[]{:S(2)}, u32[]{:S(2)}) collective-permute-start(bf16[128,512]{0,1:T(8,128)(2,1)S(1)} %pad_maximum_fusion.1), channel_id=1, source_target_pairs={{0,4},{4,8},{8,12},{12,16},{16,20},{20,24},{24,28},{1,5},{5,9},{9,... | collective-permute-start | bytes 393224 | tf_op jit(solution)/shard_map/ppermute | solution.py:13
  20.1 2.6 %copy-start.2 = (bf16[128,2048]{0,1:T(8,128)(2,1)}, bf16[128,2048]{0,1:T(8,128)(2,1)S(1)}, u32[]{:S(2)}) copy-start(bf16[128,2048]{0,1:T(8,128)(2,1)S(1)} %copy.54) | copy-start | bytes 1572868
  23.8 3.6 %collective-permute-start = (f32[2056,128]{1,0:T(8,128)}, f32[2056,128]{1,0:T(8,128)S(1)}, u32[]{:S(2)}, u32[]{:S(2)}) collective-permute-start(f32[2056,128]{1,0:T(8,128)} %select_maximum_fusion), channel_id=1, source_target_pairs={{0,4},{4,0},{8,12},{12,8},{16,20},{20,16},{24,28},{28,24},{1,5},{5... | collective-permute-start | bytes 3158024 | tf_op jit(solution)/shard_map/ppermute | solution.py:76
  26.1 2.5 %copy-start.6 = (bf16[128,2048]{1,0:T(8,128)(2,1)S(1)}, bf16[128,2048]{1,0:T(8,128)(2,1)}, u32[]{:S(2)}) copy-start(bf16[128,2048]{1,0:T(8,128)(2,1)} %param.17) | copy-start | bytes 1572868
  27.4 16.9 %copy-start.1 = (f32[2056,128]{1,0:T(8,128)}, f32[2056,128]{1,0:T(8,128)S(1)}, u32[]{:S(2)}) copy-start(f32[2056,128]{1,0:T(8,128)S(1)} %collective-permute-done) | copy-start | bytes 3158020
  28.7 13.8 %collective-permute-start.5 = (bf16[2064,128]{1,0:T(8,128)(2,1)}, bf16[2064,128]{1,0:T(8,128)(2,1)S(1)}, u32[]{:S(2)}, u32[]{:S(2)}) collective-permute-start(bf16[2064,128]{1,0:T(8,128)(2,1)} %pad_maximum_fusion), channel_id=1, source_target_pairs={{4,8},{12,16},{20,24},{0,20},{8,28},{5,9},{13,17},{21,25},{1,21},{... | collective-permute-start | bytes 1585160 | tf_op jit(solution)/shard_map/ppermute | solution.py:95
  35.4 7.2 %copy-start.3 = (bf16[128,2048]{0,1:T(8,128)(2,1)S(1)}, bf16[128,2048]{0,1:T(8,128)(2,1)}, u32[]{:S(2)}) copy-start(bf16[128,2048]{0,1:T(8,128)(2,1)} %copy-done.2) | copy-start | bytes 1572868
  35.4 7.2 %copy-start.7 = (bf16[128,2048]{1,0:T(8,128)(2,1)S(1)}, bf16[128,2048]{1,0:T(8,128)(2,1)}, u32[]{:S(2)}) copy-start(bf16[128,2048]{1,0:T(8,128)(2,1)} %param.13) | copy-start | bytes 1572868
  42.5 2.0 %collective-permute-start.6 = (bf16[2064,128]{1,0:T(8,128)(2,1)S(1)}, bf16[2064,128]{1,0:T(8,128)(2,1)}, u32[]{:S(2)}, u32[]{:S(2)}) collective-permute-start(bf16[2064,128]{1,0:T(8,128)(2,1)S(1)} %collective-permute-done.5), channel_id=1, source_target_pairs={{0,4},{4,0},{8,12},{12,8},{16,20},{20,16},{24,28},{28,24},{1,5},{5... | collective-permute-start | bytes 1585160 | tf_op jit(solution)/shard_map/ppermute | solution.py:115
  44.3 1.6 %slice-start = ((f32[2056,128]{1,0:T(8,128)}), f32[2048,128]{1,0:T(8,128)S(1)}, s32[]{:S(2)}) async-start(f32[2056,128]{1,0:T(8,128)} %copy-done.1), calls=%async_computation | async-start | bytes 2097152 | tf_op jit(solution)/shard_map/slice | solution.py:77
  44.4 1.7 %copy-start.4 = (f32[128,16,128]{0,2,1:T(8,128)S(1)}, f32[128,16,128]{0,2,1:T(8,128)}, u32[]{:S(2)}) copy-start(f32[128,16,128]{0,2,1:T(8,128)} %convolution_bitcast_fusion.1) | copy-start | bytes 3145732
  46.8 8.6 %copy-start.5 = (bf16[128,2048]{1,0:T(8,128)(2,1)S(1)}, bf16[128,2048]{1,0:T(8,128)(2,1)}, u32[]{:S(2)}) copy-start(bf16[128,2048]{1,0:T(8,128)(2,1)} %param.15) | copy-start | bytes 1572868
  46.8 8.6 %copy-start.8 = (f32[2048]{0:T(1024)S(1)}, f32[2048]{0:T(1024)}, u32[]{:S(2)}) copy-start(f32[2048]{0:T(1024)} %param.16) | copy-start | bytes 24580
  46.8 7.9 %collective-permute-start.7 = (f32[128]{0:T(128)S(1)}, f32[128]{0:T(128)S(1)}, u32[]{:S(2)}, u32[]{:S(2)}) collective-permute-start(f32[128]{0:T(128)S(1)} %get-tuple-element.30), channel_id=1, source_target_pairs={{0,1},{1,2},{2,3},{3,0},{4,5},{5,6},{6,7},{7,4},{8,9},{9,10},{10,1... | collective-permute-start | bytes 1544 | tf_op jit(solution)/shard_map/ppermute | solution.py:21
  48.4 6.3 %collective-permute-start.8 = (f32[128]{0:T(128)S(1)}, f32[128]{0:T(128)S(1)}, u32[]{:S(2)}, u32[]{:S(2)}) collective-permute-start(f32[128]{0:T(128)S(1)} %get-tuple-element.30), channel_id=1, source_target_pairs={{0,2},{1,3},{2,0},{3,1},{4,6},{5,7},{6,4},{7,5},{8,10},{9,11},{10,... | collective-permute-start | bytes 1544 | tf_op jit(solution)/shard_map/ppermute | solution.py:21
  51.0 3.8 %collective-permute-start.9 = (f32[128]{0:T(128)S(1)}, f32[128]{0:T(128)S(1)}, u32[]{:S(2)}, u32[]{:S(2)}) collective-permute-start(f32[128]{0:T(128)S(1)} %get-tuple-element.30), channel_id=1, source_target_pairs={{0,3},{1,0},{2,1},{3,2},{4,7},{5,4},{6,5},{7,6},{8,11},{9,8},{10,9... | collective-permute-start | bytes 1544 | tf_op jit(solution)/shard_map/ppermute | solution.py:21

commit v17 on v15

--- a/solution.py
+++ b/solution.py
@@ -35,7 +35,7 @@
     return jnp.sum((ends[None, :] <= positions[:, None]).astype(jnp.int32), axis=1)
 
 
-def block_terms(query, lookup_array, values, decay, docs, before):
+def block_terms(query, lookup_array, values, decay, docs, before, last):
     rows = docs.shape[0]
     level = jnp.cumsum(decay, axis=1)
     order = jnp.arange(rows)
@@ -45,11 +45,11 @@
     weights = jnp.where(same[None], scores * fade, 0.0).astype(jnp.bfloat16)
     inner = jnp.einsum("hts,shd->thd", weights, values, preferred_element_type=jnp.float32)
     carried = docs == before
-    closing = (docs == docs[-1]).astype(jnp.float32)
+    closing = (docs == last).astype(jnp.float32)
     tail = jnp.exp(level[:, -1:] - level) * closing[None, :]
     weighted = (lookup_array.astype(jnp.float32) * tail.T[:, :, None]).astype(jnp.bfloat16)
     state = jnp.einsum("shd,she->hde", weighted, values, preferred_element_type=jnp.float32)
-    shrinkage_multiplier = jnp.exp(level[:, -1]) * carried[-1].astype(jnp.float32)
+    shrinkage_multiplier = jnp.exp(level[:, -1]) * (last == before).astype(jnp.float32)
     return (inner, level, carried, shrinkage_multiplier, state)
 
 
@@ -60,13 +60,15 @@
     group = soft_q.shape[1] // (kv_here * DH)
     shard = lax.axis_index("ctx")
     positions = shard * rows + jnp.arange(rows, dtype=jnp.int32)
-    docs = document_of(positions, doc_lengths)
-    before = jnp.where(shard > 0, document_of(positions[:1] - 1, doc_lengths)[0], -1)
+    ends = jnp.cumsum(doc_lengths)
+    docs = jnp.sum((ends[None, :] <= positions[:, None]).astype(jnp.int32), axis=1)
+    last = jnp.sum((ends <= shard * rows + rows - 1).astype(jnp.int32))
+    before = jnp.where(shard > 0, jnp.sum((ends <= shard * rows - 1).astype(jnp.int32)), -1)
     query = lin_q.reshape(rows, heads_here, DH)
     lookup_array = lin_k.reshape(rows, heads_here, DH)
     values = lin_v.reshape(rows, heads_here, DH)
     inner, level, carried, shrinkage_multiplier, state = block_terms(
-        query, lookup_array, values, log_decay, docs, before
+        query, lookup_array, values, log_decay, docs, before, last
     )
     count = lax.axis_size("ctx")
     odd = (shard % 2) == 1

time: 57.1 us -> 55.9 us (0.979)
  local copies, waits for them, and re-layouts: 8 us -> 6.82 us
    slice x2 -> x0, local copies, waits for them, and re-layouts: 1.17 us -> none  [the longest x1 0.58 us: block_terms(): carried[-1].astype(jnp.float32)]
    reduce_sum x0 -> x2, other arithmetic: none -> 0.72 us  [the longest x1 0.64 us: local(): jnp.sum((ends <= shard * rows - 1).astype(jnp.int32))]
    reduce_sum x3 -> x1, other arithmetic: 0.8 us -> 0.08 us  [document_of(): jnp.sum((ends[None, :] <= positions[:, None]).astype(jnp.int32), axis=1)]
  transfers between devices with their start and end apart: 9 -> 9, of which waited for: 4 -> 4; matrix products, arithmetic and copies ran while one was open for 41% -> 40% of each run, Pallas kernels for 0% -> 0%
where the time goes in v17:
time: 55.9 us; the launch traced here: 55.3 us
  starting transfers between devices  18.1 us (32%)
  matrix products  12.4 us (22%)
  other arithmetic  9.26 us (17%)
  local copies, waits for them, and re-layouts  6.82 us (12%)
  waiting for transfers between devices  6.52 us (12%)
  between operations  2.28 us (4%)
    ppermute x4, starting transfers between devices, from_behind(): return lax.ppermute(shard, axis, pairs)  11.4 us
    sub x1, matrix products, local(): expd = jnp.where(allowed, jnp.exp(jnp.minimum(scores - top, 0.0)), 0.0)  5.36 us
    unnamed x26, local copies, waits for them, and re-layouts  4.36 us
    ppermute x2, starting transfers between devices, all_sum(): x = x + lax.ppermute(x, axis, [(i, i ^ bit) for i in range(count)])  4.24 us
    ppermute x1, waiting for transfers between devices, local(): received = lax.ppermute(packet, 'ctx', routes)  3.84 us
    dot_general x1, matrix products, local(): jnp.einsum('kgts,skd->tkgd', expd.astype(jnp.bfloat16), all_values, prefe...  3.21 us
    ppermute x2, waiting for transfers between devices, all_sum(): x = x + lax.ppermute(x, axis, [(i, i ^ bit) for i in range(count)])  1.97 us
    dot_general x1, matrix products, block_terms(): jnp.einsum('hts,shd->thd', weights, values, preferred_element_type=jnp.fl...  1.71 us
  transfers between devices with their start and end apart: 9, of which 4 were waited for; matrix products, arithmetic and copies ran while one was open for 40% of the time, Pallas kernels for 0%

profile of v17, /device:TPU:0, one launch (start us, length us, event | category | flops | bytes accessed | tf_op | source)
XLA Modules:
  0.0 55.3 jit_solution(2950050314665946564)
XLA Ops:
  0.6 0.0 copy-start
  0.6 1.0 %copy.39 = bf16[128,256]{0,1:T(8,128)(2,1)S(1)} copy(bf16[128,256]{1,0:T(8,128)(2,1)} %param.18) | data formatting | bytes 131072 | tf_op args[8]
  1.7 1.0 %copy.40 = bf16[128,256]{0,1:T(8,128)(2,1)S(1)} copy(bf16[128,256]{1,0:T(8,128)(2,1)} %param.19) | data formatting | bytes 131072 | tf_op args[9]
  2.6 4.9 %collective-permute-start.1 = (bf16[128,512]{0,1:T(8,128)(2,1)S(1)}, bf16[128,512]{0,1:T(8,128)(2,1)S(1)}, u32[]{:S(2)}, u32[]{:S(2)}) collective-permute-start(bf16[128,512]{0,1:T(8,128)(2,1)S(1)} %pad_maximum_fusion.1), channel_id=1, source_target_pairs={{0,16},{4,20},{8,24},{12,28},{1,17},{5,21},{9,25},{13,29},{2,18},{... | collective-permute-start | bytes 393224 | tf_op jit(solution)/shard_map/ppermute | solution.py:13
  7.5 2.6 %collective-permute-start.2 = (bf16[128,512]{0,1:T(8,128)(2,1)S(1)}, bf16[128,512]{0,1:T(8,128)(2,1)S(1)}, u32[]{:S(2)}, u32[]{:S(2)}) collective-permute-start(bf16[128,512]{0,1:T(8,128)(2,1)S(1)} %pad_maximum_fusion.1), channel_id=1, source_target_pairs={{0,12},{4,16},{8,20},{12,24},{16,28},{1,13},{5,17},{9,21},{13,25},... | collective-permute-start | bytes 393224 | tf_op jit(solution)/shard_map/ppermute | solution.py:13
  10.1 2.1 %collective-permute-start.3 = (bf16[128,512]{0,1:T(8,128)(2,1)S(1)}, bf16[128,512]{0,1:T(8,128)(2,1)S(1)}, u32[]{:S(2)}, u32[]{:S(2)}) collective-permute-start(bf16[128,512]{0,1:T(8,128)(2,1)S(1)} %pad_maximum_fusion.1), channel_id=1, source_target_pairs={{0,8},{4,12},{8,16},{12,20},{16,24},{20,28},{1,9},{5,13},{9,17},{1... | collective-permute-start | bytes 393224 | tf_op jit(solution)/shard_map/ppermute | solution.py:13
  12.2 1.8 %collective-permute-start.4 = (bf16[128,512]{0,1:T(8,128)(2,1)S(1)}, bf16[128,512]{0,1:T(8,128)(2,1)S(1)}, u32[]{:S(2)}, u32[]{:S(2)}) collective-permute-start(bf16[128,512]{0,1:T(8,128)(2,1)S(1)} %pad_maximum_fusion.1), channel_id=1, source_target_pairs={{0,4},{4,8},{8,12},{12,16},{16,20},{20,24},{24,28},{1,5},{5,9},{9,... | collective-permute-start | bytes 393224 | tf_op jit(solution)/shard_map/ppermute | solution.py:13
  14.1 0.8 %reduce-window.8 = s32[6,1]{0,1:T(1,128)S(1)} reduce-window(s32[6,1]{0,1:T(1,128)} %bitcast.122, s32[]{:T(128)} %constant.23.clone.1), window={size=6x1 pad=5_0x0_0}, to_apply=%region_0.0 | reduce-window | flops 30 | bytes 52 | tf_op jit(solution)/shard_map/reduce-window.3
  14.9 0.6 %fusion.64 = (s32[]{:T(128)}, s32[]{:T(128)}) fusion(s32[]{:T(128)S(6)} %sub.53, s32[6,1]{0,1:T(1,128)S(1)} %reduce-window.8, s32[]{:T(128)S(6)} %sub.52), kind=kLoop, calls=%fused_computation.89 | loop fusion | flops 34 | bytes 40 | tf_op jit(solution)/shard_map/reduce_sum | solution.py:66
  16.2 0.1 convert_reduce_fusion.1
  16.9 0.7 %compare_convert_fusion = (f32[128]{0:T(128)S(1)}, f32[128]{0:T(128)S(1)}) fusion(s32[128]{0:T(128)S(1)} %convert_reduce_fusion.1, s32[]{:T(128)S(6)} %select_n.57, s32[]{:T(128)} %get-tuple-element.19), kind=kLoop, calls=%fused_computation.84 | loop fusion | flops 512 | bytes 1544 | tf_op jit(solution)/shard_map/convert_element_type | solution.py:142
  17.6 1.3 %copy.54 = bf16[128,2048]{0,1:T(8,128)(2,1)S(1)} copy(bf16[128,2048]{1,0:T(8,128)(2,1)} %param.12) | data formatting | bytes 1048576 | tf_op jit(solution)/shard_map/reshape | solution.py:68
  18.9 0.0 copy-start.2
  18.9 1.0 %reduce_window_sum.19 = f32[16,128]{1,0:T(8,128)S(1)} reduce-window(f32[16,128]{1,0:T(8,128)} %param.14, f32[]{:T(128)} %constant.47.clone.1), window={size=1x128 pad=0_0x127_0}, to_apply=%region_2.3 | reduce-window | flops 260096 | bytes 16388 | tf_op jit(solution)/shard_map/jit(cumsum)/reduce_window_sum | solution.py:40
  19.9 0.2 slice_reduce_fusion
  20.1 0.1 multiply_bitcast_fusion
  20.2 1.4 %fusion.30 = f32[16,128,128]{2,1,0:T(8,128)S(1)} fusion(bf16[128,16,128]{0,2,1:T(8,128)(2,1)S(1)} %bitcast.111, f32[128,16]{0,1:T(8,128)S(1)} %get-tuple-element.26, bf16[128,2048]{1,0:T(8,128)(2,1)} %param.13), kind=kOutput, calls=%fused_computation.38 | convolution fusion | flops 67895296 | bytes 2105344 | tf_op jit(solution)/shard_map/shd,she->hde/dot_general | solution.py:51
  21.6 1.1 %select_maximum_fusion = f32[2056,128]{1,0:T(8,128)} fusion(f32[1,16]{1,0:T(1,128)S(1)} %bitcast.119, f32[2048,128]{1,0:T(8,128)S(1)} %bitcast.106), kind=kLoop, calls=%fused_computation.23 | loop fusion | flops 789504 | bytes 2101312 | tf_op jit(solution)/shard_map/concatenate | solution.py:83
  22.6 1.1 %collective-permute-start = (f32[2056,128]{1,0:T(8,128)}, f32[2056,128]{1,0:T(8,128)S(1)}, u32[]{:S(2)}, u32[]{:S(2)}) collective-permute-start(f32[2056,128]{1,0:T(8,128)} %select_maximum_fusion), channel_id=1, source_target_pairs={{0,4},{4,0},{8,12},{12,8},{16,20},{20,16},{24,28},{28,24},{1,5},{5... | collective-permute-start | bytes 3158024 | tf_op jit(solution)/shard_map/ppermute | solution.py:84
  23.7 0.1 convert_reduce_fusion
  23.8 0.9 %compare_and_fusion = pred[128,640]{0,1:T(8,128)(4,1)} fusion(s32[128]{0:T(128)S(1)} %iota_add_fusion.1, s32[128]{0:T(128)S(1)} %convert_reduce_fusion.1, s32[640]{0:T(1024)S(1)} %iota_add_fusion, s32[640]{0:T(1024)S(1)} %compare_select_fusion), kind=kLoop, calls=%fused_computation.59 | loop fusion | flops 245760 | bytes 88064 | tf_op jit(solution)/shard_map/and | solution.py:107
  24.7 0.0 collective-permute-done.1
  24.8 0.0 collective-permute-done.2
  24.9 0.0 copy-start.6
  25.0 0.8 %fusion.71 = (bf16[640,256]{0,1:T(8,128)(2,1)}, bf16[640,256]{0,1:T(8,128)(2,1)S(1)}) fusion(bf16[640,512]{0,1:T(8,128)(2,1)S(1)} %constant_dynamic-update-slice_fusion), kind=kLoop, calls=%fused_computation.104 | loop fusion | bytes 1310720 | tf_op jit(solution)/shard_map/slice | solution.py:109
  25.7 0.5 collective-permute-done
  26.3 0.3 select_convert_fusion.1
  26.6 0.8 %pad_maximum_fusion = bf16[2064,128]{1,0:T(8,128)(2,1)} fusion(bf16[16,128]{1,0:T(8,128)(2,1)S(1)} %fusion.62, bf16[2048,128]{1,0:T(8,128)(2,1)S(1)} %bitcast.113), kind=kLoop, calls=%fused_computation.36 | loop fusion | flops 1056768 | bytes 1056768 | tf_op jit(solution)/shard_map/concatenate | solution.py:98
  27.4 0.1 copy.57
  27.5 1.3 %collective-permute-start.5 = (bf16[2064,128]{1,0:T(8,128)(2,1)}, bf16[2064,128]{1,0:T(8,128)(2,1)S(1)}, u32[]{:S(2)}, u32[]{:S(2)}) collective-permute-start(bf16[2064,128]{1,0:T(8,128)(2,1)} %pad_maximum_fusion), channel_id=1, source_target_pairs={{4,8},{12,16},{20,24},{0,20},{8,28},{5,9},{13,17},{21,25},{1,21},{... | collective-permute-start | bytes 1585160 | tf_op jit(solution)/shard_map/ppermute | solution.py:103
  28.9 5.4 %fusion.72 = (f32[2,8,128]{2,1,0:T(8,128)S(1)}, bf16[2,8,128,640]{2,3,1,0:T(8,128)(2,1)}) fusion(pred[128,640]{0,1:T(8,128)(4,1)} %compare_and_fusion, bf16[640,2,128,1]{0,2,3,1:T(8,128)(2,1)} %bitcast.118, bf16[128,2,8,128]{3,2,1,0:T(8,128)(2,1)S(1)} %bitcast.116), kind=kOutput, calls=%fused_computation.105 | convolution fusion | flops 681575040 | bytes 3563520 | tf_op jit(solution)/shard_map/sub | solution.py:115
  34.2 3.2 %fusion.20 = bf16[128,2,8,128]{0,3,2,1:T(8,128)(2,1)} fusion(bf16[640,2,128,1]{0,2,3,1:T(8,128)(2,1)S(1)} %bitcast.117, bf16[2,8,128,640]{2,3,1,0:T(8,128)(2,1)} %get-tuple-element.30, f32[128,2,8]{0,2,1:T(8,128)S(1)} %bitcast.123), kind=kOutput, calls=%fused_computation.21 | convolution fusion | flops 336068608 | bytes 3481600 | tf_op jit(solution)/shard_map/kgts,skd->tkgd/dot_general | solution.py:117
  37.4 3.8 %collective-permute-done.5 = bf16[2064,128]{1,0:T(8,128)(2,1)S(1)} collective-permute-done((bf16[2064,128]{1,0:T(8,128)(2,1)}, bf16[2064,128]{1,0:T(8,128)(2,1)S(1)}, u32[]{:S(2)}, u32[]{:S(2)}) %collective-permute-start.5) | collective-permute-done | bytes 528416 | tf_op jit(solution)/shard_map/ppermute | solution.py:103
  41.3 0.0 collective-permute-start.6
  41.3 0.1 fusion.56
  41.4 1.7 %convolution_bitcast_fusion.1 = f32[128,16,128]{0,2,1:T(8,128)} fusion(bf16[128,16,128]{0,2,1:T(8,128)(2,1)S(1)} %bitcast.112, f32[16,128]{1,0:T(8,128)S(1)} %reduce_window_sum.19, pred[128,128]{1,0:T(8,128)(4,1)S(1)} %fusion.56, bf16[128,2048]{1,0:T(8,128)(2,1)S(1)} %copy-done.7, bf16[128,2048]{1,0:T(8,128)(2,1)S(1)} %copy-done), kind=kOutput, calls=%fused_computation.16 | convolution fusion | flops 135528448 | bytes 2646016 | tf_op jit(solution)/shard_map/hts,shd->thd/dot_general | solution.py:46
  43.1 0.2 collective-permute-done.6
  43.3 0.1 broadcast_select_fusion
  43.5 1.3 %slice_select_fusion = bf16[2048,128]{1,0:T(8,128)(2,1)S(1)} fusion(bf16[2064,128]{1,0:T(8,128)(2,1)} %collective-permute-done.6, bf16[2064,128]{1,0:T(8,128)(2,1)S(1)} %collective-permute-done.5, pred[]{:T(512)S(6)} %eq.61), kind=kLoop, calls=%fused_computation.43 | loop fusion | flops 262144 | bytes 1572865 | tf_op jit(solution)/shard_map/jit(_where)/select_n | solution.py:125
  44.8 0.1 copy-done.4
  44.8 0.7 %multiply_reduce_fusion = (f32[128]{0:T(128)S(1)}, f32[128,16,128]{0,2,1:T(8,128)S(1)}) fusion(f32[128,16,128]{0,2,1:T(8,128)S(1)} %copy-done.4, f32[128,16]{0,1:T(8,128)S(1)} %get-tuple-element.25, f32[16,128,128]{2,1,0:T(8,128)S(1)} %bitcast.108, bf16[16,128,128]{2,1,0:T(8,128)(2,1)S(1)} %bitcast.110, bf16[16,128,128]{2,1,0:T(8,128)(2,1)S(1)} %bitcast.109, ...), kind=kOutput, calls=%fused_computation.28 | convolution fusion | flops 70254464 | bytes 4727425 | tf_op jit(solution)/shard_map/thd,hde->the/dot_general | solution.py:139
  45.6 0.0 copy-start.8
  45.6 1.6 %collective-permute-start.7 = (f32[128]{0:T(128)S(1)}, f32[128]{0:T(128)S(1)}, u32[]{:S(2)}, u32[]{:S(2)}) collective-permute-start(f32[128]{0:T(128)S(1)} %get-tuple-element.31), channel_id=1, source_target_pairs={{0,1},{1,0},{2,3},{3,2},{4,5},{5,4},{6,7},{7,6},{8,9},{9,8},{10,11... | collective-permute-start | bytes 1544 | tf_op jit(solution)/shard_map/ppermute | solution.py:28
  47.2 2.0 %collective-permute-done.7 = f32[128]{0:T(128)S(1)} collective-permute-done((f32[128]{0:T(128)S(1)}, f32[128]{0:T(128)S(1)}, u32[]{:S(2)}, u32[]{:S(2)}) %collective-permute-start.7) | collective-permute-done | bytes 544 | tf_op jit(solution)/shard_map/ppermute | solution.py:28
  49.2 2.6 %collective-permute-start.8 = (f32[128]{0:T(128)S(1)}, f32[128]{0:T(128)S(1)}, u32[]{:S(2)}, u32[]{:S(2)}) collective-permute-start(f32[128]{0:T(128)S(1)} %add.93), channel_id=1, source_target_pairs={{0,2},{1,3},{2,0},{3,1},{4,6},{5,7},{6,4},{7,5},{8,10},{9,11},{10,... | collective-permute-start | bytes 1544 | tf_op jit(solution)/shard_map/ppermute | solution.py:28
  51.8 2.0 %copy.47 = bf16[128,2048]{1,0:T(8,128)(2,1)} copy(bf16[128,2048]{0,1:T(8,128)(2,1)} %bitcast.115) | data formatting | bytes 1048576
  53.8 0.3 copy.46
  54.2 1.1 %multiply_convert_fusion = bf16[128,2048]{1,0:T(8,128)(2,1)} fusion(bf16[128,2048]{1,0:T(8,128)(2,1)S(1)} %copy-done.5, f32[128,2048]{1,0:T(8,128)S(1)} %copy.46, f32[2048]{0:T(1024)S(1)} %copy-done.8, f32[128]{0:T(128)S(1)} %add_rsqrt_fusion), kind=kLoop, calls=%fused_computation.27 | loop fusion | flops 2097152 | bytes 2105856 | tf_op jit(solution)/shard_map/convert_element_type | solution.py:154
  (34 shorter events, 0.3 us)
Async XLA Ops:
  0.6 40.8 %copy-start = (bf16[128,2048]{1,0:T(8,128)(2,1)S(1)}, bf16[128,2048]{1,0:T(8,128)(2,1)}, u32[]{:S(2)}) copy-start(bf16[128,2048]{1,0:T(8,128)(2,1)} %param.11) | copy-start | bytes 1572868
  2.6 22.1 %collective-permute-start.1 = (bf16[128,512]{0,1:T(8,128)(2,1)S(1)}, bf16[128,512]{0,1:T(8,128)(2,1)S(1)}, u32[]{:S(2)}, u32[]{:S(2)}) collective-permute-start(bf16[128,512]{0,1:T(8,128)(2,1)S(1)} %pad_maximum_fusion.1), channel_id=1, source_target_pairs={{0,16},{4,20},{8,24},{12,28},{1,17},{5,21},{9,25},{13,29},{2,18},{... | collective-permute-start | bytes 393224 | tf_op jit(solution)/shard_map/ppermute | solution.py:13
  7.5 17.2 %collective-permute-start.2 = (bf16[128,512]{0,1:T(8,128)(2,1)S(1)}, bf16[128,512]{0,1:T(8,128)(2,1)S(1)}, u32[]{:S(2)}, u32[]{:S(2)}) collective-permute-start(bf16[128,512]{0,1:T(8,128)(2,1)S(1)} %pad_maximum_fusion.1), channel_id=1, source_target_pairs={{0,12},{4,16},{8,20},{12,24},{16,28},{1,13},{5,17},{9,21},{13,25},... | collective-permute-start | bytes 393224 | tf_op jit(solution)/shard_map/ppermute | solution.py:13
  10.1 14.7 %collective-permute-start.3 = (bf16[128,512]{0,1:T(8,128)(2,1)S(1)}, bf16[128,512]{0,1:T(8,128)(2,1)S(1)}, u32[]{:S(2)}, u32[]{:S(2)}) collective-permute-start(bf16[128,512]{0,1:T(8,128)(2,1)S(1)} %pad_maximum_fusion.1), channel_id=1, source_target_pairs={{0,8},{4,12},{8,16},{12,20},{16,24},{20,28},{1,9},{5,13},{9,17},{1... | collective-permute-start | bytes 393224 | tf_op jit(solution)/shard_map/ppermute | solution.py:13
  12.2 12.6 %collective-permute-start.4 = (bf16[128,512]{0,1:T(8,128)(2,1)S(1)}, bf16[128,512]{0,1:T(8,128)(2,1)S(1)}, u32[]{:S(2)}, u32[]{:S(2)}) collective-permute-start(bf16[128,512]{0,1:T(8,128)(2,1)S(1)} %pad_maximum_fusion.1), channel_id=1, source_target_pairs={{0,4},{4,8},{8,12},{12,16},{16,20},{20,24},{24,28},{1,5},{5,9},{9,... | collective-permute-start | bytes 393224 | tf_op jit(solution)/shard_map/ppermute | solution.py:13
  18.9 2.6 %copy-start.2 = (bf16[128,2048]{0,1:T(8,128)(2,1)}, bf16[128,2048]{0,1:T(8,128)(2,1)S(1)}, u32[]{:S(2)}) copy-start(bf16[128,2048]{0,1:T(8,128)(2,1)S(1)} %copy.54) | copy-start | bytes 1572868
  22.6 3.6 %collective-permute-start = (f32[2056,128]{1,0:T(8,128)}, f32[2056,128]{1,0:T(8,128)S(1)}, u32[]{:S(2)}, u32[]{:S(2)}) collective-permute-start(f32[2056,128]{1,0:T(8,128)} %select_maximum_fusion), channel_id=1, source_target_pairs={{0,4},{4,0},{8,12},{12,8},{16,20},{20,16},{24,28},{28,24},{1,5},{5... | collective-permute-start | bytes 3158024 | tf_op jit(solution)/shard_map/ppermute | solution.py:84
  24.9 2.5 %copy-start.6 = (bf16[128,2048]{1,0:T(8,128)(2,1)S(1)}, bf16[128,2048]{1,0:T(8,128)(2,1)}, u32[]{:S(2)}) copy-start(bf16[128,2048]{1,0:T(8,128)(2,1)} %param.17) | copy-start | bytes 1572868
  26.2 16.9 %copy-start.1 = (f32[2056,128]{1,0:T(8,128)}, f32[2056,128]{1,0:T(8,128)S(1)}, u32[]{:S(2)}) copy-start(f32[2056,128]{1,0:T(8,128)S(1)} %collective-permute-done) | copy-start | bytes 3158020
  27.5 13.8 %collective-permute-start.5 = (bf16[2064,128]{1,0:T(8,128)(2,1)}, bf16[2064,128]{1,0:T(8,128)(2,1)S(1)}, u32[]{:S(2)}, u32[]{:S(2)}) collective-permute-start(bf16[2064,128]{1,0:T(8,128)(2,1)} %pad_maximum_fusion), channel_id=1, source_target_pairs={{4,8},{12,16},{20,24},{0,20},{8,28},{5,9},{13,17},{21,25},{1,21},{... | collective-permute-start | bytes 1585160 | tf_op jit(solution)/shard_map/ppermute | solution.py:103
  34.2 7.2 %copy-start.3 = (bf16[128,2048]{0,1:T(8,128)(2,1)S(1)}, bf16[128,2048]{0,1:T(8,128)(2,1)}, u32[]{:S(2)}) copy-start(bf16[128,2048]{0,1:T(8,128)(2,1)} %copy-done.2) | copy-start | bytes 1572868
  34.2 7.2 %copy-start.7 = (bf16[128,2048]{1,0:T(8,128)(2,1)S(1)}, bf16[128,2048]{1,0:T(8,128)(2,1)}, u32[]{:S(2)}) copy-start(bf16[128,2048]{1,0:T(8,128)(2,1)} %param.13) | copy-start | bytes 1572868
  41.3 2.0 %collective-permute-start.6 = (bf16[2064,128]{1,0:T(8,128)(2,1)S(1)}, bf16[2064,128]{1,0:T(8,128)(2,1)}, u32[]{:S(2)}, u32[]{:S(2)}) collective-permute-start(bf16[2064,128]{1,0:T(8,128)(2,1)S(1)} %collective-permute-done.5), channel_id=1, source_target_pairs={{0,4},{4,0},{8,12},{12,8},{16,20},{20,16},{24,28},{28,24},{1,5},{5... | collective-permute-start | bytes 1585160 | tf_op jit(solution)/shard_map/ppermute | solution.py:123
  43.1 1.6 %slice-start = ((f32[2056,128]{1,0:T(8,128)}), f32[2048,128]{1,0:T(8,128)S(1)}, s32[]{:S(2)}) async-start(f32[2056,128]{1,0:T(8,128)} %copy-done.1), calls=%async_computation | async-start | bytes 2097152 | tf_op jit(solution)/shard_map/slice | solution.py:85
  43.1 1.7 %copy-start.4 = (f32[128,16,128]{0,2,1:T(8,128)S(1)}, f32[128,16,128]{0,2,1:T(8,128)}, u32[]{:S(2)}) copy-start(f32[128,16,128]{0,2,1:T(8,128)} %convolution_bitcast_fusion.1) | copy-start | bytes 3145732
  45.6 8.6 %copy-start.5 = (bf16[128,2048]{1,0:T(8,128)(2,1)S(1)}, bf16[128,2048]{1,0:T(8,128)(2,1)}, u32[]{:S(2)}) copy-start(bf16[128,2048]{1,0:T(8,128)(2,1)} %param.15) | copy-start | bytes 1572868
  45.6 8.6 %copy-start.8 = (f32[2048]{0:T(1024)S(1)}, f32[2048]{0:T(1024)}, u32[]{:S(2)}) copy-start(f32[2048]{0:T(1024)} %param.16) | copy-start | bytes 24580
  45.6 3.6 %collective-permute-start.7 = (f32[128]{0:T(128)S(1)}, f32[128]{0:T(128)S(1)}, u32[]{:S(2)}, u32[]{:S(2)}) collective-permute-start(f32[128]{0:T(128)S(1)} %get-tuple-element.31), channel_id=1, source_target_pairs={{0,1},{1,0},{2,3},{3,2},{4,5},{5,4},{6,7},{7,6},{8,9},{9,8},{10,11... | collective-permute-start | bytes 1544 | tf_op jit(solution)/shard_map/ppermute | solution.py:28
  49.2 5.0 %collective-permute-start.8 = (f32[128]{0:T(128)S(1)}, f32[128]{0:T(128)S(1)}, u32[]{:S(2)}, u32[]{:S(2)}) collective-permute-start(f32[128]{0:T(128)S(1)} %add.93), channel_id=1, source_target_pairs={{0,2},{1,3},{2,0},{3,1},{4,6},{5,7},{6,4},{7,5},{8,10},{9,11},{10,... | collective-permute-start | bytes 1544 | tf_op jit(solution)/shard_map/ppermute | solution.py:28

commit v18 on v17

--- a/solution.py
+++ b/solution.py
@@ -77,9 +77,15 @@
     n_state = heads_here * DH
     state_rows = state.reshape(n_state, DH)
     factor_rows = jnp.pad(shrinkage_multiplier[None, :], ((0, 7), (0, DH - heads_here)))
-    window = jnp.concatenate(
-        [from_behind(pair, "ctx", step) for step in range(SPAN, 0, -1)] + [pair], axis=0
+    pair_mate = lax.ppermute(pair, "ctx", [(i, i ^ 1) for i in range(count)])
+    chip_pair = jnp.concatenate(
+        [jnp.where(odd, pair_mate, pair), jnp.where(odd, pair, pair_mate)], axis=0
     )
+    chip_near = from_behind(chip_pair, "ctx", 2)
+    chip_far = from_behind(chip_pair, "ctx", 4)
+    window_even = jnp.concatenate([chip_far, chip_near], axis=0)
+    window_odd = jnp.concatenate([chip_far[rows:], chip_near, pair_mate], axis=0)
+    window = jnp.concatenate([jnp.where(odd, window_odd, window_even), pair], axis=0)
     first = jnp.concatenate([state_rows, factor_rows], axis=0)
     got = lax.ppermute(first, "ctx", [(i, i ^ 1) for i in range(count)])
     state_mate = got[:n_state]

time: 55.9 us -> 61.4 us (1.098)
  waiting for transfers between devices: 6.52 us -> 15.4 us
  local copies, waits for them, and re-layouts: 6.82 us -> 5.02 us
  starting transfers between devices: 18.1 us -> 16.4 us
    ppermute x4 -> x2, waiting for transfers between devices: 0.01 us -> 7.15 us  [from_behind(): return lax.ppermute(shard, axis, pairs)]
    ppermute x4 -> x2, starting transfers between devices: 11.4 us -> 8.22 us  [from_behind(): return lax.ppermute(shard, axis, pairs)]
    ppermute x1, starting transfers between devices: 1.32 us -> 3.33 us  [local(): received = lax.ppermute(packet, 'ctx', routes)]
    ppermute x0 -> x1, waiting for transfers between devices: none -> 1.98 us  [local(): pair_mate = lax.ppermute(pair, 'ctx', [(i, i ^ 1) for i in range(count)])]
    unnamed x26, local copies, waits for them, and re-layouts: 4.36 us -> 2.51 us
    ppermute x1, starting transfers between devices: 1.1 us -> 0.45 us  [local(): got = lax.ppermute(first, 'ctx', [(i, i ^ 1) for i in range(count)])]
  transfers between devices with their start and end apart: 9 -> 8, of which waited for: 4 -> 5; matrix products, arithmetic and copies ran while one was open for 40% -> 25% of each run, Pallas kernels for 0% -> 0%
where the time goes in v18:
time: 61.4 us; the launch traced here: 61 us
  starting transfers between devices  16.4 us (27%)
  waiting for transfers between devices  15.4 us (25%)
  matrix products  12.4 us (20%)
  other arithmetic  9.56 us (16%)
  local copies, waits for them, and re-layouts  5.02 us (8%)
  between operations  2.28 us (4%)
    ppermute x2, starting transfers between devices, from_behind(): return lax.ppermute(shard, axis, pairs)  8.22 us
    ppermute x2, waiting for transfers between devices, from_behind(): return lax.ppermute(shard, axis, pairs)  7.15 us
    sub x1, matrix products, local(): expd = jnp.where(allowed, jnp.exp(jnp.minimum(scores - top, 0.0)), 0.0)  5.37 us
    ppermute x2, starting transfers between devices, all_sum(): x = x + lax.ppermute(x, axis, [(i, i ^ bit) for i in range(count)])  4.24 us
    ppermute x1, waiting for transfers between devices, local(): received = lax.ppermute(packet, 'ctx', routes)  4.09 us
    ppermute x1, starting transfers between devices, local(): received = lax.ppermute(packet, 'ctx', routes)  3.33 us
    dot_general x1, matrix products, local(): jnp.einsum('kgts,skd->tkgd', expd.astype(jnp.bfloat16), all_values, prefe...  3.21 us
    unnamed x26, local copies, waits for them, and re-layouts  2.51 us
  transfers between devices with their start and end apart: 8, of which 5 were waited for; matrix products, arithmetic and copies ran while one was open for 25% of the time, Pallas kernels for 0%

profile of v18, /device:TPU:0, one launch (start us, length us, event | category | flops | bytes accessed | tf_op | source)
XLA Modules:
  0.0 61.0 jit_solution(369490994799916398)
XLA Ops:
  0.6 0.0 copy-start
  0.7 0.9 %reduce-window.8 = s32[6,1]{0,1:T(1,128)S(1)} reduce-window(s32[6,1]{0,1:T(1,128)} %bitcast.122, s32[]{:T(128)} %constant.23.clone.1), window={size=6x1 pad=5_0x0_0}, to_apply=%region_0.0 | reduce-window | flops 30 | bytes 52 | tf_op jit(solution)/shard_map/reduce-window.3
  1.6 0.6 %fusion.64 = (s32[]{:T(128)}, s32[]{:T(128)}) fusion(s32[]{:T(128)S(6)} %sub.53, s32[6,1]{0,1:T(1,128)S(1)} %reduce-window.8, s32[]{:T(128)S(6)} %sub.52), kind=kLoop, calls=%fused_computation.89 | loop fusion | flops 34 | bytes 40 | tf_op jit(solution)/shard_map/reduce_sum | solution.py:66
  2.8 0.1 convert_reduce_fusion.1
  3.6 0.6 %compare_convert_fusion = (f32[128]{0:T(128)S(1)}, f32[128]{0:T(128)S(1)}) fusion(s32[128]{0:T(128)S(1)} %convert_reduce_fusion.1, s32[]{:T(128)S(6)} %select_n.77, s32[]{:T(128)} %get-tuple-element.19), kind=kLoop, calls=%fused_computation.84 | loop fusion | flops 512 | bytes 1544 | tf_op jit(solution)/shard_map/convert_element_type | solution.py:148
  4.2 0.0 copy-start.8
  4.3 0.0 copy-start.9
  4.3 1.3 %copy.54 = bf16[128,2048]{0,1:T(8,128)(2,1)S(1)} copy(bf16[128,2048]{1,0:T(8,128)(2,1)} %param.12) | data formatting | bytes 1048576 | tf_op jit(solution)/shard_map/reshape | solution.py:68
  5.6 1.0 %reduce_window_sum.19 = f32[16,128]{1,0:T(8,128)S(1)} reduce-window(f32[16,128]{1,0:T(8,128)} %param.14, f32[]{:T(128)} %constant.47.clone.1), window={size=1x128 pad=0_0x127_0}, to_apply=%region_2.3 | reduce-window | flops 260096 | bytes 16388 | tf_op jit(solution)/shard_map/jit(cumsum)/reduce_window_sum | solution.py:40
  6.6 0.2 slice_reduce_fusion
  6.8 0.1 multiply_bitcast_fusion
  6.9 1.4 %fusion.30 = f32[16,128,128]{2,1,0:T(8,128)S(1)} fusion(bf16[128,16,128]{0,2,1:T(8,128)(2,1)S(1)} %bitcast.111, f32[128,16]{0,1:T(8,128)S(1)} %get-tuple-element.28, bf16[128,2048]{1,0:T(8,128)(2,1)} %param.13), kind=kOutput, calls=%fused_computation.39 | convolution fusion | flops 67895296 | bytes 2105344 | tf_op jit(solution)/shard_map/shd,she->hde/dot_general | solution.py:51
  8.3 1.1 %select_maximum_fusion = f32[2056,128]{1,0:T(8,128)} fusion(f32[1,16]{1,0:T(1,128)S(1)} %bitcast.119, f32[2048,128]{1,0:T(8,128)S(1)} %bitcast.106), kind=kLoop, calls=%fused_computation.23 | loop fusion | flops 789504 | bytes 2101312 | tf_op jit(solution)/shard_map/concatenate | solution.py:89
  9.3 0.5 collective-permute-start
  9.8 0.1 copy.39
  9.9 0.1 copy.40
  10.0 0.1 collective-permute-start.1
  10.2 0.1 convert_reduce_fusion
  10.3 2.0 %collective-permute-done.1 = bf16[128,512]{0,1:T(8,128)(2,1)S(1)} collective-permute-done((bf16[128,512]{0,1:T(8,128)(2,1)S(1)}, bf16[128,512]{0,1:T(8,128)(2,1)S(1)}, u32[]{:S(2)}, u32[]{:S(2)}) %collective-permute-start.1) | collective-permute-done | bytes 131104 | tf_op jit(solution)/shard_map/ppermute | solution.py:80
  12.3 0.1 broadcast_select_fusion.2
  12.3 4.8 %collective-permute-start.2 = (bf16[256,512]{0,1:T(8,128)(2,1)S(1)}, bf16[256,512]{0,1:T(8,128)(2,1)S(1)}, u32[]{:S(2)}, u32[]{:S(2)}) collective-permute-start(bf16[256,512]{0,1:T(8,128)(2,1)S(1)} %pad_maximum_fusion.1), channel_id=1, source_target_pairs={{0,16},{4,20},{8,24},{12,28},{1,17},{5,21},{9,25},{13,29},{2,18},{... | collective-permute-start | bytes 786440 | tf_op jit(solution)/shard_map/ppermute | solution.py:13
  17.2 3.4 %collective-permute-start.3 = (bf16[256,512]{0,1:T(8,128)(2,1)S(1)}, bf16[256,512]{0,1:T(8,128)(2,1)S(1)}, u32[]{:S(2)}, u32[]{:S(2)}) collective-permute-start(bf16[256,512]{0,1:T(8,128)(2,1)S(1)} %pad_maximum_fusion.1), channel_id=1, source_target_pairs={{0,8},{4,12},{8,16},{12,20},{16,24},{20,28},{1,9},{5,13},{9,17},{1... | collective-permute-start | bytes 786440 | tf_op jit(solution)/shard_map/ppermute | solution.py:13
  20.6 0.9 %compare_and_fusion = pred[128,640]{0,1:T(8,128)(4,1)} fusion(s32[128]{0:T(128)S(1)} %iota_add_fusion.1, s32[128]{0:T(128)S(1)} %convert_reduce_fusion.1, s32[640]{0:T(1024)S(1)} %iota_add_fusion, s32[640]{0:T(1024)S(1)} %compare_select_fusion), kind=kLoop, calls=%fused_computation.61 | loop fusion | flops 245760 | bytes 88064 | tf_op jit(solution)/shard_map/and | solution.py:113
  21.5 7.1 %collective-permute-done.2 = bf16[256,512]{0,1:T(8,128)(2,1)S(1)} collective-permute-done((bf16[256,512]{0,1:T(8,128)(2,1)S(1)}, bf16[256,512]{0,1:T(8,128)(2,1)S(1)}, u32[]{:S(2)}, u32[]{:S(2)}) %collective-permute-start.2) | collective-permute-done | bytes 262176 | tf_op jit(solution)/shard_map/ppermute | solution.py:13
  28.6 0.1 maximum_select_fusion
  28.8 0.1 maximum_maximum_fusion
  28.8 0.0 copy-start.6
  28.9 0.8 %fusion.71 = (bf16[640,256]{0,1:T(8,128)(2,1)}, bf16[640,256]{0,1:T(8,128)(2,1)S(1)}) fusion(bf16[640,512]{0,1:T(8,128)(2,1)S(1)} %maximum_maximum_fusion), kind=kLoop, calls=%fused_computation.104 | loop fusion | bytes 1310720 | tf_op jit(solution)/shard_map/slice | solution.py:115
  29.7 0.3 select_convert_fusion.1
  30.0 0.8 %pad_maximum_fusion = bf16[2064,128]{1,0:T(8,128)(2,1)} fusion(bf16[16,128]{1,0:T(8,128)(2,1)S(1)} %fusion.62, bf16[2048,128]{1,0:T(8,128)(2,1)S(1)} %bitcast.113), kind=kLoop, calls=%fused_computation.37 | loop fusion | flops 1056768 | bytes 1056768 | tf_op jit(solution)/shard_map/concatenate | solution.py:104
  30.8 0.1 copy.57
  30.9 3.3 %collective-permute-start.4 = (bf16[2064,128]{1,0:T(8,128)(2,1)}, bf16[2064,128]{1,0:T(8,128)(2,1)S(1)}, u32[]{:S(2)}, u32[]{:S(2)}) collective-permute-start(bf16[2064,128]{1,0:T(8,128)(2,1)} %pad_maximum_fusion), channel_id=1, source_target_pairs={{4,8},{12,16},{20,24},{0,20},{8,28},{5,9},{13,17},{21,25},{1,21},{... | collective-permute-start | bytes 1585160 | tf_op jit(solution)/shard_map/ppermute | solution.py:109
  34.3 5.4 %fusion.72 = (f32[2,8,128]{2,1,0:T(8,128)S(1)}, bf16[2,8,128,640]{2,3,1,0:T(8,128)(2,1)}) fusion(pred[128,640]{0,1:T(8,128)(4,1)} %compare_and_fusion, bf16[640,2,128,1]{0,2,3,1:T(8,128)(2,1)} %bitcast.118, bf16[128,2,8,128]{3,2,1,0:T(8,128)(2,1)S(1)} %bitcast.116), kind=kOutput, calls=%fused_computation.105 | convolution fusion | flops 681575040 | bytes 3563520 | tf_op jit(solution)/shard_map/sub | solution.py:121
  39.6 3.2 %fusion.20 = bf16[128,2,8,128]{0,3,2,1:T(8,128)(2,1)} fusion(bf16[640,2,128,1]{0,2,3,1:T(8,128)(2,1)S(1)} %bitcast.117, bf16[2,8,128,640]{2,3,1,0:T(8,128)(2,1)} %get-tuple-element.32, f32[128,2,8]{0,2,1:T(8,128)S(1)} %bitcast.123), kind=kOutput, calls=%fused_computation.21 | convolution fusion | flops 336068608 | bytes 3481600 | tf_op jit(solution)/shard_map/kgts,skd->tkgd/dot_general | solution.py:123
  42.9 4.1 %collective-permute-done.4 = bf16[2064,128]{1,0:T(8,128)(2,1)S(1)} collective-permute-done((bf16[2064,128]{1,0:T(8,128)(2,1)}, bf16[2064,128]{1,0:T(8,128)(2,1)S(1)}, u32[]{:S(2)}, u32[]{:S(2)}) %collective-permute-start.4) | collective-permute-done | bytes 528416 | tf_op jit(solution)/shard_map/ppermute | solution.py:109
  47.0 0.1 fusion.56
  47.1 1.7 %convolution_bitcast_fusion.1 = f32[128,16,128]{0,2,1:T(8,128)} fusion(bf16[128,16,128]{0,2,1:T(8,128)(2,1)S(1)} %bitcast.112, f32[16,128]{1,0:T(8,128)S(1)} %reduce_window_sum.19, pred[128,128]{1,0:T(8,128)(4,1)S(1)} %fusion.56, bf16[128,2048]{1,0:T(8,128)(2,1)S(1)} %copy-done.7, bf16[128,2048]{1,0:T(8,128)(2,1)S(1)} %copy-done), kind=kOutput, calls=%fused_computation.16 | convolution fusion | flops 135528448 | bytes 2646016 | tf_op jit(solution)/shard_map/hts,shd->thd/dot_general | solution.py:46
  48.8 0.2 collective-permute-done.5
  49.0 0.1 broadcast_select_fusion
  49.1 1.3 %slice_select_fusion = bf16[2048,128]{1,0:T(8,128)(2,1)S(1)} fusion(bf16[2064,128]{1,0:T(8,128)(2,1)} %collective-permute-done.5, bf16[2064,128]{1,0:T(8,128)(2,1)S(1)} %collective-permute-done.4, pred[]{:T(512)S(6)} %eq.61), kind=kLoop, calls=%fused_computation.44 | loop fusion | flops 262144 | bytes 1572865 | tf_op jit(solution)/shard_map/jit(_where)/select_n | solution.py:131
  50.4 0.1 copy-done.4
  50.5 0.7 %multiply_reduce_fusion = (f32[128]{0:T(128)S(1)}, f32[128,16,128]{0,2,1:T(8,128)S(1)}) fusion(f32[128,16,128]{0,2,1:T(8,128)S(1)} %copy-done.4, f32[128,16]{0,1:T(8,128)S(1)} %get-tuple-element.27, f32[16,128,128]{2,1,0:T(8,128)S(1)} %bitcast.108, bf16[16,128,128]{2,1,0:T(8,128)(2,1)S(1)} %bitcast.110, bf16[16,128,128]{2,1,0:T(8,128)(2,1)S(1)} %bitcast.109, ...), kind=kOutput, calls=%fused_computation.28 | convolution fusion | flops 70254464 | bytes 4727425 | tf_op jit(solution)/shard_map/thd,hde->the/dot_general | solution.py:145
  51.3 1.6 %collective-permute-start.6 = (f32[128]{0:T(128)S(1)}, f32[128]{0:T(128)S(1)}, u32[]{:S(2)}, u32[]{:S(2)}) collective-permute-start(f32[128]{0:T(128)S(1)} %get-tuple-element.33), channel_id=1, source_target_pairs={{0,1},{1,0},{2,3},{3,2},{4,5},{5,4},{6,7},{7,6},{8,9},{9,8},{10,11... | collective-permute-start | bytes 1544 | tf_op jit(solution)/shard_map/ppermute | solution.py:28
  52.9 2.0 %collective-permute-done.6 = f32[128]{0:T(128)S(1)} collective-permute-done((f32[128]{0:T(128)S(1)}, f32[128]{0:T(128)S(1)}, u32[]{:S(2)}, u32[]{:S(2)}) %collective-permute-start.6) | collective-permute-done | bytes 544 | tf_op jit(solution)/shard_map/ppermute | solution.py:28
  54.9 2.6 %collective-permute-start.7 = (f32[128]{0:T(128)S(1)}, f32[128]{0:T(128)S(1)}, u32[]{:S(2)}, u32[]{:S(2)}) collective-permute-start(f32[128]{0:T(128)S(1)} %add.93), channel_id=1, source_target_pairs={{0,2},{1,3},{2,0},{3,1},{4,6},{5,7},{6,4},{7,5},{8,10},{9,11},{10,... | collective-permute-start | bytes 1544 | tf_op jit(solution)/shard_map/ppermute | solution.py:28
  57.5 2.0 %copy.47 = bf16[128,2048]{1,0:T(8,128)(2,1)} copy(bf16[128,2048]{0,1:T(8,128)(2,1)} %bitcast.115) | data formatting | bytes 1048576
  59.5 0.3 copy.46
  59.9 1.1 %multiply_convert_fusion = bf16[128,2048]{1,0:T(8,128)(2,1)} fusion(bf16[128,2048]{1,0:T(8,128)(2,1)S(1)} %copy-done.5, f32[128,2048]{1,0:T(8,128)S(1)} %copy.46, f32[2048]{0:T(1024)S(1)} %copy-done.10, f32[128]{0:T(128)S(1)} %add_rsqrt_fusion), kind=kLoop, calls=%fused_computation.27 | loop fusion | flops 2097152 | bytes 2105856 | tf_op jit(solution)/shard_map/convert_element_type | solution.py:160
  (36 shorter events, 0.2 us)
Async XLA Ops:
  0.6 46.4 %copy-start = (bf16[128,2048]{1,0:T(8,128)(2,1)S(1)}, bf16[128,2048]{1,0:T(8,128)(2,1)}, u32[]{:S(2)}) copy-start(bf16[128,2048]{1,0:T(8,128)(2,1)} %param.11) | copy-start | bytes 1572868
  4.2 5.5 %copy-start.8 = (bf16[128,256]{1,0:T(8,128)(2,1)S(1)}, bf16[128,256]{1,0:T(8,128)(2,1)}, u32[]{:S(2)}) copy-start(bf16[128,256]{1,0:T(8,128)(2,1)} %param.18) | copy-start | bytes 196612
  4.3 5.6 %copy-start.9 = (bf16[128,256]{1,0:T(8,128)(2,1)S(1)}, bf16[128,256]{1,0:T(8,128)(2,1)}, u32[]{:S(2)}) copy-start(bf16[128,256]{1,0:T(8,128)(2,1)} %param.19) | copy-start | bytes 196612
  5.6 2.6 %copy-start.2 = (bf16[128,2048]{0,1:T(8,128)(2,1)}, bf16[128,2048]{0,1:T(8,128)(2,1)S(1)}, u32[]{:S(2)}) copy-start(bf16[128,2048]{0,1:T(8,128)(2,1)S(1)} %copy.54) | copy-start | bytes 1572868
  9.3 20.3 %collective-permute-start = (f32[2056,128]{1,0:T(8,128)}, f32[2056,128]{1,0:T(8,128)S(1)}, u32[]{:S(2)}, u32[]{:S(2)}) collective-permute-start(f32[2056,128]{1,0:T(8,128)} %select_maximum_fusion), channel_id=1, source_target_pairs={{0,4},{4,0},{8,12},{12,8},{16,20},{20,16},{24,28},{28,24},{1,5},{5... | collective-permute-start | bytes 3158024 | tf_op jit(solution)/shard_map/ppermute | solution.py:90
  10.0 2.2 %collective-permute-start.1 = (bf16[128,512]{0,1:T(8,128)(2,1)S(1)}, bf16[128,512]{0,1:T(8,128)(2,1)S(1)}, u32[]{:S(2)}, u32[]{:S(2)}) collective-permute-start(bf16[128,512]{0,1:T(8,128)(2,1)S(1)} %pad_maximum_fusion.2), channel_id=1, source_target_pairs={{0,4},{4,0},{8,12},{12,8},{16,20},{20,16},{24,28},{28,24},{1,5},{5... | collective-permute-start | bytes 393224 | tf_op jit(solution)/shard_map/ppermute | solution.py:80
  12.3 16.3 %collective-permute-start.2 = (bf16[256,512]{0,1:T(8,128)(2,1)S(1)}, bf16[256,512]{0,1:T(8,128)(2,1)S(1)}, u32[]{:S(2)}, u32[]{:S(2)}) collective-permute-start(bf16[256,512]{0,1:T(8,128)(2,1)S(1)} %pad_maximum_fusion.1), channel_id=1, source_target_pairs={{0,16},{4,20},{8,24},{12,28},{1,17},{5,21},{9,25},{13,29},{2,18},{... | collective-permute-start | bytes 786440 | tf_op jit(solution)/shard_map/ppermute | solution.py:13
  17.2 11.5 %collective-permute-start.3 = (bf16[256,512]{0,1:T(8,128)(2,1)S(1)}, bf16[256,512]{0,1:T(8,128)(2,1)S(1)}, u32[]{:S(2)}, u32[]{:S(2)}) collective-permute-start(bf16[256,512]{0,1:T(8,128)(2,1)S(1)} %pad_maximum_fusion.1), channel_id=1, source_target_pairs={{0,8},{4,12},{8,16},{12,20},{16,24},{20,28},{1,9},{5,13},{9,17},{1... | collective-permute-start | bytes 786440 | tf_op jit(solution)/shard_map/ppermute | solution.py:13
  28.8 2.0 %copy-start.6 = (bf16[128,2048]{1,0:T(8,128)(2,1)S(1)}, bf16[128,2048]{1,0:T(8,128)(2,1)}, u32[]{:S(2)}) copy-start(bf16[128,2048]{1,0:T(8,128)(2,1)} %param.17) | copy-start | bytes 1572868
  29.6 19.1 %copy-start.1 = (f32[2056,128]{1,0:T(8,128)}, f32[2056,128]{1,0:T(8,128)S(1)}, u32[]{:S(2)}) copy-start(f32[2056,128]{1,0:T(8,128)S(1)} %collective-permute-done) | copy-start | bytes 3158020
  30.9 16.0 %collective-permute-start.4 = (bf16[2064,128]{1,0:T(8,128)(2,1)}, bf16[2064,128]{1,0:T(8,128)(2,1)S(1)}, u32[]{:S(2)}, u32[]{:S(2)}) collective-permute-start(bf16[2064,128]{1,0:T(8,128)(2,1)} %pad_maximum_fusion), channel_id=1, source_target_pairs={{4,8},{12,16},{20,24},{0,20},{8,28},{5,9},{13,17},{21,25},{1,21},{... | collective-permute-start | bytes 1585160 | tf_op jit(solution)/shard_map/ppermute | solution.py:109
  39.6 7.4 %copy-start.3 = (bf16[128,2048]{0,1:T(8,128)(2,1)S(1)}, bf16[128,2048]{0,1:T(8,128)(2,1)}, u32[]{:S(2)}) copy-start(bf16[128,2048]{0,1:T(8,128)(2,1)} %copy-done.2) | copy-start | bytes 1572868
  39.6 7.4 %copy-start.7 = (bf16[128,2048]{1,0:T(8,128)(2,1)S(1)}, bf16[128,2048]{1,0:T(8,128)(2,1)}, u32[]{:S(2)}) copy-start(bf16[128,2048]{1,0:T(8,128)(2,1)} %param.13) | copy-start | bytes 1572868
  46.9 2.0 %collective-permute-start.5 = (bf16[2064,128]{1,0:T(8,128)(2,1)S(1)}, bf16[2064,128]{1,0:T(8,128)(2,1)}, u32[]{:S(2)}, u32[]{:S(2)}) collective-permute-start(bf16[2064,128]{1,0:T(8,128)(2,1)S(1)} %collective-permute-done.4), channel_id=1, source_target_pairs={{0,4},{4,0},{8,12},{12,8},{16,20},{20,16},{24,28},{28,24},{1,5},{5... | collective-permute-start | bytes 1585160 | tf_op jit(solution)/shard_map/ppermute | solution.py:129
  48.8 1.6 %slice-start = ((f32[2056,128]{1,0:T(8,128)}), f32[2048,128]{1,0:T(8,128)S(1)}, s32[]{:S(2)}) async-start(f32[2056,128]{1,0:T(8,128)} %copy-done.1), calls=%async_computation | async-start | bytes 2097152 | tf_op jit(solution)/shard_map/slice | solution.py:91
  48.8 1.7 %copy-start.4 = (f32[128,16,128]{0,2,1:T(8,128)S(1)}, f32[128,16,128]{0,2,1:T(8,128)}, u32[]{:S(2)}) copy-start(f32[128,16,128]{0,2,1:T(8,128)} %convolution_bitcast_fusion.1) | copy-start | bytes 3145732
  51.2 8.6 %copy-start.5 = (bf16[128,2048]{1,0:T(8,128)(2,1)S(1)}, bf16[128,2048]{1,0:T(8,128)(2,1)}, u32[]{:S(2)}) copy-start(bf16[128,2048]{1,0:T(8,128)(2,1)} %param.15) | copy-start | bytes 1572868
  51.2 8.6 %copy-start.10 = (f32[2048]{0:T(1024)S(1)}, f32[2048]{0:T(1024)}, u32[]{:S(2)}) copy-start(f32[2048]{0:T(1024)} %param.16) | copy-start | bytes 24580
  51.3 3.6 %collective-permute-start.6 = (f32[128]{0:T(128)S(1)}, f32[128]{0:T(128)S(1)}, u32[]{:S(2)}, u32[]{:S(2)}) collective-permute-start(f32[128]{0:T(128)S(1)} %get-tuple-element.33), channel_id=1, source_target_pairs={{0,1},{1,0},{2,3},{3,2},{4,5},{5,4},{6,7},{7,6},{8,9},{9,8},{10,11... | collective-permute-start | bytes 1544 | tf_op jit(solution)/shard_map/ppermute | solution.py:28
  54.9 5.0 %collective-permute-start.7 = (f32[128]{0:T(128)S(1)}, f32[128]{0:T(128)S(1)}, u32[]{:S(2)}, u32[]{:S(2)}) collective-permute-start(f32[128]{0:T(128)S(1)} %add.93), channel_id=1, source_target_pairs={{0,2},{1,3},{2,0},{3,1},{4,6},{5,7},{6,4},{7,5},{8,10},{9,11},{10,... | collective-permute-start | bytes 1544 | tf_op jit(solution)/shard_map/ppermute | solution.py:28

commit v19 on v17

--- a/solution.py
+++ b/solution.py
@@ -37,7 +37,9 @@
 
 def block_terms(query, lookup_array, values, decay, docs, before, last):
     rows = docs.shape[0]
-    level = jnp.cumsum(decay, axis=1)
+    span = decay.shape[1]
+    upto = (jnp.arange(span)[:, None] <= jnp.arange(span)[None, :]).astype(jnp.float32)
+    level = jnp.dot(decay, upto, precision=lax.Precision.HIGHEST)
     order = jnp.arange(rows)
     same = (docs[:, None] == docs[None, :]) & (order[None, :] <= order[:, None])
     scores = jnp.einsum("thd,shd->hts", query, lookup_array, preferred_element_type=jnp.float32)

time: 55.9 us -> 55.7 us (level)
  other arithmetic: 9.26 us -> 8.26 us
  matrix products: 12.4 us -> 13.2 us
    another operation x2 -> x1, other arithmetic: 1.83 us -> 0.83 us  [the longest x1 1 us: block_terms(): level = jnp.cumsum(decay, axis=1)]
    dot_general x0 -> x1, matrix products: none -> 0.82 us  [block_terms(): level = jnp.dot(decay, upto, precision=lax.Precision.HIGHEST)]
  transfers between devices with their start and end apart: 9 -> 9, of which waited for: 4 -> 4; matrix products, arithmetic and copies ran while one was open for 40% -> 39% of each run, Pallas kernels for 0% -> 0%
where the time goes in v19:
time: 55.7 us; the launch traced here: 55.2 us
  starting transfers between devices  18.1 us (32%)
  matrix products  13.2 us (24%)
  other arithmetic  8.26 us (15%)
  local copies, waits for them, and re-layouts  6.85 us (12%)
  waiting for transfers between devices  6.52 us (12%)
  between operations  2.28 us (4%)
    ppermute x4, starting transfers between devices, from_behind(): return lax.ppermute(shard, axis, pairs)  11.4 us
    sub x1, matrix products, local(): expd = jnp.where(allowed, jnp.exp(jnp.minimum(scores - top, 0.0)), 0.0)  5.37 us
    unnamed x26, local copies, waits for them, and re-layouts  4.36 us
    ppermute x2, starting transfers between devices, all_sum(): x = x + lax.ppermute(x, axis, [(i, i ^ bit) for i in range(count)])  4.24 us
    ppermute x1, waiting for transfers between devices, local(): received = lax.ppermute(packet, 'ctx', routes)  3.85 us
    dot_general x1, matrix products, local(): jnp.einsum('kgts,skd->tkgd', expd.astype(jnp.bfloat16), all_values, prefe...  3.21 us
    ppermute x2, waiting for transfers between devices, all_sum(): x = x + lax.ppermute(x, axis, [(i, i ^ bit) for i in range(count)])  1.97 us
    dot_general x1, matrix products, block_terms(): jnp.einsum('hts,shd->thd', weights, values, preferred_element_type=jnp.fl...  1.72 us
  transfers between devices with their start and end apart: 9, of which 4 were waited for; matrix products, arithmetic and copies ran while one was open for 39% of the time, Pallas kernels for 0%

profile of v19, /device:TPU:0, one launch (start us, length us, event | category | flops | bytes accessed | tf_op | source)
XLA Modules:
  0.0 55.2 jit_solution(16691987753943485200)
XLA Ops:
  0.6 0.0 copy-start
  0.6 1.0 %copy.39 = bf16[128,256]{0,1:T(8,128)(2,1)S(1)} copy(bf16[128,256]{1,0:T(8,128)(2,1)} %param.18) | data formatting | bytes 131072 | tf_op args[8]
  1.7 1.0 %copy.40 = bf16[128,256]{0,1:T(8,128)(2,1)S(1)} copy(bf16[128,256]{1,0:T(8,128)(2,1)} %param.19) | data formatting | bytes 131072 | tf_op args[9]
  2.6 4.9 %collective-permute-start.1 = (bf16[128,512]{0,1:T(8,128)(2,1)S(1)}, bf16[128,512]{0,1:T(8,128)(2,1)S(1)}, u32[]{:S(2)}, u32[]{:S(2)}) collective-permute-start(bf16[128,512]{0,1:T(8,128)(2,1)S(1)} %pad_maximum_fusion.1), channel_id=1, source_target_pairs={{0,16},{4,20},{8,24},{12,28},{1,17},{5,21},{9,25},{13,29},{2,18},{... | collective-permute-start | bytes 393224 | tf_op jit(solution)/shard_map/ppermute | solution.py:13
  7.5 2.6 %collective-permute-start.2 = (bf16[128,512]{0,1:T(8,128)(2,1)S(1)}, bf16[128,512]{0,1:T(8,128)(2,1)S(1)}, u32[]{:S(2)}, u32[]{:S(2)}) collective-permute-start(bf16[128,512]{0,1:T(8,128)(2,1)S(1)} %pad_maximum_fusion.1), channel_id=1, source_target_pairs={{0,12},{4,16},{8,20},{12,24},{16,28},{1,13},{5,17},{9,21},{13,25},... | collective-permute-start | bytes 393224 | tf_op jit(solution)/shard_map/ppermute | solution.py:13
  10.1 2.1 %collective-permute-start.3 = (bf16[128,512]{0,1:T(8,128)(2,1)S(1)}, bf16[128,512]{0,1:T(8,128)(2,1)S(1)}, u32[]{:S(2)}, u32[]{:S(2)}) collective-permute-start(bf16[128,512]{0,1:T(8,128)(2,1)S(1)} %pad_maximum_fusion.1), channel_id=1, source_target_pairs={{0,8},{4,12},{8,16},{12,20},{16,24},{20,28},{1,9},{5,13},{9,17},{1... | collective-permute-start | bytes 393224 | tf_op jit(solution)/shard_map/ppermute | solution.py:13
  12.2 1.8 %collective-permute-start.4 = (bf16[128,512]{0,1:T(8,128)(2,1)S(1)}, bf16[128,512]{0,1:T(8,128)(2,1)S(1)}, u32[]{:S(2)}, u32[]{:S(2)}) collective-permute-start(bf16[128,512]{0,1:T(8,128)(2,1)S(1)} %pad_maximum_fusion.1), channel_id=1, source_target_pairs={{0,4},{4,8},{8,12},{12,16},{16,20},{20,24},{24,28},{1,5},{5,9},{9,... | collective-permute-start | bytes 393224 | tf_op jit(solution)/shard_map/ppermute | solution.py:13
  14.1 0.8 %reduce-window.8 = s32[6,1]{0,1:T(1,128)S(1)} reduce-window(s32[6,1]{0,1:T(1,128)} %bitcast.122, s32[]{:T(128)} %constant.20.clone.1), window={size=6x1 pad=5_0x0_0}, to_apply=%region_0.0 | reduce-window | flops 30 | bytes 52 | tf_op jit(solution)/shard_map/reduce-window.3
  14.9 0.6 %fusion.65 = (s32[]{:T(128)}, s32[]{:T(128)}) fusion(s32[]{:T(128)S(6)} %sub.52, s32[6,1]{0,1:T(1,128)S(1)} %reduce-window.8, s32[]{:T(128)S(6)} %sub.51), kind=kLoop, calls=%fused_computation.91 | loop fusion | flops 34 | bytes 40 | tf_op jit(solution)/shard_map/reduce_sum | solution.py:68
  16.2 0.1 convert_reduce_fusion.1
  16.9 0.7 %compare_convert_fusion = (f32[128]{0:T(128)S(1)}, f32[128]{0:T(128)S(1)}) fusion(s32[128]{0:T(128)S(1)} %convert_reduce_fusion.1, s32[]{:T(128)S(6)} %select_n.57, s32[]{:T(128)} %get-tuple-element.19), kind=kLoop, calls=%fused_computation.86 | loop fusion | flops 512 | bytes 1544 | tf_op jit(solution)/shard_map/convert_element_type | solution.py:144
  17.6 0.8 %fusion.57 = f32[128,16]{0,1:T(8,128)S(1)} fusion(f32[16,128]{1,0:T(8,128)} %param.14), kind=kOutput, calls=%fused_computation.64 | convolution fusion | flops 3162112 | bytes 16384 | tf_op jit(solution)/shard_map/dot_general | solution.py:42
  18.4 1.3 %copy.54 = bf16[128,2048]{0,1:T(8,128)(2,1)S(1)} copy(bf16[128,2048]{1,0:T(8,128)(2,1)} %param.12) | data formatting | bytes 1048576 | tf_op jit(solution)/shard_map/reshape | solution.py:70
  19.8 0.0 copy-start.2
  19.8 0.2 slice_reduce_fusion
  20.0 0.1 exponential_multiply_fusion
  20.1 1.4 %fusion.30 = f32[16,128,128]{2,1,0:T(8,128)S(1)} fusion(bf16[128,16,128]{0,2,1:T(8,128)(2,1)S(1)} %bitcast.109, f32[128,16]{0,1:T(8,128)S(1)} %get-tuple-element.26, bf16[128,2048]{1,0:T(8,128)(2,1)} %param.13), kind=kOutput, calls=%fused_computation.38 | convolution fusion | flops 67895296 | bytes 2105344 | tf_op jit(solution)/shard_map/shd,she->hde/dot_general | solution.py:53
  21.4 1.1 %select_maximum_fusion = f32[2056,128]{1,0:T(8,128)} fusion(f32[1,16]{1,0:T(1,128)S(1)} %bitcast.119, f32[2048,128]{1,0:T(8,128)S(1)} %bitcast.104), kind=kLoop, calls=%fused_computation.23 | loop fusion | flops 789504 | bytes 2101312 | tf_op jit(solution)/shard_map/concatenate | solution.py:85
  22.5 1.1 %collective-permute-start = (f32[2056,128]{1,0:T(8,128)}, f32[2056,128]{1,0:T(8,128)S(1)}, u32[]{:S(2)}, u32[]{:S(2)}) collective-permute-start(f32[2056,128]{1,0:T(8,128)} %select_maximum_fusion), channel_id=1, source_target_pairs={{0,4},{4,0},{8,12},{12,8},{16,20},{20,16},{24,28},{28,24},{1,5},{5... | collective-permute-start | bytes 3158024 | tf_op jit(solution)/shard_map/ppermute | solution.py:86
  23.6 0.1 convert_reduce_fusion
  23.7 0.9 %compare_and_fusion = pred[128,640]{0,1:T(8,128)(4,1)} fusion(s32[128]{0:T(128)S(1)} %iota_add_fusion.1, s32[128]{0:T(128)S(1)} %convert_reduce_fusion.1, s32[640]{0:T(1024)S(1)} %iota_add_fusion, s32[640]{0:T(1024)S(1)} %compare_select_fusion), kind=kLoop, calls=%fused_computation.59 | loop fusion | flops 245760 | bytes 88064 | tf_op jit(solution)/shard_map/and | solution.py:109
  24.6 0.0 collective-permute-done.1
  24.6 0.0 collective-permute-done.2
  24.7 0.0 collective-permute-done.3
  24.8 0.0 copy-start.6
  24.8 0.8 %fusion.72 = (bf16[640,256]{0,1:T(8,128)(2,1)}, bf16[640,256]{0,1:T(8,128)(2,1)S(1)}) fusion(bf16[640,512]{0,1:T(8,128)(2,1)S(1)} %constant_dynamic-update-slice_fusion), kind=kLoop, calls=%fused_computation.106 | loop fusion | bytes 1310720 | tf_op jit(solution)/shard_map/slice | solution.py:111
  25.6 0.5 collective-permute-done
  26.1 0.3 select_convert_fusion.1
  26.4 0.8 %pad_maximum_fusion = bf16[2064,128]{1,0:T(8,128)(2,1)} fusion(bf16[16,128]{1,0:T(8,128)(2,1)S(1)} %fusion.63, bf16[2048,128]{1,0:T(8,128)(2,1)S(1)} %bitcast.111), kind=kLoop, calls=%fused_computation.36 | loop fusion | flops 1056768 | bytes 1056768 | tf_op jit(solution)/shard_map/concatenate | solution.py:100
  27.2 0.1 copy.57
  27.4 1.3 %collective-permute-start.5 = (bf16[2064,128]{1,0:T(8,128)(2,1)}, bf16[2064,128]{1,0:T(8,128)(2,1)S(1)}, u32[]{:S(2)}, u32[]{:S(2)}) collective-permute-start(bf16[2064,128]{1,0:T(8,128)(2,1)} %pad_maximum_fusion), channel_id=1, source_target_pairs={{4,8},{12,16},{20,24},{0,20},{8,28},{5,9},{13,17},{21,25},{1,21},{... | collective-permute-start | bytes 1585160 | tf_op jit(solution)/shard_map/ppermute | solution.py:105
  28.7 5.4 %fusion.73 = (f32[2,8,128]{2,1,0:T(8,128)S(1)}, bf16[2,8,128,640]{2,3,1,0:T(8,128)(2,1)}) fusion(pred[128,640]{0,1:T(8,128)(4,1)} %compare_and_fusion, bf16[640,2,128,1]{0,2,3,1:T(8,128)(2,1)} %bitcast.116, bf16[128,2,8,128]{3,2,1,0:T(8,128)(2,1)S(1)} %bitcast.114), kind=kOutput, calls=%fused_computation.107 | convolution fusion | flops 681575040 | bytes 3563520 | tf_op jit(solution)/shard_map/sub | solution.py:117
  34.1 3.2 %fusion.20 = bf16[128,2,8,128]{0,3,2,1:T(8,128)(2,1)} fusion(bf16[640,2,128,1]{0,2,3,1:T(8,128)(2,1)S(1)} %bitcast.115, bf16[2,8,128,640]{2,3,1,0:T(8,128)(2,1)} %get-tuple-element.30, f32[128,2,8]{0,2,1:T(8,128)S(1)} %bitcast.123), kind=kOutput, calls=%fused_computation.21 | convolution fusion | flops 336068608 | bytes 3481600 | tf_op jit(solution)/shard_map/kgts,skd->tkgd/dot_general | solution.py:119
  37.3 3.8 %collective-permute-done.5 = bf16[2064,128]{1,0:T(8,128)(2,1)S(1)} collective-permute-done((bf16[2064,128]{1,0:T(8,128)(2,1)}, bf16[2064,128]{1,0:T(8,128)(2,1)S(1)}, u32[]{:S(2)}, u32[]{:S(2)}) %collective-permute-start.5) | collective-permute-done | bytes 528416 | tf_op jit(solution)/shard_map/ppermute | solution.py:105
  41.1 0.1 fusion.56
  41.3 1.7 %convolution_bitcast_fusion.1 = f32[128,16,128]{0,2,1:T(8,128)} fusion(bf16[128,16,128]{0,2,1:T(8,128)(2,1)S(1)} %bitcast.110, f32[16,128]{1,0:T(8,128)S(1)} %bitcast.118, pred[128,128]{1,0:T(8,128)(4,1)S(1)} %fusion.56, bf16[128,2048]{1,0:T(8,128)(2,1)S(1)} %copy-done.7, bf16[128,2048]{1,0:T(8,128)(2,1)S(1)} %copy-done), kind=kOutput, calls=%fused_computation.16 | convolution fusion | flops 135528448 | bytes 2646016 | tf_op jit(solution)/shard_map/hts,shd->thd/dot_general | solution.py:48
  43.0 0.2 collective-permute-done.6
  43.2 0.1 broadcast_select_fusion
  43.3 1.3 %slice_select_fusion = bf16[2048,128]{1,0:T(8,128)(2,1)S(1)} fusion(bf16[2064,128]{1,0:T(8,128)(2,1)} %collective-permute-done.6, bf16[2064,128]{1,0:T(8,128)(2,1)S(1)} %collective-permute-done.5, pred[]{:T(512)S(6)} %eq.61), kind=kLoop, calls=%fused_computation.43 | loop fusion | flops 262144 | bytes 1572865 | tf_op jit(solution)/shard_map/jit(_where)/select_n | solution.py:127
  44.6 0.1 copy-done.4
  44.7 0.7 %multiply_reduce_fusion = (f32[128]{0:T(128)S(1)}, f32[128,16,128]{0,2,1:T(8,128)S(1)}) fusion(f32[128,16,128]{0,2,1:T(8,128)S(1)} %copy-done.4, f32[128,16]{0,1:T(8,128)S(1)} %get-tuple-element.25, f32[16,128,128]{2,1,0:T(8,128)S(1)} %bitcast.106, bf16[16,128,128]{2,1,0:T(8,128)(2,1)S(1)} %bitcast.108, bf16[16,128,128]{2,1,0:T(8,128)(2,1)S(1)} %bitcast.107, ...), kind=kOutput, calls=%fused_computation.28 | convolution fusion | flops 70254464 | bytes 4727425 | tf_op jit(solution)/shard_map/thd,hde->the/dot_general | solution.py:141
  45.4 0.0 copy-start.8
  45.4 1.6 %collective-permute-start.7 = (f32[128]{0:T(128)S(1)}, f32[128]{0:T(128)S(1)}, u32[]{:S(2)}, u32[]{:S(2)}) collective-permute-start(f32[128]{0:T(128)S(1)} %get-tuple-element.31), channel_id=1, source_target_pairs={{0,1},{1,0},{2,3},{3,2},{4,5},{5,4},{6,7},{7,6},{8,9},{9,8},{10,11... | collective-permute-start | bytes 1544 | tf_op jit(solution)/shard_map/ppermute | solution.py:28
  47.1 2.0 %collective-permute-done.7 = f32[128]{0:T(128)S(1)} collective-permute-done((f32[128]{0:T(128)S(1)}, f32[128]{0:T(128)S(1)}, u32[]{:S(2)}, u32[]{:S(2)}) %collective-permute-start.7) | collective-permute-done | bytes 544 | tf_op jit(solution)/shard_map/ppermute | solution.py:28
  49.0 2.6 %collective-permute-start.8 = (f32[128]{0:T(128)S(1)}, f32[128]{0:T(128)S(1)}, u32[]{:S(2)}, u32[]{:S(2)}) collective-permute-start(f32[128]{0:T(128)S(1)} %add.93), channel_id=1, source_target_pairs={{0,2},{1,3},{2,0},{3,1},{4,6},{5,7},{6,4},{7,5},{8,10},{9,11},{10,... | collective-permute-start | bytes 1544 | tf_op jit(solution)/shard_map/ppermute | solution.py:28
  51.6 2.0 %copy.47 = bf16[128,2048]{1,0:T(8,128)(2,1)} copy(bf16[128,2048]{0,1:T(8,128)(2,1)} %bitcast.113) | data formatting | bytes 1048576
  53.7 0.3 copy.46
  54.1 1.1 %multiply_convert_fusion = bf16[128,2048]{1,0:T(8,128)(2,1)} fusion(bf16[128,2048]{1,0:T(8,128)(2,1)S(1)} %copy-done.5, f32[128,2048]{1,0:T(8,128)S(1)} %copy.46, f32[2048]{0:T(1024)S(1)} %copy-done.8, f32[128]{0:T(128)S(1)} %add_rsqrt_fusion), kind=kLoop, calls=%fused_computation.27 | loop fusion | flops 2097152 | bytes 2105856 | tf_op jit(solution)/shard_map/convert_element_type | solution.py:156
  (34 shorter events, 0.3 us)
Async XLA Ops:
  0.6 40.6 %copy-start = (bf16[128,2048]{1,0:T(8,128)(2,1)S(1)}, bf16[128,2048]{1,0:T(8,128)(2,1)}, u32[]{:S(2)}) copy-start(bf16[128,2048]{1,0:T(8,128)(2,1)} %param.11) | copy-start | bytes 1572868
  2.6 21.9 %collective-permute-start.1 = (bf16[128,512]{0,1:T(8,128)(2,1)S(1)}, bf16[128,512]{0,1:T(8,128)(2,1)S(1)}, u32[]{:S(2)}, u32[]{:S(2)}) collective-permute-start(bf16[128,512]{0,1:T(8,128)(2,1)S(1)} %pad_maximum_fusion.1), channel_id=1, source_target_pairs={{0,16},{4,20},{8,24},{12,28},{1,17},{5,21},{9,25},{13,29},{2,18},{... | collective-permute-start | bytes 393224 | tf_op jit(solution)/shard_map/ppermute | solution.py:13
  7.5 17.1 %collective-permute-start.2 = (bf16[128,512]{0,1:T(8,128)(2,1)S(1)}, bf16[128,512]{0,1:T(8,128)(2,1)S(1)}, u32[]{:S(2)}, u32[]{:S(2)}) collective-permute-start(bf16[128,512]{0,1:T(8,128)(2,1)S(1)} %pad_maximum_fusion.1), channel_id=1, source_target_pairs={{0,12},{4,16},{8,20},{12,24},{16,28},{1,13},{5,17},{9,21},{13,25},... | collective-permute-start | bytes 393224 | tf_op jit(solution)/shard_map/ppermute | solution.py:13
  10.1 14.6 %collective-permute-start.3 = (bf16[128,512]{0,1:T(8,128)(2,1)S(1)}, bf16[128,512]{0,1:T(8,128)(2,1)S(1)}, u32[]{:S(2)}, u32[]{:S(2)}) collective-permute-start(bf16[128,512]{0,1:T(8,128)(2,1)S(1)} %pad_maximum_fusion.1), channel_id=1, source_target_pairs={{0,8},{4,12},{8,16},{12,20},{16,24},{20,28},{1,9},{5,13},{9,17},{1... | collective-permute-start | bytes 393224 | tf_op jit(solution)/shard_map/ppermute | solution.py:13
  12.2 12.5 %collective-permute-start.4 = (bf16[128,512]{0,1:T(8,128)(2,1)S(1)}, bf16[128,512]{0,1:T(8,128)(2,1)S(1)}, u32[]{:S(2)}, u32[]{:S(2)}) collective-permute-start(bf16[128,512]{0,1:T(8,128)(2,1)S(1)} %pad_maximum_fusion.1), channel_id=1, source_target_pairs={{0,4},{4,8},{8,12},{12,16},{16,20},{20,24},{24,28},{1,5},{5,9},{9,... | collective-permute-start | bytes 393224 | tf_op jit(solution)/shard_map/ppermute | solution.py:13
  19.8 1.6 %copy-start.2 = (bf16[128,2048]{0,1:T(8,128)(2,1)}, bf16[128,2048]{0,1:T(8,128)(2,1)S(1)}, u32[]{:S(2)}) copy-start(bf16[128,2048]{0,1:T(8,128)(2,1)S(1)} %copy.54) | copy-start | bytes 1572868
  22.5 3.6 %collective-permute-start = (f32[2056,128]{1,0:T(8,128)}, f32[2056,128]{1,0:T(8,128)S(1)}, u32[]{:S(2)}, u32[]{:S(2)}) collective-permute-start(f32[2056,128]{1,0:T(8,128)} %select_maximum_fusion), channel_id=1, source_target_pairs={{0,4},{4,0},{8,12},{12,8},{16,20},{20,16},{24,28},{28,24},{1,5},{5... | collective-permute-start | bytes 3158024 | tf_op jit(solution)/shard_map/ppermute | solution.py:86
  24.8 2.5 %copy-start.6 = (bf16[128,2048]{1,0:T(8,128)(2,1)S(1)}, bf16[128,2048]{1,0:T(8,128)(2,1)}, u32[]{:S(2)}) copy-start(bf16[128,2048]{1,0:T(8,128)(2,1)} %param.17) | copy-start | bytes 1572868
  26.1 16.9 %copy-start.1 = (f32[2056,128]{1,0:T(8,128)}, f32[2056,128]{1,0:T(8,128)S(1)}, u32[]{:S(2)}) copy-start(f32[2056,128]{1,0:T(8,128)S(1)} %collective-permute-done) | copy-start | bytes 3158020
  27.4 13.8 %collective-permute-start.5 = (bf16[2064,128]{1,0:T(8,128)(2,1)}, bf16[2064,128]{1,0:T(8,128)(2,1)S(1)}, u32[]{:S(2)}, u32[]{:S(2)}) collective-permute-start(bf16[2064,128]{1,0:T(8,128)(2,1)} %pad_maximum_fusion), channel_id=1, source_target_pairs={{4,8},{12,16},{20,24},{0,20},{8,28},{5,9},{13,17},{21,25},{1,21},{... | collective-permute-start | bytes 1585160 | tf_op jit(solution)/shard_map/ppermute | solution.py:105
  34.1 7.2 %copy-start.3 = (bf16[128,2048]{0,1:T(8,128)(2,1)S(1)}, bf16[128,2048]{0,1:T(8,128)(2,1)}, u32[]{:S(2)}) copy-start(bf16[128,2048]{0,1:T(8,128)(2,1)} %copy-done.2) | copy-start | bytes 1572868
  34.1 7.2 %copy-start.7 = (bf16[128,2048]{1,0:T(8,128)(2,1)S(1)}, bf16[128,2048]{1,0:T(8,128)(2,1)}, u32[]{:S(2)}) copy-start(bf16[128,2048]{1,0:T(8,128)(2,1)} %param.13) | copy-start | bytes 1572868
  41.1 2.0 %collective-permute-start.6 = (bf16[2064,128]{1,0:T(8,128)(2,1)S(1)}, bf16[2064,128]{1,0:T(8,128)(2,1)}, u32[]{:S(2)}, u32[]{:S(2)}) collective-permute-start(bf16[2064,128]{1,0:T(8,128)(2,1)S(1)} %collective-permute-done.5), channel_id=1, source_target_pairs={{0,4},{4,0},{8,12},{12,8},{16,20},{20,16},{24,28},{28,24},{1,5},{5... | collective-permute-start | bytes 1585160 | tf_op jit(solution)/shard_map/ppermute | solution.py:125
  43.0 1.6 %slice-start = ((f32[2056,128]{1,0:T(8,128)}), f32[2048,128]{1,0:T(8,128)S(1)}, s32[]{:S(2)}) async-start(f32[2056,128]{1,0:T(8,128)} %copy-done.1), calls=%async_computation | async-start | bytes 2097152 | tf_op jit(solution)/shard_map/slice | solution.py:87
  43.0 1.7 %copy-start.4 = (f32[128,16,128]{0,2,1:T(8,128)S(1)}, f32[128,16,128]{0,2,1:T(8,128)}, u32[]{:S(2)}) copy-start(f32[128,16,128]{0,2,1:T(8,128)} %convolution_bitcast_fusion.1) | copy-start | bytes 3145732
  45.4 8.6 %copy-start.5 = (bf16[128,2048]{1,0:T(8,128)(2,1)S(1)}, bf16[128,2048]{1,0:T(8,128)(2,1)}, u32[]{:S(2)}) copy-start(bf16[128,2048]{1,0:T(8,128)(2,1)} %param.15) | copy-start | bytes 1572868
  45.4 8.6 %copy-start.8 = (f32[2048]{0:T(1024)S(1)}, f32[2048]{0:T(1024)}, u32[]{:S(2)}) copy-start(f32[2048]{0:T(1024)} %param.16) | copy-start | bytes 24580
  45.4 3.6 %collective-permute-start.7 = (f32[128]{0:T(128)S(1)}, f32[128]{0:T(128)S(1)}, u32[]{:S(2)}, u32[]{:S(2)}) collective-permute-start(f32[128]{0:T(128)S(1)} %get-tuple-element.31), channel_id=1, source_target_pairs={{0,1},{1,0},{2,3},{3,2},{4,5},{5,4},{6,7},{7,6},{8,9},{9,8},{10,11... | collective-permute-start | bytes 1544 | tf_op jit(solution)/shard_map/ppermute | solution.py:28
  49.0 5.0 %collective-permute-start.8 = (f32[128]{0:T(128)S(1)}, f32[128]{0:T(128)S(1)}, u32[]{:S(2)}, u32[]{:S(2)}) collective-permute-start(f32[128]{0:T(128)S(1)} %add.93), channel_id=1, source_target_pairs={{0,2},{1,3},{2,0},{3,1},{4,6},{5,7},{6,4},{7,5},{8,10},{9,11},{10,... | collective-permute-start | bytes 1544 | tf_op jit(solution)/shard_map/ppermute | solution.py:28

commit v20 on v17

--- a/solution.py
+++ b/solution.py
@@ -72,7 +72,7 @@
     )
     count = lax.axis_size("ctx")
     odd = (shard % 2) == 1
-    pair = jnp.concatenate([soft_k, soft_v], axis=1)
+    pair = jnp.concatenate([soft_k, soft_v], axis=0)
     kv_width = soft_k.shape[1]
     n_state = heads_here * DH
     state_rows = state.reshape(n_state, DH)
@@ -106,8 +106,9 @@
     key_docs = jnp.where(key_pos >= 0, document_of(key_pos, doc_lengths), -1)
     allowed = (key_docs[None, :] == docs[:, None]) & (key_pos[None, :] <= positions[:, None])
     soft_query = soft_q.reshape(rows, kv_here, group, DH)
-    all_keys = window[:, :kv_width].reshape(span_rows, kv_here, DH)
-    all_values = window[:, kv_width:].reshape(span_rows, kv_here, DH)
+    paired = window.reshape(SPAN + 1, 2, rows, kv_width)
+    all_keys = paired[:, 0].reshape(span_rows, kv_here, DH)
+    all_values = paired[:, 1].reshape(span_rows, kv_here, DH)
     scores = jnp.einsum(
         "tkgd,skd->kgts", soft_query, all_keys, preferred_element_type=jnp.float32
     ) * DH ** (-0.5)

time: 55.9 us -> 55.6 us (level)
  waiting for transfers between devices: 6.52 us -> 5.81 us
  local copies, waits for them, and re-layouts: 6.82 us -> 7.42 us
    another operation x0 -> x2, local copies, waits for them, and re-layouts: none -> 1.6 us  [the longest x1 0.8 us: local(): all_keys = paired[:, 0].reshape(span_rows, kv_here, DH)]
    unnamed x26 -> x33, local copies, waits for them, and re-layouts: 4.36 us -> 3.29 us
    concatenate x0 -> x2, local copies, waits for them, and re-layouts: none -> 0.85 us  [the longest x1 0.84 us: local(): pair = jnp.concatenate([soft_k, soft_v], axis=0)]
    slice x1 -> x0, local copies, waits for them, and re-layouts: 0.78 us -> none  [local(): all_keys = window[:, :kv_width].reshape(span_rows, kv_here, DH)]
  transfers between devices with their start and end apart: 9 -> 9, of which waited for: 4 -> 3; matrix products, arithmetic and copies ran while one was open for 40% -> 41% of each run, Pallas kernels for 0% -> 0%
where the time goes in v20:
time: 55.6 us; the launch traced here: 55.1 us
  starting transfers between devices  18 us (32%)
  matrix products  12.3 us (22%)
  other arithmetic  9.21 us (17%)
  local copies, waits for them, and re-layouts  7.42 us (13%)
  waiting for transfers between devices  5.81 us (10%)
  between operations  2.32 us (4%)
    ppermute x4, starting transfers between devices, from_behind(): return lax.ppermute(shard, axis, pairs)  11.4 us
    sub x1, matrix products, local(): expd = jnp.where(allowed, jnp.exp(jnp.minimum(scores - top, 0.0)), 0.0)  5.2 us
    ppermute x2, starting transfers between devices, all_sum(): x = x + lax.ppermute(x, axis, [(i, i ^ bit) for i in range(count)])  4.23 us
    ppermute x1, waiting for transfers between devices, local(): received = lax.ppermute(packet, 'ctx', routes)  3.63 us
    unnamed x33, local copies, waits for them, and re-layouts  3.29 us
    dot_general x1, matrix products, local(): jnp.einsum('kgts,skd->tkgd', expd.astype(jnp.bfloat16), all_values, prefe...  3.27 us
    ppermute x2, waiting for transfers between devices, all_sum(): x = x + lax.ppermute(x, axis, [(i, i ^ bit) for i in range(count)])  1.97 us
    dot_general x1, matrix products, block_terms(): jnp.einsum('hts,shd->thd', weights, values, preferred_element_type=jnp.fl...  1.72 us
  transfers between devices with their start and end apart: 9, of which 3 were waited for; matrix products, arithmetic and copies ran while one was open for 41% of the time, Pallas kernels for 0%

profile of v20, /device:TPU:0, one launch (start us, length us, event | category | flops | bytes accessed | tf_op | source)
XLA Modules:
  0.0 55.1 jit_solution(2771511489660115671)
XLA Ops:
  0.6 0.0 copy-start
  0.6 0.9 %constant_dynamic-update-slice_fusion.1 = bf16[256,256]{1,0:T(8,128)(2,1)S(1)} fusion(bf16[128,256]{1,0:T(8,128)(2,1)} %param.18), kind=kLoop, calls=%fused_computation.69 | loop fusion | bytes 131072
  1.5 0.8 %constant_dynamic-update-slice_fusion = bf16[256,256]{1,0:T(8,128)(2,1)S(1)} fusion(bf16[256,256]{1,0:T(8,128)(2,1)S(1)} %constant_dynamic-update-slice_fusion.1, bf16[128,256]{1,0:T(8,128)(2,1)} %param.19), kind=kLoop, calls=%fused_computation.68 | loop fusion | bytes 131072 | tf_op jit(solution)/shard_map/concatenate | solution.py:75
  2.4 4.9 %collective-permute-start.1 = (bf16[256,256]{1,0:T(8,128)(2,1)S(1)}, bf16[256,256]{1,0:T(8,128)(2,1)S(1)}, u32[]{:S(2)}, u32[]{:S(2)}) collective-permute-start(bf16[256,256]{1,0:T(8,128)(2,1)S(1)} %constant_dynamic-update-slice_fusion), channel_id=1, source_target_pairs={{0,16},{4,20},{8,24},{12,28},{1,17},{5,21},{9,25},{13,29},{2,18},{... | collective-permute-start | bytes 393224 | tf_op jit(solution)/shard_map/ppermute | solution.py:13
  7.3 2.6 %collective-permute-start.2 = (bf16[256,256]{1,0:T(8,128)(2,1)S(1)}, bf16[256,256]{1,0:T(8,128)(2,1)S(1)}, u32[]{:S(2)}, u32[]{:S(2)}) collective-permute-start(bf16[256,256]{1,0:T(8,128)(2,1)S(1)} %constant_dynamic-update-slice_fusion), channel_id=1, source_target_pairs={{0,12},{4,16},{8,20},{12,24},{16,28},{1,13},{5,17},{9,21},{13,25},... | collective-permute-start | bytes 393224 | tf_op jit(solution)/shard_map/ppermute | solution.py:13
  9.8 2.1 %collective-permute-start.3 = (bf16[256,256]{1,0:T(8,128)(2,1)S(1)}, bf16[256,256]{1,0:T(8,128)(2,1)S(1)}, u32[]{:S(2)}, u32[]{:S(2)}) collective-permute-start(bf16[256,256]{1,0:T(8,128)(2,1)S(1)} %constant_dynamic-update-slice_fusion), channel_id=1, source_target_pairs={{0,8},{4,12},{8,16},{12,20},{16,24},{20,28},{1,9},{5,13},{9,17},{1... | collective-permute-start | bytes 393224 | tf_op jit(solution)/shard_map/ppermute | solution.py:13
  12.0 1.8 %collective-permute-start.4 = (bf16[256,256]{1,0:T(8,128)(2,1)S(1)}, bf16[256,256]{1,0:T(8,128)(2,1)S(1)}, u32[]{:S(2)}, u32[]{:S(2)}) collective-permute-start(bf16[256,256]{1,0:T(8,128)(2,1)S(1)} %constant_dynamic-update-slice_fusion), channel_id=1, source_target_pairs={{0,4},{4,8},{8,12},{12,16},{16,20},{20,24},{24,28},{1,5},{5,9},{9,... | collective-permute-start | bytes 393224 | tf_op jit(solution)/shard_map/ppermute | solution.py:13
  13.8 0.8 %reduce-window.8 = s32[6,1]{0,1:T(1,128)S(1)} reduce-window(s32[6,1]{0,1:T(1,128)} %bitcast.125, s32[]{:T(128)} %constant.23.clone.1), window={size=6x1 pad=5_0x0_0}, to_apply=%region_0.0 | reduce-window | flops 30 | bytes 52 | tf_op jit(solution)/shard_map/reduce-window.3
  14.7 0.6 %fusion.69 = (s32[]{:T(128)}, s32[]{:T(128)}) fusion(s32[]{:T(128)S(6)} %sub.53, s32[6,1]{0,1:T(1,128)S(1)} %reduce-window.8, s32[]{:T(128)S(6)} %sub.52), kind=kLoop, calls=%fused_computation.96 | loop fusion | flops 34 | bytes 40 | tf_op jit(solution)/shard_map/reduce_sum | solution.py:66
  15.9 0.1 convert_reduce_fusion.1
  16.7 0.7 %compare_convert_fusion = (f32[128]{0:T(128)S(1)}, f32[128]{0:T(128)S(1)}) fusion(s32[128]{0:T(128)S(1)} %convert_reduce_fusion.1, s32[]{:T(128)S(6)} %select_n.57, s32[]{:T(128)} %get-tuple-element.19), kind=kLoop, calls=%fused_computation.91 | loop fusion | flops 512 | bytes 1544 | tf_op jit(solution)/shard_map/convert_element_type | solution.py:143
  17.3 1.3 %copy.60 = bf16[128,2048]{0,1:T(8,128)(2,1)S(1)} copy(bf16[128,2048]{1,0:T(8,128)(2,1)} %param.12) | data formatting | bytes 1048576 | tf_op jit(solution)/shard_map/reshape | solution.py:68
  18.7 0.0 copy-start.2
  18.7 1.0 %reduce_window_sum.19 = f32[16,128]{1,0:T(8,128)S(1)} reduce-window(f32[16,128]{1,0:T(8,128)} %param.14, f32[]{:T(128)} %constant.47.clone.1), window={size=1x128 pad=0_0x127_0}, to_apply=%region_2.3 | reduce-window | flops 260096 | bytes 16388 | tf_op jit(solution)/shard_map/jit(cumsum)/reduce_window_sum | solution.py:40
  19.7 0.2 slice_reduce_fusion
  19.9 0.1 multiply_bitcast_fusion
  19.9 0.0 copy-start.10
  20.0 1.4 %fusion.30 = f32[16,128,128]{2,1,0:T(8,128)S(1)} fusion(bf16[128,16,128]{0,2,1:T(8,128)(2,1)S(1)} %bitcast.113, f32[128,16]{0,1:T(8,128)S(1)} %get-tuple-element.26, bf16[128,2048]{1,0:T(8,128)(2,1)} %param.13), kind=kOutput, calls=%fused_computation.38 | convolution fusion | flops 67895296 | bytes 2105344 | tf_op jit(solution)/shard_map/shd,she->hde/dot_general | solution.py:51
  21.4 1.1 %select_maximum_fusion = f32[2056,128]{1,0:T(8,128)} fusion(f32[1,16]{1,0:T(1,128)S(1)} %bitcast.122, f32[2048,128]{1,0:T(8,128)S(1)} %bitcast.108), kind=kLoop, calls=%fused_computation.23 | loop fusion | flops 789504 | bytes 2101312 | tf_op jit(solution)/shard_map/concatenate | solution.py:83
  22.4 1.1 %collective-permute-start = (f32[2056,128]{1,0:T(8,128)}, f32[2056,128]{1,0:T(8,128)S(1)}, u32[]{:S(2)}, u32[]{:S(2)}) collective-permute-start(f32[2056,128]{1,0:T(8,128)} %select_maximum_fusion), channel_id=1, source_target_pairs={{0,4},{4,0},{8,12},{12,8},{16,20},{20,16},{24,28},{28,24},{1,5},{5... | collective-permute-start | bytes 3158024 | tf_op jit(solution)/shard_map/ppermute | solution.py:84
  23.5 0.1 convert_reduce_fusion
  23.6 0.9 %compare_and_fusion = pred[128,640]{0,1:T(8,128)(4,1)} fusion(s32[128]{0:T(128)S(1)} %iota_add_fusion.1, s32[128]{0:T(128)S(1)} %convert_reduce_fusion.1, s32[640]{0:T(1024)S(1)} %iota_add_fusion, s32[640]{0:T(1024)S(1)} %compare_select_fusion), kind=kLoop, calls=%fused_computation.62 | loop fusion | flops 245760 | bytes 88064 | tf_op jit(solution)/shard_map/and | solution.py:107
  24.6 0.0 collective-permute-done.3
  24.7 0.8 %reshape_squeeze.7 = bf16[640,2,128]{2,1,0:T(2,128)(2,1)} reshape(bf16[5,1,128,256]{3,2,0,1:T(8,128)(2,1)S(1)} %get-tuple-element.24) | data formatting | bytes 655360 | tf_op jit(solution)/shard_map/reshape;squeeze | solution.py:110
  25.5 0.8 %reshape_squeeze.6 = bf16[640,2,128]{2,1,0:T(2,128)(2,1)} reshape(bf16[5,1,128,256]{3,2,0,1:T(8,128)(2,1)S(1)} %get-tuple-element.23) | data formatting | bytes 655360 | tf_op jit(solution)/shard_map/reshape;squeeze | solution.py:111
  26.3 0.0 collective-permute-done
  26.4 0.3 select_convert_fusion.1
  26.6 0.8 %pad_maximum_fusion = bf16[2064,128]{1,0:T(8,128)(2,1)} fusion(bf16[16,128]{1,0:T(8,128)(2,1)S(1)} %fusion.67, bf16[2048,128]{1,0:T(8,128)(2,1)S(1)} %bitcast.115), kind=kLoop, calls=%fused_computation.36 | loop fusion | flops 1056768 | bytes 1056768 | tf_op jit(solution)/shard_map/concatenate | solution.py:98
  27.5 0.1 copy.63
  27.6 1.3 %collective-permute-start.5 = (bf16[2064,128]{1,0:T(8,128)(2,1)}, bf16[2064,128]{1,0:T(8,128)(2,1)S(1)}, u32[]{:S(2)}, u32[]{:S(2)}) collective-permute-start(bf16[2064,128]{1,0:T(8,128)(2,1)} %pad_maximum_fusion), channel_id=1, source_target_pairs={{4,8},{12,16},{20,24},{0,20},{8,28},{5,9},{13,17},{21,25},{1,21},{... | collective-permute-start | bytes 1585160 | tf_op jit(solution)/shard_map/ppermute | solution.py:103
  29.0 5.2 %fusion.76 = (f32[2,8,128]{2,1,0:T(8,128)S(1)}, bf16[2,8,128,640]{2,3,1,0:T(8,128)(2,1)}) fusion(pred[128,640]{0,1:T(8,128)(4,1)} %compare_and_fusion, bf16[128,2,8,128]{3,2,1,0:T(8,128)(2,1)S(1)} %bitcast.119, bf16[640,2,128,1]{2,1,0,3:T(2,128)(2,1)} %bitcast.121), kind=kOutput, calls=%fused_computation.111 | convolution fusion | flops 681575040 | bytes 3563520 | tf_op jit(solution)/shard_map/sub | solution.py:116
  34.2 3.3 %fusion.20 = bf16[128,2,8,128]{0,3,2,1:T(8,128)(2,1)} fusion(bf16[2,8,128,640]{2,3,1,0:T(8,128)(2,1)} %get-tuple-element.30, f32[128,2,8]{0,2,1:T(8,128)S(1)} %bitcast.126, bf16[640,2,128,1]{2,1,0,3:T(2,128)(2,1)S(1)} %bitcast.120), kind=kOutput, calls=%fused_computation.21 | convolution fusion | flops 336068608 | bytes 3481600 | tf_op jit(solution)/shard_map/kgts,skd->tkgd/dot_general | solution.py:118
  37.4 3.6 %collective-permute-done.5 = bf16[2064,128]{1,0:T(8,128)(2,1)S(1)} collective-permute-done((bf16[2064,128]{1,0:T(8,128)(2,1)}, bf16[2064,128]{1,0:T(8,128)(2,1)S(1)}, u32[]{:S(2)}, u32[]{:S(2)}) %collective-permute-start.5) | collective-permute-done | bytes 528416 | tf_op jit(solution)/shard_map/ppermute | solution.py:103
  41.1 0.0 collective-permute-start.6
  41.1 0.1 fusion.61
  41.2 1.7 %convolution_bitcast_fusion.1 = f32[128,16,128]{0,2,1:T(8,128)} fusion(bf16[128,16,128]{0,2,1:T(8,128)(2,1)S(1)} %bitcast.114, f32[16,128]{1,0:T(8,128)S(1)} %reduce_window_sum.19, pred[128,128]{1,0:T(8,128)(4,1)S(1)} %fusion.61, bf16[128,2048]{1,0:T(8,128)(2,1)S(1)} %copy-done.7, bf16[128,2048]{1,0:T(8,128)(2,1)S(1)} %copy-done), kind=kOutput, calls=%fused_computation.16 | convolution fusion | flops 135528448 | bytes 2646016 | tf_op jit(solution)/shard_map/hts,shd->thd/dot_general | solution.py:46
  42.9 0.2 collective-permute-done.6
  43.1 0.1 broadcast_select_fusion
  43.2 1.3 %slice_select_fusion = bf16[2048,128]{1,0:T(8,128)(2,1)S(1)} fusion(bf16[2064,128]{1,0:T(8,128)(2,1)} %collective-permute-done.6, bf16[2064,128]{1,0:T(8,128)(2,1)S(1)} %collective-permute-done.5, pred[]{:T(512)S(6)} %eq.61), kind=kLoop, calls=%fused_computation.43 | loop fusion | flops 262144 | bytes 1572865 | tf_op jit(solution)/shard_map/jit(_where)/select_n | solution.py:126
  44.5 0.1 copy-done.4
  44.6 0.7 %multiply_reduce_fusion = (f32[128]{0:T(128)S(1)}, f32[128,16,128]{0,2,1:T(8,128)S(1)}) fusion(f32[128,16,128]{0,2,1:T(8,128)S(1)} %copy-done.4, f32[128,16]{0,1:T(8,128)S(1)} %get-tuple-element.25, f32[16,128,128]{2,1,0:T(8,128)S(1)} %bitcast.110, bf16[16,128,128]{2,1,0:T(8,128)(2,1)S(1)} %bitcast.112, bf16[16,128,128]{2,1,0:T(8,128)(2,1)S(1)} %bitcast.111, ...), kind=kOutput, calls=%fused_computation.28 | convolution fusion | flops 70254464 | bytes 4727425 | tf_op jit(solution)/shard_map/thd,hde->the/dot_general | solution.py:140
  45.4 0.0 copy-start.11
  45.4 1.6 %collective-permute-start.7 = (f32[128]{0:T(128)S(1)}, f32[128]{0:T(128)S(1)}, u32[]{:S(2)}, u32[]{:S(2)}) collective-permute-start(f32[128]{0:T(128)S(1)} %get-tuple-element.31), channel_id=1, source_target_pairs={{0,1},{1,0},{2,3},{3,2},{4,5},{5,4},{6,7},{7,6},{8,9},{9,8},{10,11... | collective-permute-start | bytes 1544 | tf_op jit(solution)/shard_map/ppermute | solution.py:28
  47.0 2.0 %collective-permute-done.7 = f32[128]{0:T(128)S(1)} collective-permute-done((f32[128]{0:T(128)S(1)}, f32[128]{0:T(128)S(1)}, u32[]{:S(2)}, u32[]{:S(2)}) %collective-permute-start.7) | collective-permute-done | bytes 544 | tf_op jit(solution)/shard_map/ppermute | solution.py:28
  49.0 2.6 %collective-permute-start.8 = (f32[128]{0:T(128)S(1)}, f32[128]{0:T(128)S(1)}, u32[]{:S(2)}, u32[]{:S(2)}) collective-permute-start(f32[128]{0:T(128)S(1)} %add.93), channel_id=1, source_target_pairs={{0,2},{1,3},{2,0},{3,1},{4,6},{5,7},{6,4},{7,5},{8,10},{9,11},{10,... | collective-permute-start | bytes 1544 | tf_op jit(solution)/shard_map/ppermute | solution.py:28
  51.6 2.0 %copy.49 = bf16[128,2048]{1,0:T(8,128)(2,1)} copy(bf16[128,2048]{0,1:T(8,128)(2,1)} %bitcast.118) | data formatting | bytes 1048576
  53.6 0.3 copy.48
  54.0 1.1 %multiply_convert_fusion = bf16[128,2048]{1,0:T(8,128)(2,1)} fusion(bf16[128,2048]{1,0:T(8,128)(2,1)S(1)} %copy-done.5, f32[128,2048]{1,0:T(8,128)S(1)} %copy.48, f32[2048]{0:T(1024)S(1)} %copy-done.11, f32[128]{0:T(128)S(1)} %add_rsqrt_fusion), kind=kLoop, calls=%fused_computation.27 | loop fusion | flops 2097152 | bytes 2105856 | tf_op jit(solution)/shard_map/convert_element_type | solution.py:155
  (42 shorter events, 0.2 us)
Async XLA Ops:
  0.6 40.5 %copy-start = (bf16[128,2048]{1,0:T(8,128)(2,1)S(1)}, bf16[128,2048]{1,0:T(8,128)(2,1)}, u32[]{:S(2)}) copy-start(bf16[128,2048]{1,0:T(8,128)(2,1)} %param.11) | copy-start | bytes 1572868
  2.4 22.1 %collective-permute-start.1 = (bf16[256,256]{1,0:T(8,128)(2,1)S(1)}, bf16[256,256]{1,0:T(8,128)(2,1)S(1)}, u32[]{:S(2)}, u32[]{:S(2)}) collective-permute-start(bf16[256,256]{1,0:T(8,128)(2,1)S(1)} %constant_dynamic-update-slice_fusion), channel_id=1, source_target_pairs={{0,16},{4,20},{8,24},{12,28},{1,17},{5,21},{9,25},{13,29},{2,18},{... | collective-permute-start | bytes 393224 | tf_op jit(solution)/shard_map/ppermute | solution.py:13
  7.3 17.3 %collective-permute-start.2 = (bf16[256,256]{1,0:T(8,128)(2,1)S(1)}, bf16[256,256]{1,0:T(8,128)(2,1)S(1)}, u32[]{:S(2)}, u32[]{:S(2)}) collective-permute-start(bf16[256,256]{1,0:T(8,128)(2,1)S(1)} %constant_dynamic-update-slice_fusion), channel_id=1, source_target_pairs={{0,12},{4,16},{8,20},{12,24},{16,28},{1,13},{5,17},{9,21},{13,25},... | collective-permute-start | bytes 393224 | tf_op jit(solution)/shard_map/ppermute | solution.py:13
  9.8 14.7 %collective-permute-start.3 = (bf16[256,256]{1,0:T(8,128)(2,1)S(1)}, bf16[256,256]{1,0:T(8,128)(2,1)S(1)}, u32[]{:S(2)}, u32[]{:S(2)}) collective-permute-start(bf16[256,256]{1,0:T(8,128)(2,1)S(1)} %constant_dynamic-update-slice_fusion), channel_id=1, source_target_pairs={{0,8},{4,12},{8,16},{12,20},{16,24},{20,28},{1,9},{5,13},{9,17},{1... | collective-permute-start | bytes 393224 | tf_op jit(solution)/shard_map/ppermute | solution.py:13
  12.0 12.6 %collective-permute-start.4 = (bf16[256,256]{1,0:T(8,128)(2,1)S(1)}, bf16[256,256]{1,0:T(8,128)(2,1)S(1)}, u32[]{:S(2)}, u32[]{:S(2)}) collective-permute-start(bf16[256,256]{1,0:T(8,128)(2,1)S(1)} %constant_dynamic-update-slice_fusion), channel_id=1, source_target_pairs={{0,4},{4,8},{8,12},{12,16},{16,20},{20,24},{24,28},{1,5},{5,9},{9,... | collective-permute-start | bytes 393224 | tf_op jit(solution)/shard_map/ppermute | solution.py:13
  18.7 2.7 %copy-start.2 = (bf16[128,2048]{0,1:T(8,128)(2,1)}, bf16[128,2048]{0,1:T(8,128)(2,1)S(1)}, u32[]{:S(2)}) copy-start(bf16[128,2048]{0,1:T(8,128)(2,1)S(1)} %copy.60) | copy-start | bytes 1572868
  19.9 4.7 %copy-start.9 = (bf16[128,256]{1,0:T(8,128)(2,1)S(1)}, bf16[128,256]{1,0:T(8,128)(2,1)}, u32[]{:S(2)}) copy-start(bf16[128,256]{1,0:T(8,128)(2,1)} %param.18) | copy-start | bytes 196612
  19.9 4.7 %copy-start.10 = (bf16[128,256]{1,0:T(8,128)(2,1)S(1)}, bf16[128,256]{1,0:T(8,128)(2,1)}, u32[]{:S(2)}) copy-start(bf16[128,256]{1,0:T(8,128)(2,1)} %param.19) | copy-start | bytes 196612
  22.4 3.9 %collective-permute-start = (f32[2056,128]{1,0:T(8,128)}, f32[2056,128]{1,0:T(8,128)S(1)}, u32[]{:S(2)}, u32[]{:S(2)}) collective-permute-start(f32[2056,128]{1,0:T(8,128)} %select_maximum_fusion), channel_id=1, source_target_pairs={{0,4},{4,0},{8,12},{12,8},{16,20},{20,16},{24,28},{28,24},{1,5},{5... | collective-permute-start | bytes 3158024 | tf_op jit(solution)/shard_map/ppermute | solution.py:84
  25.5 2.0 %copy-start.6 = (bf16[128,2048]{1,0:T(8,128)(2,1)S(1)}, bf16[128,2048]{1,0:T(8,128)(2,1)}, u32[]{:S(2)}) copy-start(bf16[128,2048]{1,0:T(8,128)(2,1)} %param.17) | copy-start | bytes 1572868
  26.3 16.6 %copy-start.1 = (f32[2056,128]{1,0:T(8,128)}, f32[2056,128]{1,0:T(8,128)S(1)}, u32[]{:S(2)}) copy-start(f32[2056,128]{1,0:T(8,128)S(1)} %collective-permute-done) | copy-start | bytes 3158020
  27.6 13.4 %collective-permute-start.5 = (bf16[2064,128]{1,0:T(8,128)(2,1)}, bf16[2064,128]{1,0:T(8,128)(2,1)S(1)}, u32[]{:S(2)}, u32[]{:S(2)}) collective-permute-start(bf16[2064,128]{1,0:T(8,128)(2,1)} %pad_maximum_fusion), channel_id=1, source_target_pairs={{4,8},{12,16},{20,24},{0,20},{8,28},{5,9},{13,17},{21,25},{1,21},{... | collective-permute-start | bytes 1585160 | tf_op jit(solution)/shard_map/ppermute | solution.py:103
  28.9 5.2 %copy-start.8 = (bf16[640,2,128]{2,1,0:T(2,128)(2,1)S(1)}, bf16[640,2,128]{2,1,0:T(2,128)(2,1)}, u32[]{:S(2)}) copy-start(bf16[640,2,128]{2,1,0:T(2,128)(2,1)} %reshape_squeeze.6) | copy-start | bytes 983044
  34.2 7.0 %copy-start.3 = (bf16[128,2048]{0,1:T(8,128)(2,1)S(1)}, bf16[128,2048]{0,1:T(8,128)(2,1)}, u32[]{:S(2)}) copy-start(bf16[128,2048]{0,1:T(8,128)(2,1)} %copy-done.2) | copy-start | bytes 1572868
  34.2 7.0 %copy-start.7 = (bf16[128,2048]{1,0:T(8,128)(2,1)S(1)}, bf16[128,2048]{1,0:T(8,128)(2,1)}, u32[]{:S(2)}) copy-start(bf16[128,2048]{1,0:T(8,128)(2,1)} %param.13) | copy-start | bytes 1572868
  41.1 2.0 %collective-permute-start.6 = (bf16[2064,128]{1,0:T(8,128)(2,1)S(1)}, bf16[2064,128]{1,0:T(8,128)(2,1)}, u32[]{:S(2)}, u32[]{:S(2)}) collective-permute-start(bf16[2064,128]{1,0:T(8,128)(2,1)S(1)} %collective-permute-done.5), channel_id=1, source_target_pairs={{0,4},{4,0},{8,12},{12,8},{16,20},{20,16},{24,28},{28,24},{1,5},{5... | collective-permute-start | bytes 1585160 | tf_op jit(solution)/shard_map/ppermute | solution.py:124
  42.9 1.6 %slice-start = ((f32[2056,128]{1,0:T(8,128)}), f32[2048,128]{1,0:T(8,128)S(1)}, s32[]{:S(2)}) async-start(f32[2056,128]{1,0:T(8,128)} %copy-done.1), calls=%async_computation | async-start | bytes 2097152 | tf_op jit(solution)/shard_map/slice | solution.py:85
  42.9 1.7 %copy-start.4 = (f32[128,16,128]{0,2,1:T(8,128)S(1)}, f32[128,16,128]{0,2,1:T(8,128)}, u32[]{:S(2)}) copy-start(f32[128,16,128]{0,2,1:T(8,128)} %convolution_bitcast_fusion.1) | copy-start | bytes 3145732
  45.4 8.6 %copy-start.5 = (bf16[128,2048]{1,0:T(8,128)(2,1)S(1)}, bf16[128,2048]{1,0:T(8,128)(2,1)}, u32[]{:S(2)}) copy-start(bf16[128,2048]{1,0:T(8,128)(2,1)} %param.15) | copy-start | bytes 1572868
  45.4 8.6 %copy-start.11 = (f32[2048]{0:T(1024)S(1)}, f32[2048]{0:T(1024)}, u32[]{:S(2)}) copy-start(f32[2048]{0:T(1024)} %param.16) | copy-start | bytes 24580
  45.4 3.6 %collective-permute-start.7 = (f32[128]{0:T(128)S(1)}, f32[128]{0:T(128)S(1)}, u32[]{:S(2)}, u32[]{:S(2)}) collective-permute-start(f32[128]{0:T(128)S(1)} %get-tuple-element.31), channel_id=1, source_target_pairs={{0,1},{1,0},{2,3},{3,2},{4,5},{5,4},{6,7},{7,6},{8,9},{9,8},{10,11... | collective-permute-start | bytes 1544 | tf_op jit(solution)/shard_map/ppermute | solution.py:28
  49.0 5.0 %collective-permute-start.8 = (f32[128]{0:T(128)S(1)}, f32[128]{0:T(128)S(1)}, u32[]{:S(2)}, u32[]{:S(2)}) collective-permute-start(f32[128]{0:T(128)S(1)} %add.93), channel_id=1, source_target_pairs={{0,2},{1,3},{2,0},{3,1},{4,6},{5,7},{6,4},{7,5},{8,10},{9,11},{10,... | collective-permute-start | bytes 1544 | tf_op jit(solution)/shard_map/ppermute | solution.py:28

commit v21 on v20

--- a/solution.py
+++ b/solution.py
@@ -37,7 +37,9 @@
 
 def block_terms(query, lookup_array, values, decay, docs, before, last):
     rows = docs.shape[0]
-    level = jnp.cumsum(decay, axis=1)
+    span = decay.shape[1]
+    upto = (jnp.arange(span)[:, None] <= jnp.arange(span)[None, :]).astype(jnp.float32)
+    level = jnp.dot(decay, upto, precision=lax.Precision.HIGHEST)
     order = jnp.arange(rows)
     same = (docs[:, None] == docs[None, :]) & (order[None, :] <= order[:, None])
     scores = jnp.einsum("thd,shd->hts", query, lookup_array, preferred_element_type=jnp.float32)

time: 55.6 us -> 55.4 us (level)
  other arithmetic: 9.21 us -> 8.19 us
  matrix products: 12.3 us -> 13.1 us
    another operation x2 -> x1, other arithmetic: 1.83 us -> 0.83 us  [the longest x1 1 us: block_terms(): level = jnp.cumsum(decay, axis=1)]
    dot_general x0 -> x1, matrix products: none -> 0.82 us  [block_terms(): level = jnp.dot(decay, upto, precision=lax.Precision.HIGHEST)]
where the time goes in v21:
time: 55.4 us; the launch traced here: 54.9 us
  starting transfers between devices  18 us (32%)
  matrix products  13.1 us (24%)
  other arithmetic  8.19 us (15%)
  local copies, waits for them, and re-layouts  7.42 us (13%)
  waiting for transfers between devices  5.82 us (11%)
  between operations  2.32 us (4%)
    ppermute x4, starting transfers between devices, from_behind(): return lax.ppermute(shard, axis, pairs)  11.4 us
    sub x1, matrix products, local(): expd = jnp.where(allowed, jnp.exp(jnp.minimum(scores - top, 0.0)), 0.0)  5.2 us
    ppermute x2, starting transfers between devices, all_sum(): x = x + lax.ppermute(x, axis, [(i, i ^ bit) for i in range(count)])  4.23 us
    ppermute x1, waiting for transfers between devices, local(): received = lax.ppermute(packet, 'ctx', routes)  3.63 us
    dot_general x1, matrix products, local(): jnp.einsum('kgts,skd->tkgd', expd.astype(jnp.bfloat16), all_values, prefe...  3.27 us
    unnamed x33, local copies, waits for them, and re-layouts  3.26 us
    ppermute x2, waiting for transfers between devices, all_sum(): x = x + lax.ppermute(x, axis, [(i, i ^ bit) for i in range(count)])  1.96 us
    dot_general x1, matrix products, block_terms(): jnp.einsum('hts,shd->thd', weights, values, preferred_element_type=jnp.fl...  1.7 us
  transfers between devices with their start and end apart: 9, of which 3 were waited for; matrix products, arithmetic and copies ran while one was open for 41% of the time, Pallas kernels for 0%

profile of v21, /device:TPU:0, one launch (start us, length us, event | category | flops | bytes accessed | tf_op | source)
XLA Modules:
  0.0 54.9 jit_solution(4100312833082244555)
XLA Ops:
  0.6 0.0 copy-start
  0.6 0.9 %constant_dynamic-update-slice_fusion.1 = bf16[256,256]{1,0:T(8,128)(2,1)S(1)} fusion(bf16[128,256]{1,0:T(8,128)(2,1)} %param.18), kind=kLoop, calls=%fused_computation.71 | loop fusion | bytes 131072
  1.5 0.8 %constant_dynamic-update-slice_fusion = bf16[256,256]{1,0:T(8,128)(2,1)S(1)} fusion(bf16[256,256]{1,0:T(8,128)(2,1)S(1)} %constant_dynamic-update-slice_fusion.1, bf16[128,256]{1,0:T(8,128)(2,1)} %param.19), kind=kLoop, calls=%fused_computation.70 | loop fusion | bytes 131072 | tf_op jit(solution)/shard_map/concatenate | solution.py:77
  2.4 4.9 %collective-permute-start.1 = (bf16[256,256]{1,0:T(8,128)(2,1)S(1)}, bf16[256,256]{1,0:T(8,128)(2,1)S(1)}, u32[]{:S(2)}, u32[]{:S(2)}) collective-permute-start(bf16[256,256]{1,0:T(8,128)(2,1)S(1)} %constant_dynamic-update-slice_fusion), channel_id=1, source_target_pairs={{0,16},{4,20},{8,24},{12,28},{1,17},{5,21},{9,25},{13,29},{2,18},{... | collective-permute-start | bytes 393224 | tf_op jit(solution)/shard_map/ppermute | solution.py:13
  7.3 2.6 %collective-permute-start.2 = (bf16[256,256]{1,0:T(8,128)(2,1)S(1)}, bf16[256,256]{1,0:T(8,128)(2,1)S(1)}, u32[]{:S(2)}, u32[]{:S(2)}) collective-permute-start(bf16[256,256]{1,0:T(8,128)(2,1)S(1)} %constant_dynamic-update-slice_fusion), channel_id=1, source_target_pairs={{0,12},{4,16},{8,20},{12,24},{16,28},{1,13},{5,17},{9,21},{13,25},... | collective-permute-start | bytes 393224 | tf_op jit(solution)/shard_map/ppermute | solution.py:13
  9.8 2.1 %collective-permute-start.3 = (bf16[256,256]{1,0:T(8,128)(2,1)S(1)}, bf16[256,256]{1,0:T(8,128)(2,1)S(1)}, u32[]{:S(2)}, u32[]{:S(2)}) collective-permute-start(bf16[256,256]{1,0:T(8,128)(2,1)S(1)} %constant_dynamic-update-slice_fusion), channel_id=1, source_target_pairs={{0,8},{4,12},{8,16},{12,20},{16,24},{20,28},{1,9},{5,13},{9,17},{1... | collective-permute-start | bytes 393224 | tf_op jit(solution)/shard_map/ppermute | solution.py:13
  12.0 1.8 %collective-permute-start.4 = (bf16[256,256]{1,0:T(8,128)(2,1)S(1)}, bf16[256,256]{1,0:T(8,128)(2,1)S(1)}, u32[]{:S(2)}, u32[]{:S(2)}) collective-permute-start(bf16[256,256]{1,0:T(8,128)(2,1)S(1)} %constant_dynamic-update-slice_fusion), channel_id=1, source_target_pairs={{0,4},{4,8},{8,12},{12,16},{16,20},{20,24},{24,28},{1,5},{5,9},{9,... | collective-permute-start | bytes 393224 | tf_op jit(solution)/shard_map/ppermute | solution.py:13
  13.8 0.8 %reduce-window.8 = s32[6,1]{0,1:T(1,128)S(1)} reduce-window(s32[6,1]{0,1:T(1,128)} %bitcast.125, s32[]{:T(128)} %constant.20.clone.1), window={size=6x1 pad=5_0x0_0}, to_apply=%region_0.0 | reduce-window | flops 30 | bytes 52 | tf_op jit(solution)/shard_map/reduce-window.3
  14.7 0.6 %fusion.70 = (s32[]{:T(128)}, s32[]{:T(128)}) fusion(s32[]{:T(128)S(6)} %sub.52, s32[6,1]{0,1:T(1,128)S(1)} %reduce-window.8, s32[]{:T(128)S(6)} %sub.51), kind=kLoop, calls=%fused_computation.98 | loop fusion | flops 34 | bytes 40 | tf_op jit(solution)/shard_map/reduce_sum | solution.py:68
  15.9 0.1 convert_reduce_fusion.1
  16.7 0.7 %compare_convert_fusion = (f32[128]{0:T(128)S(1)}, f32[128]{0:T(128)S(1)}) fusion(s32[128]{0:T(128)S(1)} %convert_reduce_fusion.1, s32[]{:T(128)S(6)} %select_n.57, s32[]{:T(128)} %get-tuple-element.19), kind=kLoop, calls=%fused_computation.93 | loop fusion | flops 512 | bytes 1544 | tf_op jit(solution)/shard_map/convert_element_type | solution.py:145
  17.3 0.8 %fusion.62 = f32[128,16]{0,1:T(8,128)S(1)} fusion(f32[16,128]{1,0:T(8,128)} %param.14), kind=kOutput, calls=%fused_computation.68 | convolution fusion | flops 3162112 | bytes 16384 | tf_op jit(solution)/shard_map/dot_general | solution.py:42
  18.2 1.3 %copy.60 = bf16[128,2048]{0,1:T(8,128)(2,1)S(1)} copy(bf16[128,2048]{1,0:T(8,128)(2,1)} %param.12) | data formatting | bytes 1048576 | tf_op jit(solution)/shard_map/reshape | solution.py:70
  19.5 0.0 copy-start.2
  19.5 0.2 slice_reduce_fusion
  19.7 0.1 exponential_multiply_fusion
  19.8 0.0 copy-start.10
  19.8 1.4 %fusion.30 = f32[16,128,128]{2,1,0:T(8,128)S(1)} fusion(bf16[128,16,128]{0,2,1:T(8,128)(2,1)S(1)} %bitcast.111, f32[128,16]{0,1:T(8,128)S(1)} %get-tuple-element.26, bf16[128,2048]{1,0:T(8,128)(2,1)} %param.13), kind=kOutput, calls=%fused_computation.38 | convolution fusion | flops 67895296 | bytes 2105344 | tf_op jit(solution)/shard_map/shd,she->hde/dot_general | solution.py:53
  21.2 1.0 %select_maximum_fusion = f32[2056,128]{1,0:T(8,128)} fusion(f32[1,16]{1,0:T(1,128)S(1)} %bitcast.122, f32[2048,128]{1,0:T(8,128)S(1)} %bitcast.106), kind=kLoop, calls=%fused_computation.23 | loop fusion | flops 789504 | bytes 2101312 | tf_op jit(solution)/shard_map/concatenate | solution.py:85
  22.2 1.1 %collective-permute-start = (f32[2056,128]{1,0:T(8,128)}, f32[2056,128]{1,0:T(8,128)S(1)}, u32[]{:S(2)}, u32[]{:S(2)}) collective-permute-start(f32[2056,128]{1,0:T(8,128)} %select_maximum_fusion), channel_id=1, source_target_pairs={{0,4},{4,0},{8,12},{12,8},{16,20},{20,16},{24,28},{28,24},{1,5},{5... | collective-permute-start | bytes 3158024 | tf_op jit(solution)/shard_map/ppermute | solution.py:86
  23.4 0.1 convert_reduce_fusion
  23.5 0.9 %compare_and_fusion = pred[128,640]{0,1:T(8,128)(4,1)} fusion(s32[128]{0:T(128)S(1)} %iota_add_fusion.1, s32[128]{0:T(128)S(1)} %convert_reduce_fusion.1, s32[640]{0:T(1024)S(1)} %iota_add_fusion, s32[640]{0:T(1024)S(1)} %compare_select_fusion), kind=kLoop, calls=%fused_computation.62 | loop fusion | flops 245760 | bytes 88064 | tf_op jit(solution)/shard_map/and | solution.py:109
  24.3 0.0 collective-permute-done.1
  24.4 0.0 collective-permute-done.2
  24.4 0.0 collective-permute-done.3
  24.5 0.8 %reshape_squeeze.7 = bf16[640,2,128]{2,1,0:T(2,128)(2,1)} reshape(bf16[5,1,128,256]{3,2,0,1:T(8,128)(2,1)S(1)} %get-tuple-element.24) | data formatting | bytes 655360 | tf_op jit(solution)/shard_map/reshape;squeeze | solution.py:112
  25.4 0.8 %reshape_squeeze.6 = bf16[640,2,128]{2,1,0:T(2,128)(2,1)} reshape(bf16[5,1,128,256]{3,2,0,1:T(8,128)(2,1)S(1)} %get-tuple-element.23) | data formatting | bytes 655360 | tf_op jit(solution)/shard_map/reshape;squeeze | solution.py:113
  26.2 0.3 select_convert_fusion.1
  26.5 0.8 %pad_maximum_fusion = bf16[2064,128]{1,0:T(8,128)(2,1)} fusion(bf16[16,128]{1,0:T(8,128)(2,1)S(1)} %fusion.68, bf16[2048,128]{1,0:T(8,128)(2,1)S(1)} %bitcast.113), kind=kLoop, calls=%fused_computation.36 | loop fusion | flops 1056768 | bytes 1056768 | tf_op jit(solution)/shard_map/concatenate | solution.py:100
  27.3 0.1 copy.63
  27.4 1.3 %collective-permute-start.5 = (bf16[2064,128]{1,0:T(8,128)(2,1)}, bf16[2064,128]{1,0:T(8,128)(2,1)S(1)}, u32[]{:S(2)}, u32[]{:S(2)}) collective-permute-start(bf16[2064,128]{1,0:T(8,128)(2,1)} %pad_maximum_fusion), channel_id=1, source_target_pairs={{4,8},{12,16},{20,24},{0,20},{8,28},{5,9},{13,17},{21,25},{1,21},{... | collective-permute-start | bytes 1585160 | tf_op jit(solution)/shard_map/ppermute | solution.py:105
  28.8 5.2 %fusion.77 = (f32[2,8,128]{2,1,0:T(8,128)S(1)}, bf16[2,8,128,640]{2,3,1,0:T(8,128)(2,1)}) fusion(pred[128,640]{0,1:T(8,128)(4,1)} %compare_and_fusion, bf16[128,2,8,128]{3,2,1,0:T(8,128)(2,1)S(1)} %bitcast.117, bf16[640,2,128,1]{2,1,0,3:T(2,128)(2,1)} %bitcast.119), kind=kOutput, calls=%fused_computation.113 | convolution fusion | flops 681575040 | bytes 3563520 | tf_op jit(solution)/shard_map/sub | solution.py:118
  34.0 3.3 %fusion.20 = bf16[128,2,8,128]{0,3,2,1:T(8,128)(2,1)} fusion(bf16[2,8,128,640]{2,3,1,0:T(8,128)(2,1)} %get-tuple-element.30, f32[128,2,8]{0,2,1:T(8,128)S(1)} %bitcast.126, bf16[640,2,128,1]{2,1,0,3:T(2,128)(2,1)S(1)} %bitcast.118), kind=kOutput, calls=%fused_computation.21 | convolution fusion | flops 336068608 | bytes 3481600 | tf_op jit(solution)/shard_map/kgts,skd->tkgd/dot_general | solution.py:120
  37.3 3.6 %collective-permute-done.5 = bf16[2064,128]{1,0:T(8,128)(2,1)S(1)} collective-permute-done((bf16[2064,128]{1,0:T(8,128)(2,1)}, bf16[2064,128]{1,0:T(8,128)(2,1)S(1)}, u32[]{:S(2)}, u32[]{:S(2)}) %collective-permute-start.5) | collective-permute-done | bytes 528416 | tf_op jit(solution)/shard_map/ppermute | solution.py:105
  40.9 0.1 fusion.61
  41.0 1.7 %convolution_bitcast_fusion.1 = f32[128,16,128]{0,2,1:T(8,128)} fusion(bf16[128,16,128]{0,2,1:T(8,128)(2,1)S(1)} %bitcast.112, f32[16,128]{1,0:T(8,128)S(1)} %bitcast.121, pred[128,128]{1,0:T(8,128)(4,1)S(1)} %fusion.61, bf16[128,2048]{1,0:T(8,128)(2,1)S(1)} %copy-done.7, bf16[128,2048]{1,0:T(8,128)(2,1)S(1)} %copy-done), kind=kOutput, calls=%fused_computation.16 | convolution fusion | flops 135528448 | bytes 2646016 | tf_op jit(solution)/shard_map/hts,shd->thd/dot_general | solution.py:48
  42.7 0.2 collective-permute-done.6
  42.9 0.1 broadcast_select_fusion
  43.1 1.3 %slice_select_fusion = bf16[2048,128]{1,0:T(8,128)(2,1)S(1)} fusion(bf16[2064,128]{1,0:T(8,128)(2,1)} %collective-permute-done.6, bf16[2064,128]{1,0:T(8,128)(2,1)S(1)} %collective-permute-done.5, pred[]{:T(512)S(6)} %eq.61), kind=kLoop, calls=%fused_computation.43 | loop fusion | flops 262144 | bytes 1572865 | tf_op jit(solution)/shard_map/jit(_where)/select_n | solution.py:128
  44.4 0.0 copy-done.4
  44.4 0.7 %multiply_reduce_fusion = (f32[128]{0:T(128)S(1)}, f32[128,16,128]{0,2,1:T(8,128)S(1)}) fusion(f32[128,16,128]{0,2,1:T(8,128)S(1)} %copy-done.4, f32[128,16]{0,1:T(8,128)S(1)} %get-tuple-element.25, f32[16,128,128]{2,1,0:T(8,128)S(1)} %bitcast.108, bf16[16,128,128]{2,1,0:T(8,128)(2,1)S(1)} %bitcast.110, bf16[16,128,128]{2,1,0:T(8,128)(2,1)S(1)} %bitcast.109, ...), kind=kOutput, calls=%fused_computation.28 | convolution fusion | flops 70254464 | bytes 4727425 | tf_op jit(solution)/shard_map/thd,hde->the/dot_general | solution.py:142
  45.2 0.0 copy-start.11
  45.2 1.6 %collective-permute-start.7 = (f32[128]{0:T(128)S(1)}, f32[128]{0:T(128)S(1)}, u32[]{:S(2)}, u32[]{:S(2)}) collective-permute-start(f32[128]{0:T(128)S(1)} %get-tuple-element.31), channel_id=1, source_target_pairs={{0,1},{1,0},{2,3},{3,2},{4,5},{5,4},{6,7},{7,6},{8,9},{9,8},{10,11... | collective-permute-start | bytes 1544 | tf_op jit(solution)/shard_map/ppermute | solution.py:28
  46.8 2.0 %collective-permute-done.7 = f32[128]{0:T(128)S(1)} collective-permute-done((f32[128]{0:T(128)S(1)}, f32[128]{0:T(128)S(1)}, u32[]{:S(2)}, u32[]{:S(2)}) %collective-permute-start.7) | collective-permute-done | bytes 544 | tf_op jit(solution)/shard_map/ppermute | solution.py:28
  48.8 2.6 %collective-permute-start.8 = (f32[128]{0:T(128)S(1)}, f32[128]{0:T(128)S(1)}, u32[]{:S(2)}, u32[]{:S(2)}) collective-permute-start(f32[128]{0:T(128)S(1)} %add.93), channel_id=1, source_target_pairs={{0,2},{1,3},{2,0},{3,1},{4,6},{5,7},{6,4},{7,5},{8,10},{9,11},{10,... | collective-permute-start | bytes 1544 | tf_op jit(solution)/shard_map/ppermute | solution.py:28
  51.4 2.0 %copy.49 = bf16[128,2048]{1,0:T(8,128)(2,1)} copy(bf16[128,2048]{0,1:T(8,128)(2,1)} %bitcast.116) | data formatting | bytes 1048576
  53.4 0.3 copy.48
  53.8 1.1 %multiply_convert_fusion = bf16[128,2048]{1,0:T(8,128)(2,1)} fusion(bf16[128,2048]{1,0:T(8,128)(2,1)S(1)} %copy-done.5, f32[128,2048]{1,0:T(8,128)S(1)} %copy.48, f32[2048]{0:T(1024)S(1)} %copy-done.11, f32[128]{0:T(128)S(1)} %add_rsqrt_fusion), kind=kLoop, calls=%fused_computation.27 | loop fusion | flops 2097152 | bytes 2105856 | tf_op jit(solution)/shard_map/convert_element_type | solution.py:157
  (42 shorter events, 0.2 us)
Async XLA Ops:
  0.6 40.4 %copy-start = (bf16[128,2048]{1,0:T(8,128)(2,1)S(1)}, bf16[128,2048]{1,0:T(8,128)(2,1)}, u32[]{:S(2)}) copy-start(bf16[128,2048]{1,0:T(8,128)(2,1)} %param.11) | copy-start | bytes 1572868
  2.4 21.9 %collective-permute-start.1 = (bf16[256,256]{1,0:T(8,128)(2,1)S(1)}, bf16[256,256]{1,0:T(8,128)(2,1)S(1)}, u32[]{:S(2)}, u32[]{:S(2)}) collective-permute-start(bf16[256,256]{1,0:T(8,128)(2,1)S(1)} %constant_dynamic-update-slice_fusion), channel_id=1, source_target_pairs={{0,16},{4,20},{8,24},{12,28},{1,17},{5,21},{9,25},{13,29},{2,18},{... | collective-permute-start | bytes 393224 | tf_op jit(solution)/shard_map/ppermute | solution.py:13
  7.3 17.1 %collective-permute-start.2 = (bf16[256,256]{1,0:T(8,128)(2,1)S(1)}, bf16[256,256]{1,0:T(8,128)(2,1)S(1)}, u32[]{:S(2)}, u32[]{:S(2)}) collective-permute-start(bf16[256,256]{1,0:T(8,128)(2,1)S(1)} %constant_dynamic-update-slice_fusion), channel_id=1, source_target_pairs={{0,12},{4,16},{8,20},{12,24},{16,28},{1,13},{5,17},{9,21},{13,25},... | collective-permute-start | bytes 393224 | tf_op jit(solution)/shard_map/ppermute | solution.py:13
  9.8 14.5 %collective-permute-start.3 = (bf16[256,256]{1,0:T(8,128)(2,1)S(1)}, bf16[256,256]{1,0:T(8,128)(2,1)S(1)}, u32[]{:S(2)}, u32[]{:S(2)}) collective-permute-start(bf16[256,256]{1,0:T(8,128)(2,1)S(1)} %constant_dynamic-update-slice_fusion), channel_id=1, source_target_pairs={{0,8},{4,12},{8,16},{12,20},{16,24},{20,28},{1,9},{5,13},{9,17},{1... | collective-permute-start | bytes 393224 | tf_op jit(solution)/shard_map/ppermute | solution.py:13
  12.0 12.4 %collective-permute-start.4 = (bf16[256,256]{1,0:T(8,128)(2,1)S(1)}, bf16[256,256]{1,0:T(8,128)(2,1)S(1)}, u32[]{:S(2)}, u32[]{:S(2)}) collective-permute-start(bf16[256,256]{1,0:T(8,128)(2,1)S(1)} %constant_dynamic-update-slice_fusion), channel_id=1, source_target_pairs={{0,4},{4,8},{8,12},{12,16},{16,20},{20,24},{24,28},{1,5},{5,9},{9,... | collective-permute-start | bytes 393224 | tf_op jit(solution)/shard_map/ppermute | solution.py:13
  19.5 1.7 %copy-start.2 = (bf16[128,2048]{0,1:T(8,128)(2,1)}, bf16[128,2048]{0,1:T(8,128)(2,1)S(1)}, u32[]{:S(2)}) copy-start(bf16[128,2048]{0,1:T(8,128)(2,1)S(1)} %copy.60) | copy-start | bytes 1572868
  19.8 4.7 %copy-start.9 = (bf16[128,256]{1,0:T(8,128)(2,1)S(1)}, bf16[128,256]{1,0:T(8,128)(2,1)}, u32[]{:S(2)}) copy-start(bf16[128,256]{1,0:T(8,128)(2,1)} %param.18) | copy-start | bytes 196612
  19.8 4.7 %copy-start.10 = (bf16[128,256]{1,0:T(8,128)(2,1)S(1)}, bf16[128,256]{1,0:T(8,128)(2,1)}, u32[]{:S(2)}) copy-start(bf16[128,256]{1,0:T(8,128)(2,1)} %param.19) | copy-start | bytes 196612
  22.2 3.9 %collective-permute-start = (f32[2056,128]{1,0:T(8,128)}, f32[2056,128]{1,0:T(8,128)S(1)}, u32[]{:S(2)}, u32[]{:S(2)}) collective-permute-start(f32[2056,128]{1,0:T(8,128)} %select_maximum_fusion), channel_id=1, source_target_pairs={{0,4},{4,0},{8,12},{12,8},{16,20},{20,16},{24,28},{28,24},{1,5},{5... | collective-permute-start | bytes 3158024 | tf_op jit(solution)/shard_map/ppermute | solution.py:86
  25.3 2.0 %copy-start.6 = (bf16[128,2048]{1,0:T(8,128)(2,1)S(1)}, bf16[128,2048]{1,0:T(8,128)(2,1)}, u32[]{:S(2)}) copy-start(bf16[128,2048]{1,0:T(8,128)(2,1)} %param.17) | copy-start | bytes 1572868
  26.2 16.6 %copy-start.1 = (f32[2056,128]{1,0:T(8,128)}, f32[2056,128]{1,0:T(8,128)S(1)}, u32[]{:S(2)}) copy-start(f32[2056,128]{1,0:T(8,128)S(1)} %collective-permute-done) | copy-start | bytes 3158020
  27.4 13.5 %collective-permute-start.5 = (bf16[2064,128]{1,0:T(8,128)(2,1)}, bf16[2064,128]{1,0:T(8,128)(2,1)S(1)}, u32[]{:S(2)}, u32[]{:S(2)}) collective-permute-start(bf16[2064,128]{1,0:T(8,128)(2,1)} %pad_maximum_fusion), channel_id=1, source_target_pairs={{4,8},{12,16},{20,24},{0,20},{8,28},{5,9},{13,17},{21,25},{1,21},{... | collective-permute-start | bytes 1585160 | tf_op jit(solution)/shard_map/ppermute | solution.py:105
  28.8 5.2 %copy-start.8 = (bf16[640,2,128]{2,1,0:T(2,128)(2,1)S(1)}, bf16[640,2,128]{2,1,0:T(2,128)(2,1)}, u32[]{:S(2)}) copy-start(bf16[640,2,128]{2,1,0:T(2,128)(2,1)} %reshape_squeeze.6) | copy-start | bytes 983044
  34.0 7.0 %copy-start.3 = (bf16[128,2048]{0,1:T(8,128)(2,1)S(1)}, bf16[128,2048]{0,1:T(8,128)(2,1)}, u32[]{:S(2)}) copy-start(bf16[128,2048]{0,1:T(8,128)(2,1)} %copy-done.2) | copy-start | bytes 1572868
  34.0 7.0 %copy-start.7 = (bf16[128,2048]{1,0:T(8,128)(2,1)S(1)}, bf16[128,2048]{1,0:T(8,128)(2,1)}, u32[]{:S(2)}) copy-start(bf16[128,2048]{1,0:T(8,128)(2,1)} %param.13) | copy-start | bytes 1572868
  40.9 2.0 %collective-permute-start.6 = (bf16[2064,128]{1,0:T(8,128)(2,1)S(1)}, bf16[2064,128]{1,0:T(8,128)(2,1)}, u32[]{:S(2)}, u32[]{:S(2)}) collective-permute-start(bf16[2064,128]{1,0:T(8,128)(2,1)S(1)} %collective-permute-done.5), channel_id=1, source_target_pairs={{0,4},{4,0},{8,12},{12,8},{16,20},{20,16},{24,28},{28,24},{1,5},{5... | collective-permute-start | bytes 1585160 | tf_op jit(solution)/shard_map/ppermute | solution.py:126
  42.7 1.6 %slice-start = ((f32[2056,128]{1,0:T(8,128)}), f32[2048,128]{1,0:T(8,128)S(1)}, s32[]{:S(2)}) async-start(f32[2056,128]{1,0:T(8,128)} %copy-done.1), calls=%async_computation | async-start | bytes 2097152 | tf_op jit(solution)/shard_map/slice | solution.py:87
  42.7 1.7 %copy-start.4 = (f32[128,16,128]{0,2,1:T(8,128)S(1)}, f32[128,16,128]{0,2,1:T(8,128)}, u32[]{:S(2)}) copy-start(f32[128,16,128]{0,2,1:T(8,128)} %convolution_bitcast_fusion.1) | copy-start | bytes 3145732
  45.2 8.6 %copy-start.5 = (bf16[128,2048]{1,0:T(8,128)(2,1)S(1)}, bf16[128,2048]{1,0:T(8,128)(2,1)}, u32[]{:S(2)}) copy-start(bf16[128,2048]{1,0:T(8,128)(2,1)} %param.15) | copy-start | bytes 1572868
  45.2 8.6 %copy-start.11 = (f32[2048]{0:T(1024)S(1)}, f32[2048]{0:T(1024)}, u32[]{:S(2)}) copy-start(f32[2048]{0:T(1024)} %param.16) | copy-start | bytes 24580
  45.2 3.6 %collective-permute-start.7 = (f32[128]{0:T(128)S(1)}, f32[128]{0:T(128)S(1)}, u32[]{:S(2)}, u32[]{:S(2)}) collective-permute-start(f32[128]{0:T(128)S(1)} %get-tuple-element.31), channel_id=1, source_target_pairs={{0,1},{1,0},{2,3},{3,2},{4,5},{5,4},{6,7},{7,6},{8,9},{9,8},{10,11... | collective-permute-start | bytes 1544 | tf_op jit(solution)/shard_map/ppermute | solution.py:28
  48.8 5.0 %collective-permute-start.8 = (f32[128]{0:T(128)S(1)}, f32[128]{0:T(128)S(1)}, u32[]{:S(2)}, u32[]{:S(2)}) collective-permute-start(f32[128]{0:T(128)S(1)} %add.93), channel_id=1, source_target_pairs={{0,2},{1,3},{2,0},{3,1},{4,6},{5,7},{6,4},{7,5},{8,10},{9,11},{10,... | collective-permute-start | bytes 1544 | tf_op jit(solution)/shard_map/ppermute | solution.py:28

commit v22 on v20

--- a/solution.py
+++ b/solution.py
@@ -72,7 +72,7 @@
     )
     count = lax.axis_size("ctx")
     odd = (shard % 2) == 1
-    pair = jnp.concatenate([soft_k, soft_v], axis=0)
+    pair = jnp.stack([soft_k, soft_v])
     kv_width = soft_k.shape[1]
     n_state = heads_here * DH
     state_rows = state.reshape(n_state, DH)

time: 55.6 us -> 54.8 us (0.986)
  local copies, waits for them, and re-layouts: 7.42 us -> 5.66 us
  other arithmetic: 9.21 us -> 10.2 us
    another operation x1 -> x2, other arithmetic: 0.83 us -> 1.77 us  [the longest x1 0.94 us: local(): pair = jnp.stack([soft_k, soft_v])]
    unnamed x33 -> x32, local copies, waits for them, and re-layouts: 3.29 us -> 2.37 us
    concatenate x1 -> x0, local copies, waits for them, and re-layouts: 0.84 us -> none  [local(): pair = jnp.concatenate([soft_k, soft_v], axis=0)]
  transfers between devices with their start and end apart: 9 -> 9, of which waited for: 3 -> 3; matrix products, arithmetic and copies ran while one was open for 41% -> 42% of each run, Pallas kernels for 0% -> 0%
where the time goes in v22:
time: 54.8 us; the launch traced here: 54.3 us
  starting transfers between devices  18.1 us (33%)
  matrix products  12.3 us (22%)
  other arithmetic  10.2 us (19%)
  waiting for transfers between devices  5.8 us (11%)
  local copies, waits for them, and re-layouts  5.66 us (10%)
  between operations  2.32 us (4%)
    ppermute x4, starting transfers between devices, from_behind(): return lax.ppermute(shard, axis, pairs)  11.4 us
    sub x1, matrix products, local(): expd = jnp.where(allowed, jnp.exp(jnp.minimum(scores - top, 0.0)), 0.0)  5.2 us
    ppermute x2, starting transfers between devices, all_sum(): x = x + lax.ppermute(x, axis, [(i, i ^ bit) for i in range(count)])  4.24 us
    ppermute x1, waiting for transfers between devices, local(): received = lax.ppermute(packet, 'ctx', routes)  3.62 us
    dot_general x1, matrix products, local(): jnp.einsum('kgts,skd->tkgd', expd.astype(jnp.bfloat16), all_values, prefe...  3.27 us
    unnamed x32, local copies, waits for them, and re-layouts  2.37 us
    ppermute x2, waiting for transfers between devices, all_sum(): x = x + lax.ppermute(x, axis, [(i, i ^ bit) for i in range(count)])  1.96 us
    dot_general x1, matrix products, block_terms(): jnp.einsum('hts,shd->thd', weights, values, preferred_element_type=jnp.fl...  1.71 us
  transfers between devices with their start and end apart: 9, of which 3 were waited for; matrix products, arithmetic and copies ran while one was open for 42% of the time, Pallas kernels for 0%

profile of v22, /device:TPU:0, one launch (start us, length us, event | category | flops | bytes accessed | tf_op | source)
XLA Modules:
  0.0 54.3 jit_solution(6953906071113193497)
XLA Ops:
  0.6 0.0 copy-start
  0.6 0.9 %pad_maximum_fusion.1 = bf16[2,128,256]{2,1,0:T(8,128)(2,1)S(1)} fusion(bf16[1,128,256]{2,1,0:T(8,128)(2,1)} %bitcast.127, bf16[1,128,256]{2,1,0:T(8,128)(2,1)} %bitcast.126), kind=kLoop, calls=%fused_computation.65 | loop fusion | flops 65536 | bytes 262144 | tf_op jit(solution)/shard_map/stack | solution.py:75
  1.6 4.9 %collective-permute-start.1 = (bf16[2,128,256]{2,1,0:T(8,128)(2,1)S(1)}, bf16[2,128,256]{2,1,0:T(8,128)(2,1)S(1)}, u32[]{:S(2)}, u32[]{:S(2)}) collective-permute-start(bf16[2,128,256]{2,1,0:T(8,128)(2,1)S(1)} %pad_maximum_fusion.1), channel_id=1, source_target_pairs={{0,16},{4,20},{8,24},{12,28},{1,17},{5,21},{9,25},{13,29},{2,18},{... | collective-permute-start | bytes 393224 | tf_op jit(solution)/shard_map/ppermute | solution.py:13
  6.5 2.6 %collective-permute-start.2 = (bf16[2,128,256]{2,1,0:T(8,128)(2,1)S(1)}, bf16[2,128,256]{2,1,0:T(8,128)(2,1)S(1)}, u32[]{:S(2)}, u32[]{:S(2)}) collective-permute-start(bf16[2,128,256]{2,1,0:T(8,128)(2,1)S(1)} %pad_maximum_fusion.1), channel_id=1, source_target_pairs={{0,12},{4,16},{8,20},{12,24},{16,28},{1,13},{5,17},{9,21},{13,25},... | collective-permute-start | bytes 393224 | tf_op jit(solution)/shard_map/ppermute | solution.py:13
  9.0 2.1 %collective-permute-start.3 = (bf16[2,128,256]{2,1,0:T(8,128)(2,1)S(1)}, bf16[2,128,256]{2,1,0:T(8,128)(2,1)S(1)}, u32[]{:S(2)}, u32[]{:S(2)}) collective-permute-start(bf16[2,128,256]{2,1,0:T(8,128)(2,1)S(1)} %pad_maximum_fusion.1), channel_id=1, source_target_pairs={{0,8},{4,12},{8,16},{12,20},{16,24},{20,28},{1,9},{5,13},{9,17},{1... | collective-permute-start | bytes 393224 | tf_op jit(solution)/shard_map/ppermute | solution.py:13
  11.2 1.8 %collective-permute-start.4 = (bf16[2,128,256]{2,1,0:T(8,128)(2,1)S(1)}, bf16[2,128,256]{2,1,0:T(8,128)(2,1)S(1)}, u32[]{:S(2)}, u32[]{:S(2)}) collective-permute-start(bf16[2,128,256]{2,1,0:T(8,128)(2,1)S(1)} %pad_maximum_fusion.1), channel_id=1, source_target_pairs={{0,4},{4,8},{8,12},{12,16},{16,20},{20,24},{24,28},{1,5},{5,9},{9,... | collective-permute-start | bytes 393224 | tf_op jit(solution)/shard_map/ppermute | solution.py:13
  13.0 0.8 %reduce-window.8 = s32[6,1]{0,1:T(1,128)S(1)} reduce-window(s32[6,1]{0,1:T(1,128)} %bitcast.131, s32[]{:T(128)} %constant.23.clone.1), window={size=6x1 pad=5_0x0_0}, to_apply=%region_0.0 | reduce-window | flops 30 | bytes 52 | tf_op jit(solution)/shard_map/reduce-window.3
  13.9 0.6 %fusion.69 = (s32[]{:T(128)}, s32[]{:T(128)}) fusion(s32[]{:T(128)S(6)} %sub.53, s32[6,1]{0,1:T(1,128)S(1)} %reduce-window.8, s32[]{:T(128)S(6)} %sub.52), kind=kLoop, calls=%fused_computation.95 | loop fusion | flops 34 | bytes 40 | tf_op jit(solution)/shard_map/reduce_sum | solution.py:66
  15.2 0.1 convert_reduce_fusion.1
  15.9 0.7 %compare_convert_fusion = (f32[128]{0:T(128)S(1)}, f32[128]{0:T(128)S(1)}) fusion(s32[128]{0:T(128)S(1)} %convert_reduce_fusion.1, s32[]{:T(128)S(6)} %select_n.57, s32[]{:T(128)} %get-tuple-element.19), kind=kLoop, calls=%fused_computation.90 | loop fusion | flops 512 | bytes 1544 | tf_op jit(solution)/shard_map/convert_element_type | solution.py:143
  16.6 1.3 %copy.60 = bf16[128,2048]{0,1:T(8,128)(2,1)S(1)} copy(bf16[128,2048]{1,0:T(8,128)(2,1)} %param.12) | data formatting | bytes 1048576 | tf_op jit(solution)/shard_map/reshape | solution.py:68
  17.9 0.0 copy-start.2
  17.9 1.0 %reduce_window_sum.19 = f32[16,128]{1,0:T(8,128)S(1)} reduce-window(f32[16,128]{1,0:T(8,128)} %param.14, f32[]{:T(128)} %constant.47.clone.1), window={size=1x128 pad=0_0x127_0}, to_apply=%region_2.3 | reduce-window | flops 260096 | bytes 16388 | tf_op jit(solution)/shard_map/jit(cumsum)/reduce_window_sum | solution.py:40
  18.9 0.2 slice_reduce_fusion
  19.1 0.1 multiply_bitcast_fusion
  19.2 0.0 copy-start.10
  19.2 1.4 %fusion.30 = f32[16,128,128]{2,1,0:T(8,128)S(1)} fusion(bf16[128,16,128]{0,2,1:T(8,128)(2,1)S(1)} %bitcast.117, f32[128,16]{0,1:T(8,128)S(1)} %get-tuple-element.26, bf16[128,2048]{1,0:T(8,128)(2,1)} %param.13), kind=kOutput, calls=%fused_computation.38 | convolution fusion | flops 67895296 | bytes 2105344 | tf_op jit(solution)/shard_map/shd,she->hde/dot_general | solution.py:51
  20.6 1.1 %select_maximum_fusion = f32[2056,128]{1,0:T(8,128)} fusion(f32[1,16]{1,0:T(1,128)S(1)} %bitcast.128, f32[2048,128]{1,0:T(8,128)S(1)} %bitcast.112), kind=kLoop, calls=%fused_computation.23 | loop fusion | flops 789504 | bytes 2101312 | tf_op jit(solution)/shard_map/concatenate | solution.py:83
  21.6 1.1 %collective-permute-start = (f32[2056,128]{1,0:T(8,128)}, f32[2056,128]{1,0:T(8,128)S(1)}, u32[]{:S(2)}, u32[]{:S(2)}) collective-permute-start(f32[2056,128]{1,0:T(8,128)} %select_maximum_fusion), channel_id=1, source_target_pairs={{0,4},{4,0},{8,12},{12,8},{16,20},{20,16},{24,28},{28,24},{1,5},{5... | collective-permute-start | bytes 3158024 | tf_op jit(solution)/shard_map/ppermute | solution.py:84
  22.7 0.1 convert_reduce_fusion
  22.8 0.9 %compare_and_fusion = pred[128,640]{0,1:T(8,128)(4,1)} fusion(s32[128]{0:T(128)S(1)} %iota_add_fusion.1, s32[128]{0:T(128)S(1)} %convert_reduce_fusion.1, s32[640]{0:T(1024)S(1)} %iota_add_fusion, s32[640]{0:T(1024)S(1)} %compare_select_fusion), kind=kLoop, calls=%fused_computation.62 | loop fusion | flops 245760 | bytes 88064 | tf_op jit(solution)/shard_map/and | solution.py:107
  23.7 0.0 collective-permute-done.1
  23.7 0.0 collective-permute-done.2
  23.8 0.0 collective-permute-done.3
  23.9 0.8 %reshape_squeeze.7 = bf16[640,2,128]{2,1,0:T(2,128)(2,1)} reshape(bf16[5,1,128,256]{3,2,0,1:T(8,128)(2,1)S(1)} %get-tuple-element.24) | data formatting | bytes 655360 | tf_op jit(solution)/shard_map/reshape;squeeze | solution.py:110
  24.7 0.8 %reshape_squeeze.6 = bf16[640,2,128]{2,1,0:T(2,128)(2,1)} reshape(bf16[5,1,128,256]{3,2,0,1:T(8,128)(2,1)S(1)} %get-tuple-element.23) | data formatting | bytes 655360 | tf_op jit(solution)/shard_map/reshape;squeeze | solution.py:111
  25.5 0.0 collective-permute-done
  25.6 0.3 select_convert_fusion.1
  25.9 0.8 %pad_maximum_fusion = bf16[2064,128]{1,0:T(8,128)(2,1)} fusion(bf16[16,128]{1,0:T(8,128)(2,1)S(1)} %fusion.67, bf16[2048,128]{1,0:T(8,128)(2,1)S(1)} %bitcast.119), kind=kLoop, calls=%fused_computation.36 | loop fusion | flops 1056768 | bytes 1056768 | tf_op jit(solution)/shard_map/concatenate | solution.py:98
  26.7 0.1 copy.63
  26.8 1.3 %collective-permute-start.5 = (bf16[2064,128]{1,0:T(8,128)(2,1)}, bf16[2064,128]{1,0:T(8,128)(2,1)S(1)}, u32[]{:S(2)}, u32[]{:S(2)}) collective-permute-start(bf16[2064,128]{1,0:T(8,128)(2,1)} %pad_maximum_fusion), channel_id=1, source_target_pairs={{4,8},{12,16},{20,24},{0,20},{8,28},{5,9},{13,17},{21,25},{1,21},{... | collective-permute-start | bytes 1585160 | tf_op jit(solution)/shard_map/ppermute | solution.py:103
  28.2 5.2 %fusion.76 = (f32[2,8,128]{2,1,0:T(8,128)S(1)}, bf16[2,8,128,640]{2,3,1,0:T(8,128)(2,1)}) fusion(pred[128,640]{0,1:T(8,128)(4,1)} %compare_and_fusion, bf16[128,2,8,128]{3,2,1,0:T(8,128)(2,1)S(1)} %bitcast.123, bf16[640,2,128,1]{2,1,0,3:T(2,128)(2,1)} %bitcast.125), kind=kOutput, calls=%fused_computation.110 | convolution fusion | flops 681575040 | bytes 3563520 | tf_op jit(solution)/shard_map/sub | solution.py:116
  33.4 3.3 %fusion.20 = bf16[128,2,8,128]{0,3,2,1:T(8,128)(2,1)} fusion(bf16[2,8,128,640]{2,3,1,0:T(8,128)(2,1)} %get-tuple-element.30, f32[128,2,8]{0,2,1:T(8,128)S(1)} %bitcast.132, bf16[640,2,128,1]{2,1,0,3:T(2,128)(2,1)S(1)} %bitcast.124), kind=kOutput, calls=%fused_computation.21 | convolution fusion | flops 336068608 | bytes 3481600 | tf_op jit(solution)/shard_map/kgts,skd->tkgd/dot_general | solution.py:118
  36.7 3.6 %collective-permute-done.5 = bf16[2064,128]{1,0:T(8,128)(2,1)S(1)} collective-permute-done((bf16[2064,128]{1,0:T(8,128)(2,1)}, bf16[2064,128]{1,0:T(8,128)(2,1)S(1)}, u32[]{:S(2)}, u32[]{:S(2)}) %collective-permute-start.5) | collective-permute-done | bytes 528416 | tf_op jit(solution)/shard_map/ppermute | solution.py:103
  40.3 0.1 fusion.61
  40.4 1.7 %convolution_bitcast_fusion.1 = f32[128,16,128]{0,2,1:T(8,128)} fusion(bf16[128,16,128]{0,2,1:T(8,128)(2,1)S(1)} %bitcast.118, f32[16,128]{1,0:T(8,128)S(1)} %reduce_window_sum.19, pred[128,128]{1,0:T(8,128)(4,1)S(1)} %fusion.61, bf16[128,2048]{1,0:T(8,128)(2,1)S(1)} %copy-done.7, bf16[128,2048]{1,0:T(8,128)(2,1)S(1)} %copy-done), kind=kOutput, calls=%fused_computation.16 | convolution fusion | flops 135528448 | bytes 2646016 | tf_op jit(solution)/shard_map/hts,shd->thd/dot_general | solution.py:46
  42.1 0.2 collective-permute-done.6
  42.3 0.1 broadcast_select_fusion
  42.5 1.3 %slice_select_fusion = bf16[2048,128]{1,0:T(8,128)(2,1)S(1)} fusion(bf16[2064,128]{1,0:T(8,128)(2,1)} %collective-permute-done.6, bf16[2064,128]{1,0:T(8,128)(2,1)S(1)} %collective-permute-done.5, pred[]{:T(512)S(6)} %eq.61), kind=kLoop, calls=%fused_computation.43 | loop fusion | flops 262144 | bytes 1572865 | tf_op jit(solution)/shard_map/jit(_where)/select_n | solution.py:126
  43.8 0.1 copy-done.4
  43.8 0.7 %multiply_reduce_fusion = (f32[128]{0:T(128)S(1)}, f32[128,16,128]{0,2,1:T(8,128)S(1)}) fusion(f32[128,16,128]{0,2,1:T(8,128)S(1)} %copy-done.4, f32[128,16]{0,1:T(8,128)S(1)} %get-tuple-element.25, f32[16,128,128]{2,1,0:T(8,128)S(1)} %bitcast.114, bf16[16,128,128]{2,1,0:T(8,128)(2,1)S(1)} %bitcast.116, bf16[16,128,128]{2,1,0:T(8,128)(2,1)S(1)} %bitcast.115, ...), kind=kOutput, calls=%fused_computation.28 | convolution fusion | flops 70254464 | bytes 4727425 | tf_op jit(solution)/shard_map/thd,hde->the/dot_general | solution.py:140
  44.6 0.0 copy-start.11
  44.6 1.6 %collective-permute-start.7 = (f32[128]{0:T(128)S(1)}, f32[128]{0:T(128)S(1)}, u32[]{:S(2)}, u32[]{:S(2)}) collective-permute-start(f32[128]{0:T(128)S(1)} %get-tuple-element.31), channel_id=1, source_target_pairs={{0,1},{1,0},{2,3},{3,2},{4,5},{5,4},{6,7},{7,6},{8,9},{9,8},{10,11... | collective-permute-start | bytes 1544 | tf_op jit(solution)/shard_map/ppermute | solution.py:28
  46.2 2.0 %collective-permute-done.7 = f32[128]{0:T(128)S(1)} collective-permute-done((f32[128]{0:T(128)S(1)}, f32[128]{0:T(128)S(1)}, u32[]{:S(2)}, u32[]{:S(2)}) %collective-permute-start.7) | collective-permute-done | bytes 544 | tf_op jit(solution)/shard_map/ppermute | solution.py:28
  48.2 2.6 %collective-permute-start.8 = (f32[128]{0:T(128)S(1)}, f32[128]{0:T(128)S(1)}, u32[]{:S(2)}, u32[]{:S(2)}) collective-permute-start(f32[128]{0:T(128)S(1)} %add.93), channel_id=1, source_target_pairs={{0,2},{1,3},{2,0},{3,1},{4,6},{5,7},{6,4},{7,5},{8,10},{9,11},{10,... | collective-permute-start | bytes 1544 | tf_op jit(solution)/shard_map/ppermute | solution.py:28
  50.8 2.0 %copy.49 = bf16[128,2048]{1,0:T(8,128)(2,1)} copy(bf16[128,2048]{0,1:T(8,128)(2,1)} %bitcast.122) | data formatting | bytes 1048576
  52.8 0.3 copy.48
  53.2 1.1 %multiply_convert_fusion = bf16[128,2048]{1,0:T(8,128)(2,1)} fusion(bf16[128,2048]{1,0:T(8,128)(2,1)S(1)} %copy-done.5, f32[128,2048]{1,0:T(8,128)S(1)} %copy.48, f32[2048]{0:T(1024)S(1)} %copy-done.11, f32[128]{0:T(128)S(1)} %add_rsqrt_fusion), kind=kLoop, calls=%fused_computation.27 | loop fusion | flops 2097152 | bytes 2105856 | tf_op jit(solution)/shard_map/convert_element_type | solution.py:155
  (41 shorter events, 0.2 us)
Async XLA Ops:
  0.6 39.7 %copy-start = (bf16[128,2048]{1,0:T(8,128)(2,1)S(1)}, bf16[128,2048]{1,0:T(8,128)(2,1)}, u32[]{:S(2)}) copy-start(bf16[128,2048]{1,0:T(8,128)(2,1)} %param.11) | copy-start | bytes 1572868
  1.6 22.1 %collective-permute-start.1 = (bf16[2,128,256]{2,1,0:T(8,128)(2,1)S(1)}, bf16[2,128,256]{2,1,0:T(8,128)(2,1)S(1)}, u32[]{:S(2)}, u32[]{:S(2)}) collective-permute-start(bf16[2,128,256]{2,1,0:T(8,128)(2,1)S(1)} %pad_maximum_fusion.1), channel_id=1, source_target_pairs={{0,16},{4,20},{8,24},{12,28},{1,17},{5,21},{9,25},{13,29},{2,18},{... | collective-permute-start | bytes 393224 | tf_op jit(solution)/shard_map/ppermute | solution.py:13
  6.5 17.3 %collective-permute-start.2 = (bf16[2,128,256]{2,1,0:T(8,128)(2,1)S(1)}, bf16[2,128,256]{2,1,0:T(8,128)(2,1)S(1)}, u32[]{:S(2)}, u32[]{:S(2)}) collective-permute-start(bf16[2,128,256]{2,1,0:T(8,128)(2,1)S(1)} %pad_maximum_fusion.1), channel_id=1, source_target_pairs={{0,12},{4,16},{8,20},{12,24},{16,28},{1,13},{5,17},{9,21},{13,25},... | collective-permute-start | bytes 393224 | tf_op jit(solution)/shard_map/ppermute | solution.py:13
  9.0 14.7 %collective-permute-start.3 = (bf16[2,128,256]{2,1,0:T(8,128)(2,1)S(1)}, bf16[2,128,256]{2,1,0:T(8,128)(2,1)S(1)}, u32[]{:S(2)}, u32[]{:S(2)}) collective-permute-start(bf16[2,128,256]{2,1,0:T(8,128)(2,1)S(1)} %pad_maximum_fusion.1), channel_id=1, source_target_pairs={{0,8},{4,12},{8,16},{12,20},{16,24},{20,28},{1,9},{5,13},{9,17},{1... | collective-permute-start | bytes 393224 | tf_op jit(solution)/shard_map/ppermute | solution.py:13
  11.2 12.6 %collective-permute-start.4 = (bf16[2,128,256]{2,1,0:T(8,128)(2,1)S(1)}, bf16[2,128,256]{2,1,0:T(8,128)(2,1)S(1)}, u32[]{:S(2)}, u32[]{:S(2)}) collective-permute-start(bf16[2,128,256]{2,1,0:T(8,128)(2,1)S(1)} %pad_maximum_fusion.1), channel_id=1, source_target_pairs={{0,4},{4,8},{8,12},{12,16},{16,20},{20,24},{24,28},{1,5},{5,9},{9,... | collective-permute-start | bytes 393224 | tf_op jit(solution)/shard_map/ppermute | solution.py:13
  17.9 2.7 %copy-start.2 = (bf16[128,2048]{0,1:T(8,128)(2,1)}, bf16[128,2048]{0,1:T(8,128)(2,1)S(1)}, u32[]{:S(2)}) copy-start(bf16[128,2048]{0,1:T(8,128)(2,1)S(1)} %copy.60) | copy-start | bytes 1572868
  19.2 4.7 %copy-start.9 = (bf16[128,256]{1,0:T(8,128)(2,1)S(1)}, bf16[128,256]{1,0:T(8,128)(2,1)}, u32[]{:S(2)}) copy-start(bf16[128,256]{1,0:T(8,128)(2,1)} %param.18) | copy-start | bytes 196612
  19.2 4.7 %copy-start.10 = (bf16[128,256]{1,0:T(8,128)(2,1)S(1)}, bf16[128,256]{1,0:T(8,128)(2,1)}, u32[]{:S(2)}) copy-start(bf16[128,256]{1,0:T(8,128)(2,1)} %param.19) | copy-start | bytes 196612
  21.6 3.9 %collective-permute-start = (f32[2056,128]{1,0:T(8,128)}, f32[2056,128]{1,0:T(8,128)S(1)}, u32[]{:S(2)}, u32[]{:S(2)}) collective-permute-start(f32[2056,128]{1,0:T(8,128)} %select_maximum_fusion), channel_id=1, source_target_pairs={{0,4},{4,0},{8,12},{12,8},{16,20},{20,16},{24,28},{28,24},{1,5},{5... | collective-permute-start | bytes 3158024 | tf_op jit(solution)/shard_map/ppermute | solution.py:84
  24.7 2.0 %copy-start.6 = (bf16[128,2048]{1,0:T(8,128)(2,1)S(1)}, bf16[128,2048]{1,0:T(8,128)(2,1)}, u32[]{:S(2)}) copy-start(bf16[128,2048]{1,0:T(8,128)(2,1)} %param.17) | copy-start | bytes 1572868
  25.5 16.6 %copy-start.1 = (f32[2056,128]{1,0:T(8,128)}, f32[2056,128]{1,0:T(8,128)S(1)}, u32[]{:S(2)}) copy-start(f32[2056,128]{1,0:T(8,128)S(1)} %collective-permute-done) | copy-start | bytes 3158020
  26.8 13.5 %collective-permute-start.5 = (bf16[2064,128]{1,0:T(8,128)(2,1)}, bf16[2064,128]{1,0:T(8,128)(2,1)S(1)}, u32[]{:S(2)}, u32[]{:S(2)}) collective-permute-start(bf16[2064,128]{1,0:T(8,128)(2,1)} %pad_maximum_fusion), channel_id=1, source_target_pairs={{4,8},{12,16},{20,24},{0,20},{8,28},{5,9},{13,17},{21,25},{1,21},{... | collective-permute-start | bytes 1585160 | tf_op jit(solution)/shard_map/ppermute | solution.py:103
  28.2 5.2 %copy-start.8 = (bf16[640,2,128]{2,1,0:T(2,128)(2,1)S(1)}, bf16[640,2,128]{2,1,0:T(2,128)(2,1)}, u32[]{:S(2)}) copy-start(bf16[640,2,128]{2,1,0:T(2,128)(2,1)} %reshape_squeeze.6) | copy-start | bytes 983044
  33.4 7.0 %copy-start.3 = (bf16[128,2048]{0,1:T(8,128)(2,1)S(1)}, bf16[128,2048]{0,1:T(8,128)(2,1)}, u32[]{:S(2)}) copy-start(bf16[128,2048]{0,1:T(8,128)(2,1)} %copy-done.2) | copy-start | bytes 1572868
  33.4 7.0 %copy-start.7 = (bf16[128,2048]{1,0:T(8,128)(2,1)S(1)}, bf16[128,2048]{1,0:T(8,128)(2,1)}, u32[]{:S(2)}) copy-start(bf16[128,2048]{1,0:T(8,128)(2,1)} %param.13) | copy-start | bytes 1572868
  40.3 2.0 %collective-permute-start.6 = (bf16[2064,128]{1,0:T(8,128)(2,1)S(1)}, bf16[2064,128]{1,0:T(8,128)(2,1)}, u32[]{:S(2)}, u32[]{:S(2)}) collective-permute-start(bf16[2064,128]{1,0:T(8,128)(2,1)S(1)} %collective-permute-done.5), channel_id=1, source_target_pairs={{0,4},{4,0},{8,12},{12,8},{16,20},{20,16},{24,28},{28,24},{1,5},{5... | collective-permute-start | bytes 1585160 | tf_op jit(solution)/shard_map/ppermute | solution.py:124
  42.1 1.6 %slice-start = ((f32[2056,128]{1,0:T(8,128)}), f32[2048,128]{1,0:T(8,128)S(1)}, s32[]{:S(2)}) async-start(f32[2056,128]{1,0:T(8,128)} %copy-done.1), calls=%async_computation | async-start | bytes 2097152 | tf_op jit(solution)/shard_map/slice | solution.py:85
  42.1 1.7 %copy-start.4 = (f32[128,16,128]{0,2,1:T(8,128)S(1)}, f32[128,16,128]{0,2,1:T(8,128)}, u32[]{:S(2)}) copy-start(f32[128,16,128]{0,2,1:T(8,128)} %convolution_bitcast_fusion.1) | copy-start | bytes 3145732
  44.6 8.6 %copy-start.5 = (bf16[128,2048]{1,0:T(8,128)(2,1)S(1)}, bf16[128,2048]{1,0:T(8,128)(2,1)}, u32[]{:S(2)}) copy-start(bf16[128,2048]{1,0:T(8,128)(2,1)} %param.15) | copy-start | bytes 1572868
  44.6 8.6 %copy-start.11 = (f32[2048]{0:T(1024)S(1)}, f32[2048]{0:T(1024)}, u32[]{:S(2)}) copy-start(f32[2048]{0:T(1024)} %param.16) | copy-start | bytes 24580
  44.6 3.6 %collective-permute-start.7 = (f32[128]{0:T(128)S(1)}, f32[128]{0:T(128)S(1)}, u32[]{:S(2)}, u32[]{:S(2)}) collective-permute-start(f32[128]{0:T(128)S(1)} %get-tuple-element.31), channel_id=1, source_target_pairs={{0,1},{1,0},{2,3},{3,2},{4,5},{5,4},{6,7},{7,6},{8,9},{9,8},{10,11... | collective-permute-start | bytes 1544 | tf_op jit(solution)/shard_map/ppermute | solution.py:28
  48.2 5.0 %collective-permute-start.8 = (f32[128]{0:T(128)S(1)}, f32[128]{0:T(128)S(1)}, u32[]{:S(2)}, u32[]{:S(2)}) collective-permute-start(f32[128]{0:T(128)S(1)} %add.93), channel_id=1, source_target_pairs={{0,2},{1,3},{2,0},{3,1},{4,6},{5,7},{6,4},{7,5},{8,10},{9,11},{10,... | collective-permute-start | bytes 1544 | tf_op jit(solution)/shard_map/ppermute | solution.py:28

commit v23 on v22

--- a/solution.py
+++ b/solution.py
@@ -76,14 +76,17 @@
     kv_width = soft_k.shape[1]
     n_state = heads_here * DH
     state_rows = state.reshape(n_state, DH)
-    factor_rows = jnp.pad(shrinkage_multiplier[None, :], ((0, 7), (0, DH - heads_here)))
+    decay_mate = lax.ppermute(log_decay, "ctx", [(i, i ^ 1) for i in range(count)])
+    mate_start = (shard ^ 1) * rows
+    mate_last = jnp.sum((ends <= mate_start + rows - 1).astype(jnp.int32))
+    mate_before = jnp.where(mate_start > 0, jnp.sum((ends <= mate_start - 1).astype(jnp.int32)), -1)
+    factor_mate = jnp.exp(jnp.cumsum(decay_mate, axis=1)[:, -1]) * (mate_last == mate_before).astype(
+        jnp.float32
+    )
     window = jnp.concatenate(
         [from_behind(pair, "ctx", step) for step in range(SPAN, 0, -1)] + [pair], axis=0
     )
-    first = jnp.concatenate([state_rows, factor_rows], axis=0)
-    got = lax.ppermute(first, "ctx", [(i, i ^ 1) for i in range(count)])
-    state_mate = got[:n_state]
-    factor_mate = got[n_state, :heads_here]
+    state_mate = lax.ppermute(state_rows, "ctx", [(i, i ^ 1) for i in range(count)])
     state_cube = state_rows.reshape(state.shape)
     mate_cube = state_mate.reshape(state.shape)
     chip_state = jnp.where(

time: 54.8 us -> 66 us (1.20)
  local copies, waits for them, and re-layouts: 5.66 us -> 13.1 us
  matrix products: 12.3 us -> 13.6 us
  between operations: 2.32 us -> 3.55 us
  waiting for transfers between devices: 5.8 us -> 4.64 us
  other arithmetic: 10.2 us -> 11.3 us
  starting transfers between devices: 18.1 us -> 18.9 us
    unnamed x32 -> x38, local copies, waits for them, and re-layouts: 2.37 us -> 8.83 us
    ppermute x4, starting transfers between devices: 11.4 us -> 12.8 us  [from_behind(): return lax.ppermute(shard, axis, pairs)]
    mul x1 -> x2, other arithmetic: 0.01 us -> 1.24 us  [block_terms(): jnp.exp(level[:, -1]) * (last == before).astype(jnp.float32)]
    select_n x1, other arithmetic: 1.28 us -> 0.07 us  [local(): far = jnp.where(odd, received, mate_packet)]
    slice x1, other arithmetic: 0.19 us -> 1.32 us  [local(): jnp.cumsum(decay_mate, axis=1)[:, -1]]
    concatenate x1 -> x0, other arithmetic: 1.06 us -> none  [local(): first = jnp.concatenate([state_rows, factor_rows], axis=0)]
    dot_general x1, matrix products: 1.71 us -> 2.75 us  [block_terms(): jnp.einsum('hts,shd->thd', weights, values, preferred_element_type=jnp.fl...]
    another operation x1, local copies, waits for them, and re-layouts: 0.8 us -> 1.78 us  [local(): all_keys = paired[:, 0].reshape(span_rows, kv_here, DH)]
  transfers between devices with their start and end apart: 9 -> 10, of which waited for: 3 -> 2; matrix products, arithmetic and copies ran while one was open for 42% -> 48% of each run, Pallas kernels for 0% -> 0%
where the time goes in v23:
time: 66 us; the launch traced here: 65.1 us
  starting transfers between devices  18.9 us (29%)
  matrix products  13.6 us (21%)
  local copies, waits for them, and re-layouts  13.1 us (20%)
  other arithmetic  11.3 us (17%)
  waiting for transfers between devices  4.64 us (7%)
  between operations  3.55 us (5%)
    ppermute x4, starting transfers between devices, from_behind(): return lax.ppermute(shard, axis, pairs)  12.8 us
    unnamed x38, local copies, waits for them, and re-layouts  8.83 us
    sub x1, matrix products, local(): expd = jnp.where(allowed, jnp.exp(jnp.minimum(scores - top, 0.0)), 0.0)  5.6 us
    ppermute x2, starting transfers between devices, all_sum(): x = x + lax.ppermute(x, axis, [(i, i ^ bit) for i in range(count)])  4.24 us
    dot_general x1, matrix products, local(): jnp.einsum('kgts,skd->tkgd', expd.astype(jnp.bfloat16), all_values, prefe...  3.18 us
    dot_general x1, matrix products, block_terms(): jnp.einsum('hts,shd->thd', weights, values, preferred_element_type=jnp.fl...  2.75 us
    ppermute x1, waiting for transfers between devices, local(): received = lax.ppermute(packet, 'ctx', routes)  2.66 us
    ppermute x2, waiting for transfers between devices, all_sum(): x = x + lax.ppermute(x, axis, [(i, i ^ bit) for i in range(count)])  1.96 us
  transfers between devices with their start and end apart: 10, of which 2 were waited for; matrix products, arithmetic and copies ran while one was open for 48% of the time, Pallas kernels for 0%

profile of v23, /device:TPU:0, one launch (start us, length us, event | category | flops | bytes accessed | tf_op | source)
XLA Modules:
  0.0 65.1 jit_solution(9347292303949685860)
XLA Ops:
  0.7 0.9 %pad_maximum_fusion.1 = bf16[2,128,256]{2,1,0:T(8,128)(2,1)S(1)} fusion(bf16[1,128,256]{2,1,0:T(8,128)(2,1)} %bitcast.133, bf16[1,128,256]{2,1,0:T(8,128)(2,1)} %bitcast.132), kind=kLoop, calls=%fused_computation.63 | loop fusion | flops 65536 | bytes 262144 | tf_op jit(solution)/shard_map/stack | solution.py:75
  1.6 5.5 %collective-permute-start.1 = (bf16[2,128,256]{2,1,0:T(8,128)(2,1)S(1)}, bf16[2,128,256]{2,1,0:T(8,128)(2,1)}, u32[]{:S(2)}, u32[]{:S(2)}) collective-permute-start(bf16[2,128,256]{2,1,0:T(8,128)(2,1)S(1)} %pad_maximum_fusion.1), channel_id=1, source_target_pairs={{0,16},{4,20},{8,24},{12,28},{1,17},{5,21},{9,25},{13,29},{2,18},{... | collective-permute-start | bytes 393224 | tf_op jit(solution)/shard_map/ppermute | solution.py:13
  7.1 3.2 %collective-permute-start.2 = (bf16[2,128,256]{2,1,0:T(8,128)(2,1)S(1)}, bf16[2,128,256]{2,1,0:T(8,128)(2,1)}, u32[]{:S(2)}, u32[]{:S(2)}) collective-permute-start(bf16[2,128,256]{2,1,0:T(8,128)(2,1)S(1)} %pad_maximum_fusion.1), channel_id=1, source_target_pairs={{0,12},{4,16},{8,20},{12,24},{16,28},{1,13},{5,17},{9,21},{13,25},... | collective-permute-start | bytes 393224 | tf_op jit(solution)/shard_map/ppermute | solution.py:13
  10.3 2.8 %collective-permute-start.3 = (bf16[2,128,256]{2,1,0:T(8,128)(2,1)S(1)}, bf16[2,128,256]{2,1,0:T(8,128)(2,1)}, u32[]{:S(2)}, u32[]{:S(2)}) collective-permute-start(bf16[2,128,256]{2,1,0:T(8,128)(2,1)S(1)} %pad_maximum_fusion.1), channel_id=1, source_target_pairs={{0,8},{4,12},{8,16},{12,20},{16,24},{20,28},{1,9},{5,13},{9,17},{1... | collective-permute-start | bytes 393224 | tf_op jit(solution)/shard_map/ppermute | solution.py:13
  13.1 1.3 %collective-permute-start.4 = (bf16[2,128,256]{2,1,0:T(8,128)(2,1)S(1)}, bf16[2,128,256]{2,1,0:T(8,128)(2,1)S(1)}, u32[]{:S(2)}, u32[]{:S(2)}) collective-permute-start(bf16[2,128,256]{2,1,0:T(8,128)(2,1)S(1)} %pad_maximum_fusion.1), channel_id=1, source_target_pairs={{0,4},{4,8},{8,12},{12,16},{16,20},{20,24},{24,28},{1,5},{5,9},{9,... | collective-permute-start | bytes 393224 | tf_op jit(solution)/shard_map/ppermute | solution.py:13
  14.4 0.2 collective-permute-start
  14.6 0.8 %reduce-window.8 = s32[6,1]{0,1:T(1,128)S(1)} reduce-window(s32[6,1]{0,1:T(1,128)} %bitcast.136, s32[]{:T(128)} %constant.46.clone.1), window={size=6x1 pad=5_0x0_0}, to_apply=%region_0.0 | reduce-window | flops 30 | bytes 52 | tf_op jit(solution)/shard_map/reduce-window.3
  15.4 0.7 %fusion.71 = (s32[]{:T(128)}, s32[]{:T(128)}, s32[]{:T(128)}, s32[]{:T(128)}) fusion(s32[]{:T(128)S(6)} %sub.63, s32[6,1]{0,1:T(1,128)S(1)} %reduce-window.8, s32[]{:T(128)S(6)} %sub.59, s32[]{:T(128)S(6)} %sub.60, s32[]{:T(128)S(6)} %sub.62), kind=kLoop, calls=%fused_computation.97 | loop fusion | flops 68 | bytes 56 | tf_op jit(solution)/shard_map/reduce_sum | solution.py:66
  16.8 0.1 convert_reduce_fusion.1
  17.5 0.6 compare_convert_fusion
  18.2 1.0 %reduce_window_sum.21 = f32[16,128]{1,0:T(8,128)S(1)} reduce-window(f32[16,128]{1,0:T(8,128)} %param.14, f32[]{:T(128)} %constant.50.clone.1), window={size=1x128 pad=0_0x127_0}, to_apply=%region_2.3 | reduce-window | flops 260096 | bytes 16388 | tf_op jit(solution)/shard_map/jit(cumsum)/reduce_window_sum | solution.py:40
  19.1 1.3 %copy.60 = bf16[128,2048]{0,1:T(8,128)(2,1)S(1)} copy(bf16[128,2048]{1,0:T(8,128)(2,1)} %param.12) | data formatting | bytes 1048576 | tf_op jit(solution)/shard_map/reshape | solution.py:68
  20.5 0.1 convert_reduce_fusion
  20.6 0.9 %compare_and_fusion = pred[128,640]{0,1:T(8,128)(4,1)} fusion(s32[128]{0:T(128)S(1)} %iota_add_fusion.1, s32[128]{0:T(128)S(1)} %convert_reduce_fusion.1, s32[640]{0:T(1024)S(1)} %iota_add_fusion, s32[640]{0:T(1024)S(1)} %compare_select_fusion), kind=kLoop, calls=%fused_computation.60 | loop fusion | flops 245760 | bytes 88064 | tf_op jit(solution)/shard_map/and | solution.py:110
  21.4 0.7 %multiply_reduce_fusion.1 = (f32[16]{0:T(128)}, f32[16]{0:T(128)S(1)}) fusion(f32[16,128]{1,0:T(8,128)S(1)} %reduce_window_sum.21, f32[]{:T(128)S(6)} %convert_element_type.141), kind=kLoop, calls=%fused_computation.79 | loop fusion | flops 16 | bytes 196 | tf_op jit(solution)/shard_map/mul | solution.py:52
  22.1 0.1 multiply_bitcast_fusion
  22.2 1.3 %fusion.30 = f32[16,128,128]{2,1,0:T(8,128)S(1)} fusion(bf16[128,16,128]{0,2,1:T(8,128)(2,1)S(1)} %bitcast.123, f32[128,16]{0,1:T(8,128)S(1)} %get-tuple-element.27, bf16[128,2048]{1,0:T(8,128)(2,1)} %param.13), kind=kOutput, calls=%fused_computation.36 | convolution fusion | flops 67895296 | bytes 2105344 | tf_op jit(solution)/shard_map/shd,she->hde/dot_general | solution.py:51
  23.6 0.5 exponential_multiply_fusion
  25.4 0.6 copy-done.11
  26.0 0.4 collective-permute-start.5
  26.4 1.3 %slice.27 = f32[16]{0:T(128)} reduce(f32[16,128]{1,0:T(8,128)} %copy-done.11, f32[]{:T(128)} %constant.50.clone.1), dimensions={1}, to_apply=%region_3.4 | reduce | flops 2032 | bytes 8260 | tf_op jit(solution)/shard_map/slice | solution.py:83
  27.7 0.7 %fusion.77 = (bf16[1,16]{1,0:T(2,128)(2,1)S(1)}, f32[16]{0:T(128)S(1)}) fusion(f32[16]{0:T(128)} %get-tuple-element.16, f32[]{:T(128)S(6)} %convert_element_type.137, f32[16]{0:T(128)} %slice.27), kind=kLoop, calls=%fused_computation.111 | loop fusion | flops 48 | bytes 228 | tf_op jit(solution)/shard_map/convert_element_type | solution.py:98
  28.4 0.6 subtract_convert_fusion
  29.0 0.6 fusion.67
  29.6 0.9 %constant_dynamic-update-slice_fusion.5 = bf16[10,128,256]{2,1,0:T(8,128)(2,1)S(1)} fusion(bf16[2,128,256]{2,1,0:T(8,128)(2,1)} %collective-permute-done.1), kind=kLoop, calls=%fused_computation.72 | loop fusion | bytes 262144
  30.5 0.9 %constant_dynamic-update-slice_fusion.4 = bf16[10,128,256]{2,1,0:T(8,128)(2,1)S(1)} fusion(bf16[10,128,256]{2,1,0:T(8,128)(2,1)S(1)} %constant_dynamic-update-slice_fusion.5, bf16[2,128,256]{2,1,0:T(8,128)(2,1)} %collective-permute-done.2), kind=kLoop, calls=%fused_computation.71 | loop fusion | bytes 262144
  31.5 0.9 %constant_dynamic-update-slice_fusion.3 = bf16[10,128,256]{2,1,0:T(8,128)(2,1)S(1)} fusion(bf16[10,128,256]{2,1,0:T(8,128)(2,1)S(1)} %constant_dynamic-update-slice_fusion.4, bf16[2,128,256]{2,1,0:T(8,128)(2,1)} %collective-permute-done.3), kind=kLoop, calls=%fused_computation.70 | loop fusion | bytes 262144
  32.5 0.8 %slice_bitcast_fusion.1 = (bf16[5,1,128,256]{3,2,0,1:T(8,128)(2,1)S(1)}, bf16[5,1,128,256]{3,2,0,1:T(8,128)(2,1)}) fusion(bf16[5,2,128,256]{3,2,1,0:T(8,128)(2,1)S(1)} %bitcast.126), kind=kLoop, calls=%fused_computation.58 | loop fusion | bytes 1310720
  33.3 1.8 %reshape_squeeze.7 = bf16[640,2,128]{2,1,0:T(2,128)(2,1)} reshape(bf16[5,1,128,256]{3,2,0,1:T(8,128)(2,1)} %get-tuple-element.25) | data formatting | bytes 655360 | tf_op jit(solution)/shard_map/reshape;squeeze | solution.py:113
  35.0 0.8 %reshape_squeeze.6 = bf16[640,2,128]{2,1,0:T(2,128)(2,1)} reshape(bf16[5,1,128,256]{3,2,0,1:T(8,128)(2,1)S(1)} %get-tuple-element.24) | data formatting | bytes 655360 | tf_op jit(solution)/shard_map/reshape;squeeze | solution.py:114
  35.9 0.3 select_convert_fusion.1
  36.2 0.7 %copy-done.3 = bf16[128,2048]{1,0:T(8,128)(2,1)S(1)} copy-done((bf16[128,2048]{1,0:T(8,128)(2,1)S(1)}, bf16[128,2048]{1,0:T(8,128)(2,1)}, u32[]{:S(2)}) %copy-start.3) | copy-done | bytes 524312
  36.9 0.9 %copy.63 = bf16[16,8,16,128]{3,2,1,0:T(8,128)(2,1)} copy(bf16[16,8,16,128]{3,1,2,0:T(8,128)(2,1)S(1)} %bitcast.127) | data formatting | bytes 1048576
  37.8 1.3 %collective-permute-start.6 = (bf16[2064,128]{1,0:T(8,128)(2,1)S(1)}, bf16[2064,128]{1,0:T(8,128)(2,1)S(1)}, u32[]{:S(2)}, u32[]{:S(2)}) collective-permute-start(bf16[2064,128]{1,0:T(8,128)(2,1)S(1)} %pad_maximum_fusion), channel_id=1, source_target_pairs={{4,8},{12,16},{20,24},{0,20},{8,28},{5,9},{13,17},{21,25},{1,21},{... | collective-permute-start | bytes 1585160 | tf_op jit(solution)/shard_map/ppermute | solution.py:106
  39.1 5.6 %fusion.78 = (f32[2,8,128]{2,1,0:T(8,128)S(1)}, bf16[2,8,128,640]{2,3,1,0:T(8,128)(2,1)}) fusion(pred[128,640]{0,1:T(8,128)(4,1)} %compare_and_fusion, bf16[128,2,8,128]{3,2,1,0:T(8,128)(2,1)} %bitcast.129, bf16[640,2,128,1]{2,1,0,3:T(2,128)(2,1)} %bitcast.131), kind=kOutput, calls=%fused_computation.112 | convolution fusion | flops 681575040 | bytes 3563520 | tf_op jit(solution)/shard_map/sub | solution.py:119
  44.7 3.2 %fusion.20 = bf16[128,2,8,128]{0,3,2,1:T(8,128)(2,1)} fusion(bf16[2,8,128,640]{2,3,1,0:T(8,128)(2,1)} %get-tuple-element.31, f32[128,2,8]{0,2,1:T(8,128)S(1)} %bitcast.137, bf16[640,2,128,1]{2,1,0,3:T(2,128)(2,1)S(1)} %bitcast.130), kind=kOutput, calls=%fused_computation.21 | convolution fusion | flops 336068608 | bytes 3481600 | tf_op jit(solution)/shard_map/kgts,skd->tkgd/dot_general | solution.py:121
  47.9 2.7 %collective-permute-done.6 = bf16[2064,128]{1,0:T(8,128)(2,1)S(1)} collective-permute-done((bf16[2064,128]{1,0:T(8,128)(2,1)S(1)}, bf16[2064,128]{1,0:T(8,128)(2,1)S(1)}, u32[]{:S(2)}, u32[]{:S(2)}) %collective-permute-start.6) | collective-permute-done | bytes 528416 | tf_op jit(solution)/shard_map/ppermute | solution.py:106
  50.6 0.1 fusion.61
  50.7 2.8 %convolution_bitcast_fusion.1 = f32[128,16,128]{0,2,1:T(8,128)} fusion(bf16[128,16,128]{0,2,1:T(8,128)(2,1)S(1)} %bitcast.124, f32[16,128]{1,0:T(8,128)S(1)} %reduce_window_sum.21, pred[128,128]{1,0:T(8,128)(4,1)S(1)} %fusion.61, bf16[128,2048]{1,0:T(8,128)(2,1)} %param.13, bf16[128,2048]{1,0:T(8,128)(2,1)S(1)} %copy-done), kind=kOutput, calls=%fused_computation.16 | convolution fusion | flops 135528448 | bytes 2646016 | tf_op jit(solution)/shard_map/hts,shd->thd/dot_general | solution.py:46
  53.5 0.1 slice_select_fusion
  53.6 1.0 %copy-done.1 = f32[128,16,128]{0,2,1:T(8,128)S(1)} copy-done((f32[128,16,128]{0,2,1:T(8,128)S(1)}, f32[128,16,128]{0,2,1:T(8,128)}, u32[]{:S(2)}) %copy-start.1) | copy-done | bytes 1048600
  54.7 0.7 %multiply_reduce_fusion = (f32[128]{0:T(128)S(1)}, f32[128,16,128]{0,2,1:T(8,128)S(1)}) fusion(f32[128,16,128]{0,2,1:T(8,128)S(1)} %copy-done.1, f32[128,16]{0,1:T(8,128)S(1)} %get-tuple-element.26, f32[16,128,128]{2,1,0:T(8,128)S(1)} %bitcast.119, bf16[16,128,128]{2,1,0:T(8,128)(2,1)S(1)} %bitcast.122, bf16[16,128,128]{2,1,0:T(8,128)(2,1)S(1)} %bitcast.121, ...), kind=kOutput, calls=%fused_computation.26 | convolution fusion | flops 70254464 | bytes 4727425 | tf_op jit(solution)/shard_map/thd,hde->the/dot_general | solution.py:143
  55.4 1.6 %collective-permute-start.8 = (f32[128]{0:T(128)S(1)}, f32[128]{0:T(128)S(1)}, u32[]{:S(2)}, u32[]{:S(2)}) collective-permute-start(f32[128]{0:T(128)S(1)} %get-tuple-element.32), channel_id=1, source_target_pairs={{0,1},{1,0},{2,3},{3,2},{4,5},{5,4},{6,7},{7,6},{8,9},{9,8},{10,11... | collective-permute-start | bytes 1544 | tf_op jit(solution)/shard_map/ppermute | solution.py:28
  57.1 2.0 %collective-permute-done.8 = f32[128]{0:T(128)S(1)} collective-permute-done((f32[128]{0:T(128)S(1)}, f32[128]{0:T(128)S(1)}, u32[]{:S(2)}, u32[]{:S(2)}) %collective-permute-start.8) | collective-permute-done | bytes 544 | tf_op jit(solution)/shard_map/ppermute | solution.py:28
  59.0 2.6 %collective-permute-start.9 = (f32[128]{0:T(128)S(1)}, f32[128]{0:T(128)S(1)}, u32[]{:S(2)}, u32[]{:S(2)}) collective-permute-start(f32[128]{0:T(128)S(1)} %add.96), channel_id=1, source_target_pairs={{0,2},{1,3},{2,0},{3,1},{4,6},{5,7},{6,4},{7,5},{8,10},{9,11},{10,... | collective-permute-start | bytes 1544 | tf_op jit(solution)/shard_map/ppermute | solution.py:28
  61.6 2.0 %copy.49 = bf16[128,2048]{1,0:T(8,128)(2,1)} copy(bf16[128,2048]{0,1:T(8,128)(2,1)} %bitcast.128) | data formatting | bytes 1048576
  63.7 0.3 copy.48
  64.0 1.1 %multiply_convert_fusion = bf16[128,2048]{1,0:T(8,128)(2,1)} fusion(bf16[128,2048]{1,0:T(8,128)(2,1)S(1)} %copy-done.2, f32[128,2048]{1,0:T(8,128)S(1)} %copy.48, f32[2048]{0:T(1024)S(1)} %copy-done.8, f32[128]{0:T(128)S(1)} %add_rsqrt_fusion), kind=kLoop, calls=%fused_computation.25 | loop fusion | flops 2097152 | bytes 2105856 | tf_op jit(solution)/shard_map/convert_element_type | solution.py:158
  (48 shorter events, 0.3 us)
Async XLA Ops:
  0.6 50.0 %copy-start = (bf16[128,2048]{1,0:T(8,128)(2,1)S(1)}, bf16[128,2048]{1,0:T(8,128)(2,1)}, u32[]{:S(2)}) copy-start(bf16[128,2048]{1,0:T(8,128)(2,1)} %param.11) | copy-start | bytes 1572868
  0.6 31.8 %copy-start.5 = (bf16[128,256]{1,0:T(8,128)(2,1)S(1)}, bf16[128,256]{1,0:T(8,128)(2,1)}, u32[]{:S(2)}) copy-start(bf16[128,256]{1,0:T(8,128)(2,1)} %param.18) | copy-start | bytes 196612
  0.7 31.8 %copy-start.6 = (bf16[128,256]{1,0:T(8,128)(2,1)S(1)}, bf16[128,256]{1,0:T(8,128)(2,1)}, u32[]{:S(2)}) copy-start(bf16[128,256]{1,0:T(8,128)(2,1)} %param.19) | copy-start | bytes 196612
  1.6 28.0 %collective-permute-start.1 = (bf16[2,128,256]{2,1,0:T(8,128)(2,1)S(1)}, bf16[2,128,256]{2,1,0:T(8,128)(2,1)}, u32[]{:S(2)}, u32[]{:S(2)}) collective-permute-start(bf16[2,128,256]{2,1,0:T(8,128)(2,1)S(1)} %pad_maximum_fusion.1), channel_id=1, source_target_pairs={{0,16},{4,20},{8,24},{12,28},{1,17},{5,21},{9,25},{13,29},{2,18},{... | collective-permute-start | bytes 393224 | tf_op jit(solution)/shard_map/ppermute | solution.py:13
  7.1 23.4 %collective-permute-start.2 = (bf16[2,128,256]{2,1,0:T(8,128)(2,1)S(1)}, bf16[2,128,256]{2,1,0:T(8,128)(2,1)}, u32[]{:S(2)}, u32[]{:S(2)}) collective-permute-start(bf16[2,128,256]{2,1,0:T(8,128)(2,1)S(1)} %pad_maximum_fusion.1), channel_id=1, source_target_pairs={{0,12},{4,16},{8,20},{12,24},{16,28},{1,13},{5,17},{9,21},{13,25},... | collective-permute-start | bytes 393224 | tf_op jit(solution)/shard_map/ppermute | solution.py:13
  10.3 21.1 %collective-permute-start.3 = (bf16[2,128,256]{2,1,0:T(8,128)(2,1)S(1)}, bf16[2,128,256]{2,1,0:T(8,128)(2,1)}, u32[]{:S(2)}, u32[]{:S(2)}) collective-permute-start(bf16[2,128,256]{2,1,0:T(8,128)(2,1)S(1)} %pad_maximum_fusion.1), channel_id=1, source_target_pairs={{0,8},{4,12},{8,16},{12,20},{16,24},{20,28},{1,9},{5,13},{9,17},{1... | collective-permute-start | bytes 393224 | tf_op jit(solution)/shard_map/ppermute | solution.py:13
  13.1 19.3 %collective-permute-start.4 = (bf16[2,128,256]{2,1,0:T(8,128)(2,1)S(1)}, bf16[2,128,256]{2,1,0:T(8,128)(2,1)S(1)}, u32[]{:S(2)}, u32[]{:S(2)}) collective-permute-start(bf16[2,128,256]{2,1,0:T(8,128)(2,1)S(1)} %pad_maximum_fusion.1), channel_id=1, source_target_pairs={{0,4},{4,8},{8,12},{12,16},{16,20},{20,24},{24,28},{1,5},{5,9},{9,... | collective-permute-start | bytes 393224 | tf_op jit(solution)/shard_map/ppermute | solution.py:13
  14.4 10.9 %collective-permute-start = (f32[16,128]{1,0:T(8,128)}, f32[16,128]{1,0:T(8,128)S(1)}, u32[]{:S(2)}, u32[]{:S(2)}) collective-permute-start(f32[16,128]{1,0:T(8,128)} %param.14), channel_id=1, source_target_pairs={{0,4},{4,0},{8,12},{12,8},{16,20},{20,16},{24,28},{28,24},{1,5},{5... | collective-permute-start | bytes 24584 | tf_op jit(solution)/shard_map/ppermute | solution.py:79
  16.9 8.5 %copy-start.9 = (s32[128]{0:T(128)}, s32[128]{0:T(128)S(1)}, u32[]{:S(2)}) copy-start(s32[128]{0:T(128)S(1)} %convert_reduce_fusion.1) | copy-start | bytes 1540
  25.4 0.6 copy-start.11
  26.0 9.9 %collective-permute-start.5 = (f32[2048,128]{1,0:T(8,128)S(1)}, f32[2048,128]{1,0:T(8,128)S(1)}, u32[]{:S(2)}, u32[]{:S(2)}) collective-permute-start(f32[2048,128]{1,0:T(8,128)S(1)} %bitcast.118), channel_id=1, source_target_pairs={{0,4},{4,0},{8,12},{12,8},{16,20},{20,16},{24,28},{28,24},{1,5},{5... | collective-permute-start | bytes 3145736 | tf_op jit(solution)/shard_map/ppermute | solution.py:89
  28.4 4.1 %copy-start.12 = (f32[16]{0:T(128)}, f32[16]{0:T(128)S(1)}, u32[]{:S(2)}) copy-start(f32[16]{0:T(128)S(1)} %get-tuple-element.23) | copy-start | bytes 196
  32.4 3.4 %copy-start.14 = (f32[16]{0:T(128)S(1)}, f32[16]{0:T(128)}, u32[]{:S(2)}) copy-start(f32[16]{0:T(128)} %exponential_multiply_fusion) | copy-start | bytes 196
  32.5 3.4 %copy-start.13 = (f32[16]{0:T(128)S(1)}, f32[16]{0:T(128)}, u32[]{:S(2)}) copy-start(f32[16]{0:T(128)} %copy-done.12) | copy-start | bytes 196
  32.5 3.7 %copy-start.7 = (bf16[16,128]{1,0:T(8,128)(2,1)S(1)}, bf16[16,128]{1,0:T(8,128)(2,1)}, u32[]{:S(2)}) copy-start(bf16[16,128]{1,0:T(8,128)(2,1)} %fusion.67) | copy-start | bytes 12292
  35.8 1.0 %copy-start.3 = (bf16[128,2048]{1,0:T(8,128)(2,1)S(1)}, bf16[128,2048]{1,0:T(8,128)(2,1)}, u32[]{:S(2)}) copy-start(bf16[128,2048]{1,0:T(8,128)(2,1)} %param.17) | copy-start | bytes 1572868
  37.8 12.8 %collective-permute-start.6 = (bf16[2064,128]{1,0:T(8,128)(2,1)S(1)}, bf16[2064,128]{1,0:T(8,128)(2,1)S(1)}, u32[]{:S(2)}, u32[]{:S(2)}) collective-permute-start(bf16[2064,128]{1,0:T(8,128)(2,1)S(1)} %pad_maximum_fusion), channel_id=1, source_target_pairs={{4,8},{12,16},{20,24},{0,20},{8,28},{5,9},{13,17},{21,25},{1,21},{... | collective-permute-start | bytes 1585160 | tf_op jit(solution)/shard_map/ppermute | solution.py:106
  39.1 5.6 %copy-start.4 = (bf16[640,2,128]{2,1,0:T(2,128)(2,1)S(1)}, bf16[640,2,128]{2,1,0:T(2,128)(2,1)}, u32[]{:S(2)}) copy-start(bf16[640,2,128]{2,1,0:T(2,128)(2,1)} %reshape_squeeze.6) | copy-start | bytes 983044
  44.7 5.9 %copy-start.10 = (s32[128]{0:T(128)S(1)}, s32[128]{0:T(128)}, u32[]{:S(2)}) copy-start(s32[128]{0:T(128)} %copy-done.9) | copy-start | bytes 1540
  50.6 2.9 %collective-permute-start.7 = (bf16[2064,128]{1,0:T(8,128)(2,1)S(1)}, bf16[2064,128]{1,0:T(8,128)(2,1)S(1)}, u32[]{:S(2)}, u32[]{:S(2)}) collective-permute-start(bf16[2064,128]{1,0:T(8,128)(2,1)S(1)} %collective-permute-done.6), channel_id=1, source_target_pairs={{0,4},{4,0},{8,12},{12,8},{16,20},{20,16},{24,28},{28,24},{1,5},{5... | collective-permute-start | bytes 1585160 | tf_op jit(solution)/shard_map/ppermute | solution.py:127
  53.4 1.2 %copy-start.1 = (f32[128,16,128]{0,2,1:T(8,128)S(1)}, f32[128,16,128]{0,2,1:T(8,128)}, u32[]{:S(2)}) copy-start(f32[128,16,128]{0,2,1:T(8,128)} %convolution_bitcast_fusion.1) | copy-start | bytes 3145732
  55.4 8.6 %copy-start.2 = (bf16[128,2048]{1,0:T(8,128)(2,1)S(1)}, bf16[128,2048]{1,0:T(8,128)(2,1)}, u32[]{:S(2)}) copy-start(bf16[128,2048]{1,0:T(8,128)(2,1)} %param.15) | copy-start | bytes 1572868
  55.4 8.6 %copy-start.8 = (f32[2048]{0:T(1024)S(1)}, f32[2048]{0:T(1024)}, u32[]{:S(2)}) copy-start(f32[2048]{0:T(1024)} %param.16) | copy-start | bytes 24580
  55.4 3.6 %collective-permute-start.8 = (f32[128]{0:T(128)S(1)}, f32[128]{0:T(128)S(1)}, u32[]{:S(2)}, u32[]{:S(2)}) collective-permute-start(f32[128]{0:T(128)S(1)} %get-tuple-element.32), channel_id=1, source_target_pairs={{0,1},{1,0},{2,3},{3,2},{4,5},{5,4},{6,7},{7,6},{8,9},{9,8},{10,11... | collective-permute-start | bytes 1544 | tf_op jit(solution)/shard_map/ppermute | solution.py:28
  59.0 5.0 %collective-permute-start.9 = (f32[128]{0:T(128)S(1)}, f32[128]{0:T(128)S(1)}, u32[]{:S(2)}, u32[]{:S(2)}) collective-permute-start(f32[128]{0:T(128)S(1)} %add.96), channel_id=1, source_target_pairs={{0,2},{1,3},{2,0},{3,1},{4,6},{5,7},{6,4},{7,5},{8,10},{9,11},{10,... | collective-permute-start | bytes 1544 | tf_op jit(solution)/shard_map/ppermute | solution.py:28

commit v24 on v21

--- a/solution.py
+++ b/solution.py
@@ -15,19 +15,13 @@
 
 def all_sum(x, axis):
     count = lax.axis_size(axis)
-    if count & (count - 1):
-        me = lax.axis_index(axis)
-        parts = [x]
-        for by in range(1, count):
-            parts.append(lax.ppermute(x, axis, [(i, (i + by) % count) for i in range(count)]))
-        stacked = jnp.stack(parts)
-        order = (me - jnp.arange(count)) % count
-        return jnp.sum(stacked[order], axis=0)
-    bit = 1
-    while bit < count:
-        x = x + lax.ppermute(x, axis, [(i, i ^ bit) for i in range(count)])
-        bit *= 2
-    return x
+    me = lax.axis_index(axis)
+    parts = [x]
+    for by in range(1, count):
+        parts.append(lax.ppermute(x, axis, [(i, (i + by) % count) for i in range(count)]))
+    stacked = jnp.stack(parts)
+    order = (me - jnp.arange(count)) % count
+    return jnp.sum(stacked[order], axis=0)
 
 
 def document_of(positions, doc_lengths):
@@ -74,7 +68,7 @@
     )
     count = lax.axis_size("ctx")
     odd = (shard % 2) == 1
-    pair = jnp.concatenate([soft_k, soft_v], axis=0)
+    pair = jnp.stack([soft_k, soft_v])
     kv_width = soft_k.shape[1]
     n_state = heads_here * DH
     state_rows = state.reshape(n_state, DH)

time: 55.4 us -> 54.7 us (0.987)
  waiting for transfers between devices: 5.82 us -> 3.83 us
  starting transfers between devices: 18 us -> 19.4 us
  local copies, waits for them, and re-layouts: 7.42 us -> 6.27 us
  other arithmetic: 8.19 us -> 9.2 us
    ppermute x2 -> x3, waiting for transfers between devices: 1.96 us -> 0.01 us  [all_sum(): lax.ppermute(x, axis, [(i, (i + by) % count) for i in range(count)])]
    ppermute x2 -> x3, starting transfers between devices: 4.23 us -> 5.58 us  [all_sum(): lax.ppermute(x, axis, [(i, (i + by) % count) for i in range(count)])]
    another operation x1 -> x3, other arithmetic: 0.83 us -> 1.79 us  [the longest x1 0.94 us: local(): pair = jnp.stack([soft_k, soft_v])]
    unnamed x33 -> x32, local copies, waits for them, and re-layouts: 3.26 us -> 2.39 us
    concatenate x1 -> x0, local copies, waits for them, and re-layouts: 0.84 us -> none  [local(): pair = jnp.concatenate([soft_k, soft_v], axis=0)]
    gather x0 -> x1, local copies, waits for them, and re-layouts: none -> 0.56 us  [all_sum(): return jnp.sum(stacked[order], axis=0)]
  transfers between devices with their start and end apart: 9 -> 10, of which waited for: 3 -> 2; matrix products, arithmetic and copies ran while one was open for 41% -> 41% of each run, Pallas kernels for 0% -> 0%
where the time goes in v24:
time: 54.7 us; the launch traced here: 54.2 us
  starting transfers between devices  19.4 us (35%)
  matrix products  13.1 us (24%)
  other arithmetic  9.2 us (17%)
  local copies, waits for them, and re-layouts  6.27 us (11%)
  waiting for transfers between devices  3.83 us (7%)
  between operations  2.33 us (4%)
    ppermute x4, starting transfers between devices, from_behind(): return lax.ppermute(shard, axis, pairs)  11.4 us
    ppermute x3, starting transfers between devices, all_sum(): lax.ppermute(x, axis, [(i, (i + by) % count) for i in range(count)])  5.58 us
    sub x1, matrix products, local(): expd = jnp.where(allowed, jnp.exp(jnp.minimum(scores - top, 0.0)), 0.0)  5.2 us
    ppermute x1, waiting for transfers between devices, local(): received = lax.ppermute(packet, 'ctx', routes)  3.62 us
    dot_general x1, matrix products, local(): jnp.einsum('kgts,skd->tkgd', expd.astype(jnp.bfloat16), all_values, prefe...  3.27 us
    unnamed x32, local copies, waits for them, and re-layouts  2.39 us
    dot_general x1, matrix products, block_terms(): jnp.einsum('hts,shd->thd', weights, values, preferred_element_type=jnp.fl...  1.72 us
    dot_general x1, matrix products, block_terms(): jnp.einsum('shd,she->hde', weighted, values, preferred_element_type=jnp.f...  1.38 us
  transfers between devices with their start and end apart: 10, of which 2 were waited for; matrix products, arithmetic and copies ran while one was open for 41% of the time, Pallas kernels for 0%

profile of v24, /device:TPU:0, one launch (start us, length us, event | category | flops | bytes accessed | tf_op | source)
XLA Modules:
  0.0 54.2 jit_solution(7638782483897816153)
XLA Ops:
  0.6 0.0 copy-start
  0.6 0.9 %pad_maximum_fusion.1 = bf16[2,128,256]{2,1,0:T(8,128)(2,1)S(1)} fusion(bf16[1,128,256]{2,1,0:T(8,128)(2,1)} %bitcast.131, bf16[1,128,256]{2,1,0:T(8,128)(2,1)} %bitcast.130), kind=kLoop, calls=%fused_computation.66 | loop fusion | flops 65536 | bytes 262144 | tf_op jit(solution)/shard_map/stack | solution.py:71
  1.6 4.9 %collective-permute-start.1 = (bf16[2,128,256]{2,1,0:T(8,128)(2,1)S(1)}, bf16[2,128,256]{2,1,0:T(8,128)(2,1)S(1)}, u32[]{:S(2)}, u32[]{:S(2)}) collective-permute-start(bf16[2,128,256]{2,1,0:T(8,128)(2,1)S(1)} %pad_maximum_fusion.1), channel_id=1, source_target_pairs={{0,16},{4,20},{8,24},{12,28},{1,17},{5,21},{9,25},{13,29},{2,18},{... | collective-permute-start | bytes 393224 | tf_op jit(solution)/shard_map/ppermute | solution.py:13
  6.5 2.6 %collective-permute-start.2 = (bf16[2,128,256]{2,1,0:T(8,128)(2,1)S(1)}, bf16[2,128,256]{2,1,0:T(8,128)(2,1)S(1)}, u32[]{:S(2)}, u32[]{:S(2)}) collective-permute-start(bf16[2,128,256]{2,1,0:T(8,128)(2,1)S(1)} %pad_maximum_fusion.1), channel_id=1, source_target_pairs={{0,12},{4,16},{8,20},{12,24},{16,28},{1,13},{5,17},{9,21},{13,25},... | collective-permute-start | bytes 393224 | tf_op jit(solution)/shard_map/ppermute | solution.py:13
  9.0 2.1 %collective-permute-start.3 = (bf16[2,128,256]{2,1,0:T(8,128)(2,1)S(1)}, bf16[2,128,256]{2,1,0:T(8,128)(2,1)S(1)}, u32[]{:S(2)}, u32[]{:S(2)}) collective-permute-start(bf16[2,128,256]{2,1,0:T(8,128)(2,1)S(1)} %pad_maximum_fusion.1), channel_id=1, source_target_pairs={{0,8},{4,12},{8,16},{12,20},{16,24},{20,28},{1,9},{5,13},{9,17},{1... | collective-permute-start | bytes 393224 | tf_op jit(solution)/shard_map/ppermute | solution.py:13
  11.2 1.8 %collective-permute-start.4 = (bf16[2,128,256]{2,1,0:T(8,128)(2,1)S(1)}, bf16[2,128,256]{2,1,0:T(8,128)(2,1)S(1)}, u32[]{:S(2)}, u32[]{:S(2)}) collective-permute-start(bf16[2,128,256]{2,1,0:T(8,128)(2,1)S(1)} %pad_maximum_fusion.1), channel_id=1, source_target_pairs={{0,4},{4,8},{8,12},{12,16},{16,20},{20,24},{24,28},{1,5},{5,9},{9,... | collective-permute-start | bytes 393224 | tf_op jit(solution)/shard_map/ppermute | solution.py:13
  13.0 0.8 %reduce-window.8 = s32[6,1]{0,1:T(1,128)S(1)} reduce-window(s32[6,1]{0,1:T(1,128)} %bitcast.141, s32[]{:T(128)} %constant.56.clone.1), window={size=6x1 pad=5_0x0_0}, to_apply=%region_0.0 | reduce-window | flops 30 | bytes 52 | tf_op jit(solution)/shard_map/reduce-window.3
  13.9 0.6 %fusion.70 = (s32[]{:T(128)}, s32[]{:T(128)}) fusion(s32[]{:T(128)S(6)} %sub.65, s32[6,1]{0,1:T(1,128)S(1)} %reduce-window.8, s32[]{:T(128)S(6)} %sub.64), kind=kLoop, calls=%fused_computation.104 | loop fusion | flops 34 | bytes 40 | tf_op jit(solution)/shard_map/reduce_sum | solution.py:62
  15.2 0.1 convert_reduce_fusion.1
  15.9 0.7 %compare_convert_fusion = (f32[128]{0:T(128)S(1)}, f32[128]{0:T(128)S(1)}) fusion(s32[128]{0:T(128)S(1)} %convert_reduce_fusion.1, s32[]{:T(128)S(6)} %select_n.80, s32[]{:T(128)} %get-tuple-element.19), kind=kLoop, calls=%fused_computation.99 | loop fusion | flops 512 | bytes 1544 | tf_op jit(solution)/shard_map/convert_element_type | solution.py:139
  16.6 0.8 %fusion.62 = f32[128,16]{0,1:T(8,128)S(1)} fusion(f32[16,128]{1,0:T(8,128)} %param.14), kind=kOutput, calls=%fused_computation.70 | convolution fusion | flops 3162112 | bytes 16384 | tf_op jit(solution)/shard_map/dot_general | solution.py:36
  17.4 1.3 %copy.60 = bf16[128,2048]{0,1:T(8,128)(2,1)S(1)} copy(bf16[128,2048]{1,0:T(8,128)(2,1)} %param.12) | data formatting | bytes 1048576 | tf_op jit(solution)/shard_map/reshape | solution.py:64
  18.7 0.0 copy-start.2
  18.7 0.2 slice_reduce_fusion
  18.9 0.1 exponential_multiply_fusion
  19.0 0.0 copy-start.10
  19.0 1.4 %fusion.30 = f32[16,128,128]{2,1,0:T(8,128)S(1)} fusion(bf16[128,16,128]{0,2,1:T(8,128)(2,1)S(1)} %bitcast.121, f32[128,16]{0,1:T(8,128)S(1)} %get-tuple-element.26, bf16[128,2048]{1,0:T(8,128)(2,1)} %param.13), kind=kOutput, calls=%fused_computation.39 | convolution fusion | flops 67895296 | bytes 2105344 | tf_op jit(solution)/shard_map/shd,she->hde/dot_general | solution.py:47
  20.4 1.1 %select_maximum_fusion = f32[2056,128]{1,0:T(8,128)} fusion(f32[1,16]{1,0:T(1,128)S(1)} %bitcast.134, f32[2048,128]{1,0:T(8,128)S(1)} %bitcast.116), kind=kLoop, calls=%fused_computation.24 | loop fusion | flops 789504 | bytes 2101312 | tf_op jit(solution)/shard_map/concatenate | solution.py:79
  21.5 1.1 %collective-permute-start = (f32[2056,128]{1,0:T(8,128)}, f32[2056,128]{1,0:T(8,128)S(1)}, u32[]{:S(2)}, u32[]{:S(2)}) collective-permute-start(f32[2056,128]{1,0:T(8,128)} %select_maximum_fusion), channel_id=1, source_target_pairs={{0,4},{4,0},{8,12},{12,8},{16,20},{20,16},{24,28},{28,24},{1,5},{5... | collective-permute-start | bytes 3158024 | tf_op jit(solution)/shard_map/ppermute | solution.py:80
  22.6 0.1 convert_reduce_fusion
  22.7 0.9 %compare_and_fusion = pred[128,640]{0,1:T(8,128)(4,1)} fusion(s32[128]{0:T(128)S(1)} %iota_add_fusion.1, s32[128]{0:T(128)S(1)} %convert_reduce_fusion.1, s32[640]{0:T(1024)S(1)} %iota_add_fusion, s32[640]{0:T(1024)S(1)} %compare_select_fusion), kind=kLoop, calls=%fused_computation.63 | loop fusion | flops 245760 | bytes 88064 | tf_op jit(solution)/shard_map/and | solution.py:103
  23.6 0.0 collective-permute-done.1
  23.6 0.0 collective-permute-done.2
  23.6 0.0 collective-permute-done.3
  23.8 0.8 %reshape_squeeze.7 = bf16[640,2,128]{2,1,0:T(2,128)(2,1)} reshape(bf16[5,1,128,256]{3,2,0,1:T(8,128)(2,1)S(1)} %get-tuple-element.24) | data formatting | bytes 655360 | tf_op jit(solution)/shard_map/reshape;squeeze | solution.py:106
  24.6 0.8 %reshape_squeeze.6 = bf16[640,2,128]{2,1,0:T(2,128)(2,1)} reshape(bf16[5,1,128,256]{3,2,0,1:T(8,128)(2,1)S(1)} %get-tuple-element.23) | data formatting | bytes 655360 | tf_op jit(solution)/shard_map/reshape;squeeze | solution.py:107
  25.4 0.3 select_convert_fusion.1
  25.7 0.8 %pad_maximum_fusion = bf16[2064,128]{1,0:T(8,128)(2,1)} fusion(bf16[16,128]{1,0:T(8,128)(2,1)S(1)} %fusion.68, bf16[2048,128]{1,0:T(8,128)(2,1)S(1)} %bitcast.123), kind=kLoop, calls=%fused_computation.37 | loop fusion | flops 1056768 | bytes 1056768 | tf_op jit(solution)/shard_map/concatenate | solution.py:94
  26.6 0.1 copy.63
  26.7 1.3 %collective-permute-start.5 = (bf16[2064,128]{1,0:T(8,128)(2,1)}, bf16[2064,128]{1,0:T(8,128)(2,1)S(1)}, u32[]{:S(2)}, u32[]{:S(2)}) collective-permute-start(bf16[2064,128]{1,0:T(8,128)(2,1)} %pad_maximum_fusion), channel_id=1, source_target_pairs={{4,8},{12,16},{20,24},{0,20},{8,28},{5,9},{13,17},{21,25},{1,21},{... | collective-permute-start | bytes 1585160 | tf_op jit(solution)/shard_map/ppermute | solution.py:99
  28.0 5.2 %fusion.79 = (f32[2,8,128]{2,1,0:T(8,128)S(1)}, bf16[2,8,128,640]{2,3,1,0:T(8,128)(2,1)}) fusion(pred[128,640]{0,1:T(8,128)(4,1)} %compare_and_fusion, bf16[128,2,8,128]{3,2,1,0:T(8,128)(2,1)S(1)} %bitcast.127, bf16[640,2,128,1]{2,1,0,3:T(2,128)(2,1)} %bitcast.129), kind=kOutput, calls=%fused_computation.121 | convolution fusion | flops 681575040 | bytes 3563520 | tf_op jit(solution)/shard_map/sub | solution.py:112
  33.2 3.3 %fusion.20 = bf16[128,2,8,128]{0,3,2,1:T(8,128)(2,1)} fusion(bf16[2,8,128,640]{2,3,1,0:T(8,128)(2,1)} %get-tuple-element.30, f32[128,2,8]{0,2,1:T(8,128)S(1)} %bitcast.142, bf16[640,2,128,1]{2,1,0,3:T(2,128)(2,1)S(1)} %bitcast.128), kind=kOutput, calls=%fused_computation.22 | convolution fusion | flops 336068608 | bytes 3481600 | tf_op jit(solution)/shard_map/kgts,skd->tkgd/dot_general | solution.py:114
  36.5 3.6 %collective-permute-done.5 = bf16[2064,128]{1,0:T(8,128)(2,1)S(1)} collective-permute-done((bf16[2064,128]{1,0:T(8,128)(2,1)}, bf16[2064,128]{1,0:T(8,128)(2,1)S(1)}, u32[]{:S(2)}, u32[]{:S(2)}) %collective-permute-start.5) | collective-permute-done | bytes 528416 | tf_op jit(solution)/shard_map/ppermute | solution.py:99
  40.1 0.1 fusion.61
  40.3 1.7 %convolution_bitcast_fusion.1 = f32[128,16,128]{0,2,1:T(8,128)} fusion(bf16[128,16,128]{0,2,1:T(8,128)(2,1)S(1)} %bitcast.122, f32[16,128]{1,0:T(8,128)S(1)} %bitcast.133, pred[128,128]{1,0:T(8,128)(4,1)S(1)} %fusion.61, bf16[128,2048]{1,0:T(8,128)(2,1)S(1)} %copy-done.7, bf16[128,2048]{1,0:T(8,128)(2,1)S(1)} %copy-done), kind=kOutput, calls=%fused_computation.17 | convolution fusion | flops 135528448 | bytes 2646016 | tf_op jit(solution)/shard_map/hts,shd->thd/dot_general | solution.py:42
  42.0 0.2 collective-permute-done.6
  42.2 0.1 broadcast_select_fusion
  42.3 1.3 %slice_select_fusion = bf16[2048,128]{1,0:T(8,128)(2,1)S(1)} fusion(bf16[2064,128]{1,0:T(8,128)(2,1)} %collective-permute-done.6, bf16[2064,128]{1,0:T(8,128)(2,1)S(1)} %collective-permute-done.5, pred[]{:T(512)S(6)} %eq.63), kind=kLoop, calls=%fused_computation.44 | loop fusion | flops 262144 | bytes 1572865 | tf_op jit(solution)/shard_map/jit(_where)/select_n | solution.py:122
  43.6 0.1 copy-done.4
  43.7 0.7 %multiply_reduce_fusion = (f32[128]{0:T(128)S(1)}, f32[128,16,128]{0,2,1:T(8,128)S(1)}) fusion(f32[128,16,128]{0,2,1:T(8,128)S(1)} %copy-done.4, f32[128,16]{0,1:T(8,128)S(1)} %get-tuple-element.25, f32[16,128,128]{2,1,0:T(8,128)S(1)} %bitcast.118, bf16[16,128,128]{2,1,0:T(8,128)(2,1)S(1)} %bitcast.120, bf16[16,128,128]{2,1,0:T(8,128)(2,1)S(1)} %bitcast.119, ...), kind=kOutput, calls=%fused_computation.29 | convolution fusion | flops 70254464 | bytes 4727425 | tf_op jit(solution)/shard_map/thd,hde->the/dot_general | solution.py:136
  44.4 0.0 copy-start.11
  44.4 1.6 %collective-permute-start.7 = (f32[128]{0:T(128)S(1)}, f32[128]{0:T(128)S(1)}, u32[]{:S(2)}, u32[]{:S(2)}) collective-permute-start(f32[128]{0:T(128)S(1)} %get-tuple-element.31), channel_id=1, source_target_pairs={{0,1},{1,2},{2,3},{3,0},{4,5},{5,6},{6,7},{7,4},{8,9},{9,10},{10,1... | collective-permute-start | bytes 1544 | tf_op jit(solution)/shard_map/ppermute | solution.py:21
  46.1 2.6 %collective-permute-start.8 = (f32[128]{0:T(128)S(1)}, f32[128]{0:T(128)S(1)}, u32[]{:S(2)}, u32[]{:S(2)}) collective-permute-start(f32[128]{0:T(128)S(1)} %get-tuple-element.31), channel_id=1, source_target_pairs={{0,2},{1,3},{2,0},{3,1},{4,6},{5,7},{6,4},{7,5},{8,10},{9,11},{10,... | collective-permute-start | bytes 1544 | tf_op jit(solution)/shard_map/ppermute | solution.py:21
  48.7 1.4 %collective-permute-start.9 = (f32[128]{0:T(128)S(1)}, f32[128]{0:T(128)S(1)}, u32[]{:S(2)}, u32[]{:S(2)}) collective-permute-start(f32[128]{0:T(128)S(1)} %get-tuple-element.31), channel_id=1, source_target_pairs={{0,3},{1,0},{2,1},{3,2},{4,7},{5,4},{6,5},{7,6},{8,11},{9,8},{10,9... | collective-permute-start | bytes 1544 | tf_op jit(solution)/shard_map/ppermute | solution.py:21
  50.0 2.0 %copy.49 = bf16[128,2048]{1,0:T(8,128)(2,1)} copy(bf16[128,2048]{0,1:T(8,128)(2,1)} %bitcast.126) | data formatting | bytes 1048576
  52.1 0.3 copy.48
  52.4 0.6 %gather_fusion = f32[4,128]{1,0:T(4,128)S(1)} fusion(f32[4,128]{1,0:T(4,128)S(1)} %pad_maximum_fusion.2, s32[1024]{0:T(1024)S(1)} %pad_clamp_fusion), kind=kCustom, calls=%fused_computation | custom fusion | bytes 4112 | tf_op jit(solution)/shard_map/gather | solution.py:24
  53.1 1.1 %multiply_convert_fusion = bf16[128,2048]{1,0:T(8,128)(2,1)} fusion(bf16[128,2048]{1,0:T(8,128)(2,1)S(1)} %copy-done.5, f32[128,2048]{1,0:T(8,128)S(1)} %copy.48, f32[2048]{0:T(1024)S(1)} %copy-done.11, f32[128]{0:T(128)S(1)} %add_rsqrt_fusion), kind=kLoop, calls=%fused_computation.28 | loop fusion | flops 2097152 | bytes 2105856 | tf_op jit(solution)/shard_map/convert_element_type | solution.py:151
  (47 shorter events, 0.3 us)
Async XLA Ops:
  0.6 39.6 %copy-start = (bf16[128,2048]{1,0:T(8,128)(2,1)S(1)}, bf16[128,2048]{1,0:T(8,128)(2,1)}, u32[]{:S(2)}) copy-start(bf16[128,2048]{1,0:T(8,128)(2,1)} %param.11) | copy-start | bytes 1572868
  1.6 22.0 %collective-permute-start.1 = (bf16[2,128,256]{2,1,0:T(8,128)(2,1)S(1)}, bf16[2,128,256]{2,1,0:T(8,128)(2,1)S(1)}, u32[]{:S(2)}, u32[]{:S(2)}) collective-permute-start(bf16[2,128,256]{2,1,0:T(8,128)(2,1)S(1)} %pad_maximum_fusion.1), channel_id=1, source_target_pairs={{0,16},{4,20},{8,24},{12,28},{1,17},{5,21},{9,25},{13,29},{2,18},{... | collective-permute-start | bytes 393224 | tf_op jit(solution)/shard_map/ppermute | solution.py:13
  6.5 17.1 %collective-permute-start.2 = (bf16[2,128,256]{2,1,0:T(8,128)(2,1)S(1)}, bf16[2,128,256]{2,1,0:T(8,128)(2,1)S(1)}, u32[]{:S(2)}, u32[]{:S(2)}) collective-permute-start(bf16[2,128,256]{2,1,0:T(8,128)(2,1)S(1)} %pad_maximum_fusion.1), channel_id=1, source_target_pairs={{0,12},{4,16},{8,20},{12,24},{16,28},{1,13},{5,17},{9,21},{13,25},... | collective-permute-start | bytes 393224 | tf_op jit(solution)/shard_map/ppermute | solution.py:13
  9.0 14.6 %collective-permute-start.3 = (bf16[2,128,256]{2,1,0:T(8,128)(2,1)S(1)}, bf16[2,128,256]{2,1,0:T(8,128)(2,1)S(1)}, u32[]{:S(2)}, u32[]{:S(2)}) collective-permute-start(bf16[2,128,256]{2,1,0:T(8,128)(2,1)S(1)} %pad_maximum_fusion.1), channel_id=1, source_target_pairs={{0,8},{4,12},{8,16},{12,20},{16,24},{20,28},{1,9},{5,13},{9,17},{1... | collective-permute-start | bytes 393224 | tf_op jit(solution)/shard_map/ppermute | solution.py:13
  11.2 12.5 %collective-permute-start.4 = (bf16[2,128,256]{2,1,0:T(8,128)(2,1)S(1)}, bf16[2,128,256]{2,1,0:T(8,128)(2,1)S(1)}, u32[]{:S(2)}, u32[]{:S(2)}) collective-permute-start(bf16[2,128,256]{2,1,0:T(8,128)(2,1)S(1)} %pad_maximum_fusion.1), channel_id=1, source_target_pairs={{0,4},{4,8},{8,12},{12,16},{16,20},{20,24},{24,28},{1,5},{5,9},{9,... | collective-permute-start | bytes 393224 | tf_op jit(solution)/shard_map/ppermute | solution.py:13
  18.7 1.7 %copy-start.2 = (bf16[128,2048]{0,1:T(8,128)(2,1)}, bf16[128,2048]{0,1:T(8,128)(2,1)S(1)}, u32[]{:S(2)}) copy-start(bf16[128,2048]{0,1:T(8,128)(2,1)S(1)} %copy.60) | copy-start | bytes 1572868
  19.0 4.7 %copy-start.9 = (bf16[128,256]{1,0:T(8,128)(2,1)S(1)}, bf16[128,256]{1,0:T(8,128)(2,1)}, u32[]{:S(2)}) copy-start(bf16[128,256]{1,0:T(8,128)(2,1)} %param.18) | copy-start | bytes 196612
  19.0 4.7 %copy-start.10 = (bf16[128,256]{1,0:T(8,128)(2,1)S(1)}, bf16[128,256]{1,0:T(8,128)(2,1)}, u32[]{:S(2)}) copy-start(bf16[128,256]{1,0:T(8,128)(2,1)} %param.19) | copy-start | bytes 196612
  21.5 3.9 %collective-permute-start = (f32[2056,128]{1,0:T(8,128)}, f32[2056,128]{1,0:T(8,128)S(1)}, u32[]{:S(2)}, u32[]{:S(2)}) collective-permute-start(f32[2056,128]{1,0:T(8,128)} %select_maximum_fusion), channel_id=1, source_target_pairs={{0,4},{4,0},{8,12},{12,8},{16,20},{20,16},{24,28},{28,24},{1,5},{5... | collective-permute-start | bytes 3158024 | tf_op jit(solution)/shard_map/ppermute | solution.py:80
  24.6 2.0 %copy-start.6 = (bf16[128,2048]{1,0:T(8,128)(2,1)S(1)}, bf16[128,2048]{1,0:T(8,128)(2,1)}, u32[]{:S(2)}) copy-start(bf16[128,2048]{1,0:T(8,128)(2,1)} %param.17) | copy-start | bytes 1572868
  25.4 16.6 %copy-start.1 = (f32[2056,128]{1,0:T(8,128)}, f32[2056,128]{1,0:T(8,128)S(1)}, u32[]{:S(2)}) copy-start(f32[2056,128]{1,0:T(8,128)S(1)} %collective-permute-done) | copy-start | bytes 3158020
  26.7 13.4 %collective-permute-start.5 = (bf16[2064,128]{1,0:T(8,128)(2,1)}, bf16[2064,128]{1,0:T(8,128)(2,1)S(1)}, u32[]{:S(2)}, u32[]{:S(2)}) collective-permute-start(bf16[2064,128]{1,0:T(8,128)(2,1)} %pad_maximum_fusion), channel_id=1, source_target_pairs={{4,8},{12,16},{20,24},{0,20},{8,28},{5,9},{13,17},{21,25},{1,21},{... | collective-permute-start | bytes 1585160 | tf_op jit(solution)/shard_map/ppermute | solution.py:99
  28.0 5.2 %copy-start.8 = (bf16[640,2,128]{2,1,0:T(2,128)(2,1)S(1)}, bf16[640,2,128]{2,1,0:T(2,128)(2,1)}, u32[]{:S(2)}) copy-start(bf16[640,2,128]{2,1,0:T(2,128)(2,1)} %reshape_squeeze.6) | copy-start | bytes 983044
  33.2 7.0 %copy-start.3 = (bf16[128,2048]{0,1:T(8,128)(2,1)S(1)}, bf16[128,2048]{0,1:T(8,128)(2,1)}, u32[]{:S(2)}) copy-start(bf16[128,2048]{0,1:T(8,128)(2,1)} %copy-done.2) | copy-start | bytes 1572868
  33.2 7.0 %copy-start.7 = (bf16[128,2048]{1,0:T(8,128)(2,1)S(1)}, bf16[128,2048]{1,0:T(8,128)(2,1)}, u32[]{:S(2)}) copy-start(bf16[128,2048]{1,0:T(8,128)(2,1)} %param.13) | copy-start | bytes 1572868
  40.1 2.0 %collective-permute-start.6 = (bf16[2064,128]{1,0:T(8,128)(2,1)S(1)}, bf16[2064,128]{1,0:T(8,128)(2,1)}, u32[]{:S(2)}, u32[]{:S(2)}) collective-permute-start(bf16[2064,128]{1,0:T(8,128)(2,1)S(1)} %collective-permute-done.5), channel_id=1, source_target_pairs={{0,4},{4,0},{8,12},{12,8},{16,20},{20,16},{24,28},{28,24},{1,5},{5... | collective-permute-start | bytes 1585160 | tf_op jit(solution)/shard_map/ppermute | solution.py:120
  42.0 1.6 %slice-start = ((f32[2056,128]{1,0:T(8,128)}), f32[2048,128]{1,0:T(8,128)S(1)}, s32[]{:S(2)}) async-start(f32[2056,128]{1,0:T(8,128)} %copy-done.1), calls=%async_computation | async-start | bytes 2097152 | tf_op jit(solution)/shard_map/slice | solution.py:81
  42.0 1.7 %copy-start.4 = (f32[128,16,128]{0,2,1:T(8,128)S(1)}, f32[128,16,128]{0,2,1:T(8,128)}, u32[]{:S(2)}) copy-start(f32[128,16,128]{0,2,1:T(8,128)} %convolution_bitcast_fusion.1) | copy-start | bytes 3145732
  44.4 8.6 %copy-start.5 = (bf16[128,2048]{1,0:T(8,128)(2,1)S(1)}, bf16[128,2048]{1,0:T(8,128)(2,1)}, u32[]{:S(2)}) copy-start(bf16[128,2048]{1,0:T(8,128)(2,1)} %param.15) | copy-start | bytes 1572868
  44.4 8.6 %copy-start.11 = (f32[2048]{0:T(1024)S(1)}, f32[2048]{0:T(1024)}, u32[]{:S(2)}) copy-start(f32[2048]{0:T(1024)} %param.16) | copy-start | bytes 24580
  44.4 8.0 %collective-permute-start.7 = (f32[128]{0:T(128)S(1)}, f32[128]{0:T(128)S(1)}, u32[]{:S(2)}, u32[]{:S(2)}) collective-permute-start(f32[128]{0:T(128)S(1)} %get-tuple-element.31), channel_id=1, source_target_pairs={{0,1},{1,2},{2,3},{3,0},{4,5},{5,6},{6,7},{7,4},{8,9},{9,10},{10,1... | collective-permute-start | bytes 1544 | tf_op jit(solution)/shard_map/ppermute | solution.py:21
  46.1 6.3 %collective-permute-start.8 = (f32[128]{0:T(128)S(1)}, f32[128]{0:T(128)S(1)}, u32[]{:S(2)}, u32[]{:S(2)}) collective-permute-start(f32[128]{0:T(128)S(1)} %get-tuple-element.31), channel_id=1, source_target_pairs={{0,2},{1,3},{2,0},{3,1},{4,6},{5,7},{6,4},{7,5},{8,10},{9,11},{10,... | collective-permute-start | bytes 1544 | tf_op jit(solution)/shard_map/ppermute | solution.py:21
  48.7 3.8 %collective-permute-start.9 = (f32[128]{0:T(128)S(1)}, f32[128]{0:T(128)S(1)}, u32[]{:S(2)}, u32[]{:S(2)}) collective-permute-start(f32[128]{0:T(128)S(1)} %get-tuple-element.31), channel_id=1, source_target_pairs={{0,3},{1,0},{2,1},{3,2},{4,7},{5,4},{6,5},{7,6},{8,11},{9,8},{10,9... | collective-permute-start | bytes 1544 | tf_op jit(solution)/shard_map/ppermute | solution.py:21
